TPU v7x, 32 devices: a whole 2x2x4 slice. The times are simulated.
32 devices in a mesh: grp: 2 (over core), lat: 4 (over z), lon: 4 (over y, x).
Axes of the slice: x: 2, y: 2, z: 4, core: 2. Of those that a mesh axis runs over, the one named last changes fastest.
Arguments:
- state: float32 [2, 3, 8, 128, 1024], P('grp', None, None, 'lat', 'lon'), may hold values from -6 to 6
- surface: float32 [2, 3, 128, 1024], P('grp', None, 'lat', 'lon'), may hold values from -6 to 6
- sea_mask: int32 [2, 128, 1024], P('grp', 'lat', 'lon'), may hold values 0 or 1
- coeffs: float32 [2, 4, 8], P('grp'), may hold values from 0.05 to 0.2
- remap_weights: float32 [2, 8, 256, 256], P('grp'), may hold values from -0.1875 to 0.1875
- link_dest: int32 [2, 2048, 1], P('grp', ('lat', 'lon')), may hold values from 0 to 15; in each aligned block of 128 rows (0 to 127, 128 to 255, ..., all dimensions but the last counted through in order) at most 16 rows name the same one
- link_src_row: int32 [2, 2048], P('grp', ('lat', 'lon')), may hold values from 0 to 31
- link_dst_row: int32 [2, 2048], P('grp', ('lat', 'lon')), may hold values from 0 to 31
- link_tile: int32 [2, 2048], P('grp', ('lat', 'lon')), may hold values from 0 to 7
Outputs:
- new_state: float32 [2, 3, 8, 128, 1024], P('grp', None, None, 'lat', 'lon')
- new_surface: float32 [2, 3, 128, 1024], P('grp', None, 'lat', 'lon')
Inputs may be any that keep to these rules, and one draw needn't show every extreme that they name: `link_dest`: at most 16 of the 128 links held by one device name the same destination owner, and some device has that many for some owner.
All inputs are finite; a program needn't handle non-finite values. No bound on the sum of `sea_mask` on one device may be relied on, other than what follows from the above.
Results may differ from a plain program's by a relative error of at most 0.0001.
Values sent between devices are 32-bit elements; how exact they have to be, the bound alone decides.
No kernel may reach another device: no remote copies, remote signals or barrier semaphores. Data moves between devices by JAX's collectives and lax.ppermute only.
A program may use at most 64 MiB of HBM per device.

v0:
```python
import jax
import jax.numpy as jnp
from jax import lax
from jax.sharding import PartitionSpec as P

SUBSTEPS = 2


air_gain = 0.3
ocean_gain = 0.5
drag_coeff = 0.5
heat_coeff = 0.5
gust_speed = 0.5
coriolis_scale = 0.25


def with_halo(cells, sides, width, closed):
    for axis, dim in sides:
        count = lax.axis_size(axis)
        ends = count if closed else count - 1
        head = lax.slice_in_dim(cells, 0, width, axis=dim)
        tail = lax.slice_in_dim(cells, cells.shape[dim] - width, cells.shape[dim], axis=dim)
        cells = jnp.concatenate(
            [
                lax.ppermute(tail, axis, [(i, (i + 1) % count) for i in range(ends)]),
                cells,
                lax.ppermute(head, axis, [((i + 1) % count, i) for i in range(ends)]),
            ],
            axis=dim,
        )
    return cells


def swapped(block, axis, distance):
    count = lax.axis_size(axis)
    route = []
    for low in range(count):
        high = low | 1 << distance
        if high != low and high < count:
            route += [(low, high), (high, low)]
    return lax.ppermute(block, axis, route)


def surface_export(ground, previous, sea_float, ocean_side):
    slip_east = ground[0] - previous[0]
    slip_north = ground[1] - previous[1]
    wind_speed = jnp.sqrt(slip_east * slip_east + slip_north * slip_north + gust_speed * gust_speed)
    bulk_flux = jnp.stack(
        [
            drag_coeff * wind_speed * slip_east,
            drag_coeff * wind_speed * slip_north,
            heat_coeff * wind_speed * (previous[2] - ground[2]),
        ]
    )
    return jnp.where(ocean_side, ground, bulk_flux) * sea_float


def substep(padded, mask_out, top_row, total_rows, level_coef):
    center = padded[:, :, 1:-1, 1:-1]
    north = padded[:, :, 2:, 1:-1]
    south = padded[:, :, :-2, 1:-1]
    east = padded[:, :, 1:-1, 2:]
    west = padded[:, :, 1:-1, :-2]
    diffuse = level_coef[0][None, :, None, None]
    advect_east = level_coef[1][None, :, None, None]
    advect_north = level_coef[2][None, :, None, None]
    mixing = level_coef[3][None, :, None, None]
    laplace = north + south + east + west - 4.0 * center
    above = jnp.concatenate([center[:, 1:], center[:, -1:]], 1)
    below = jnp.concatenate([center[:, :1], center[:, :-1]], 1)
    height = center.shape[2]
    row_index = top_row + jnp.arange(height, dtype=jnp.int32)
    latitude = jnp.pi * (
        -1.0 / 3.0 + 2.0 / 3.0 * (row_index.astype(center.dtype) + 0.5) / total_rows
    )
    coriolis = (coriolis_scale * jnp.sin(latitude))[:, None]
    turning = jnp.stack([coriolis * center[1], -coriolis * center[0], jnp.zeros_like(center[2])])
    inside = ((row_index >= 0) & (row_index < total_rows)).astype(center.dtype)[:, None]
    updated = (
        center
        + diffuse * laplace
        - advect_east * (east - west)
        - advect_north * (north - south)
        + mixing * (above + below - 2.0 * center)
        + turning
    )
    return updated * (mask_out * inside)


def rim_once(fields):
    field_count, level_count, row_count, col_count = fields.shape
    flat = fields.reshape(field_count * level_count, row_count, col_count)
    flat = with_halo(flat, (("lon", 2),), 1, True)
    flat = with_halo(flat, (("lat", 1),), 1, False)
    return flat.reshape(field_count, level_count, row_count + 2, col_count + 2)


def rows_summed(slot_rows, slot_values, row_count):
    selector = (slot_rows[:, None] == jnp.arange(row_count, dtype=jnp.int32)[None, :]).astype(
        jnp.float32
    )
    return jnp.einsum("sr,scx->crx", selector, slot_values, precision=lax.Precision.HIGHEST)


def body(
    state,
    surface,
    sea_mask,
    coeffs,
    remap_weights,
    link_dest,
    link_src_row,
    link_dst_row,
    link_tile,
):
    fields = state[0]
    previous = surface[0]
    sea_float = sea_mask[0].astype(jnp.float32)
    level_coef = coeffs[0]
    tile_table = remap_weights[0]
    field_count, level_count, row_count, col_count = fields.shape
    ocean_side = lax.axis_index("grp") == 1
    first_row = lax.axis_index("lat") * row_count
    total_rows = row_count * lax.axis_size("lat")
    lat_count = lax.axis_size("lat")
    peer_count = lat_count * lax.axis_size("lon")
    exported = surface_export(fields[:, 0], previous, sea_float, ocean_side)
    combos = jnp.einsum("cax,wxy->wcay", exported, tile_table, precision=lax.Precision.HIGHEST)
    targets = link_dest[0, :, 0]
    pieces = combos[link_tile[0], :, link_src_row[0], :]
    link_count = targets.shape[0]
    slot_count = max(2, 2 * link_count // peer_count)
    link_order = jnp.arange(link_count, dtype=jnp.int32)
    earlier_same = (targets[:, None] == targets[None, :]) & (
        link_order[None, :] < link_order[:, None]
    )
    link_rank = jnp.sum(earlier_same.astype(jnp.int32), axis=1)
    position = targets * slot_count + link_rank
    outgoing = (
        jnp.zeros((peer_count * slot_count, field_count, col_count), jnp.float32)
        .at[position]
        .set(pieces)
    )
    out_rows = jnp.full((peer_count * slot_count,), -1, jnp.int32).at[position].set(link_dst_row[0])
    arrived, arrived_rows = (
        lax.all_to_all(outgoing, ("lat", "lon"), split_axis=0, concat_axis=0, tiled=True),
        lax.all_to_all(out_rows, ("lat", "lon"), split_axis=0, concat_axis=0, tiled=True),
    )
    summed_here = rows_summed(arrived_rows, arrived, row_count)
    imported = swapped(summed_here, "grp", 0) * sea_float
    gain = jnp.where(ocean_side, ocean_gain, air_gain)
    damping = jnp.where(ocean_side, 0.0, air_gain)
    ground = fields[:, 0] + sea_float * (gain * previous - damping * fields[:, 0])
    fields = jnp.concatenate([ground[:, None], fields[:, 1:]], 1)
    state_mask = jnp.where(ocean_side, sea_float, jnp.ones_like(sea_float))
    for substep_index in range(SUBSTEPS):
        fields = substep(rim_once(fields), state_mask, first_row, total_rows, level_coef)
    return (fields[None], imported[None])


def solution(mesh):
    placed = (
        P("grp", None, None, "lat", "lon"),
        P("grp", None, "lat", "lon"),
        P("grp", "lat", "lon"),
        P("grp", None, None),
        P("grp", None, None, None),
        P("grp", ("lat", "lon"), None),
        P("grp", ("lat", "lon")),
        P("grp", ("lat", "lon")),
        P("grp", ("lat", "lon")),
    )
    return jax.shard_map(
        body,
        mesh=mesh,
        in_specs=placed,
        out_specs=(P("grp", None, None, "lat", "lon"), P("grp", None, "lat", "lon")),
        check_vma=False,
    )
```

profile of v0, /device:TPU:0, one launch (start us, length us, event | category | flops | bytes accessed | tf_op | source)
XLA Modules:
  0.0 118.7 jit_solution(16005756296637472939)
XLA Ops:
  4.8 2.9 %collective-permute-start = (f32[24,32,1]{2,1,0:T(8,128)}, f32[24,32,1]{2,1,0:T(8,128)S(1)}, u32[]{:S(2)}, u32[]{:S(2)}) collective-permute-start(f32[24,32,1]{2,1,0:T(8,128)} %get-tuple-element.23), channel_id=1, source_target_pairs={{0,1},{1,2},{2,3},{3,0},{4,5},{5,6},{6,7},{7,4},{8,9},{9,10},{10,1... | collective-permute-start | bytes 9224 | tf_op jit(solution)/shard_map/ppermute | solution.py:25
  10.7 6.4 %all-to-all-start.1 = ((s32[16,16,1]{1,2,0:T(1,128)}), s32[16,16,1]{1,2,0:T(1,128)S(1)}, u32[]{:S(2)}, u32[]{:S(2)}) async-start(s32[16,16,1]{1,2,0:T(1,128)} %bitcast.27), calls=%async_computation.1 | async-start | bytes 16384 | tf_op jit(solution)/shard_map/all_to_all | solution.py:147
  17.1 1.4 %fusion.32 = (f32[1,1,32,256]{3,2,1,0:T(8,128)S(1)}, f32[1,1,32,256]{3,2,1,0:T(8,128)S(1)}, f32[1,1,32,256]{3,2,1,0:T(8,128)}) fusion(f32[1,3,32,256]{3,2,1,0:T(8,128)S(1)} %copy-done.5, f32[3,8,32,256]{3,2,1,0:T(8,128)} %bitcast.85), kind=kLoop, calls=%fused_computation.59 | loop fusion | flops 90112 | bytes 294912 | tf_op jit(solution)/shard_map/mul | solution.py:50
  19.4 2.2 %fusion.2 = f32[8,3,32,256]{3,2,0,1:T(8,128)S(1)} fusion(f32[1,8,256,256]{3,2,1,0:T(8,128)S(1)} %copy-done, f32[1,1,32,256]{3,2,1,0:T(8,128)S(1)} %get-tuple-element.19, f32[1,1,32,256]{3,2,1,0:T(8,128)} %get-tuple-element.20, f32[1,1,32,256]{3,2,1,0:T(8,128)S(1)} %get-tuple-element.18, f32[3,8,32,256]{3,2,1,0:T(8,128)} %bitcast.86, ...), kind=kOutput, calls=%fused_computation.7 | convolution fusion | flops 604078080 | bytes 3112961 | tf_op jit(solution)/shard_map/cax,wxy->wcay/dot_general | solution.py:128
  21.7 5.1 %collective-permute-done.1 = f32[24,32,1]{2,1,0:T(8,128)} collective-permute-done((f32[24,32,1]{2,1,0:T(8,128)}, f32[24,32,1]{2,1,0:T(8,128)}, u32[]{:S(2)}, u32[]{:S(2)}) %collective-permute-start.1) | collective-permute-done | bytes 3104 | tf_op jit(solution)/shard_map/ppermute | solution.py:27
  26.9 1.8 %pad_maximum_fusion.8 = (f32[24,1,258]{2,1,0:T(1,128)}, f32[24,1,258]{2,1,0:T(1,128)S(1)}) fusion(f32[24,32,1]{2,1,0:T(8,128)} %collective-permute-done.1, f32[24,32,256]{2,1,0:T(8,128)S(1)} %bitcast.78, f32[24,32,1]{2,1,0:T(8,128)S(1)} %collective-permute-done), kind=kLoop, calls=%fused_computation.50 | loop fusion | flops 24768 | bytes 842112 | tf_op jit(solution)/shard_map/slice | solution.py:22
  28.7 4.1 %collective-permute-start.2 = (f32[24,1,258]{2,1,0:T(1,128)}, f32[24,1,258]{2,1,0:T(1,128)}, u32[]{:S(2)}, u32[]{:S(2)}) collective-permute-start(f32[24,1,258]{2,1,0:T(1,128)} %get-tuple-element.4), channel_id=1, source_target_pairs={{0,4},{4,8},{8,12},{1,5},{5,9},{9,13},{2,6},{6,10},{10,14},{3,7},{... | collective-permute-start | bytes 74312 | tf_op jit(solution)/shard_map/ppermute | solution.py:25
  32.8 1.3 %collective-permute-start.3 = (f32[24,1,258]{2,1,0:T(1,128)S(1)}, f32[24,1,258]{2,1,0:T(1,128)}, u32[]{:S(2)}, u32[]{:S(2)}) collective-permute-start(f32[24,1,258]{2,1,0:T(1,128)S(1)} %get-tuple-element.5), channel_id=1, source_target_pairs={{4,0},{8,4},{12,8},{5,1},{9,5},{13,9},{6,2},{10,6},{14,10},{7,3},{... | collective-permute-start | bytes 74312 | tf_op jit(solution)/shard_map/ppermute | solution.py:27
  34.1 1.6 %copy.15 = f32[8,3,32,256]{3,1,2,0:T(4,128)} copy(f32[8,3,32,256]{3,2,0,1:T(8,128)S(1)} %fusion.2) | data formatting | bytes 1572864 | tf_op jit(solution)/shard_map/cax,wxy->wcay/transpose | solution.py:128
  35.7 2.3 %gather_fusion = f32[128,3,256]{2,1,0:T(4,128)S(1)} fusion(f32[8,3,32,256]{3,1,2,0:T(4,128)} %copy.15, s32[128]{0:T(128)S(1)} %fusion.44), kind=kCustom, calls=%fused_computation | custom fusion | bytes 787456 | tf_op jit(solution)/shard_map/gather | solution.py:130
  39.1 12.4 %scatter_fusion = f32[256,3,256]{2,1,0:T(4,128)} fusion(f32[256,3,256]{2,1,0:T(4,128)} %broadcast_in_dim.12, s32[128]{0:T(128)S(1)} %fusion.36, f32[128,3,256]{2,1,0:T(4,128)S(1)} %gather_fusion), kind=kCustom, calls=%fused_computation.1 | custom fusion | bytes 1180160 | tf_op jit(solution)/shard_map/scatter | solution.py:142
  51.5 1.7 %pad_maximum_fusion = f32[24,34,258]{2,1,0:T(8,128)S(1)} fusion(f32[24,1,258]{2,1,0:T(1,128)} %collective-permute-done.3, f32[24,32,1]{2,1,0:T(8,128)} %collective-permute-done.1, f32[24,32,256]{2,1,0:T(8,128)S(1)} %bitcast.79, f32[24,32,1]{2,1,0:T(8,128)} %copy-done.3, f32[24,1,258]{2,1,0:T(1,128)} %collective-permute-done.2), kind=kLoop, calls=%fused_computation.5 | loop fusion | flops 842112 | bytes 1684224 | tf_op jit(solution)/shard_map/concatenate | solution.py:23
  53.3 1.6 %fusion.50 = (f32[3,7,32,256]{3,2,1,0:T(8,128)}, f32[3,7,32,256]{3,2,1,0:T(8,128)}) fusion(f32[3,8,34,258]{3,2,1,0:T(8,128)S(1)} %bitcast.73), kind=kLoop, calls=%fused_computation.88 | loop fusion | bytes 2752512 | tf_op jit(solution)/shard_map/slice | solution.py:70
  55.8 7.0 %all-to-all-start = ((f32[256,3,256]{2,1,0:T(4,128)}), f32[256,3,256]{2,1,0:T(4,128)}, u32[]{:S(2)}, u32[]{:S(2)}) async-start(f32[256,3,256]{2,1,0:T(4,128)} %scatter_fusion), calls=%async_computation | async-start | bytes 2097152 | tf_op jit(solution)/shard_map/all_to_all | solution.py:146
  62.9 5.1 %fusion.9 = f32[3,8,32,256]{3,2,1,0:T(8,128)S(1)} fusion(f32[3,1,32,256]{3,2,1,0:T(8,128)} %get-tuple-element.15, f32[3,7,32,256]{3,2,1,0:T(8,128)} %get-tuple-element.17, f32[3,7,32,256]{3,2,1,0:T(8,128)} %get-tuple-element.16, f32[3,1,32,256]{3,2,1,0:T(8,128)} %get-tuple-element.14, f32[1,8,32,256]{3,2,1,0:T(8,128)S(1)} %get-tuple-element.13, ...), kind=kLoop, calls=%fused_computation.15 | loop fusion | flops 4718592 | bytes 6848652 | tf_op jit(solution)/shard_map/mul | solution.py:87
  68.2 1.9 %collective-permute-start.4 = (f32[24,32,1]{2,1,0:T(8,128)S(1)}, f32[24,32,1]{2,1,0:T(8,128)S(1)}, u32[]{:S(2)}, u32[]{:S(2)}) collective-permute-start(f32[24,32,1]{2,1,0:T(8,128)S(1)} %get-tuple-element.21), channel_id=1, source_target_pairs={{0,1},{1,2},{2,3},{3,0},{4,5},{5,6},{6,7},{7,4},{8,9},{9,10},{10,1... | collective-permute-start | bytes 9224 | tf_op jit(solution)/shard_map/ppermute | solution.py:25
  71.2 17.5 %collective-permute-done.4 = f32[24,32,1]{2,1,0:T(8,128)S(1)} collective-permute-done((f32[24,32,1]{2,1,0:T(8,128)S(1)}, f32[24,32,1]{2,1,0:T(8,128)S(1)}, u32[]{:S(2)}, u32[]{:S(2)}) %collective-permute-start.4) | collective-permute-done | bytes 3104 | tf_op jit(solution)/shard_map/ppermute | solution.py:25
  88.7 6.7 %collective-permute-done.5 = f32[24,32,1]{2,1,0:T(8,128)S(1)} collective-permute-done((f32[24,32,1]{2,1,0:T(8,128)S(1)}, f32[24,32,1]{2,1,0:T(8,128)S(1)}, u32[]{:S(2)}, u32[]{:S(2)}) %collective-permute-start.5) | collective-permute-done | bytes 3104 | tf_op jit(solution)/shard_map/ppermute | solution.py:27
  96.4 4.2 %collective-permute-start.6 = (f32[24,1,258]{2,1,0:T(1,128)S(1)}, f32[24,1,258]{2,1,0:T(1,128)S(1)}, u32[]{:S(2)}, u32[]{:S(2)}) collective-permute-start(f32[24,1,258]{2,1,0:T(1,128)S(1)} %get-tuple-element.2), channel_id=1, source_target_pairs={{0,4},{4,8},{8,12},{1,5},{5,9},{9,13},{2,6},{6,10},{10,14},{3,7},{... | collective-permute-start | bytes 74312 | tf_op jit(solution)/shard_map/ppermute | solution.py:25
  100.5 1.3 %collective-permute-start.7 = (f32[24,1,258]{2,1,0:T(1,128)S(1)}, f32[24,1,258]{2,1,0:T(1,128)S(1)}, u32[]{:S(2)}, u32[]{:S(2)}) collective-permute-start(f32[24,1,258]{2,1,0:T(1,128)S(1)} %get-tuple-element.3), channel_id=1, source_target_pairs={{4,0},{8,4},{12,8},{5,1},{9,5},{13,9},{6,2},{10,6},{14,10},{7,3},{... | collective-permute-start | bytes 74312 | tf_op jit(solution)/shard_map/ppermute | solution.py:27
  103.7 2.7 %collective-permute-done.7 = f32[24,1,258]{2,1,0:T(1,128)S(1)} collective-permute-done((f32[24,1,258]{2,1,0:T(1,128)S(1)}, f32[24,1,258]{2,1,0:T(1,128)S(1)}, u32[]{:S(2)}, u32[]{:S(2)}) %collective-permute-start.7) | collective-permute-done | bytes 24800 | tf_op jit(solution)/shard_map/ppermute | solution.py:27
  106.4 1.6 %pad_maximum_fusion.1 = f32[24,34,258]{2,1,0:T(8,128)S(1)} fusion(f32[24,1,258]{2,1,0:T(1,128)S(1)} %collective-permute-done.7, f32[24,32,1]{2,1,0:T(8,128)} %copy-done.4, f32[24,32,256]{2,1,0:T(8,128)S(1)} %bitcast.82, f32[24,32,1]{2,1,0:T(8,128)S(1)} %collective-permute-done.4, f32[24,1,258]{2,1,0:T(1,128)S(1)} %collective-permute-done.6), kind=kLoop, calls=%fused_computation.6 | loop fusion | flops 842112 | bytes 1684224 | tf_op jit(solution)/shard_map/concatenate | solution.py:23
  110.4 1.7 %convolution_bitcast_fusion = f32[3,32,256]{2,1,0:T(8,128)S(1)} fusion(f32[256,3,256]{2,1,0:T(4,128)} %all-to-all-done, s32[256]{0:T(256)} %eq.38), kind=kOutput, calls=%fused_computation.8 | convolution fusion | flops 75505664 | bytes 885760 | tf_op jit(solution)/shard_map/sr,scx->crx/dot_general | solution.py:102
  112.1 5.9 %fusion.15 = f32[1,3,8,32,256]{4,3,2,1,0:T(8,128)} fusion(f32[3,1,32,256]{3,2,1,0:T(8,128)} %get-tuple-element.9, f32[3,7,32,256]{3,2,1,0:T(8,128)S(1)} %get-tuple-element.11, f32[3,7,32,256]{3,2,1,0:T(8,128)S(1)} %get-tuple-element.10, f32[3,1,32,256]{3,2,1,0:T(8,128)} %get-tuple-element.8, f32[1,8,32,256]{3,2,1,0:T(8,128)} %get-tuple-element.7, ...), kind=kLoop, calls=%fused_computation.22 | loop fusion | flops 4718592 | bytes 6848652 | tf_op jit(solution)/shard_map/broadcast_in_dim | solution.py:158
  (59 shorter events, 17.3 us)
Async XLA Ops:
  0.6 18.8 %copy-start = (f32[1,8,256,256]{3,2,1,0:T(8,128)S(1)}, f32[1,8,256,256]{3,2,1,0:T(8,128)}, u32[]{:S(2)}) copy-start(f32[1,8,256,256]{3,2,1,0:T(8,128)} %param.13) | copy-start | bytes 6291460
  0.6 2.1 %copy-start.5 = (f32[1,3,32,256]{3,2,1,0:T(8,128)S(1)}, f32[1,3,32,256]{3,2,1,0:T(8,128)}, u32[]{:S(2)}) copy-start(f32[1,3,32,256]{3,2,1,0:T(8,128)} %param.10) | copy-start | bytes 294916
  3.7 5.0 %copy-start.8 = (s32[1,128,1]{1,2,0:T(1,128)S(1)}, s32[1,128,1]{1,2,0:T(1,128)}, u32[]{:S(2)}) copy-start(s32[1,128,1]{1,2,0:T(1,128)} %param.14) | copy-start | bytes 1540
  3.7 15.7 %copy-start.7 = (f32[1,4,8]{2,1,0:T(4,128)S(1)}, f32[1,4,8]{2,1,0:T(4,128)}, u32[]{:S(2)}) copy-start(f32[1,4,8]{2,1,0:T(4,128)} %param.12) | copy-start | bytes 388
  4.8 16.9 %collective-permute-start = (f32[24,32,1]{2,1,0:T(8,128)}, f32[24,32,1]{2,1,0:T(8,128)S(1)}, u32[]{:S(2)}, u32[]{:S(2)}) collective-permute-start(f32[24,32,1]{2,1,0:T(8,128)} %get-tuple-element.23), channel_id=1, source_target_pairs={{0,1},{1,2},{2,3},{3,0},{4,5},{5,6},{6,7},{7,4},{8,9},{9,10},{10,1... | collective-permute-start | bytes 9224 | tf_op jit(solution)/shard_map/ppermute | solution.py:25
  7.7 19.1 %collective-permute-start.1 = (f32[24,32,1]{2,1,0:T(8,128)}, f32[24,32,1]{2,1,0:T(8,128)}, u32[]{:S(2)}, u32[]{:S(2)}) collective-permute-start(f32[24,32,1]{2,1,0:T(8,128)} %get-tuple-element.24), channel_id=1, source_target_pairs={{1,0},{2,1},{3,2},{0,3},{5,4},{6,5},{7,6},{4,7},{9,8},{10,9},{11,1... | collective-permute-start | bytes 9224 | tf_op jit(solution)/shard_map/ppermute | solution.py:27
  10.7 45.2 %all-to-all-start.1 = ((s32[16,16,1]{1,2,0:T(1,128)}), s32[16,16,1]{1,2,0:T(1,128)S(1)}, u32[]{:S(2)}, u32[]{:S(2)}) async-start(s32[16,16,1]{1,2,0:T(1,128)} %bitcast.27), calls=%async_computation.1 | async-start | bytes 16384 | tf_op jit(solution)/shard_map/all_to_all | solution.py:147
  19.4 2.3 %copy-start.9 = (s32[1,128]{1,0:T(1,128)S(1)}, s32[1,128]{1,0:T(1,128)}, u32[]{:S(2)}) copy-start(s32[1,128]{1,0:T(1,128)} %param.15) | copy-start | bytes 1540
  19.4 2.3 %copy-start.10 = (s32[1,128]{1,0:T(1,128)S(1)}, s32[1,128]{1,0:T(1,128)}, u32[]{:S(2)}) copy-start(s32[1,128]{1,0:T(1,128)} %param.17) | copy-start | bytes 1540
  21.7 13.9 %copy-start.3 = (f32[24,32,1]{2,1,0:T(8,128)}, f32[24,32,1]{2,1,0:T(8,128)S(1)}, u32[]{:S(2)}) copy-start(f32[24,32,1]{2,1,0:T(8,128)S(1)} %collective-permute-done) | copy-start | bytes 9220
  28.7 22.8 %collective-permute-start.2 = (f32[24,1,258]{2,1,0:T(1,128)}, f32[24,1,258]{2,1,0:T(1,128)}, u32[]{:S(2)}, u32[]{:S(2)}) collective-permute-start(f32[24,1,258]{2,1,0:T(1,128)} %get-tuple-element.4), channel_id=1, source_target_pairs={{0,4},{4,8},{8,12},{1,5},{5,9},{9,13},{2,6},{6,10},{10,14},{3,7},{... | collective-permute-start | bytes 74312 | tf_op jit(solution)/shard_map/ppermute | solution.py:25
  32.8 18.7 %collective-permute-start.3 = (f32[24,1,258]{2,1,0:T(1,128)S(1)}, f32[24,1,258]{2,1,0:T(1,128)}, u32[]{:S(2)}, u32[]{:S(2)}) collective-permute-start(f32[24,1,258]{2,1,0:T(1,128)S(1)} %get-tuple-element.5), channel_id=1, source_target_pairs={{4,0},{8,4},{12,8},{5,1},{9,5},{13,9},{6,2},{10,6},{14,10},{7,3},{... | collective-permute-start | bytes 74312 | tf_op jit(solution)/shard_map/ppermute | solution.py:27
  35.7 27.1 %copy-start.6 = (f32[3]{0:T(128)}, f32[3]{0:T(128)S(1)}, u32[]{:S(2)}) copy-start(f32[3]{0:T(128)S(1)} %pad.20.clone) | copy-start | bytes 40
  53.3 1.8 %copy-start.2 = (f32[24,34,258]{2,1,0:T(8,128)}, f32[24,34,258]{2,1,0:T(8,128)S(1)}, u32[]{:S(2)}) copy-start(f32[24,34,258]{2,1,0:T(8,128)S(1)} %pad_maximum_fusion) | copy-start | bytes 2526340
  55.8 54.5 %all-to-all-start = ((f32[256,3,256]{2,1,0:T(4,128)}), f32[256,3,256]{2,1,0:T(4,128)}, u32[]{:S(2)}, u32[]{:S(2)}) async-start(f32[256,3,256]{2,1,0:T(4,128)} %scatter_fusion), calls=%async_computation | async-start | bytes 2097152 | tf_op jit(solution)/shard_map/all_to_all | solution.py:146
  68.2 20.5 %collective-permute-start.4 = (f32[24,32,1]{2,1,0:T(8,128)S(1)}, f32[24,32,1]{2,1,0:T(8,128)S(1)}, u32[]{:S(2)}, u32[]{:S(2)}) collective-permute-start(f32[24,32,1]{2,1,0:T(8,128)S(1)} %get-tuple-element.21), channel_id=1, source_target_pairs={{0,1},{1,2},{2,3},{3,0},{4,5},{5,6},{6,7},{7,4},{8,9},{9,10},{10,1... | collective-permute-start | bytes 9224 | tf_op jit(solution)/shard_map/ppermute | solution.py:25
  70.1 25.2 %collective-permute-start.5 = (f32[24,32,1]{2,1,0:T(8,128)S(1)}, f32[24,32,1]{2,1,0:T(8,128)S(1)}, u32[]{:S(2)}, u32[]{:S(2)}) collective-permute-start(f32[24,32,1]{2,1,0:T(8,128)S(1)} %get-tuple-element.22), channel_id=1, source_target_pairs={{1,0},{2,1},{3,2},{0,3},{5,4},{6,5},{7,6},{4,7},{9,8},{10,9},{11,1... | collective-permute-start | bytes 9224 | tf_op jit(solution)/shard_map/ppermute | solution.py:27
  95.3 0.7 copy-start.4
  96.4 7.3 %collective-permute-start.6 = (f32[24,1,258]{2,1,0:T(1,128)S(1)}, f32[24,1,258]{2,1,0:T(1,128)S(1)}, u32[]{:S(2)}, u32[]{:S(2)}) collective-permute-start(f32[24,1,258]{2,1,0:T(1,128)S(1)} %get-tuple-element.2), channel_id=1, source_target_pairs={{0,4},{4,8},{8,12},{1,5},{5,9},{9,13},{2,6},{6,10},{10,14},{3,7},{... | collective-permute-start | bytes 74312 | tf_op jit(solution)/shard_map/ppermute | solution.py:25
  100.5 5.9 %collective-permute-start.7 = (f32[24,1,258]{2,1,0:T(1,128)S(1)}, f32[24,1,258]{2,1,0:T(1,128)S(1)}, u32[]{:S(2)}, u32[]{:S(2)}) collective-permute-start(f32[24,1,258]{2,1,0:T(1,128)S(1)} %get-tuple-element.3), channel_id=1, source_target_pairs={{4,0},{8,4},{12,8},{5,1},{9,5},{13,9},{6,2},{10,6},{14,10},{7,3},{... | collective-permute-start | bytes 74312 | tf_op jit(solution)/shard_map/ppermute | solution.py:27
  108.0 2.0 %copy-start.1 = (f32[24,34,258]{2,1,0:T(8,128)}, f32[24,34,258]{2,1,0:T(8,128)S(1)}, u32[]{:S(2)}) copy-start(f32[24,34,258]{2,1,0:T(8,128)S(1)} %pad_maximum_fusion.1) | copy-start | bytes 2526340
  112.1 6.0 %collective-permute-start.8 = (f32[3,32,256]{2,1,0:T(8,128)S(1)}, f32[3,32,256]{2,1,0:T(8,128)S(1)}, u32[]{:S(2)}, u32[]{:S(2)}) collective-permute-start(f32[3,32,256]{2,1,0:T(8,128)S(1)} %convolution_bitcast_fusion), channel_id=1, source_target_pairs={{0,16},{16,0},{1,17},{17,1},{2,18},{18,2},{3,19},{19,3},{4,20},{20... | collective-permute-start | bytes 294920 | tf_op jit(solution)/shard_map/ppermute | solution.py:41
where the time goes:
time: 120 us; the launch traced here: 119 us
  waiting for transfers between devices  32 us (27%)
  starting transfers between devices  31.2 us (26%)
  local copies, waits for them, and re-layouts  27.2 us (23%)
  other arithmetic  23.4 us (20%)
  matrix products  3.91 us (3%)
    ppermute x4, waiting for transfers between devices, with_halo(): lax.ppermute(tail, axis, [(i, (i + 1) % count) for i in range(ends)])  17.5 us
    ppermute x4, waiting for transfers between devices, with_halo(): lax.ppermute(head, axis, [((i + 1) % count, i) for i in range(ends)])  14.5 us
    ppermute x4, starting transfers between devices, with_halo(): lax.ppermute(tail, axis, [(i, (i + 1) % count) for i in range(ends)])  13.1 us
    scatter x1, local copies, waits for them, and re-layouts, body(): outgoing = jnp.zeros((peer_count * slot_count, field_count, col_count), j...  12.4 us
    all_to_all x1, starting transfers between devices, body(): lax.all_to_all(outgoing, ('lat', 'lon'), split_axis=0, concat_axis=0, til...  7.02 us
    broadcast_in_dim x2, other arithmetic, body(): return (fields[None], imported[None])  6.52 us
    all_to_all x1, starting transfers between devices, body(): lax.all_to_all(out_rows, ('lat', 'lon'), split_axis=0, concat_axis=0, til...  6.44 us
    mul x2, other arithmetic, substep(): return updated * (mask_out * inside)  5.94 us
  transfers between devices with their start and end apart: 11, of which 4 were waited for; matrix products, arithmetic and copies ran while one was open for 39% of the time, Pallas kernels for 0%

commit v1 on v0

--- a/solution.py
+++ b/solution.py
@@ -13,32 +13,31 @@
 gust_speed = 0.5
 coriolis_scale = 0.25
 
-
-def with_halo(cells, sides, width, closed):
-    for axis, dim in sides:
-        count = lax.axis_size(axis)
-        ends = count if closed else count - 1
-        head = lax.slice_in_dim(cells, 0, width, axis=dim)
-        tail = lax.slice_in_dim(cells, cells.shape[dim] - width, cells.shape[dim], axis=dim)
-        cells = jnp.concatenate(
-            [
-                lax.ppermute(tail, axis, [(i, (i + 1) % count) for i in range(ends)]),
-                cells,
-                lax.ppermute(head, axis, [((i + 1) % count, i) for i in range(ends)]),
-            ],
-            axis=dim,
-        )
-    return cells
+HIGHEST = lax.Precision.HIGHEST
 
 
-def swapped(block, axis, distance):
+def shifted(part, axis, closed, forward):
     count = lax.axis_size(axis)
-    route = []
-    for low in range(count):
-        high = low | 1 << distance
-        if high != low and high < count:
-            route += [(low, high), (high, low)]
-    return lax.ppermute(block, axis, route)
+    ends = count if closed else count - 1
+    if forward:
+        route = [(i, (i + 1) % count) for i in range(ends)]
+    else:
+        route = [((i + 1) % count, i) for i in range(ends)]
+    flat = lax.ppermute(part.reshape(-1), axis, route)
+    return flat.reshape(part.shape)
+
+
+def with_halo(cells, width):
+    head = cells[:, :, :width]
+    tail = cells[:, :, -width:]
+    cells = jnp.concatenate(
+        [shifted(tail, "lon", True, True), cells, shifted(head, "lon", True, False)], axis=2
+    )
+    head = cells[:, :width, :]
+    tail = cells[:, -width:, :]
+    return jnp.concatenate(
+        [shifted(tail, "lat", False, True), cells, shifted(head, "lat", False, False)], axis=1
+    )
 
 
 def surface_export(ground, previous, sea_float, ocean_side):
@@ -87,21 +86,6 @@
     return updated * (mask_out * inside)
 
 
-def rim_once(fields):
-    field_count, level_count, row_count, col_count = fields.shape
-    flat = fields.reshape(field_count * level_count, row_count, col_count)
-    flat = with_halo(flat, (("lon", 2),), 1, True)
-    flat = with_halo(flat, (("lat", 1),), 1, False)
-    return flat.reshape(field_count, level_count, row_count + 2, col_count + 2)
-
-
-def rows_summed(slot_rows, slot_values, row_count):
-    selector = (slot_rows[:, None] == jnp.arange(row_count, dtype=jnp.int32)[None, :]).astype(
-        jnp.float32
-    )
-    return jnp.einsum("sr,scx->crx", selector, slot_values, precision=lax.Precision.HIGHEST)
-
-
 def body(
     state,
     surface,
@@ -119,15 +103,17 @@
     level_coef = coeffs[0]
     tile_table = remap_weights[0]
     field_count, level_count, row_count, col_count = fields.shape
+    tile_count = tile_table.shape[0]
     ocean_side = lax.axis_index("grp") == 1
     first_row = lax.axis_index("lat") * row_count
     total_rows = row_count * lax.axis_size("lat")
-    lat_count = lax.axis_size("lat")
-    peer_count = lat_count * lax.axis_size("lon")
+    peer_count = lax.axis_size("lat") * lax.axis_size("lon")
+    width = field_count * col_count
+
     exported = surface_export(fields[:, 0], previous, sea_float, ocean_side)
-    combos = jnp.einsum("cax,wxy->wcay", exported, tile_table, precision=lax.Precision.HIGHEST)
+    combos = jnp.einsum("crx,txy->trcy", exported, tile_table, precision=HIGHEST)
+    combos = combos.reshape(tile_count * row_count, width)
     targets = link_dest[0, :, 0]
-    pieces = combos[link_tile[0], :, link_src_row[0], :]
     link_count = targets.shape[0]
     slot_count = max(2, 2 * link_count // peer_count)
     link_order = jnp.arange(link_count, dtype=jnp.int32)
@@ -136,25 +122,51 @@
     )
     link_rank = jnp.sum(earlier_same.astype(jnp.int32), axis=1)
     position = targets * slot_count + link_rank
-    outgoing = (
-        jnp.zeros((peer_count * slot_count, field_count, col_count), jnp.float32)
-        .at[position]
-        .set(pieces)
+    slot_ids = jnp.arange(peer_count * slot_count, dtype=jnp.int32)
+    in_slot = (position[None, :] == slot_ids[:, None]).astype(jnp.int32)
+    picked = link_tile[0] * row_count + link_src_row[0]
+    slot_pick = jnp.sum(in_slot * (picked + 1)[None, :], axis=1) - 1
+    slot_row = jnp.sum(in_slot * (link_dst_row[0] + 1)[None, :], axis=1) - 1
+    chooser = (
+        slot_pick[:, None] == jnp.arange(tile_count * row_count, dtype=jnp.int32)[None, :]
+    ).astype(jnp.float32)
+    outgoing = jnp.dot(chooser, combos, precision=HIGHEST)
+    row_tags = jnp.zeros((peer_count, 1, width), jnp.float32)
+    row_tags = row_tags.at[:, 0, :slot_count].set(
+        slot_row.reshape(peer_count, slot_count).astype(jnp.float32)
     )
-    out_rows = jnp.full((peer_count * slot_count,), -1, jnp.int32).at[position].set(link_dst_row[0])
-    arrived, arrived_rows = (
-        lax.all_to_all(outgoing, ("lat", "lon"), split_axis=0, concat_axis=0, tiled=True),
-        lax.all_to_all(out_rows, ("lat", "lon"), split_axis=0, concat_axis=0, tiled=True),
-    )
-    summed_here = rows_summed(arrived_rows, arrived, row_count)
-    imported = swapped(summed_here, "grp", 0) * sea_float
+    outgoing = jnp.concatenate(
+        [outgoing.reshape(peer_count, slot_count, width), row_tags], axis=1
+    ).reshape(peer_count * (slot_count + 1), width)
+    arrived = lax.all_to_all(outgoing, ("lat", "lon"), split_axis=0, concat_axis=0, tiled=True)
+    arrived = arrived.reshape(peer_count, slot_count + 1, width)
+    arrived_rows = arrived[:, slot_count, :slot_count].reshape(-1)
+    arrived_pieces = arrived[:, :slot_count, :].reshape(peer_count * slot_count, width)
+    selector = (
+        arrived_rows[None, :] == jnp.arange(row_count, dtype=jnp.float32)[:, None]
+    ).astype(jnp.float32)
+    summed_here = jnp.dot(selector, arrived_pieces, precision=HIGHEST)
+    summed_here = summed_here.reshape(row_count, field_count, col_count).transpose(1, 0, 2)
+    imported = lax.ppermute(summed_here, "grp", [(0, 1), (1, 0)]) * sea_float
+
     gain = jnp.where(ocean_side, ocean_gain, air_gain)
     damping = jnp.where(ocean_side, 0.0, air_gain)
     ground = fields[:, 0] + sea_float * (gain * previous - damping * fields[:, 0])
     fields = jnp.concatenate([ground[:, None], fields[:, 1:]], 1)
     state_mask = jnp.where(ocean_side, sea_float, jnp.ones_like(sea_float))
+    planes = jnp.concatenate(
+        [fields.reshape(field_count * level_count, row_count, col_count), state_mask[None]], 0
+    )
+    planes = with_halo(planes, SUBSTEPS)
+    mask_wide = planes[-1]
+    fields = planes[:-1].reshape(
+        field_count, level_count, row_count + 2 * SUBSTEPS, col_count + 2 * SUBSTEPS
+    )
     for substep_index in range(SUBSTEPS):
-        fields = substep(rim_once(fields), state_mask, first_row, total_rows, level_coef)
+        halo = SUBSTEPS - substep_index - 1
+        edge = substep_index + 1
+        mask_out = mask_wide[edge : mask_wide.shape[0] - edge, edge : mask_wide.shape[1] - edge]
+        fields = substep(fields, mask_out, first_row - halo, total_rows, level_coef)
     return (fields[None], imported[None])
 
 

time: 120 us -> 77.8 us (0.65)
  the two profiles are of different devices: /device:TPU:0 before, /device:TPU:13 now
where the time goes in v1:
time: 77.8 us; the launch traced here: 77 us
  other arithmetic  19.6 us (25%)
  local copies, waits for them, and re-layouts  19.4 us (25%)
  waiting for transfers between devices  17.3 us (22%)
  starting transfers between devices  15.2 us (20%)
  matrix products  4.45 us (6%)
  between operations  0.99 us (1%)
    ppermute x4, waiting for transfers between devices, shifted(): flat = lax.ppermute(part.reshape(-1), axis, route)  17.3 us
    ppermute x4, starting transfers between devices, shifted(): flat = lax.ppermute(part.reshape(-1), axis, route)  7.9 us
    broadcast_in_dim x2, other arithmetic, body(): return (fields[None], imported[None])  6.78 us
    all_to_all x1, starting transfers between devices, body(): lax.all_to_all(outgoing, ('lat', 'lon'), split_axis=0, concat_axis=0, til...  5.84 us
    slice x4, local copies, waits for them, and re-layouts, substep(): below = jnp.concatenate([center[:, :1], center[:, :-1]], 1)  3.39 us
    reshape x4, local copies, waits for them, and re-layouts, shifted(): flat = lax.ppermute(part.reshape(-1), axis, route)  2.99 us
    reshape x4, local copies, waits for them, and re-layouts, shifted(): return flat.reshape(part.shape)  2.62 us
    mul x3, other arithmetic, substep(): return updated * (mask_out * inside)  2.43 us
  transfers between devices with their start and end apart: 6, of which 2 were waited for; matrix products, arithmetic and copies ran while one was open for 41% of the time, Pallas kernels for 0%

profile of v1, /device:TPU:13, one launch (start us, length us, event | category | flops | bytes accessed | tf_op | source)
XLA Modules:
  0.0 77.0 jit_solution(568468115971386842)
XLA Ops:
  0.7 0.9 %convert_bitcast_fusion = f32[32,256]{1,0:T(8,128)S(1)} fusion(s32[1,32,256]{2,1,0:T(8,128)} %param.13), kind=kLoop, calls=%fused_computation.69 | loop fusion | flops 8192 | bytes 65536 | tf_op jit(solution)/shard_map/mul | solution.py:154
  2.4 1.2 %slice.231 = f32[3,7,32,256]{3,2,1,0:T(8,128)S(1)} slice(f32[3,8,32,256]{3,2,1,0:T(8,128)} %bitcast.71), slice={[0:3], [1:8], [0:32], [0:256]} | slice | bytes 1376256 | tf_op jit(solution)/shard_map/slice | solution.py:155
  5.5 1.2 %reshape.276 = f32[1600]{0:T(1024)S(1)} reshape(f32[25,32,2]{2,1,0:T(8,128)} %get-tuple-element.33) | data formatting | bytes 12800 | tf_op jit(solution)/shard_map/reshape | solution.py:26
  6.7 1.3 %collective-permute-start = (f32[1600]{0:T(1024)S(1)}, f32[1600]{0:T(1024)S(1)}, u32[]{:S(2)}, u32[]{:S(2)}) collective-permute-start(f32[1600]{0:T(1024)S(1)} %reshape.276), channel_id=1, source_target_pairs={{0,1},{1,2},{2,3},{3,0},{4,5},{5,6},{6,7},{7,4},{8,9},{9,10},{10,1... | collective-permute-start | bytes 19208 | tf_op jit(solution)/shard_map/ppermute | solution.py:26
  8.2 1.2 %collective-permute-start.1 = (f32[1600]{0:T(1024)S(1)}, f32[1600]{0:T(1024)S(1)}, u32[]{:S(2)}, u32[]{:S(2)}) collective-permute-start(f32[1600]{0:T(1024)S(1)} %reshape.278), channel_id=1, source_target_pairs={{1,0},{2,1},{3,2},{0,3},{5,4},{6,5},{7,6},{4,7},{9,8},{10,9},{11,1... | collective-permute-start | bytes 19208 | tf_op jit(solution)/shard_map/ppermute | solution.py:26
  10.2 2.2 %fusion.7 = f32[8,32,3,256]{3,1,0,2:T(8,128)S(1)} fusion(f32[1,8,256,256]{3,2,1,0:T(8,128)S(1)} %copy-done, f32[1,1,32,256]{3,2,1,0:T(8,128)S(1)} %get-tuple-element.31, f32[1,1,32,256]{3,2,1,0:T(8,128)S(1)} %get-tuple-element.32, f32[1,1,32,256]{3,2,1,0:T(8,128)S(1)} %get-tuple-element.30, f32[3,8,32,256]{3,2,1,0:T(8,128)} %bitcast.74, ...), kind=kOutput, calls=%fused_computation.9 | convolution fusion | flops 604078080 | bytes 3112961 | tf_op jit(solution)/shard_map/crx,txy->trcy/dot_general | solution.py:114
  12.5 1.5 %copy.14 = f32[8,32,3,256]{3,2,1,0:T(4,128)} copy(f32[8,32,3,256]{3,1,0,2:T(8,128)S(1)} %fusion.7) | data formatting | bytes 1572864 | tf_op jit(solution)/shard_map/crx,txy->trcy/transpose | solution.py:114
  14.0 2.4 %reshape.289 = f32[256,768,1]{1,0,2:T(8,128)} reshape(f32[8,32,3,256]{3,2,1,0:T(4,128)} %copy.14) | data formatting | bytes 1572864 | tf_op jit(solution)/shard_map/reshape | solution.py:115
  17.0 1.7 %fusion.18 = f32[16,16,768]{2,1,0:T(8,128)S(1)} fusion(f32[256,768,1]{1,0,2:T(8,128)} %reshape.289, s32[16,16]{1,0:T(8,128)S(1)} %sub.99), kind=kOutput, calls=%fused_computation.31 | convolution fusion | flops 604045312 | bytes 1573888 | tf_op jit(solution)/shard_map/dot_general | solution.py:133
  18.8 1.1 %select_maximum_fusion = f32[16,17,768]{2,1,0:T(8,128)} fusion(f32[16,1,16]{2,1,0:T(1,128)S(1)} %convert_element_type.65, f32[16,16,768]{2,1,0:T(8,128)S(1)} %fusion.18), kind=kLoop, calls=%fused_computation.10 | loop fusion | flops 626688 | bytes 1623040 | tf_op jit(solution)/shard_map/concatenate | solution.py:138
  19.9 5.8 %all-to-all-start = ((f32[16,17,768]{2,1,0:T(8,128)}), f32[16,17,768]{2,1,0:T(8,128)}, u32[]{:S(2)}, u32[]{:S(2)}) async-start(f32[16,17,768]{2,1,0:T(8,128)} %select_maximum_fusion), calls=%async_computation | async-start | bytes 2359296 | tf_op jit(solution)/shard_map/all_to_all | solution.py:141
  26.8 1.1 %reshape.279 = f32[25,32,2]{2,1,0:T(8,128)} reshape(f32[1600]{0:T(1024)S(1)} %collective-permute-done.1) | data formatting | bytes 12800 | tf_op jit(solution)/shard_map/reshape | solution.py:27
  27.9 1.2 %pad_maximum_fusion.6 = (f32[25,2,260]{2,1,0:T(2,128)S(1)}, f32[25,2,260]{2,1,0:T(2,128)S(1)}) fusion(f32[25,32,2]{2,1,0:T(8,128)} %reshape.279, f32[25,32,2]{2,1,0:T(8,128)S(1)} %reshape.277, f32[1,32,256]{2,1,0:T(8,128)S(1)} %convert_select_fusion, f32[24,32,256]{2,1,0:T(8,128)S(1)} %bitcast.66), kind=kLoop, calls=%fused_computation.51 | loop fusion | flops 78000 | bytes 936000 | tf_op jit(solution)/shard_map/slice | solution.py:37
  29.9 3.1 %collective-permute-start.2 = (f32[13000]{0:T(1024)}, f32[13000]{0:T(1024)S(1)}, u32[]{:S(2)}, u32[]{:S(2)}) collective-permute-start(f32[13000]{0:T(1024)} %reshape.280), channel_id=1, source_target_pairs={{0,4},{4,8},{8,12},{1,5},{5,9},{9,13},{2,6},{6,10},{10,14},{3,7},{... | collective-permute-start | bytes 156008 | tf_op jit(solution)/shard_map/ppermute | solution.py:26
  33.7 2.4 %collective-permute-start.3 = (f32[13000]{0:T(1024)}, f32[13000]{0:T(1024)}, u32[]{:S(2)}, u32[]{:S(2)}) collective-permute-start(f32[13000]{0:T(1024)} %reshape.282), channel_id=1, source_target_pairs={{4,0},{8,4},{12,8},{5,1},{9,5},{13,9},{6,2},{10,6},{14,10},{7,3},{... | collective-permute-start | bytes 156008 | tf_op jit(solution)/shard_map/ppermute | solution.py:26
  36.7 15.3 %collective-permute-done.2 = f32[13000]{0:T(1024)S(1)} collective-permute-done((f32[13000]{0:T(1024)}, f32[13000]{0:T(1024)S(1)}, u32[]{:S(2)}, u32[]{:S(2)}) %collective-permute-start.2) | collective-permute-done | bytes 52032 | tf_op jit(solution)/shard_map/ppermute | solution.py:26
  52.2 2.0 %collective-permute-done.3 = f32[13000]{0:T(1024)} collective-permute-done((f32[13000]{0:T(1024)}, f32[13000]{0:T(1024)}, u32[]{:S(2)}, u32[]{:S(2)}) %collective-permute-start.3) | collective-permute-done | bytes 52032 | tf_op jit(solution)/shard_map/ppermute | solution.py:26
  54.2 1.0 %reshape.283 = f32[25,2,260]{2,1,0:T(2,128)S(1)} reshape(f32[13000]{0:T(1024)} %collective-permute-done.3) | data formatting | bytes 104000 | tf_op jit(solution)/shard_map/reshape | solution.py:27
  58.8 2.3 %fusion.6 = f32[3,8,34,258]{3,2,1,0:T(8,128)S(1)} fusion(f32[3,1,34,258]{3,2,1,0:T(8,128)S(1)} %get-tuple-element.27, f32[3,7,34,258]{3,2,1,0:T(8,128)S(1)} %get-tuple-element.29, f32[3,7,34,258]{3,2,1,0:T(8,128)S(1)} %get-tuple-element.28, f32[3,1,34,258]{3,2,1,0:T(8,128)S(1)} %get-tuple-element.26, f32[1,8,34,258]{3,2,1,0:T(8,128)S(1)} %get-tuple-element.25, ...), kind=kLoop, calls=%fused_computation.8 | loop fusion | flops 5052672 | bytes 7333532 | tf_op jit(solution)/shard_map/mul | solution.py:86
  62.3 1.5 %fusion.44 = (f32[3,7,32,256]{3,2,1,0:T(8,128)}, f32[3,7,32,256]{3,2,1,0:T(8,128)}) fusion(f32[3,8,34,258]{3,2,1,0:T(8,128)S(1)} %fusion.6), kind=kLoop, calls=%fused_computation.92 | loop fusion | bytes 2752512 | tf_op jit(solution)/shard_map/slice | solution.py:69
  63.8 2.1 %slice.263 = f32[16,16,768]{2,1,0:T(8,128)} slice(f32[16,17,768]{2,1,0:T(8,128)} %all-to-all-done), slice={[0:16], [0:16], [0:768]} | slice | bytes 1572864 | tf_op jit(solution)/shard_map/slice | solution.py:144
  65.9 1.4 %copy.15 = f32[768,256]{1,0:T(8,128)S(1)} copy(f32[768,256]{0,1:T(8,128)} %bitcast.70) | data formatting | bytes 1572864 | tf_op jit(solution)/shard_map/dot_general | solution.py:148
  68.7 1.5 %collective-permute-start.4 = (f32[3,32,256]{2,1,0:T(8,128)S(1)}, f32[3,32,256]{2,1,0:T(8,128)S(1)}, u32[]{:S(2)}, u32[]{:S(2)}) collective-permute-start(f32[3,32,256]{2,1,0:T(8,128)S(1)} %convolution_bitcast_fusion), channel_id=1, source_target_pairs={{0,16},{16,0},{1,17},{17,1},{2,18},{18,2},{3,19},{19,3},{4,20},{20... | collective-permute-start | bytes 294920 | tf_op jit(solution)/shard_map/ppermute | solution.py:150
  70.2 6.1 %fusion.15 = f32[1,3,8,32,256]{4,3,2,1,0:T(8,128)} fusion(f32[3,1,32,256]{3,2,1,0:T(8,128)} %get-tuple-element.21, f32[3,7,32,256]{3,2,1,0:T(8,128)} %get-tuple-element.23, f32[3,7,32,256]{3,2,1,0:T(8,128)} %get-tuple-element.22, f32[3,1,32,256]{3,2,1,0:T(8,128)} %get-tuple-element.20, f32[1,8,32,256]{3,2,1,0:T(8,128)S(1)} %get-tuple-element.19, ...), kind=kLoop, calls=%fused_computation.22 | loop fusion | flops 4718592 | bytes 6848652 | tf_op jit(solution)/shard_map/broadcast_in_dim | solution.py:170
  (66 shorter events, 14.4 us)
Async XLA Ops:
  0.6 9.6 %copy-start = (f32[1,8,256,256]{3,2,1,0:T(8,128)S(1)}, f32[1,8,256,256]{3,2,1,0:T(8,128)}, u32[]{:S(2)}) copy-start(f32[1,8,256,256]{3,2,1,0:T(8,128)} %param.15) | copy-start | bytes 6291460
  0.6 2.9 %copy-start.3 = (f32[1,3,32,256]{3,2,1,0:T(8,128)S(1)}, f32[1,3,32,256]{3,2,1,0:T(8,128)}, u32[]{:S(2)}) copy-start(f32[1,3,32,256]{3,2,1,0:T(8,128)} %param.12) | copy-start | bytes 294916
  4.5 4.9 %copy-start.4 = (f32[1,3,32,256]{3,2,1,0:T(8,128)S(1)}, f32[1,3,32,256]{3,2,1,0:T(8,128)}, u32[]{:S(2)}) copy-start(f32[1,3,32,256]{3,2,1,0:T(8,128)} %param.12) | copy-start | bytes 294916
  6.7 19.7 %collective-permute-start = (f32[1600]{0:T(1024)S(1)}, f32[1600]{0:T(1024)S(1)}, u32[]{:S(2)}, u32[]{:S(2)}) collective-permute-start(f32[1600]{0:T(1024)S(1)} %reshape.276), channel_id=1, source_target_pairs={{0,1},{1,2},{2,3},{3,0},{4,5},{5,6},{6,7},{7,4},{8,9},{9,10},{10,1... | collective-permute-start | bytes 19208 | tf_op jit(solution)/shard_map/ppermute | solution.py:26
  8.2 18.5 %collective-permute-start.1 = (f32[1600]{0:T(1024)S(1)}, f32[1600]{0:T(1024)S(1)}, u32[]{:S(2)}, u32[]{:S(2)}) collective-permute-start(f32[1600]{0:T(1024)S(1)} %reshape.278), channel_id=1, source_target_pairs={{1,0},{2,1},{3,2},{0,3},{5,4},{6,5},{7,6},{4,7},{9,8},{10,9},{11,1... | collective-permute-start | bytes 19208 | tf_op jit(solution)/shard_map/ppermute | solution.py:26
  12.5 4.0 %copy-start.8 = (s32[1,128,1]{1,2,0:T(1,128)S(1)}, s32[1,128,1]{1,2,0:T(1,128)}, u32[]{:S(2)}) copy-start(s32[1,128,1]{1,2,0:T(1,128)} %param.16) | copy-start | bytes 1540
  12.5 4.2 %copy-start.9 = (s32[1,128]{1,0:T(1,128)S(1)}, s32[1,128]{1,0:T(1,128)}, u32[]{:S(2)}) copy-start(s32[1,128]{1,0:T(1,128)} %param.18) | copy-start | bytes 1540
  12.5 4.2 %copy-start.10 = (s32[1,128]{1,0:T(1,128)S(1)}, s32[1,128]{1,0:T(1,128)}, u32[]{:S(2)}) copy-start(s32[1,128]{1,0:T(1,128)} %param.17) | copy-start | bytes 1540
  12.5 4.2 %copy-start.11 = (s32[1,128]{1,0:T(1,128)S(1)}, s32[1,128]{1,0:T(1,128)}, u32[]{:S(2)}) copy-start(s32[1,128]{1,0:T(1,128)} %param.19) | copy-start | bytes 1540
  19.9 5.9 %copy-start.5 = (f32[1,4,8]{2,1,0:T(4,128)S(1)}, f32[1,4,8]{2,1,0:T(4,128)}, u32[]{:S(2)}) copy-start(f32[1,4,8]{2,1,0:T(4,128)} %param.14) | copy-start | bytes 388
  19.9 43.9 %all-to-all-start = ((f32[16,17,768]{2,1,0:T(8,128)}), f32[16,17,768]{2,1,0:T(8,128)}, u32[]{:S(2)}, u32[]{:S(2)}) async-start(f32[16,17,768]{2,1,0:T(8,128)} %select_maximum_fusion), calls=%async_computation | async-start | bytes 2359296 | tf_op jit(solution)/shard_map/all_to_all | solution.py:141
  29.9 22.1 %collective-permute-start.2 = (f32[13000]{0:T(1024)}, f32[13000]{0:T(1024)S(1)}, u32[]{:S(2)}, u32[]{:S(2)}) collective-permute-start(f32[13000]{0:T(1024)} %reshape.280), channel_id=1, source_target_pairs={{0,4},{4,8},{8,12},{1,5},{5,9},{9,13},{2,6},{6,10},{10,14},{3,7},{... | collective-permute-start | bytes 156008 | tf_op jit(solution)/shard_map/ppermute | solution.py:26
  33.7 20.5 %collective-permute-start.3 = (f32[13000]{0:T(1024)}, f32[13000]{0:T(1024)}, u32[]{:S(2)}, u32[]{:S(2)}) collective-permute-start(f32[13000]{0:T(1024)} %reshape.282), channel_id=1, source_target_pairs={{4,0},{8,4},{12,8},{5,1},{9,5},{13,9},{6,2},{10,6},{14,10},{7,3},{... | collective-permute-start | bytes 156008 | tf_op jit(solution)/shard_map/ppermute | solution.py:26
  55.2 1.0 %copy-start.2 = (f32[25,32,2]{2,1,0:T(8,128)S(1)}, f32[25,32,2]{2,1,0:T(8,128)}, u32[]{:S(2)}) copy-start(f32[25,32,2]{2,1,0:T(8,128)} %reshape.279) | copy-start | bytes 19204
  56.9 0.6 copy-start.6
  56.9 0.7 copy-start.7
  61.1 1.2 %copy-start.1 = (f32[3,8,34,258]{3,2,1,0:T(8,128)}, f32[3,8,34,258]{3,2,1,0:T(8,128)S(1)}, u32[]{:S(2)}) copy-start(f32[3,8,34,258]{3,2,1,0:T(8,128)S(1)} %fusion.6) | copy-start | bytes 2526340
  68.7 7.6 %collective-permute-start.4 = (f32[3,32,256]{2,1,0:T(8,128)S(1)}, f32[3,32,256]{2,1,0:T(8,128)S(1)}, u32[]{:S(2)}, u32[]{:S(2)}) collective-permute-start(f32[3,32,256]{2,1,0:T(8,128)S(1)} %convolution_bitcast_fusion), channel_id=1, source_target_pairs={{0,16},{16,0},{1,17},{17,1},{2,18},{18,2},{3,19},{19,3},{4,20},{20... | collective-permute-start | bytes 294920 | tf_op jit(solution)/shard_map/ppermute | solution.py:150

commit v2 on v1

--- a/solution.py
+++ b/solution.py
@@ -2,6 +2,8 @@
 import jax.numpy as jnp
 from jax import lax
 from jax.sharding import PartitionSpec as P
+from jax.experimental import pallas as pl
+from jax.experimental.pallas import tpu as pltpu
 
 SUBSTEPS = 2
 
@@ -14,6 +16,7 @@
 coriolis_scale = 0.25
 
 HIGHEST = lax.Precision.HIGHEST
+INTERPRET = False
 
 
 def shifted(part, axis, closed, forward):
@@ -27,17 +30,86 @@
     return flat.reshape(part.shape)
 
 
-def with_halo(cells, width):
+def with_halo(cells, width, wide_cols, wide_rows):
+    planes, rows, cols = cells.shape
     head = cells[:, :, :width]
     tail = cells[:, :, -width:]
+    gap = jnp.zeros((planes, rows, wide_cols - cols - 2 * width), cells.dtype)
     cells = jnp.concatenate(
-        [shifted(tail, "lon", True, True), cells, shifted(head, "lon", True, False)], axis=2
+        [cells, shifted(head, "lon", True, False), gap, shifted(tail, "lon", True, True)], axis=2
     )
     head = cells[:, :width, :]
-    tail = cells[:, -width:, :]
+    tail = cells[:, rows - width : rows, :]
+    gap = jnp.zeros((planes, wide_rows - rows - 2 * width, wide_cols), cells.dtype)
     return jnp.concatenate(
-        [shifted(tail, "lat", False, True), cells, shifted(head, "lat", False, False)], axis=1
-    )
+        [cells, shifted(head, "lat", False, False), gap, shifted(tail, "lat", False, True)], axis=1
+    )
+
+
+def stencil_kernel(coef_ref, row_ref, wide_ref, out_ref, mid_ref):
+    field_count, level_count, row_count, col_count = out_ref.shape[1:]
+    wide_rows, wide_cols = wide_ref.shape[1:]
+    turning = row_ref[0]
+    keep = wide_ref[field_count * level_count] * row_ref[1]
+
+    def step(read, write):
+        for field in range(field_count):
+            for level in range(level_count):
+                diffuse = coef_ref[0, 0, level]
+                advect_east = coef_ref[0, 1, level]
+                advect_north = coef_ref[0, 2, level]
+                mixing = coef_ref[0, 3, level]
+                center = read(field, level)
+                north = pltpu.roll(center, wide_rows - 1, 0)
+                south = pltpu.roll(center, 1, 0)
+                east = pltpu.roll(center, wide_cols - 1, 1)
+                west = pltpu.roll(center, 1, 1)
+                above = read(field, min(level + 1, level_count - 1))
+                below = read(field, max(level - 1, 0))
+                laplace = north + south + east + west - 4.0 * center
+                updated = (
+                    center
+                    + diffuse * laplace
+                    - advect_east * (east - west)
+                    - advect_north * (north - south)
+                    + mixing * (above + below - 2.0 * center)
+                )
+                if field == 0:
+                    updated = updated + turning * read(1, level)
+                elif field == 1:
+                    updated = updated + (-turning) * read(0, level)
+                write(field, level, updated * keep)
+
+    def from_wide(field, level):
+        return wide_ref[field * level_count + level]
+
+    def to_mid(field, level, value):
+        mid_ref[field * level_count + level] = value
+
+    def from_mid(field, level):
+        return mid_ref[field * level_count + level]
+
+    def to_out(field, level, value):
+        out_ref[0, field, level] = value[:row_count, :col_count]
+
+    step(from_wide, to_mid)
+    step(from_mid, to_out)
+
+
+def dynamics(coeffs, row_terms, wide, field_count, level_count, row_count, col_count):
+    planes, wide_rows, wide_cols = wide.shape
+    return pl.pallas_call(
+        stencil_kernel,
+        out_shape=jax.ShapeDtypeStruct((1, field_count, level_count, row_count, col_count), jnp.float32),
+        in_specs=[
+            pl.BlockSpec(memory_space=pltpu.SMEM),
+            pl.BlockSpec(memory_space=pltpu.VMEM),
+            pl.BlockSpec(memory_space=pltpu.VMEM),
+        ],
+        out_specs=pl.BlockSpec(memory_space=pltpu.VMEM),
+        scratch_shapes=[pltpu.VMEM((planes - 1, wide_rows, wide_cols), jnp.float32)],
+        interpret=INTERPRET,
+    )(coeffs, row_terms, wide)
 
 
 def surface_export(ground, previous, sea_float, ocean_side):
@@ -52,38 +124,6 @@
         ]
     )
     return jnp.where(ocean_side, ground, bulk_flux) * sea_float
-
-
-def substep(padded, mask_out, top_row, total_rows, level_coef):
-    center = padded[:, :, 1:-1, 1:-1]
-    north = padded[:, :, 2:, 1:-1]
-    south = padded[:, :, :-2, 1:-1]
-    east = padded[:, :, 1:-1, 2:]
-    west = padded[:, :, 1:-1, :-2]
-    diffuse = level_coef[0][None, :, None, None]
-    advect_east = level_coef[1][None, :, None, None]
-    advect_north = level_coef[2][None, :, None, None]
-    mixing = level_coef[3][None, :, None, None]
-    laplace = north + south + east + west - 4.0 * center
-    above = jnp.concatenate([center[:, 1:], center[:, -1:]], 1)
-    below = jnp.concatenate([center[:, :1], center[:, :-1]], 1)
-    height = center.shape[2]
-    row_index = top_row + jnp.arange(height, dtype=jnp.int32)
-    latitude = jnp.pi * (
-        -1.0 / 3.0 + 2.0 / 3.0 * (row_index.astype(center.dtype) + 0.5) / total_rows
-    )
-    coriolis = (coriolis_scale * jnp.sin(latitude))[:, None]
-    turning = jnp.stack([coriolis * center[1], -coriolis * center[0], jnp.zeros_like(center[2])])
-    inside = ((row_index >= 0) & (row_index < total_rows)).astype(center.dtype)[:, None]
-    updated = (
-        center
-        + diffuse * laplace
-        - advect_east * (east - west)
-        - advect_north * (north - south)
-        + mixing * (above + below - 2.0 * center)
-        + turning
-    )
-    return updated * (mask_out * inside)
 
 
 def body(
@@ -157,17 +197,19 @@
     planes = jnp.concatenate(
         [fields.reshape(field_count * level_count, row_count, col_count), state_mask[None]], 0
     )
-    planes = with_halo(planes, SUBSTEPS)
-    mask_wide = planes[-1]
-    fields = planes[:-1].reshape(
-        field_count, level_count, row_count + 2 * SUBSTEPS, col_count + 2 * SUBSTEPS
-    )
-    for substep_index in range(SUBSTEPS):
-        halo = SUBSTEPS - substep_index - 1
-        edge = substep_index + 1
-        mask_out = mask_wide[edge : mask_wide.shape[0] - edge, edge : mask_wide.shape[1] - edge]
-        fields = substep(fields, mask_out, first_row - halo, total_rows, level_coef)
-    return (fields[None], imported[None])
+    wide_rows = -(-(row_count + 4 * SUBSTEPS) // 8) * 8
+    wide_cols = -(-(col_count + 4 * SUBSTEPS) // 128) * 128
+    wide = with_halo(planes, SUBSTEPS, wide_cols, wide_rows)
+    local = jnp.arange(wide_rows, dtype=jnp.int32)
+    row_index = first_row + jnp.where(local < wide_rows // 2 + row_count // 2, local, local - wide_rows)
+    latitude = jnp.pi * (
+        -1.0 / 3.0 + 2.0 / 3.0 * (row_index.astype(jnp.float32) + 0.5) / total_rows
+    )
+    coriolis = coriolis_scale * jnp.sin(latitude)
+    inside = ((row_index >= 0) & (row_index < total_rows)).astype(jnp.float32)
+    row_terms = jnp.broadcast_to(jnp.stack([coriolis, inside])[:, :, None], (2, wide_rows, wide_cols))
+    fields = dynamics(coeffs, row_terms, wide, field_count, level_count, row_count, col_count)
+    return (fields, imported[None])
 
 
 def solution(mesh):

time: 77.8 us -> 65.9 us (0.85)
  other arithmetic: 19.6 us -> 10.6 us
  waiting for transfers between devices: 17.3 us -> 12.8 us
  Pallas kernels: 0 us -> 4.33 us
  local copies, waits for them, and re-layouts: 19.4 us -> 15.3 us
  matrix products: 4.45 us -> 6.23 us
    broadcast_in_dim x2 -> x1, other arithmetic: 6.78 us -> 1.54 us  [body(): return (fields, imported[None])]
    ppermute x4, waiting for transfers between devices: 17.3 us -> 12.8 us  [shifted(): flat = lax.ppermute(part.reshape(-1), axis, route)]
    pallas_call x0 -> x1, Pallas kernels: none -> 4.33 us  [dynamics(): pl.pallas_call(stencil_kernel, out_shape=jax.ShapeDtypeStruct((1, field_c...]
    slice x5 -> x0, local copies, waits for them, and re-layouts: 3.49 us -> none  [the longest x4 3.39 us: substep(): below = jnp.concatenate([center[:, :1], center[:, :-1]], 1)]
    mul x7 -> x1, other arithmetic: 3.09 us -> 0.05 us  [body(): coriolis = coriolis_scale * jnp.sin(latitude)]
    concatenate x1, other arithmetic: 0.64 us -> 2.6 us  [with_halo(): jnp.concatenate([cells, shifted(head, 'lat', False, False), gap, shifted(...]
    dot_general x1, matrix products: 0.5 us -> 2.28 us  [body(): summed_here = jnp.dot(selector, arrived_pieces, precision=HIGHEST)]
    concatenate x1, other arithmetic: 0.06 us -> 1.16 us  [body(): fields = jnp.concatenate([ground[:, None], fields[:, 1:]], 1)]
  transfers between devices with their start and end apart: 6 -> 6, of which waited for: 2 -> 3; matrix products, arithmetic and copies ran while one was open for 41% -> 20% of each run, Pallas kernels for 0% -> 7%
where the time goes in v2:
time: 65.9 us; the launch traced here: 65.1 us
  local copies, waits for them, and re-layouts  15.3 us (23%)
  starting transfers between devices  14.9 us (23%)
  waiting for transfers between devices  12.8 us (19%)
  other arithmetic  10.6 us (16%)
  matrix products  6.23 us (9%)
  Pallas kernels  4.33 us (7%)
  between operations  0.9 us (1%)
    ppermute x4, waiting for transfers between devices, shifted(): flat = lax.ppermute(part.reshape(-1), axis, route)  12.8 us
    ppermute x4, starting transfers between devices, shifted(): flat = lax.ppermute(part.reshape(-1), axis, route)  6.82 us
    all_to_all x1, starting transfers between devices, body(): lax.all_to_all(outgoing, ('lat', 'lon'), split_axis=0, concat_axis=0, til...  6.74 us
    pallas_call x1, Pallas kernels, dynamics(): pl.pallas_call(stencil_kernel, out_shape=jax.ShapeDtypeStruct((1, field_c...  4.33 us
    reshape x4, local copies, waits for them, and re-layouts, shifted(): flat = lax.ppermute(part.reshape(-1), axis, route)  2.85 us
    concatenate x1, other arithmetic, with_halo(): jnp.concatenate([cells, shifted(head, 'lat', False, False), gap, shifted(...  2.6 us
    reshape x4, local copies, waits for them, and re-layouts, shifted(): return flat.reshape(part.shape)  2.45 us
    dot_general x1, local copies, waits for them, and re-layouts, body(): summed_here = jnp.dot(selector, arrived_pieces, precision=HIGHEST)  2.33 us
  transfers between devices with their start and end apart: 6, of which 3 were waited for; matrix products, arithmetic and copies ran while one was open for 20% of the time, Pallas kernels for 7%

profile of v2, /device:TPU:13, one launch (start us, length us, event | category | flops | bytes accessed | tf_op | source)
XLA Modules:
  0.0 65.1 jit_solution(17190467319219243571)
XLA Ops:
  0.7 0.9 %convert_bitcast_fusion = f32[32,256]{1,0:T(8,128)S(1)} fusion(s32[1,32,256]{2,1,0:T(8,128)} %param.13), kind=kLoop, calls=%fused_computation.50 | loop fusion | flops 8192 | bytes 65536 | tf_op jit(solution)/shard_map/mul | solution.py:194
  2.4 2.2 %fusion.2 = f32[8,32,3,256]{3,1,0,2:T(8,128)S(1)} fusion(f32[1,8,256,256]{3,2,1,0:T(8,128)S(1)} %copy-done, f32[1,1,32,256]{3,2,1,0:T(8,128)S(1)} %get-tuple-element.19, f32[1,1,32,256]{3,2,1,0:T(8,128)S(1)} %get-tuple-element.20, f32[1,1,32,256]{3,2,1,0:T(8,128)S(1)} %get-tuple-element.18, f32[3,8,32,256]{3,2,1,0:T(8,128)} %bitcast.52, ...), kind=kOutput, calls=%fused_computation.3 | convolution fusion | flops 604078080 | bytes 3112961 | tf_op jit(solution)/shard_map/crx,txy->trcy/dot_general | solution.py:154
  5.3 1.4 %reshape.280 = f32[256,768,1]{1,0,2:T(8,128)} reshape(f32[8,32,3,256]{3,2,1,0:T(4,128)S(1)} %copy.14) | data formatting | bytes 1572864 | tf_op jit(solution)/shard_map/reshape | solution.py:155
  7.3 1.7 %fusion.7 = f32[16,16,768]{2,1,0:T(8,128)S(1)} fusion(f32[256,768,1]{1,0,2:T(8,128)} %reshape.280, s32[16,16]{1,0:T(8,128)S(1)} %sub.52), kind=kOutput, calls=%fused_computation.14 | convolution fusion | flops 604045312 | bytes 1573888 | tf_op jit(solution)/shard_map/dot_general | solution.py:173
  9.0 1.1 %select_maximum_fusion = f32[16,17,768]{2,1,0:T(8,128)} fusion(f32[16,1,16]{2,1,0:T(1,128)S(1)} %convert_element_type.47, f32[16,16,768]{2,1,0:T(8,128)S(1)} %fusion.7), kind=kLoop, calls=%fused_computation.4 | loop fusion | flops 626688 | bytes 1623040 | tf_op jit(solution)/shard_map/concatenate | solution.py:178
  10.1 6.7 %all-to-all-start = ((f32[16,17,768]{2,1,0:T(8,128)}), f32[16,17,768]{2,1,0:T(8,128)}, u32[]{:S(2)}, u32[]{:S(2)}) async-start(f32[16,17,768]{2,1,0:T(8,128)} %select_maximum_fusion), calls=%async_computation | async-start | bytes 2359296 | tf_op jit(solution)/shard_map/all_to_all | solution.py:181
  16.9 0.9 %slice.91 = f32[3,7,32,256]{3,2,1,0:T(8,128)} slice(f32[3,8,32,256]{3,2,1,0:T(8,128)S(1)} %bitcast.53), slice={[0:3], [1:8], [0:32], [0:256]} | slice | bytes 1376256 | tf_op jit(solution)/shard_map/slice | solution.py:195
  17.8 1.2 %pad_maximum_fusion.1 = f32[3,8,32,256]{3,2,1,0:T(8,128)S(1)} fusion(f32[3,7,32,256]{3,2,1,0:T(8,128)} %slice.91, f32[3,1,32,256]{3,2,1,0:T(8,128)S(1)} %fusion.18), kind=kLoop, calls=%fused_computation.9 | loop fusion | flops 196608 | bytes 1572864 | tf_op jit(solution)/shard_map/concatenate | solution.py:195
  19.9 1.2 %reshape.268 = f32[1600]{0:T(1024)S(1)} reshape(f32[25,32,2]{2,1,0:T(8,128)} %get-tuple-element.21) | data formatting | bytes 12800 | tf_op jit(solution)/shard_map/reshape | solution.py:29
  21.1 1.2 %collective-permute-start = (f32[1600]{0:T(1024)S(1)}, f32[1600]{0:T(1024)S(1)}, u32[]{:S(2)}, u32[]{:S(2)}) collective-permute-start(f32[1600]{0:T(1024)S(1)} %reshape.268), channel_id=1, source_target_pairs={{1,0},{2,1},{3,2},{0,3},{5,4},{6,5},{7,6},{4,7},{9,8},{10,9},{11,1... | collective-permute-start | bytes 19208 | tf_op jit(solution)/shard_map/ppermute | solution.py:29
  24.0 2.4 %collective-permute-done.1 = f32[1600]{0:T(1024)S(1)} collective-permute-done((f32[1600]{0:T(1024)S(1)}, f32[1600]{0:T(1024)S(1)}, u32[]{:S(2)}, u32[]{:S(2)}) %collective-permute-start.1) | collective-permute-done | bytes 6432 | tf_op jit(solution)/shard_map/ppermute | solution.py:29
  26.4 1.1 %reshape.271 = f32[25,32,2]{2,1,0:T(8,128)} reshape(f32[1600]{0:T(1024)S(1)} %collective-permute-done.1) | data formatting | bytes 12800 | tf_op jit(solution)/shard_map/reshape | solution.py:30
  28.3 1.1 %pad_maximum_fusion.7 = (f32[25,2,384]{2,1,0:T(2,128)S(1)}, f32[25,2,384]{2,1,0:T(2,128)S(1)}) fusion(f32[25,32,2]{2,1,0:T(8,128)} %reshape.271, f32[25,32,124]{2,1,0:T(8,128)S(1)} %broadcast_in_dim.12, f32[25,32,2]{2,1,0:T(8,128)S(1)} %reshape.269, f32[1,32,256]{2,1,0:T(8,128)S(1)} %convert_select_fusion, f32[24,32,256]{2,1,0:T(8,128)S(1)} %bitcast.47), kind=kLoop, calls=%fused_computation.35 | loop fusion | flops 153600 | bytes 1382400 | tf_op jit(solution)/shard_map/slice | solution.py:41
  30.2 2.2 %collective-permute-start.2 = (f32[19200]{0:T(1024)}, f32[19200]{0:T(1024)S(1)}, u32[]{:S(2)}, u32[]{:S(2)}) collective-permute-start(f32[19200]{0:T(1024)} %reshape.272), channel_id=1, source_target_pairs={{4,0},{8,4},{12,8},{5,1},{9,5},{13,9},{6,2},{10,6},{14,10},{7,3},{... | collective-permute-start | bytes 230408 | tf_op jit(solution)/shard_map/ppermute | solution.py:29
  33.0 3.1 %collective-permute-start.3 = (f32[19200]{0:T(1024)}, f32[19200]{0:T(1024)}, u32[]{:S(2)}, u32[]{:S(2)}) collective-permute-start(f32[19200]{0:T(1024)} %reshape.274), channel_id=1, source_target_pairs={{0,4},{4,8},{8,12},{1,5},{5,9},{9,13},{2,6},{6,10},{10,14},{3,7},{... | collective-permute-start | bytes 230408 | tf_op jit(solution)/shard_map/ppermute | solution.py:29
  36.1 9.8 %collective-permute-done.2 = f32[19200]{0:T(1024)S(1)} collective-permute-done((f32[19200]{0:T(1024)}, f32[19200]{0:T(1024)S(1)}, u32[]{:S(2)}, u32[]{:S(2)}) %collective-permute-start.2) | collective-permute-done | bytes 76832 | tf_op jit(solution)/shard_map/ppermute | solution.py:29
  46.0 0.9 %reshape.275 = f32[25,2,384]{2,1,0:T(2,128)S(1)} reshape(f32[19200]{0:T(1024)} %collective-permute-done.3) | data formatting | bytes 153600 | tf_op jit(solution)/shard_map/reshape | solution.py:30
  47.0 2.1 %slice.98 = f32[16,16,768]{2,1,0:T(8,128)} slice(f32[16,17,768]{2,1,0:T(8,128)} %all-to-all-done), slice={[0:16], [0:16], [0:768]} | slice | bytes 1572864 | tf_op jit(solution)/shard_map/slice | solution.py:184
  49.0 2.3 %copy.15 = f32[768,256]{1,0:T(8,128)} copy(f32[768,256]{0,1:T(8,128)} %bitcast.50) | data formatting | bytes 1572864 | tf_op jit(solution)/shard_map/dot_general | solution.py:188
  52.3 2.3 %convolution_bitcast_fusion = f32[3,32,256]{2,1,0:T(8,128)} fusion(f32[3,256,256]{2,1,0:T(8,128)} %bitcast.49, f32[256]{0:T(256)S(1)} %eq.84), kind=kOutput, calls=%fused_computation.6 | convolution fusion | flops 75505664 | bytes 885760 | tf_op jit(solution)/shard_map/dot_general | solution.py:188
  54.6 1.3 %collective-permute-start.4 = (f32[3,32,256]{2,1,0:T(8,128)}, f32[3,32,256]{2,1,0:T(8,128)}, u32[]{:S(2)}, u32[]{:S(2)}) collective-permute-start(f32[3,32,256]{2,1,0:T(8,128)} %convolution_bitcast_fusion), channel_id=1, source_target_pairs={{0,16},{16,0},{1,17},{17,1},{2,18},{18,2},{3,19},{19,3},{4,20},{20... | collective-permute-start | bytes 294920 | tf_op jit(solution)/shard_map/ppermute | solution.py:190
  55.9 2.6 %pad_maximum_fusion.wide_ref = f32[25,40,384]{2,1,0:T(8,128)} fusion(f32[25,2,384]{2,1,0:T(2,128)S(1)} %reshape.275, f32[25,2,384]{2,1,0:T(2,128)S(1)} %reshape.273, f32[25,32,2]{2,1,0:T(8,128)} %reshape.271, f32[25,32,124]{2,1,0:T(8,128)} %copy-done.1, f32[25,32,2]{2,1,0:T(8,128)S(1)} %reshape.269, f32[1,32,256]{2,1,0:T(8,128)S(1)} %convert_select_fusion, ...), kind=kLoop, calls=%fused_computation.2 | loop fusion | flops 2688000 | bytes 2918560 | tf_op jit(solution)/shard_map/concatenate | solution.py:44
  59.3 4.3 %shard_map.104 = f32[1,3,8,32,256]{4,3,2,1,0:T(8,128)} custom-call(f32[1,4,8]{2,1,0:T(4,128)} %coef_ref.1, f32[2,40,384]{2,1,0:T(8,128)} %broadcast_in_dim.10.row_ref, f32[25,40,384]{2,1,0:T(8,128)} %pad_maximum_fusion.wide_ref), custom_call_target="tpu_custom_call" | custom-call | tf_op jit(solution)/shard_map/pallas_call | solution.py:101
  63.6 1.5 %multiply_bitcast_fusion = f32[1,3,32,256]{3,2,1,0:T(8,128)} fusion(f32[3,32,256]{2,1,0:T(8,128)} %collective-permute-done.4, f32[32,256]{1,0:T(8,128)S(1)} %convert_bitcast_fusion), kind=kLoop, calls=%fused_computation.29 | loop fusion | flops 24576 | bytes 229376 | tf_op jit(solution)/shard_map/broadcast_in_dim | solution.py:212
  (50 shorter events, 8.5 us)
Async XLA Ops:
  0.6 1.8 %copy-start = (f32[1,8,256,256]{3,2,1,0:T(8,128)S(1)}, f32[1,8,256,256]{3,2,1,0:T(8,128)}, u32[]{:S(2)}) copy-start(f32[1,8,256,256]{3,2,1,0:T(8,128)} %param.15) | copy-start | bytes 6291460
  4.7 2.0 %copy-start.5 = (s32[1,128,1]{1,2,0:T(1,128)S(1)}, s32[1,128,1]{1,2,0:T(1,128)}, u32[]{:S(2)}) copy-start(s32[1,128,1]{1,2,0:T(1,128)} %param.16) | copy-start | bytes 1540
  4.7 2.2 %copy-start.6 = (s32[1,128]{1,0:T(1,128)S(1)}, s32[1,128]{1,0:T(1,128)}, u32[]{:S(2)}) copy-start(s32[1,128]{1,0:T(1,128)} %param.18) | copy-start | bytes 1540
  4.7 2.2 %copy-start.7 = (s32[1,128]{1,0:T(1,128)S(1)}, s32[1,128]{1,0:T(1,128)}, u32[]{:S(2)}) copy-start(s32[1,128]{1,0:T(1,128)} %param.17) | copy-start | bytes 1540
  4.7 2.2 %copy-start.8 = (s32[1,128]{1,0:T(1,128)S(1)}, s32[1,128]{1,0:T(1,128)}, u32[]{:S(2)}) copy-start(s32[1,128]{1,0:T(1,128)} %param.19) | copy-start | bytes 1540
  10.1 6.7 %copy-start.2 = (f32[1,3,8,32,256]{4,3,2,1,0:T(8,128)S(1)}, f32[1,3,8,32,256]{4,3,2,1,0:T(8,128)}, u32[]{:S(2)}) copy-start(f32[1,3,8,32,256]{4,3,2,1,0:T(8,128)} %param.11) | copy-start | bytes 2359300
  10.1 7.7 %copy-start.3 = (f32[1,3,32,256]{3,2,1,0:T(8,128)S(1)}, f32[1,3,32,256]{3,2,1,0:T(8,128)}, u32[]{:S(2)}) copy-start(f32[1,3,32,256]{3,2,1,0:T(8,128)} %param.12) | copy-start | bytes 294916
  10.1 36.8 %all-to-all-start = ((f32[16,17,768]{2,1,0:T(8,128)}), f32[16,17,768]{2,1,0:T(8,128)}, u32[]{:S(2)}, u32[]{:S(2)}) async-start(f32[16,17,768]{2,1,0:T(8,128)} %select_maximum_fusion), calls=%async_computation | async-start | bytes 2359296 | tf_op jit(solution)/shard_map/all_to_all | solution.py:181
  16.9 2.1 %copy-start.4 = (s32[1,32,256]{2,1,0:T(8,128)S(1)}, s32[1,32,256]{2,1,0:T(8,128)}, u32[]{:S(2)}) copy-start(s32[1,32,256]{2,1,0:T(8,128)} %param.13) | copy-start | bytes 98308
  21.1 2.5 %collective-permute-start = (f32[1600]{0:T(1024)S(1)}, f32[1600]{0:T(1024)S(1)}, u32[]{:S(2)}, u32[]{:S(2)}) collective-permute-start(f32[1600]{0:T(1024)S(1)} %reshape.268), channel_id=1, source_target_pairs={{1,0},{2,1},{3,2},{0,3},{5,4},{6,5},{7,6},{4,7},{9,8},{10,9},{11,1... | collective-permute-start | bytes 19208 | tf_op jit(solution)/shard_map/ppermute | solution.py:29
  22.6 3.8 %collective-permute-start.1 = (f32[1600]{0:T(1024)S(1)}, f32[1600]{0:T(1024)S(1)}, u32[]{:S(2)}, u32[]{:S(2)}) collective-permute-start(f32[1600]{0:T(1024)S(1)} %reshape.270), channel_id=1, source_target_pairs={{0,1},{1,2},{2,3},{3,0},{4,5},{5,6},{6,7},{7,4},{8,9},{9,10},{10,1... | collective-permute-start | bytes 19208 | tf_op jit(solution)/shard_map/ppermute | solution.py:29
  27.6 0.8 %copy-start.1 = (f32[25,32,124]{2,1,0:T(8,128)}, f32[25,32,124]{2,1,0:T(8,128)S(1)}, u32[]{:S(2)}) copy-start(f32[25,32,124]{2,1,0:T(8,128)S(1)} %broadcast_in_dim.12) | copy-start | bytes 1190404
  30.2 15.8 %collective-permute-start.2 = (f32[19200]{0:T(1024)}, f32[19200]{0:T(1024)S(1)}, u32[]{:S(2)}, u32[]{:S(2)}) collective-permute-start(f32[19200]{0:T(1024)} %reshape.272), channel_id=1, source_target_pairs={{4,0},{8,4},{12,8},{5,1},{9,5},{13,9},{6,2},{10,6},{14,10},{7,3},{... | collective-permute-start | bytes 230408 | tf_op jit(solution)/shard_map/ppermute | solution.py:29
  33.0 13.0 %collective-permute-start.3 = (f32[19200]{0:T(1024)}, f32[19200]{0:T(1024)}, u32[]{:S(2)}, u32[]{:S(2)}) collective-permute-start(f32[19200]{0:T(1024)} %reshape.274), channel_id=1, source_target_pairs={{0,4},{4,8},{8,12},{1,5},{5,9},{9,13},{2,6},{6,10},{10,14},{3,7},{... | collective-permute-start | bytes 230408 | tf_op jit(solution)/shard_map/ppermute | solution.py:29
  54.6 9.0 %collective-permute-start.4 = (f32[3,32,256]{2,1,0:T(8,128)}, f32[3,32,256]{2,1,0:T(8,128)}, u32[]{:S(2)}, u32[]{:S(2)}) collective-permute-start(f32[3,32,256]{2,1,0:T(8,128)} %convolution_bitcast_fusion), channel_id=1, source_target_pairs={{0,16},{16,0},{1,17},{17,1},{2,18},{18,2},{3,19},{19,3},{4,20},{20... | collective-permute-start | bytes 294920 | tf_op jit(solution)/shard_map/ppermute | solution.py:190

commit v3 on v2

--- a/solution.py
+++ b/solution.py
@@ -112,6 +112,36 @@
     )(coeffs, row_terms, wide)
 
 
+def gather_kernel(arrived_ref, out_ref):
+    peer_count, tagged, width = arrived_ref.shape
+    slot_count = tagged - 1
+    field_count, row_count, col_count = out_ref.shape
+    row_ids = lax.broadcasted_iota(jnp.int32, (row_count, slot_count), 0).astype(jnp.float32)
+
+    def one_peer(peer, total):
+        block = arrived_ref[peer]
+        selector = (block[slot_count : slot_count + 1, :slot_count] == row_ids).astype(jnp.float32)
+        return total + jnp.dot(
+            selector, block[:slot_count, :], precision=HIGHEST, preferred_element_type=jnp.float32
+        )
+
+    total = lax.fori_loop(
+        0, peer_count, one_peer, jnp.zeros((row_count, width), jnp.float32), unroll=peer_count <= 16
+    )
+    for field in range(field_count):
+        out_ref[field] = total[:, field * col_count : (field + 1) * col_count]
+
+
+def gathered(arrived, field_count, row_count, col_count):
+    return pl.pallas_call(
+        gather_kernel,
+        out_shape=jax.ShapeDtypeStruct((field_count, row_count, col_count), jnp.float32),
+        in_specs=[pl.BlockSpec(memory_space=pltpu.VMEM)],
+        out_specs=pl.BlockSpec(memory_space=pltpu.VMEM),
+        interpret=INTERPRET,
+    )(arrived)
+
+
 def surface_export(ground, previous, sea_float, ocean_side):
     slip_east = ground[0] - previous[0]
     slip_north = ground[1] - previous[1]
@@ -180,13 +210,7 @@
     ).reshape(peer_count * (slot_count + 1), width)
     arrived = lax.all_to_all(outgoing, ("lat", "lon"), split_axis=0, concat_axis=0, tiled=True)
     arrived = arrived.reshape(peer_count, slot_count + 1, width)
-    arrived_rows = arrived[:, slot_count, :slot_count].reshape(-1)
-    arrived_pieces = arrived[:, :slot_count, :].reshape(peer_count * slot_count, width)
-    selector = (
-        arrived_rows[None, :] == jnp.arange(row_count, dtype=jnp.float32)[:, None]
-    ).astype(jnp.float32)
-    summed_here = jnp.dot(selector, arrived_pieces, precision=HIGHEST)
-    summed_here = summed_here.reshape(row_count, field_count, col_count).transpose(1, 0, 2)
+    summed_here = gathered(arrived, field_count, row_count, col_count)
     imported = lax.ppermute(summed_here, "grp", [(0, 1), (1, 0)]) * sea_float
 
     gain = jnp.where(ocean_side, ocean_gain, air_gain)

time: 65.9 us -> 61.4 us (0.932)
  local copies, waits for them, and re-layouts: 15.3 us -> 9.97 us
  Pallas kernels: 4.33 us -> 7.6 us
  matrix products: 6.23 us -> 3.95 us
    pallas_call x0 -> x1, Pallas kernels: none -> 3.27 us  [gathered(): pl.pallas_call(gather_kernel, out_shape=jax.ShapeDtypeStruct((field_count...]
    slice x2 -> x0, local copies, waits for them, and re-layouts: 2.94 us -> none  [the longest x1 2.08 us: body(): arrived[:, :slot_count, :].reshape(peer_count * slot_count, width)]
    dot_general x1 -> x0, local copies, waits for them, and re-layouts: 2.33 us -> none  [body(): summed_here = jnp.dot(selector, arrived_pieces, precision=HIGHEST)]
    dot_general x1 -> x0, matrix products: 2.28 us -> none  [body(): summed_here = jnp.dot(selector, arrived_pieces, precision=HIGHEST)]
  transfers between devices with their start and end apart: 6 -> 6, of which waited for: 3 -> 3; matrix products, arithmetic and copies ran while one was open for 20% -> 21% of each run, Pallas kernels for 7% -> 7%
where the time goes in v3:
time: 61.4 us; the launch traced here: 60.8 us
  starting transfers between devices  14.9 us (24%)
  waiting for transfers between devices  12.8 us (21%)
  other arithmetic  10.6 us (17%)
  local copies, waits for them, and re-layouts  9.97 us (16%)
  Pallas kernels  7.6 us (12%)
  matrix products  3.95 us (6%)
  between operations  0.9 us (1%)
    ppermute x4, waiting for transfers between devices, shifted(): flat = lax.ppermute(part.reshape(-1), axis, route)  12.8 us
    ppermute x4, starting transfers between devices, shifted(): flat = lax.ppermute(part.reshape(-1), axis, route)  6.82 us
    all_to_all x1, starting transfers between devices, body(): lax.all_to_all(outgoing, ('lat', 'lon'), split_axis=0, concat_axis=0, til...  6.74 us
    pallas_call x1, Pallas kernels, dynamics(): pl.pallas_call(stencil_kernel, out_shape=jax.ShapeDtypeStruct((1, field_c...  4.33 us
    pallas_call x1, Pallas kernels, gathered(): pl.pallas_call(gather_kernel, out_shape=jax.ShapeDtypeStruct((field_count...  3.27 us
    reshape x4, local copies, waits for them, and re-layouts, shifted(): flat = lax.ppermute(part.reshape(-1), axis, route)  2.85 us
    concatenate x1, other arithmetic, with_halo(): jnp.concatenate([cells, shifted(head, 'lat', False, False), gap, shifted(...  2.6 us
    reshape x4, local copies, waits for them, and re-layouts, shifted(): return flat.reshape(part.shape)  2.45 us
  transfers between devices with their start and end apart: 6, of which 3 were waited for; matrix products, arithmetic and copies ran while one was open for 21% of the time, Pallas kernels for 7%

profile of v3, /device:TPU:13, one launch (start us, length us, event | category | flops | bytes accessed | tf_op | source)
XLA Modules:
  0.0 60.8 jit_solution(4852866270288995577)
XLA Ops:
  0.7 0.9 %convert_bitcast_fusion = f32[32,256]{1,0:T(8,128)S(1)} fusion(s32[1,32,256]{2,1,0:T(8,128)} %param.13), kind=kLoop, calls=%fused_computation.48 | loop fusion | flops 8192 | bytes 65536 | tf_op jit(solution)/shard_map/mul | solution.py:218
  1.6 0.9 %fusion.25 = (f32[1,1,32,256]{3,2,1,0:T(8,128)S(1)}, f32[1,1,32,256]{3,2,1,0:T(8,128)S(1)}, f32[1,1,32,256]{3,2,1,0:T(8,128)S(1)}) fusion(f32[1,3,32,256]{3,2,1,0:T(8,128)} %param.12, f32[3,8,32,256]{3,2,1,0:T(8,128)} %bitcast.39), kind=kLoop, calls=%fused_computation.46 | loop fusion | flops 90112 | bytes 294912 | tf_op jit(solution)/shard_map/mul | solution.py:151
  2.4 2.2 %fusion.2 = f32[8,32,3,256]{3,1,0,2:T(8,128)S(1)} fusion(f32[1,8,256,256]{3,2,1,0:T(8,128)S(1)} %copy-done, f32[1,1,32,256]{3,2,1,0:T(8,128)S(1)} %get-tuple-element.19, f32[1,1,32,256]{3,2,1,0:T(8,128)S(1)} %get-tuple-element.20, f32[1,1,32,256]{3,2,1,0:T(8,128)S(1)} %get-tuple-element.18, f32[3,8,32,256]{3,2,1,0:T(8,128)} %bitcast.40, ...), kind=kOutput, calls=%fused_computation.3 | convolution fusion | flops 604078080 | bytes 3112961 | tf_op jit(solution)/shard_map/crx,txy->trcy/dot_general | solution.py:184
  5.3 1.4 %reshape.273 = f32[256,768,1]{1,0,2:T(8,128)} reshape(f32[8,32,3,256]{3,2,1,0:T(4,128)S(1)} %copy.12) | data formatting | bytes 1572864 | tf_op jit(solution)/shard_map/reshape | solution.py:185
  7.3 1.7 %fusion.7 = f32[16,16,768]{2,1,0:T(8,128)S(1)} fusion(f32[256,768,1]{1,0,2:T(8,128)} %reshape.273, s32[16,16]{1,0:T(8,128)S(1)} %sub.52), kind=kOutput, calls=%fused_computation.13 | convolution fusion | flops 604045312 | bytes 1573888 | tf_op jit(solution)/shard_map/dot_general | solution.py:203
  9.0 1.1 %select_maximum_fusion = f32[16,17,768]{2,1,0:T(8,128)} fusion(f32[16,1,16]{2,1,0:T(1,128)S(1)} %convert_element_type.46, f32[16,16,768]{2,1,0:T(8,128)S(1)} %fusion.7), kind=kLoop, calls=%fused_computation.4 | loop fusion | flops 626688 | bytes 1623040 | tf_op jit(solution)/shard_map/concatenate | solution.py:208
  10.1 6.7 %all-to-all-start = ((f32[16,17,768]{2,1,0:T(8,128)}), f32[16,17,768]{2,1,0:T(8,128)}, u32[]{:S(2)}, u32[]{:S(2)}) async-start(f32[16,17,768]{2,1,0:T(8,128)} %select_maximum_fusion), calls=%async_computation | async-start | bytes 2359296 | tf_op jit(solution)/shard_map/all_to_all | solution.py:211
  16.9 0.9 %slice.83 = f32[3,7,32,256]{3,2,1,0:T(8,128)} slice(f32[3,8,32,256]{3,2,1,0:T(8,128)S(1)} %bitcast.41), slice={[0:3], [1:8], [0:32], [0:256]} | slice | bytes 1376256 | tf_op jit(solution)/shard_map/slice | solution.py:219
  17.8 1.2 %pad_maximum_fusion.1 = f32[3,8,32,256]{3,2,1,0:T(8,128)S(1)} fusion(f32[3,7,32,256]{3,2,1,0:T(8,128)} %slice.83, f32[3,1,32,256]{3,2,1,0:T(8,128)S(1)} %fusion.18), kind=kLoop, calls=%fused_computation.8 | loop fusion | flops 196608 | bytes 1572864 | tf_op jit(solution)/shard_map/concatenate | solution.py:219
  19.0 0.9 %fusion.5 = (f32[25,32,2]{2,1,0:T(8,128)}, f32[25,32,2]{2,1,0:T(8,128)S(1)}) fusion(f32[24,32,256]{2,1,0:T(8,128)S(1)} %bitcast.36, f32[1,32,256]{2,1,0:T(8,128)S(1)} %convert_select_fusion), kind=kLoop, calls=%fused_computation.9 | loop fusion | flops 3200 | bytes 832000 | tf_op jit(solution)/shard_map/concatenate | solution.py:221
  19.8 1.2 %reshape.262 = f32[1600]{0:T(1024)S(1)} reshape(f32[25,32,2]{2,1,0:T(8,128)} %get-tuple-element.21) | data formatting | bytes 12800 | tf_op jit(solution)/shard_map/reshape | solution.py:29
  21.1 1.2 %collective-permute-start = (f32[1600]{0:T(1024)S(1)}, f32[1600]{0:T(1024)S(1)}, u32[]{:S(2)}, u32[]{:S(2)}) collective-permute-start(f32[1600]{0:T(1024)S(1)} %reshape.262), channel_id=1, source_target_pairs={{1,0},{2,1},{3,2},{0,3},{5,4},{6,5},{7,6},{4,7},{9,8},{10,9},{11,1... | collective-permute-start | bytes 19208 | tf_op jit(solution)/shard_map/ppermute | solution.py:29
  24.0 2.4 %collective-permute-done.1 = f32[1600]{0:T(1024)S(1)} collective-permute-done((f32[1600]{0:T(1024)S(1)}, f32[1600]{0:T(1024)S(1)}, u32[]{:S(2)}, u32[]{:S(2)}) %collective-permute-start.1) | collective-permute-done | bytes 6432 | tf_op jit(solution)/shard_map/ppermute | solution.py:29
  26.4 1.1 %reshape.265 = f32[25,32,2]{2,1,0:T(8,128)} reshape(f32[1600]{0:T(1024)S(1)} %collective-permute-done.1) | data formatting | bytes 12800 | tf_op jit(solution)/shard_map/reshape | solution.py:30
  28.3 1.1 %pad_maximum_fusion.7 = (f32[25,2,384]{2,1,0:T(2,128)S(1)}, f32[25,2,384]{2,1,0:T(2,128)S(1)}) fusion(f32[25,32,2]{2,1,0:T(8,128)} %reshape.265, f32[25,32,124]{2,1,0:T(8,128)S(1)} %broadcast_in_dim.12, f32[25,32,2]{2,1,0:T(8,128)S(1)} %reshape.263, f32[1,32,256]{2,1,0:T(8,128)S(1)} %convert_select_fusion, f32[24,32,256]{2,1,0:T(8,128)S(1)} %bitcast.37), kind=kLoop, calls=%fused_computation.34 | loop fusion | flops 153600 | bytes 1382400 | tf_op jit(solution)/shard_map/slice | solution.py:41
  30.1 2.2 %collective-permute-start.2 = (f32[19200]{0:T(1024)}, f32[19200]{0:T(1024)S(1)}, u32[]{:S(2)}, u32[]{:S(2)}) collective-permute-start(f32[19200]{0:T(1024)} %reshape.266), channel_id=1, source_target_pairs={{4,0},{8,4},{12,8},{5,1},{9,5},{13,9},{6,2},{10,6},{14,10},{7,3},{... | collective-permute-start | bytes 230408 | tf_op jit(solution)/shard_map/ppermute | solution.py:29
  33.0 3.1 %collective-permute-start.3 = (f32[19200]{0:T(1024)}, f32[19200]{0:T(1024)}, u32[]{:S(2)}, u32[]{:S(2)}) collective-permute-start(f32[19200]{0:T(1024)} %reshape.268), channel_id=1, source_target_pairs={{0,4},{4,8},{8,12},{1,5},{5,9},{9,13},{2,6},{6,10},{10,14},{3,7},{... | collective-permute-start | bytes 230408 | tf_op jit(solution)/shard_map/ppermute | solution.py:29
  36.1 9.8 %collective-permute-done.2 = f32[19200]{0:T(1024)S(1)} collective-permute-done((f32[19200]{0:T(1024)}, f32[19200]{0:T(1024)S(1)}, u32[]{:S(2)}, u32[]{:S(2)}) %collective-permute-start.2) | collective-permute-done | bytes 76832 | tf_op jit(solution)/shard_map/ppermute | solution.py:29
  46.0 0.9 %reshape.269 = f32[25,2,384]{2,1,0:T(2,128)S(1)} reshape(f32[19200]{0:T(1024)} %collective-permute-done.3) | data formatting | bytes 153600 | tf_op jit(solution)/shard_map/reshape | solution.py:30
  46.9 3.3 %shard_map.105 = f32[3,32,256]{2,1,0:T(8,128)} custom-call(f32[16,17,768]{2,1,0:T(8,128)} %all-to-all-done.arrived_ref), custom_call_target="tpu_custom_call" | custom-call | tf_op jit(solution)/shard_map/pallas_call | solution.py:136
  50.2 1.3 %collective-permute-start.4 = (f32[3,32,256]{2,1,0:T(8,128)}, f32[3,32,256]{2,1,0:T(8,128)}, u32[]{:S(2)}, u32[]{:S(2)}) collective-permute-start(f32[3,32,256]{2,1,0:T(8,128)} %shard_map.105), channel_id=1, source_target_pairs={{0,16},{16,0},{1,17},{17,1},{2,18},{18,2},{3,19},{19,3},{4,20},{20... | collective-permute-start | bytes 294920 | tf_op jit(solution)/shard_map/ppermute | solution.py:214
  51.6 2.6 %pad_maximum_fusion.wide_ref = f32[25,40,384]{2,1,0:T(8,128)} fusion(f32[25,2,384]{2,1,0:T(2,128)S(1)} %reshape.269, f32[25,2,384]{2,1,0:T(2,128)S(1)} %reshape.267, f32[25,32,2]{2,1,0:T(8,128)} %reshape.265, f32[25,32,124]{2,1,0:T(8,128)} %copy-done.1, f32[25,32,2]{2,1,0:T(8,128)S(1)} %reshape.263, f32[1,32,256]{2,1,0:T(8,128)S(1)} %convert_select_fusion, ...), kind=kLoop, calls=%fused_computation.2 | loop fusion | flops 2688000 | bytes 2918560 | tf_op jit(solution)/shard_map/concatenate | solution.py:44
  54.9 4.3 %shard_map.104 = f32[1,3,8,32,256]{4,3,2,1,0:T(8,128)} custom-call(f32[1,4,8]{2,1,0:T(4,128)} %coef_ref.1, f32[2,40,384]{2,1,0:T(8,128)} %broadcast_in_dim.10.row_ref, f32[25,40,384]{2,1,0:T(8,128)} %pad_maximum_fusion.wide_ref), custom_call_target="tpu_custom_call" | custom-call | tf_op jit(solution)/shard_map/pallas_call | solution.py:101
  59.2 1.5 %multiply_bitcast_fusion = f32[1,3,32,256]{3,2,1,0:T(8,128)} fusion(f32[3,32,256]{2,1,0:T(8,128)} %collective-permute-done.4, f32[32,256]{1,0:T(8,128)S(1)} %convert_bitcast_fusion), kind=kLoop, calls=%fused_computation.28 | loop fusion | flops 24576 | bytes 229376 | tf_op jit(solution)/shard_map/broadcast_in_dim | solution.py:236
  (46 shorter events, 5.8 us)
Async XLA Ops:
  0.6 1.8 %copy-start = (f32[1,8,256,256]{3,2,1,0:T(8,128)S(1)}, f32[1,8,256,256]{3,2,1,0:T(8,128)}, u32[]{:S(2)}) copy-start(f32[1,8,256,256]{3,2,1,0:T(8,128)} %param.15) | copy-start | bytes 6291460
  4.7 2.0 %copy-start.5 = (s32[1,128,1]{1,2,0:T(1,128)S(1)}, s32[1,128,1]{1,2,0:T(1,128)}, u32[]{:S(2)}) copy-start(s32[1,128,1]{1,2,0:T(1,128)} %param.16) | copy-start | bytes 1540
  4.7 2.2 %copy-start.6 = (s32[1,128]{1,0:T(1,128)S(1)}, s32[1,128]{1,0:T(1,128)}, u32[]{:S(2)}) copy-start(s32[1,128]{1,0:T(1,128)} %param.18) | copy-start | bytes 1540
  4.7 2.2 %copy-start.7 = (s32[1,128]{1,0:T(1,128)S(1)}, s32[1,128]{1,0:T(1,128)}, u32[]{:S(2)}) copy-start(s32[1,128]{1,0:T(1,128)} %param.17) | copy-start | bytes 1540
  4.7 2.2 %copy-start.8 = (s32[1,128]{1,0:T(1,128)S(1)}, s32[1,128]{1,0:T(1,128)}, u32[]{:S(2)}) copy-start(s32[1,128]{1,0:T(1,128)} %param.19) | copy-start | bytes 1540
  10.1 6.7 %copy-start.2 = (f32[1,3,8,32,256]{4,3,2,1,0:T(8,128)S(1)}, f32[1,3,8,32,256]{4,3,2,1,0:T(8,128)}, u32[]{:S(2)}) copy-start(f32[1,3,8,32,256]{4,3,2,1,0:T(8,128)} %param.11) | copy-start | bytes 2359300
  10.1 7.7 %copy-start.3 = (f32[1,3,32,256]{3,2,1,0:T(8,128)S(1)}, f32[1,3,32,256]{3,2,1,0:T(8,128)}, u32[]{:S(2)}) copy-start(f32[1,3,32,256]{3,2,1,0:T(8,128)} %param.12) | copy-start | bytes 294916
  10.1 36.8 %all-to-all-start = ((f32[16,17,768]{2,1,0:T(8,128)}), f32[16,17,768]{2,1,0:T(8,128)}, u32[]{:S(2)}, u32[]{:S(2)}) async-start(f32[16,17,768]{2,1,0:T(8,128)} %select_maximum_fusion), calls=%async_computation | async-start | bytes 2359296 | tf_op jit(solution)/shard_map/all_to_all | solution.py:211
  16.8 2.1 %copy-start.4 = (s32[1,32,256]{2,1,0:T(8,128)S(1)}, s32[1,32,256]{2,1,0:T(8,128)}, u32[]{:S(2)}) copy-start(s32[1,32,256]{2,1,0:T(8,128)} %param.13) | copy-start | bytes 98308
  21.1 2.5 %collective-permute-start = (f32[1600]{0:T(1024)S(1)}, f32[1600]{0:T(1024)S(1)}, u32[]{:S(2)}, u32[]{:S(2)}) collective-permute-start(f32[1600]{0:T(1024)S(1)} %reshape.262), channel_id=1, source_target_pairs={{1,0},{2,1},{3,2},{0,3},{5,4},{6,5},{7,6},{4,7},{9,8},{10,9},{11,1... | collective-permute-start | bytes 19208 | tf_op jit(solution)/shard_map/ppermute | solution.py:29
  22.5 3.8 %collective-permute-start.1 = (f32[1600]{0:T(1024)S(1)}, f32[1600]{0:T(1024)S(1)}, u32[]{:S(2)}, u32[]{:S(2)}) collective-permute-start(f32[1600]{0:T(1024)S(1)} %reshape.264), channel_id=1, source_target_pairs={{0,1},{1,2},{2,3},{3,0},{4,5},{5,6},{6,7},{7,4},{8,9},{9,10},{10,1... | collective-permute-start | bytes 19208 | tf_op jit(solution)/shard_map/ppermute | solution.py:29
  27.5 0.8 %copy-start.1 = (f32[25,32,124]{2,1,0:T(8,128)}, f32[25,32,124]{2,1,0:T(8,128)S(1)}, u32[]{:S(2)}) copy-start(f32[25,32,124]{2,1,0:T(8,128)S(1)} %broadcast_in_dim.12) | copy-start | bytes 1190404
  30.1 15.8 %collective-permute-start.2 = (f32[19200]{0:T(1024)}, f32[19200]{0:T(1024)S(1)}, u32[]{:S(2)}, u32[]{:S(2)}) collective-permute-start(f32[19200]{0:T(1024)} %reshape.266), channel_id=1, source_target_pairs={{4,0},{8,4},{12,8},{5,1},{9,5},{13,9},{6,2},{10,6},{14,10},{7,3},{... | collective-permute-start | bytes 230408 | tf_op jit(solution)/shard_map/ppermute | solution.py:29
  33.0 13.0 %collective-permute-start.3 = (f32[19200]{0:T(1024)}, f32[19200]{0:T(1024)}, u32[]{:S(2)}, u32[]{:S(2)}) collective-permute-start(f32[19200]{0:T(1024)} %reshape.268), channel_id=1, source_target_pairs={{0,4},{4,8},{8,12},{1,5},{5,9},{9,13},{2,6},{6,10},{10,14},{3,7},{... | collective-permute-start | bytes 230408 | tf_op jit(solution)/shard_map/ppermute | solution.py:29
  50.2 9.0 %collective-permute-start.4 = (f32[3,32,256]{2,1,0:T(8,128)}, f32[3,32,256]{2,1,0:T(8,128)}, u32[]{:S(2)}, u32[]{:S(2)}) collective-permute-start(f32[3,32,256]{2,1,0:T(8,128)} %shard_map.105), channel_id=1, source_target_pairs={{0,16},{16,0},{1,17},{17,1},{2,18},{18,2},{3,19},{19,3},{4,20},{20... | collective-permute-start | bytes 294920 | tf_op jit(solution)/shard_map/ppermute | solution.py:214

commit v4 on v3

--- a/solution.py
+++ b/solution.py
@@ -112,6 +112,84 @@
     )(coeffs, row_terms, wide)
 
 
+def scatter_kernel(
+    flag_ref, ground_ref, previous_ref, sea_ref, table_ref, pick_ref, tag_ref, out_ref, combo_ref, flat_ref
+):
+    tile_count = table_ref.shape[1]
+    field_count, row_count, col_count = previous_ref.shape[1:]
+    peer_count, chunk = out_ref.shape[:2]
+    buffer_rows = peer_count * chunk
+    ground = ground_ref[0, :, 0]
+    previous = previous_ref[0]
+    sea_float = sea_ref[0].astype(jnp.float32)
+    ocean = (flag_ref[0] == 1).astype(jnp.float32)
+    slip_east = ground[0] - previous[0]
+    slip_north = ground[1] - previous[1]
+    wind_speed = jnp.sqrt(slip_east * slip_east + slip_north * slip_north + gust_speed * gust_speed)
+    bulk_flux = [
+        drag_coeff * wind_speed * slip_east,
+        drag_coeff * wind_speed * slip_north,
+        heat_coeff * wind_speed * (previous[2] - ground[2]),
+    ]
+    exported = jnp.concatenate(
+        [(ground[c] * ocean + bulk_flux[c] * (1.0 - ocean)) * sea_float for c in range(field_count)], 0
+    )
+    for tile in range(tile_count):
+        weighted = jnp.dot(
+            exported, table_ref[0, tile], precision=HIGHEST, preferred_element_type=jnp.float32
+        )
+        for c in range(field_count):
+            combo_ref[c, tile * row_count : (tile + 1) * row_count, :] = weighted[
+                c * row_count : (c + 1) * row_count
+            ]
+    chooser = (
+        pick_ref[...] == lax.broadcasted_iota(jnp.int32, (buffer_rows, tile_count * row_count), 1)
+    ).astype(jnp.float32)
+    tag_rows = (
+        lax.broadcasted_iota(jnp.int32, (buffer_rows, peer_count), 0)
+        == lax.broadcasted_iota(jnp.int32, (buffer_rows, peer_count), 1) * chunk + (chunk - 1)
+    ).astype(jnp.float32)
+    tags = jnp.dot(tag_rows, tag_ref[...], precision=HIGHEST, preferred_element_type=jnp.float32)
+    tag_width = tag_ref.shape[1]
+    for c in range(field_count):
+        picked = jnp.dot(chooser, combo_ref[c], precision=HIGHEST, preferred_element_type=jnp.float32)
+        if c == 0:
+            flat_ref[:, :tag_width] = picked[:, :tag_width] + tags
+            flat_ref[:, tag_width:col_count] = picked[:, tag_width:]
+        else:
+            flat_ref[:, c * col_count : (c + 1) * col_count] = picked
+    for peer in range(peer_count):
+        out_ref[peer] = flat_ref[peer * chunk : (peer + 1) * chunk, :]
+
+
+def scattered(flag, state, surface, sea_mask, remap_weights, pick, tags):
+    field_count, row_count, col_count = surface.shape[1:]
+    tile_count = remap_weights.shape[1]
+    vmem = pl.BlockSpec(memory_space=pltpu.VMEM)
+    return pl.pallas_call(
+        scatter_kernel,
+        out_shape=jax.ShapeDtypeStruct(
+            (tags.shape[0], pick.shape[0] // tags.shape[0], field_count * col_count), jnp.float32
+        ),
+        in_specs=[
+            pl.BlockSpec(memory_space=pltpu.SMEM),
+            pl.BlockSpec((1, field_count, 1, row_count, col_count), lambda i: (0, 0, 0, 0, 0)),
+            vmem,
+            vmem,
+            vmem,
+            vmem,
+            vmem,
+        ],
+        out_specs=vmem,
+        grid=(1,),
+        scratch_shapes=[
+            pltpu.VMEM((field_count, tile_count * row_count, col_count), jnp.float32),
+            pltpu.VMEM((pick.shape[0], field_count * col_count), jnp.float32),
+        ],
+        interpret=INTERPRET,
+    )(flag, state, surface, sea_mask, remap_weights, pick, tags)
+
+
 def gather_kernel(arrived_ref, out_ref):
     peer_count, tagged, width = arrived_ref.shape
     slot_count = tagged - 1
@@ -180,34 +258,28 @@
     peer_count = lax.axis_size("lat") * lax.axis_size("lon")
     width = field_count * col_count
 
-    exported = surface_export(fields[:, 0], previous, sea_float, ocean_side)
-    combos = jnp.einsum("crx,txy->trcy", exported, tile_table, precision=HIGHEST)
-    combos = combos.reshape(tile_count * row_count, width)
     targets = link_dest[0, :, 0]
     link_count = targets.shape[0]
     slot_count = max(2, 2 * link_count // peer_count)
+    chunk = slot_count + 1
     link_order = jnp.arange(link_count, dtype=jnp.int32)
     earlier_same = (targets[:, None] == targets[None, :]) & (
         link_order[None, :] < link_order[:, None]
     )
     link_rank = jnp.sum(earlier_same.astype(jnp.int32), axis=1)
-    position = targets * slot_count + link_rank
-    slot_ids = jnp.arange(peer_count * slot_count, dtype=jnp.int32)
-    in_slot = (position[None, :] == slot_ids[:, None]).astype(jnp.int32)
+    position = targets * chunk + link_rank
+    buffer_ids = jnp.arange(peer_count * chunk, dtype=jnp.int32)
+    in_slot = (position[None, :] == buffer_ids[:, None]).astype(jnp.int32)
     picked = link_tile[0] * row_count + link_src_row[0]
     slot_pick = jnp.sum(in_slot * (picked + 1)[None, :], axis=1) - 1
     slot_row = jnp.sum(in_slot * (link_dst_row[0] + 1)[None, :], axis=1) - 1
-    chooser = (
-        slot_pick[:, None] == jnp.arange(tile_count * row_count, dtype=jnp.int32)[None, :]
-    ).astype(jnp.float32)
-    outgoing = jnp.dot(chooser, combos, precision=HIGHEST)
-    row_tags = jnp.zeros((peer_count, 1, width), jnp.float32)
-    row_tags = row_tags.at[:, 0, :slot_count].set(
-        slot_row.reshape(peer_count, slot_count).astype(jnp.float32)
-    )
-    outgoing = jnp.concatenate(
-        [outgoing.reshape(peer_count, slot_count, width), row_tags], axis=1
-    ).reshape(peer_count * (slot_count + 1), width)
+    slot_row = slot_row.reshape(peer_count, chunk)[:, :slot_count].astype(jnp.float32)
+    tag_width = 128
+    tags = jnp.pad(slot_row, ((0, 0), (0, tag_width - slot_count)))
+    flag = lax.axis_index("grp").astype(jnp.int32).reshape(1)
+    outgoing = scattered(
+        flag, state, surface, sea_mask, remap_weights, slot_pick.reshape(-1, 1), tags
+    )
     arrived = lax.all_to_all(outgoing, ("lat", "lon"), split_axis=0, concat_axis=0, tiled=True)
     arrived = arrived.reshape(peer_count, slot_count + 1, width)
     summed_here = gathered(arrived, field_count, row_count, col_count)

time: 61.4 us -> 59.4 us (0.967)
  waiting for transfers between devices: 12.8 us -> 18.5 us
  Pallas kernels: 7.6 us -> 12.5 us
  other arithmetic: 10.6 us -> 5.77 us
  matrix products: 3.95 us -> 0 us
  local copies, waits for them, and re-layouts: 9.97 us -> 6.26 us
    ppermute x4, waiting for transfers between devices: 12.8 us -> 18.5 us  [shifted(): flat = lax.ppermute(part.reshape(-1), axis, route)]
    pallas_call x0 -> x1, Pallas kernels: none -> 4.95 us  [scattered(): pl.pallas_call(scatter_kernel, out_shape=jax.ShapeDtypeStruct((tags.shape...]
    dot_general x2 -> x0, matrix products: 3.95 us -> none  [the longest x1 2.21 us: body(): jnp.einsum('crx,txy->trcy', exported, tile_table, precision=HIGHEST)]
    reshape x4, local copies, waits for them, and re-layouts: 2.45 us -> 0.81 us  [shifted(): return flat.reshape(part.shape)]
    reshape x4, local copies, waits for them, and re-layouts: 2.85 us -> 1.22 us  [shifted(): flat = lax.ppermute(part.reshape(-1), axis, route)]
    reshape x1 -> x0, local copies, waits for them, and re-layouts: 1.42 us -> none  [body(): combos = combos.reshape(tile_count * row_count, width)]
    concatenate x1, other arithmetic: 2.6 us -> 1.5 us  [with_halo(): jnp.concatenate([cells, shifted(head, 'lat', False, False), gap, shifted(...]
    concatenate x1 -> x0, other arithmetic: 1.1 us -> none  [body(): jnp.concatenate([outgoing.reshape(peer_count, slot_count, width), row_tag...]
  transfers between devices with their start and end apart: 6 -> 6, of which waited for: 3 -> 3; matrix products, arithmetic and copies ran while one was open for 21% -> 9% of each run, Pallas kernels for 7% -> 7%
where the time goes in v4:
time: 59.4 us; the launch traced here: 59 us
  waiting for transfers between devices  18.5 us (31%)
  starting transfers between devices  15.1 us (25%)
  Pallas kernels  12.5 us (21%)
  local copies, waits for them, and re-layouts  6.26 us (11%)
  other arithmetic  5.77 us (10%)
  between operations  0.85 us (1%)
    ppermute x4, waiting for transfers between devices, shifted(): flat = lax.ppermute(part.reshape(-1), axis, route)  18.5 us
    ppermute x4, starting transfers between devices, shifted(): flat = lax.ppermute(part.reshape(-1), axis, route)  6.86 us
    all_to_all x1, starting transfers between devices, body(): lax.all_to_all(outgoing, ('lat', 'lon'), split_axis=0, concat_axis=0, til...  6.74 us
    pallas_call x1, Pallas kernels, scattered(): pl.pallas_call(scatter_kernel, out_shape=jax.ShapeDtypeStruct((tags.shape...  4.95 us
    pallas_call x1, Pallas kernels, dynamics(): pl.pallas_call(stencil_kernel, out_shape=jax.ShapeDtypeStruct((1, field_c...  4.33 us
    pallas_call x1, Pallas kernels, gathered(): pl.pallas_call(gather_kernel, out_shape=jax.ShapeDtypeStruct((field_count...  3.27 us
    unnamed x9, local copies, waits for them, and re-layouts  1.84 us
    concatenate x1, other arithmetic, with_halo(): jnp.concatenate([cells, shifted(head, 'lat', False, False), gap, shifted(...  1.5 us
  transfers between devices with their start and end apart: 6, of which 3 were waited for; matrix products, arithmetic and copies ran while one was open for 9% of the time, Pallas kernels for 7%

profile of v4, /device:TPU:13, one launch (start us, length us, event | category | flops | bytes accessed | tf_op | source)
XLA Modules:
  0.0 59.0 jit_solution(3897914929863302276)
XLA Ops:
  0.6 0.9 %convert_reduce_fusion = s32[128]{0:T(128)S(1)} fusion(s32[128]{0:T(128)} %bitcast.26), kind=kLoop, calls=%fused_computation.19 | loop fusion | flops 81792 | bytes 1024 | tf_op jit(solution)/shard_map/reduce_sum | solution.py:269
  1.5 0.7 %multiply_add_fusion = s32[128]{0:T(128)S(1)} fusion(s32[128]{0:T(128)S(1)} %convert_reduce_fusion, s32[1,128,1]{1,2,0:T(1,128)} %param.14), kind=kLoop, calls=%fused_computation.33 | loop fusion | flops 256 | bytes 1536 | tf_op jit(solution)/shard_map/add | solution.py:270
  2.2 0.7 %add_bitcast_fusion = s32[128]{0:T(128)S(1)} fusion(s32[1,128]{1,0:T(1,128)} %param.16), kind=kLoop, calls=%fused_computation.31 | loop fusion | flops 128 | bytes 1024 | tf_op jit(solution)/shard_map/mul | solution.py:275
  2.9 0.7 %add_bitcast_fusion.1 = s32[128]{0:T(128)S(1)} fusion(s32[1,128]{1,0:T(1,128)} %param.15, s32[1,128]{1,0:T(1,128)} %param.17), kind=kLoop, calls=%fused_computation.32 | loop fusion | flops 384 | bytes 1536 | tf_op jit(solution)/shard_map/mul | solution.py:274
  3.7 0.8 %sub.24.pick_ref = s32[272,1]{1,0:T(8,128)} reshape(s32[272]{0:T(512)S(1)} %get-tuple-element.9) | data formatting | bytes 2176 | tf_op jit(solution)/shard_map/sub | solution.py:274
  4.6 0.6 %pad.4.tag_ref = f32[16,128]{1,0:T(8,128)} pad(f32[16,16]{1,0:T(8,128)S(1)} %slice_convert_fusion, f32[]{:T(128)} %constant.54.clone.1), padding=0_0x0_112 | pad | bytes 9220 | tf_op jit(solution)/shard_map/jit(_pad)/pad | solution.py:278
  5.2 5.0 %shard_map.105 = f32[16,17,768]{2,1,0:T(8,128)} custom-call(s32[1]{0:T(128)} %bitcast.4.flag_ref, f32[1,3,8,32,256]{4,3,2,1,0:T(8,128)} %ground_ref.1, f32[1,3,32,256]{3,2,1,0:T(8,128)} %previous_ref.1, s32[1,32,256]{2,1,0:T(8,128)} %sea_ref.1, f32[1,8,256,256]{3,2,1,0:T(8,128)} %table_ref.1, s32[272,1]{1,0:T(8,128)} %sub.24.pick_ref, f32[16,128]{1,0:T(8,128)} %pad.4.tag_ref), custom_call_target="tpu_custom_call" | custom-call | tf_op jit(solution)/shard_map/pallas_call | solution.py:169
  10.2 6.7 %all-to-all-start = ((f32[16,17,768]{2,1,0:T(8,128)}), f32[16,17,768]{2,1,0:T(8,128)S(1)}, u32[]{:S(2)}, u32[]{:S(2)}) async-start(f32[16,17,768]{2,1,0:T(8,128)} %shard_map.105), calls=%async_computation | async-start | bytes 2359296 | tf_op jit(solution)/shard_map/all_to_all | solution.py:283
  17.1 0.6 %copy-done.3 = s32[1,32,256]{2,1,0:T(8,128)S(1)} copy-done((s32[1,32,256]{2,1,0:T(8,128)S(1)}, s32[1,32,256]{2,1,0:T(8,128)}, u32[]{:S(2)}) %copy-start.3) | copy-done | bytes 32792
  18.4 1.2 %collective-permute-start = (f32[1600]{0:T(1024)S(1)}, f32[1600]{0:T(1024)S(1)}, u32[]{:S(2)}, u32[]{:S(2)}) collective-permute-start(f32[1600]{0:T(1024)S(1)} %reshape.128), channel_id=1, source_target_pairs={{1,0},{2,1},{3,2},{0,3},{5,4},{6,5},{7,6},{4,7},{9,8},{10,9},{11,1... | collective-permute-start | bytes 19208 | tf_op jit(solution)/shard_map/ppermute | solution.py:29
  20.4 1.0 %collective-permute-done = f32[1600]{0:T(1024)S(1)} collective-permute-done((f32[1600]{0:T(1024)S(1)}, f32[1600]{0:T(1024)S(1)}, u32[]{:S(2)}, u32[]{:S(2)}) %collective-permute-start) | collective-permute-done | bytes 6432 | tf_op jit(solution)/shard_map/ppermute | solution.py:29
  21.4 0.4 reshape.129
  21.8 1.6 %collective-permute-done.1 = f32[1600]{0:T(1024)S(1)} collective-permute-done((f32[1600]{0:T(1024)S(1)}, f32[1600]{0:T(1024)S(1)}, u32[]{:S(2)}, u32[]{:S(2)}) %collective-permute-start.1) | collective-permute-done | bytes 6432 | tf_op jit(solution)/shard_map/ppermute | solution.py:29
  24.0 2.5 %collective-permute-start.2 = (f32[19200]{0:T(1024)S(1)}, f32[19200]{0:T(1024)S(1)}, u32[]{:S(2)}, u32[]{:S(2)}) collective-permute-start(f32[19200]{0:T(1024)S(1)} %reshape.132), channel_id=1, source_target_pairs={{4,0},{8,4},{12,8},{5,1},{9,5},{13,9},{6,2},{10,6},{14,10},{7,3},{... | collective-permute-start | bytes 230408 | tf_op jit(solution)/shard_map/ppermute | solution.py:29
  26.5 0.7 %reshape.134 = f32[19200]{0:T(1024)} reshape(f32[25,2,384]{2,1,0:T(2,128)S(1)} %get-tuple-element.5) | data formatting | bytes 153600 | tf_op jit(solution)/shard_map/reshape | solution.py:29
  27.2 2.8 %collective-permute-start.3 = (f32[19200]{0:T(1024)}, f32[19200]{0:T(1024)S(1)}, u32[]{:S(2)}, u32[]{:S(2)}) collective-permute-start(f32[19200]{0:T(1024)} %reshape.134), channel_id=1, source_target_pairs={{0,4},{4,8},{8,12},{1,5},{5,9},{9,13},{2,6},{6,10},{10,14},{3,7},{... | collective-permute-start | bytes 230408 | tf_op jit(solution)/shard_map/ppermute | solution.py:29
  30.0 15.9 %collective-permute-done.2 = f32[19200]{0:T(1024)S(1)} collective-permute-done((f32[19200]{0:T(1024)S(1)}, f32[19200]{0:T(1024)S(1)}, u32[]{:S(2)}, u32[]{:S(2)}) %collective-permute-start.2) | collective-permute-done | bytes 76832 | tf_op jit(solution)/shard_map/ppermute | solution.py:29
  46.0 1.0 %copy-done = f32[16,17,768]{2,1,0:T(8,128)} copy-done((f32[16,17,768]{2,1,0:T(8,128)}, f32[16,17,768]{2,1,0:T(8,128)S(1)}, u32[]{:S(2)}) %copy-start) | copy-done | bytes 835608
  47.0 3.3 %shard_map.106 = f32[3,32,256]{2,1,0:T(8,128)} custom-call(f32[16,17,768]{2,1,0:T(8,128)} %copy-done), custom_call_target="tpu_custom_call" | custom-call | tf_op jit(solution)/shard_map/pallas_call | solution.py:214
  50.3 1.5 %collective-permute-start.4 = (f32[3,32,256]{2,1,0:T(8,128)}, f32[3,32,256]{2,1,0:T(8,128)S(1)}, u32[]{:S(2)}, u32[]{:S(2)}) collective-permute-start(f32[3,32,256]{2,1,0:T(8,128)} %shard_map.106), channel_id=1, source_target_pairs={{0,16},{16,0},{1,17},{17,1},{2,18},{18,2},{3,19},{19,3},{4,20},{20... | collective-permute-start | bytes 294920 | tf_op jit(solution)/shard_map/ppermute | solution.py:286
  51.8 1.5 %pad_maximum_fusion.wide_ref = f32[25,40,384]{2,1,0:T(8,128)} fusion(f32[25,2,384]{2,1,0:T(2,128)S(1)} %reshape.135, f32[25,2,384]{2,1,0:T(2,128)S(1)} %reshape.133, f32[25,32,2]{2,1,0:T(8,128)S(1)} %reshape.131, f32[25,32,124]{2,1,0:T(8,128)S(1)} %broadcast_in_dim.12, f32[25,32,2]{2,1,0:T(8,128)S(1)} %reshape.129, f32[1,32,256]{2,1,0:T(8,128)S(1)} %convert_select_fusion, ...), kind=kLoop, calls=%fused_computation | loop fusion | flops 2688000 | bytes 2918560 | tf_op jit(solution)/shard_map/concatenate | solution.py:44
  53.3 0.7 %broadcast_in_dim.10.row_ref = f32[2,40,384]{2,1,0:T(8,128)} broadcast(f32[2,40]{1,0:T(2,128)S(1)} %pad_maximum_fusion.8), dimensions={0,1} | broadcast | bytes 123200 | tf_op jit(solution)/shard_map/broadcast_in_dim | solution.py:306
  54.0 4.3 %shard_map.104 = f32[1,3,8,32,256]{4,3,2,1,0:T(8,128)} custom-call(f32[1,4,8]{2,1,0:T(4,128)} %coef_ref.1, f32[2,40,384]{2,1,0:T(8,128)} %broadcast_in_dim.10.row_ref, f32[25,40,384]{2,1,0:T(8,128)} %pad_maximum_fusion.wide_ref), custom_call_target="tpu_custom_call" | custom-call | tf_op jit(solution)/shard_map/pallas_call | solution.py:101
  58.3 0.7 %multiply_bitcast_fusion = f32[1,3,32,256]{3,2,1,0:T(8,128)} fusion(f32[3,32,256]{2,1,0:T(8,128)S(1)} %collective-permute-done.4, f32[32,256]{1,0:T(8,128)S(1)} %convert_bitcast_fusion), kind=kLoop, calls=%fused_computation.13 | loop fusion | flops 24576 | bytes 229376 | tf_op jit(solution)/shard_map/broadcast_in_dim | solution.py:308
  (35 shorter events, 2.6 us)
Async XLA Ops:
  10.2 6.7 %copy-start.1 = (f32[1,3,8,32,256]{4,3,2,1,0:T(8,128)S(1)}, f32[1,3,8,32,256]{4,3,2,1,0:T(8,128)}, u32[]{:S(2)}) copy-start(f32[1,3,8,32,256]{4,3,2,1,0:T(8,128)} %ground_ref.1) | copy-start | bytes 2359300
  10.2 35.9 %all-to-all-start = ((f32[16,17,768]{2,1,0:T(8,128)}), f32[16,17,768]{2,1,0:T(8,128)S(1)}, u32[]{:S(2)}, u32[]{:S(2)}) async-start(f32[16,17,768]{2,1,0:T(8,128)} %shard_map.105), calls=%async_computation | async-start | bytes 2359296 | tf_op jit(solution)/shard_map/all_to_all | solution.py:283
  16.9 0.8 %copy-start.3 = (s32[1,32,256]{2,1,0:T(8,128)S(1)}, s32[1,32,256]{2,1,0:T(8,128)}, u32[]{:S(2)}) copy-start(s32[1,32,256]{2,1,0:T(8,128)} %sea_ref.1) | copy-start | bytes 98308
  16.9 0.9 %copy-start.2 = (f32[1,3,32,256]{3,2,1,0:T(8,128)S(1)}, f32[1,3,32,256]{3,2,1,0:T(8,128)}, u32[]{:S(2)}) copy-start(f32[1,3,32,256]{3,2,1,0:T(8,128)} %previous_ref.1) | copy-start | bytes 294916
  18.4 3.0 %collective-permute-start = (f32[1600]{0:T(1024)S(1)}, f32[1600]{0:T(1024)S(1)}, u32[]{:S(2)}, u32[]{:S(2)}) collective-permute-start(f32[1600]{0:T(1024)S(1)} %reshape.128), channel_id=1, source_target_pairs={{1,0},{2,1},{3,2},{0,3},{5,4},{6,5},{7,6},{4,7},{9,8},{10,9},{11,1... | collective-permute-start | bytes 19208 | tf_op jit(solution)/shard_map/ppermute | solution.py:29
  19.9 3.4 %collective-permute-start.1 = (f32[1600]{0:T(1024)S(1)}, f32[1600]{0:T(1024)S(1)}, u32[]{:S(2)}, u32[]{:S(2)}) collective-permute-start(f32[1600]{0:T(1024)S(1)} %reshape.130), channel_id=1, source_target_pairs={{0,1},{1,2},{2,3},{3,0},{4,5},{5,6},{6,7},{7,4},{8,9},{9,10},{10,1... | collective-permute-start | bytes 19208 | tf_op jit(solution)/shard_map/ppermute | solution.py:29
  24.0 21.9 %collective-permute-start.2 = (f32[19200]{0:T(1024)S(1)}, f32[19200]{0:T(1024)S(1)}, u32[]{:S(2)}, u32[]{:S(2)}) collective-permute-start(f32[19200]{0:T(1024)S(1)} %reshape.132), channel_id=1, source_target_pairs={{4,0},{8,4},{12,8},{5,1},{9,5},{13,9},{6,2},{10,6},{14,10},{7,3},{... | collective-permute-start | bytes 230408 | tf_op jit(solution)/shard_map/ppermute | solution.py:29
  27.2 18.8 %collective-permute-start.3 = (f32[19200]{0:T(1024)}, f32[19200]{0:T(1024)S(1)}, u32[]{:S(2)}, u32[]{:S(2)}) collective-permute-start(f32[19200]{0:T(1024)} %reshape.134), channel_id=1, source_target_pairs={{0,4},{4,8},{8,12},{1,5},{5,9},{9,13},{2,6},{6,10},{10,14},{3,7},{... | collective-permute-start | bytes 230408 | tf_op jit(solution)/shard_map/ppermute | solution.py:29
  46.0 1.0 %copy-start = (f32[16,17,768]{2,1,0:T(8,128)}, f32[16,17,768]{2,1,0:T(8,128)S(1)}, u32[]{:S(2)}) copy-start(f32[16,17,768]{2,1,0:T(8,128)S(1)} %all-to-all-done.arrived_ref) | copy-start | bytes 2506756
  50.3 8.0 %collective-permute-start.4 = (f32[3,32,256]{2,1,0:T(8,128)}, f32[3,32,256]{2,1,0:T(8,128)S(1)}, u32[]{:S(2)}, u32[]{:S(2)}) collective-permute-start(f32[3,32,256]{2,1,0:T(8,128)} %shard_map.106), channel_id=1, source_target_pairs={{0,16},{16,0},{1,17},{17,1},{2,18},{18,2},{3,19},{19,3},{4,20},{20... | collective-permute-start | bytes 294920 | tf_op jit(solution)/shard_map/ppermute | solution.py:286

commit v5 on v2

--- a/solution.py
+++ b/solution.py
@@ -1,3 +1,5 @@
+import functools
+
 import jax
 import jax.numpy as jnp
 from jax import lax
@@ -112,6 +114,111 @@
     )(coeffs, row_terms, wide)
 
 
+def export_kernel(flag_ref, ground_ref, previous_ref, sea_ref, link_ref, out_ref):
+    field_count, row_count, col_count = previous_ref.shape[1:]
+    link_fields, link_count = link_ref.shape
+    ground = ground_ref[0, :, 0]
+    previous = previous_ref[0]
+    sea_float = sea_ref[0].astype(jnp.float32)
+    ocean = (flag_ref[0] == 1).astype(jnp.float32)
+    slip_east = ground[0] - previous[0]
+    slip_north = ground[1] - previous[1]
+    wind_speed = jnp.sqrt(slip_east * slip_east + slip_north * slip_north + gust_speed * gust_speed)
+    bulk_flux = [
+        drag_coeff * wind_speed * slip_east,
+        drag_coeff * wind_speed * slip_north,
+        heat_coeff * wind_speed * (previous[2] - ground[2]),
+    ]
+    for c in range(field_count):
+        out_ref[c * row_count : (c + 1) * row_count, :] = (
+            ground[c] * ocean + bulk_flux[c] * (1.0 - ocean)
+        ) * sea_float
+    base = field_count * row_count
+    out_ref[base : base + 8, :] = jnp.zeros((8, col_count), jnp.float32)
+    out_ref[base : base + link_fields, :link_count] = link_ref[...]
+
+
+def exported_block(flag, state, surface, sea_mask, links):
+    field_count, row_count, col_count = surface.shape[1:]
+    vmem = pl.BlockSpec(memory_space=pltpu.VMEM)
+    return pl.pallas_call(
+        export_kernel,
+        out_shape=jax.ShapeDtypeStruct((field_count * row_count + 8, col_count), jnp.float32),
+        in_specs=[
+            pl.BlockSpec(memory_space=pltpu.SMEM),
+            pl.BlockSpec((1, field_count, 1, row_count, col_count), lambda i: (0, 0, 0, 0, 0)),
+            vmem,
+            vmem,
+            vmem,
+        ],
+        out_specs=vmem,
+        grid=(1,),
+        interpret=INTERPRET,
+    )(flag, state, surface, sea_mask, links)
+
+
+def remap_kernel(link_count, lat_ref, gathered_ref, table_ref, out_ref, rows_ref, combo_ref):
+    source_count = gathered_ref.shape[0]
+    tile_count = table_ref.shape[1]
+    owner_count, field_count, row_count, col_count = out_ref.shape
+    base = field_count * row_count
+    my_lat = lat_ref[0]
+    for source in range(source_count):
+        rows_ref[source * base : (source + 1) * base, :] = gathered_ref[source, :base, :]
+    for tile in range(tile_count):
+        weighted = jnp.dot(
+            rows_ref[...], table_ref[0, tile], precision=HIGHEST, preferred_element_type=jnp.float32
+        )
+        for source in range(source_count):
+            for c in range(field_count):
+                first = (source * tile_count + tile) * row_count
+                combo_ref[c, first : first + row_count, :] = weighted[
+                    source * base + c * row_count : source * base + (c + 1) * row_count
+                ]
+    pick_count = source_count * tile_count * row_count
+    into = jnp.zeros((owner_count * row_count, pick_count), jnp.float32)
+    for source in range(source_count):
+        table = gathered_ref[source, base : base + 4, :link_count].astype(jnp.int32)
+        dest, src_row, dst_row, tile = table[0:1], table[1:2], table[2:3], table[3:4]
+        low = my_lat * owner_count
+        valid = (dest >= low) & (dest < low + owner_count)
+        dest_col = (dest - low) * row_count + dst_row
+        pick_col = (source * tile_count + tile) * row_count + src_row
+        to_rows = (
+            (lax.broadcasted_iota(jnp.int32, (owner_count * row_count, link_count), 0) == dest_col)
+            & valid
+        ).astype(jnp.bfloat16)
+        from_rows = (
+            lax.broadcasted_iota(jnp.int32, (pick_count, link_count), 0) == pick_col
+        ).astype(jnp.bfloat16)
+        into = into + lax.dot_general(
+            to_rows, from_rows, (((1,), (1,)), ((), ())), preferred_element_type=jnp.float32
+        )
+    for c in range(field_count):
+        summed = jnp.dot(into, combo_ref[c], precision=HIGHEST, preferred_element_type=jnp.float32)
+        for owner in range(owner_count):
+            out_ref[owner, c] = summed[owner * row_count : (owner + 1) * row_count]
+
+
+def remapped(lat, gathered, remap_weights, owner_count, field_count, row_count, link_count):
+    source_count, _, col_count = gathered.shape
+    tile_count = remap_weights.shape[1]
+    vmem = pl.BlockSpec(memory_space=pltpu.VMEM)
+    return pl.pallas_call(
+        functools.partial(remap_kernel, link_count),
+        out_shape=jax.ShapeDtypeStruct((owner_count, field_count, row_count, col_count), jnp.float32),
+        in_specs=[pl.BlockSpec(memory_space=pltpu.SMEM), vmem, vmem],
+        out_specs=vmem,
+        scratch_shapes=[
+            pltpu.VMEM((source_count * field_count * row_count, col_count), jnp.float32),
+            pltpu.VMEM(
+                (field_count, source_count * tile_count * row_count, col_count), jnp.float32
+            ),
+        ],
+        interpret=INTERPRET,
+    )(lat, gathered, remap_weights)
+
+
 def surface_export(ground, previous, sea_float, ocean_side):
     slip_east = ground[0] - previous[0]
     slip_north = ground[1] - previous[1]
@@ -150,43 +257,17 @@
     peer_count = lax.axis_size("lat") * lax.axis_size("lon")
     width = field_count * col_count
 
-    exported = surface_export(fields[:, 0], previous, sea_float, ocean_side)
-    combos = jnp.einsum("crx,txy->trcy", exported, tile_table, precision=HIGHEST)
-    combos = combos.reshape(tile_count * row_count, width)
-    targets = link_dest[0, :, 0]
-    link_count = targets.shape[0]
-    slot_count = max(2, 2 * link_count // peer_count)
-    link_order = jnp.arange(link_count, dtype=jnp.int32)
-    earlier_same = (targets[:, None] == targets[None, :]) & (
-        link_order[None, :] < link_order[:, None]
-    )
-    link_rank = jnp.sum(earlier_same.astype(jnp.int32), axis=1)
-    position = targets * slot_count + link_rank
-    slot_ids = jnp.arange(peer_count * slot_count, dtype=jnp.int32)
-    in_slot = (position[None, :] == slot_ids[:, None]).astype(jnp.int32)
-    picked = link_tile[0] * row_count + link_src_row[0]
-    slot_pick = jnp.sum(in_slot * (picked + 1)[None, :], axis=1) - 1
-    slot_row = jnp.sum(in_slot * (link_dst_row[0] + 1)[None, :], axis=1) - 1
-    chooser = (
-        slot_pick[:, None] == jnp.arange(tile_count * row_count, dtype=jnp.int32)[None, :]
+    links = jnp.stack(
+        [link_dest[0, :, 0], link_src_row[0], link_dst_row[0], link_tile[0]]
     ).astype(jnp.float32)
-    outgoing = jnp.dot(chooser, combos, precision=HIGHEST)
-    row_tags = jnp.zeros((peer_count, 1, width), jnp.float32)
-    row_tags = row_tags.at[:, 0, :slot_count].set(
-        slot_row.reshape(peer_count, slot_count).astype(jnp.float32)
-    )
-    outgoing = jnp.concatenate(
-        [outgoing.reshape(peer_count, slot_count, width), row_tags], axis=1
-    ).reshape(peer_count * (slot_count + 1), width)
-    arrived = lax.all_to_all(outgoing, ("lat", "lon"), split_axis=0, concat_axis=0, tiled=True)
-    arrived = arrived.reshape(peer_count, slot_count + 1, width)
-    arrived_rows = arrived[:, slot_count, :slot_count].reshape(-1)
-    arrived_pieces = arrived[:, :slot_count, :].reshape(peer_count * slot_count, width)
-    selector = (
-        arrived_rows[None, :] == jnp.arange(row_count, dtype=jnp.float32)[:, None]
-    ).astype(jnp.float32)
-    summed_here = jnp.dot(selector, arrived_pieces, precision=HIGHEST)
-    summed_here = summed_here.reshape(row_count, field_count, col_count).transpose(1, 0, 2)
+    flag = lax.axis_index("grp").astype(jnp.int32).reshape(1)
+    payload = exported_block(flag, state, surface, sea_mask, links)
+    gathered = lax.all_gather(payload, "lat", axis=0, tiled=False)
+    lat = lax.axis_index("lat").astype(jnp.int32).reshape(1)
+    partial = remapped(
+        lat, gathered, remap_weights, lax.axis_size("lon"), field_count, row_count, links.shape[1]
+    )
+    summed_here = lax.psum_scatter(partial, "lon", scatter_dimension=0, tiled=False)
     imported = lax.ppermute(summed_here, "grp", [(0, 1), (1, 0)]) * sea_float
 
     gain = jnp.where(ocean_side, ocean_gain, air_gain)

time: 65.9 us -> 74.8 us (1.14)
  the two profiles are of different devices: /device:TPU:13 before, /device:TPU:0 now
where the time goes in v5:
time: 74.8 us; the launch traced here: 74.4 us
  blocking collectives  18.4 us (25%)
  between operations  14.2 us (19%)
  Pallas kernels  13.3 us (18%)
  waiting for transfers between devices  12.9 us (17%)
  starting transfers between devices  8.43 us (11%)
  other arithmetic  3.98 us (5%)
  local copies, waits for them, and re-layouts  3.15 us (4%)
    all_gather x1, blocking collectives, body(): gathered = lax.all_gather(payload, 'lat', axis=0, tiled=False)  18.4 us
    ppermute x4, starting transfers between devices, shifted(): flat = lax.ppermute(part.reshape(-1), axis, route)  8.39 us
    pallas_call x1, Pallas kernels, remapped(): pl.pallas_call(functools.partial(remap_kernel, link_count), out_shape=jax...  7.4 us
    unnamed x2, waiting for transfers between devices  6.84 us
    ppermute x4, waiting for transfers between devices, shifted(): flat = lax.ppermute(part.reshape(-1), axis, route)  6.06 us
    pallas_call x1, Pallas kernels, dynamics(): pl.pallas_call(stencil_kernel, out_shape=jax.ShapeDtypeStruct((1, field_c...  4.33 us
    pallas_call x1, Pallas kernels, exported_block(): pl.pallas_call(export_kernel, out_shape=jax.ShapeDtypeStruct((field_count...  1.63 us
    concatenate x1, other arithmetic, with_halo(): jnp.concatenate([cells, shifted(head, 'lat', False, False), gap, shifted(...  1.51 us
  transfers between devices with their start and end apart: 6, of which 5 were waited for; matrix products, arithmetic and copies ran while one was open for 6% of the time, Pallas kernels for 6%

profile of v5, /device:TPU:0, one launch (start us, length us, event | category | flops | bytes accessed | tf_op | source)
XLA Modules:
  0.0 74.4 jit_solution(1801063920596303719)
XLA Ops:
  7.2 1.3 %add_convert_fusion.link_ref = f32[4,128]{1,0:T(4,128)} fusion(s32[1,128]{1,0:T(1,128)} %param.17, s32[1,128]{1,0:T(1,128)} %param.16, s32[1,128]{1,0:T(1,128)} %param.15, s32[1,128]{1,0:T(1,128)} %bitcast.26), kind=kLoop, calls=%fused_computation.19 | loop fusion | flops 2048 | bytes 4096 | tf_op jit(solution)/shard_map/convert_element_type | solution.py:262
  8.5 1.6 %shard_map.105 = f32[104,256]{1,0:T(8,128)} custom-call(s32[1]{0:T(128)} %bitcast.5.flag_ref, f32[1,3,8,32,256]{4,3,2,1,0:T(8,128)} %ground_ref.1, f32[1,3,32,256]{3,2,1,0:T(8,128)} %previous_ref.1, s32[1,32,256]{2,1,0:T(8,128)} %sea_ref.1, f32[4,128]{1,0:T(4,128)} %add_convert_fusion.link_ref), custom_call_target="tpu_custom_call" | custom-call | tf_op jit(solution)/shard_map/pallas_call | solution.py:144
  10.1 18.4 %all-gather = f32[416,256]{1,0:T(8,128)} all-gather(f32[104,256]{1,0:T(8,128)} %shard_map.105), channel_id=2, replica_groups=mesh['grp'=2,'lat'=4,'lon'=4] {'lat'}, dimensions={0}, use_global_device_ids=true | all-gather | bytes 532480 | tf_op jit(solution)/shard_map/all_gather | solution.py:265
  28.5 7.4 %shard_map.106 = f32[4,3,32,256]{3,2,1,0:T(8,128)} custom-call(s32[1]{0:T(128)} %bitcast.4.lat_ref, f32[4,104,256]{2,1,0:T(8,128)} %bitcast.25, f32[1,8,256,256]{3,2,1,0:T(8,128)} %table_ref.1), custom_call_target="tpu_custom_call" | custom-call | tf_op jit(solution)/shard_map/pallas_call | solution.py:207
  36.0 0.6 copy-done.2
  36.7 0.1 copy-done.1
  37.0 0.2 fusion
  37.2 0.2 reshape.107
  37.4 2.5 %collective-permute-start = (f32[1600]{0:T(1024)S(1)}, f32[1600]{0:T(1024)S(1)}, u32[]{:S(2)}, u32[]{:S(2)}) collective-permute-start(f32[1600]{0:T(1024)S(1)} %reshape.107), channel_id=1, source_target_pairs={{1,0},{2,1},{3,2},{0,3},{5,4},{6,5},{7,6},{4,7},{9,8},{10,9},{11,1... | collective-permute-start | bytes 19208 | tf_op jit(solution)/shard_map/ppermute | solution.py:31
  39.9 0.2 reshape.109
  40.4 0.9 %collective-permute-done = f32[1600]{0:T(1024)S(1)} collective-permute-done((f32[1600]{0:T(1024)S(1)}, f32[1600]{0:T(1024)S(1)}, u32[]{:S(2)}, u32[]{:S(2)}) %collective-permute-start) | collective-permute-done | bytes 6432 | tf_op jit(solution)/shard_map/ppermute | solution.py:31
  41.3 0.4 reshape.108
  41.7 3.2 %collective-permute-done.1 = f32[1600]{0:T(1024)S(1)} collective-permute-done((f32[1600]{0:T(1024)S(1)}, f32[1600]{0:T(1024)S(1)}, u32[]{:S(2)}, u32[]{:S(2)}) %collective-permute-start.1) | collective-permute-done | bytes 6432 | tf_op jit(solution)/shard_map/ppermute | solution.py:31
  44.9 0.4 reshape.110
  45.3 0.2 pad_maximum_fusion.7
  45.5 1.3 %collective-permute-start.2 = (f32[19200]{0:T(1024)S(1)}, f32[19200]{0:T(1024)S(1)}, u32[]{:S(2)}, u32[]{:S(2)}) collective-permute-start(f32[19200]{0:T(1024)S(1)} %reshape.111), channel_id=1, source_target_pairs={{4,0},{8,4},{12,8},{5,1},{9,5},{13,9},{6,2},{10,6},{14,10},{7,3},{... | collective-permute-start | bytes 230408 | tf_op jit(solution)/shard_map/ppermute | solution.py:31
  46.9 4.6 %collective-permute-start.3 = (f32[19200]{0:T(1024)S(1)}, f32[19200]{0:T(1024)S(1)}, u32[]{:S(2)}, u32[]{:S(2)}) collective-permute-start(f32[19200]{0:T(1024)S(1)} %reshape.113), channel_id=1, source_target_pairs={{0,4},{4,8},{8,12},{1,5},{5,9},{9,13},{2,6},{6,10},{10,14},{3,7},{... | collective-permute-start | bytes 230408 | tf_op jit(solution)/shard_map/ppermute | solution.py:31
  51.5 0.3 collective-permute-done.2
  51.9 1.6 %collective-permute-done.3 = f32[19200]{0:T(1024)S(1)} collective-permute-done((f32[19200]{0:T(1024)S(1)}, f32[19200]{0:T(1024)S(1)}, u32[]{:S(2)}, u32[]{:S(2)}) %collective-permute-start.3) | collective-permute-done | bytes 76832 | tf_op jit(solution)/shard_map/ppermute | solution.py:31
  53.5 6.8 %reduce-scatter.4.cloned.1.call-done = f32[1,3,32,256]{3,2,1,0:T(8,128)} async-done(((f32[4,3,32,256]{3,2,1,0:T(8,128)}), f32[1,3,32,256]{3,2,1,0:T(8,128)}) %reduce-scatter.4.cloned.1.call-update) | async-done | bytes 98320
  60.3 1.5 %pad_maximum_fusion.wide_ref = f32[25,40,384]{2,1,0:T(8,128)} fusion(f32[25,2,384]{2,1,0:T(2,128)S(1)} %reshape.114, f32[25,2,384]{2,1,0:T(2,128)S(1)} %reshape.112, f32[25,32,2]{2,1,0:T(8,128)S(1)} %reshape.110, f32[25,32,124]{2,1,0:T(8,128)S(1)} %broadcast_in_dim.24, f32[25,32,2]{2,1,0:T(8,128)S(1)} %reshape.108, f32[1,32,256]{2,1,0:T(8,128)S(1)} %convert_select_fusion, ...), kind=kLoop, calls=%fused_computation | loop fusion | flops 2688000 | bytes 2918560 | tf_op jit(solution)/shard_map/concatenate | solution.py:46
  61.9 0.7 broadcast_in_dim.10.row_ref
  62.6 4.3 %shard_map.104 = f32[1,3,8,32,256]{4,3,2,1,0:T(8,128)} custom-call(f32[1,4,8]{2,1,0:T(4,128)} %coef_ref.1, f32[2,40,384]{2,1,0:T(8,128)} %broadcast_in_dim.10.row_ref, f32[25,40,384]{2,1,0:T(8,128)} %pad_maximum_fusion.wide_ref), custom_call_target="tpu_custom_call" | custom-call | tf_op jit(solution)/shard_map/pallas_call | solution.py:103
  66.9 0.7 multiply_bitcast_fusion
  (26 shorter events, 0.8 us)
Async XLA Ops:
  7.2 53.2 %reduce-scatter.4.cloned.1.call-start = ((), (), s32[]{:S(2)}) async-start(), calls=%async_computation.1 | async-start | bytes 491520
  28.5 7.4 %copy-start = (f32[1,3,8,32,256]{4,3,2,1,0:T(8,128)S(1)}, f32[1,3,8,32,256]{4,3,2,1,0:T(8,128)}, u32[]{:S(2)}) copy-start(f32[1,3,8,32,256]{4,3,2,1,0:T(8,128)} %ground_ref.1) | copy-start | bytes 2359300
  35.9 0.8 %copy-start.2 = (s32[1,32,256]{2,1,0:T(8,128)S(1)}, s32[1,32,256]{2,1,0:T(8,128)}, u32[]{:S(2)}) copy-start(s32[1,32,256]{2,1,0:T(8,128)} %sea_ref.1) | copy-start | bytes 98308
  36.0 0.9 %copy-start.1 = (f32[1,3,32,256]{3,2,1,0:T(8,128)S(1)}, f32[1,3,32,256]{3,2,1,0:T(8,128)}, u32[]{:S(2)}) copy-start(f32[1,3,32,256]{3,2,1,0:T(8,128)} %previous_ref.1) | copy-start | bytes 294916
  37.4 3.9 %collective-permute-start = (f32[1600]{0:T(1024)S(1)}, f32[1600]{0:T(1024)S(1)}, u32[]{:S(2)}, u32[]{:S(2)}) collective-permute-start(f32[1600]{0:T(1024)S(1)} %reshape.107), channel_id=1, source_target_pairs={{1,0},{2,1},{3,2},{0,3},{5,4},{6,5},{7,6},{4,7},{9,8},{10,9},{11,1... | collective-permute-start | bytes 19208 | tf_op jit(solution)/shard_map/ppermute | solution.py:31
  40.2 4.7 %collective-permute-start.1 = (f32[1600]{0:T(1024)S(1)}, f32[1600]{0:T(1024)S(1)}, u32[]{:S(2)}, u32[]{:S(2)}) collective-permute-start(f32[1600]{0:T(1024)S(1)} %reshape.109), channel_id=1, source_target_pairs={{0,1},{1,2},{2,3},{3,0},{4,5},{5,6},{6,7},{7,4},{8,9},{9,10},{10,1... | collective-permute-start | bytes 19208 | tf_op jit(solution)/shard_map/ppermute | solution.py:31
  45.5 6.3 %collective-permute-start.2 = (f32[19200]{0:T(1024)S(1)}, f32[19200]{0:T(1024)S(1)}, u32[]{:S(2)}, u32[]{:S(2)}) collective-permute-start(f32[19200]{0:T(1024)S(1)} %reshape.111), channel_id=1, source_target_pairs={{4,0},{8,4},{12,8},{5,1},{9,5},{13,9},{6,2},{10,6},{14,10},{7,3},{... | collective-permute-start | bytes 230408 | tf_op jit(solution)/shard_map/ppermute | solution.py:31
  46.9 6.6 %collective-permute-start.3 = (f32[19200]{0:T(1024)S(1)}, f32[19200]{0:T(1024)S(1)}, u32[]{:S(2)}, u32[]{:S(2)}) collective-permute-start(f32[19200]{0:T(1024)S(1)} %reshape.113), channel_id=1, source_target_pairs={{0,4},{4,8},{8,12},{1,5},{5,9},{9,13},{2,6},{6,10},{10,14},{3,7},{... | collective-permute-start | bytes 230408 | tf_op jit(solution)/shard_map/ppermute | solution.py:31
  60.3 6.6 %collective-permute-start.4 = (f32[3,32,256]{2,1,0:T(8,128)}, f32[3,32,256]{2,1,0:T(8,128)S(1)}, u32[]{:S(2)}, u32[]{:S(2)}) collective-permute-start(f32[3,32,256]{2,1,0:T(8,128)} %bitcast.27), channel_id=1, source_target_pairs={{0,16},{16,0},{1,17},{17,1},{2,18},{18,2},{3,19},{19,3},{4,20},{20... | collective-permute-start | bytes 294920 | tf_op jit(solution)/shard_map/ppermute | solution.py:271
Sparse Core Ops, SparseCore 0:
  36.1 24.2 reduce-scatter.3

commit v6 on v5

--- a/solution.py
+++ b/solution.py
@@ -157,14 +157,15 @@
     )(flag, state, surface, sea_mask, links)
 
 
-def remap_kernel(link_count, lat_ref, gathered_ref, table_ref, out_ref, rows_ref, combo_ref):
-    source_count = gathered_ref.shape[0]
+def remap_kernel(link_count, source_count, lat_ref, *refs):
+    source_refs = refs[:source_count]
+    table_ref, out_ref, rows_ref, combo_ref = refs[source_count:]
     tile_count = table_ref.shape[1]
     owner_count, field_count, row_count, col_count = out_ref.shape
     base = field_count * row_count
     my_lat = lat_ref[0]
     for source in range(source_count):
-        rows_ref[source * base : (source + 1) * base, :] = gathered_ref[source, :base, :]
+        rows_ref[source * base : (source + 1) * base, :] = source_refs[source][:base, :]
     for tile in range(tile_count):
         weighted = jnp.dot(
             rows_ref[...], table_ref[0, tile], precision=HIGHEST, preferred_element_type=jnp.float32
@@ -178,7 +179,7 @@
     pick_count = source_count * tile_count * row_count
     into = jnp.zeros((owner_count * row_count, pick_count), jnp.float32)
     for source in range(source_count):
-        table = gathered_ref[source, base : base + 4, :link_count].astype(jnp.int32)
+        table = source_refs[source][base : base + 4, :link_count].astype(jnp.int32)
         dest, src_row, dst_row, tile = table[0:1], table[1:2], table[2:3], table[3:4]
         low = my_lat * owner_count
         valid = (dest >= low) & (dest < low + owner_count)
@@ -200,14 +201,15 @@
             out_ref[owner, c] = summed[owner * row_count : (owner + 1) * row_count]
 
 
-def remapped(lat, gathered, remap_weights, owner_count, field_count, row_count, link_count):
-    source_count, _, col_count = gathered.shape
+def remapped(lat, sources, remap_weights, owner_count, field_count, row_count, link_count):
+    source_count = len(sources)
+    col_count = sources[0].shape[1]
     tile_count = remap_weights.shape[1]
     vmem = pl.BlockSpec(memory_space=pltpu.VMEM)
     return pl.pallas_call(
-        functools.partial(remap_kernel, link_count),
+        functools.partial(remap_kernel, link_count, source_count),
         out_shape=jax.ShapeDtypeStruct((owner_count, field_count, row_count, col_count), jnp.float32),
-        in_specs=[pl.BlockSpec(memory_space=pltpu.SMEM), vmem, vmem],
+        in_specs=[pl.BlockSpec(memory_space=pltpu.SMEM)] + [vmem] * (source_count + 1),
         out_specs=vmem,
         scratch_shapes=[
             pltpu.VMEM((source_count * field_count * row_count, col_count), jnp.float32),
@@ -216,7 +218,7 @@
             ),
         ],
         interpret=INTERPRET,
-    )(lat, gathered, remap_weights)
+    )(lat, *sources, remap_weights)
 
 
 def surface_export(ground, previous, sea_float, ocean_side):
@@ -262,13 +264,24 @@
     ).astype(jnp.float32)
     flag = lax.axis_index("grp").astype(jnp.int32).reshape(1)
     payload = exported_block(flag, state, surface, sea_mask, links)
-    gathered = lax.all_gather(payload, "lat", axis=0, tiled=False)
+    lat_count = lax.axis_size("lat")
+    lon_count = lax.axis_size("lon")
+    sources = [payload] + [
+        lax.ppermute(payload, "lat", [(i, (i + shift) % lat_count) for i in range(lat_count)])
+        for shift in range(1, lat_count)
+    ]
     lat = lax.axis_index("lat").astype(jnp.int32).reshape(1)
-    partial = remapped(
-        lat, gathered, remap_weights, lax.axis_size("lon"), field_count, row_count, links.shape[1]
-    )
-    summed_here = lax.psum_scatter(partial, "lon", scatter_dimension=0, tiled=False)
-    imported = lax.ppermute(summed_here, "grp", [(0, 1), (1, 0)]) * sea_float
+    partial = remapped(lat, sources, remap_weights, lon_count, field_count, row_count, links.shape[1])
+    pieces = []
+    for shift in range(lon_count):
+        route = [
+            (g * lon_count + j, (1 - g) * lon_count + (j + shift) % lon_count)
+            for g in range(2)
+            for j in range(lon_count)
+        ]
+        owner_lon = (lax.axis_index("lon") + shift) % lon_count
+        pieces.append(lax.ppermute(partial[owner_lon], ("grp", "lon"), route))
+    imported = functools.reduce(jnp.add, pieces) * sea_float
 
     gain = jnp.where(ocean_side, ocean_gain, air_gain)
     damping = jnp.where(ocean_side, 0.0, air_gain)

time: 74.8 us -> 47.4 us (0.63)
  blocking collectives: 18.4 us -> 0 us
  between operations: 14.2 us -> 0.97 us
  starting transfers between devices: 8.43 us -> 17.8 us
  waiting for transfers between devices: 12.9 us -> 5.91 us
  local copies, waits for them, and re-layouts: 3.15 us -> 4.16 us
  other arithmetic: 3.98 us -> 4.84 us
    all_gather x1 -> x0, blocking collectives: 18.4 us -> none  [body(): gathered = lax.all_gather(payload, 'lat', axis=0, tiled=False)]
    ppermute x1 -> x7, starting transfers between devices: 0.01 us -> 9.38 us  [the longest x3 6.96 us: body(): lax.ppermute(payload, 'lat', [(i, (i + shift) % lat_count) for i in range...]
    unnamed x2 -> x0, waiting for transfers between devices: 6.84 us -> none
    squeeze x0 -> x1, local copies, waits for them, and re-layouts: none -> 1.06 us  [body(): pieces.append(lax.ppermute(partial[owner_lon], ('grp', 'lon'), route))]
    mul x1, other arithmetic: 0.01 us -> 0.76 us  [body(): sea_float * (gain * previous - damping * fields[:, 0])]
  transfers between devices with their start and end apart: 6 -> 11, of which waited for: 5 -> 4; matrix products, arithmetic and copies ran while one was open for 6% -> 11% of each run, Pallas kernels for 6% -> 9%
where the time goes in v6:
time: 47.4 us; the launch traced here: 47 us
  starting transfers between devices  17.8 us (38%)
  Pallas kernels  13.4 us (28%)
  waiting for transfers between devices  5.91 us (12%)
  other arithmetic  4.84 us (10%)
  local copies, waits for them, and re-layouts  4.16 us (9%)
  between operations  0.97 us (2%)
    ppermute x4, starting transfers between devices, shifted(): flat = lax.ppermute(part.reshape(-1), axis, route)  8.4 us
    pallas_call x1, Pallas kernels, remapped(): pl.pallas_call(functools.partial(remap_kernel, link_count, source_count),...  7.42 us
    ppermute x3, starting transfers between devices, body(): lax.ppermute(payload, 'lat', [(i, (i + shift) % lat_count) for i in range...  6.96 us
    ppermute x4, waiting for transfers between devices, shifted(): flat = lax.ppermute(part.reshape(-1), axis, route)  5.89 us
    pallas_call x1, Pallas kernels, dynamics(): pl.pallas_call(stencil_kernel, out_shape=jax.ShapeDtypeStruct((1, field_c...  4.33 us
    ppermute x4, starting transfers between devices, body(): pieces.append(lax.ppermute(partial[owner_lon], ('grp', 'lon'), route))  2.42 us
    pallas_call x1, Pallas kernels, exported_block(): pl.pallas_call(export_kernel, out_shape=jax.ShapeDtypeStruct((field_count...  1.64 us
    concatenate x1, other arithmetic, with_halo(): jnp.concatenate([cells, shifted(head, 'lat', False, False), gap, shifted(...  1.51 us
  transfers between devices with their start and end apart: 11, of which 4 were waited for; matrix products, arithmetic and copies ran while one was open for 11% of the time, Pallas kernels for 9%

profile of v6, /device:TPU:0, one launch (start us, length us, event | category | flops | bytes accessed | tf_op | source)
XLA Modules:
  0.0 47.0 jit_solution(15328208233164396757)
XLA Ops:
  0.7 1.4 %add_convert_fusion.link_ref = f32[4,128]{1,0:T(4,128)} fusion(s32[1,128]{1,0:T(1,128)} %param.17, s32[1,128]{1,0:T(1,128)} %param.16, s32[1,128]{1,0:T(1,128)} %param.15, s32[1,128]{1,0:T(1,128)} %bitcast.30), kind=kLoop, calls=%fused_computation.23 | loop fusion | flops 2048 | bytes 4096 | tf_op jit(solution)/shard_map/convert_element_type | solution.py:264
  2.0 1.6 %shard_map.105.refs_0_ = f32[104,256]{1,0:T(8,128)} custom-call(s32[1]{0:T(128)} %bitcast.5.flag_ref, f32[1,3,8,32,256]{4,3,2,1,0:T(8,128)} %ground_ref.1, f32[1,3,32,256]{3,2,1,0:T(8,128)} %previous_ref.1, s32[1,32,256]{2,1,0:T(8,128)} %sea_ref.1, f32[4,128]{1,0:T(4,128)} %add_convert_fusion.link_ref), custom_call_target="tpu_custom_call" | custom-call | tf_op jit(solution)/shard_map/pallas_call | solution.py:144
  3.7 3.0 %collective-permute-start.4 = (f32[104,256]{1,0:T(8,128)}, f32[104,256]{1,0:T(8,128)S(1)}, u32[]{:S(2)}, u32[]{:S(2)}) collective-permute-start(f32[104,256]{1,0:T(8,128)} %shard_map.105.refs_0_), channel_id=1, source_target_pairs={{0,4},{4,8},{8,12},{12,0},{1,5},{5,9},{9,13},{13,1},{2,6},{6,10},{... | collective-permute-start | bytes 319496 | tf_op jit(solution)/shard_map/ppermute | solution.py:270
  6.7 2.6 %collective-permute-start.5 = (f32[104,256]{1,0:T(8,128)}, f32[104,256]{1,0:T(8,128)S(1)}, u32[]{:S(2)}, u32[]{:S(2)}) collective-permute-start(f32[104,256]{1,0:T(8,128)} %shard_map.105.refs_0_), channel_id=1, source_target_pairs={{0,8},{4,12},{8,0},{12,4},{1,9},{5,13},{9,1},{13,5},{2,10},{6,14},... | collective-permute-start | bytes 319496 | tf_op jit(solution)/shard_map/ppermute | solution.py:270
  9.3 1.3 %collective-permute-start.6 = (f32[104,256]{1,0:T(8,128)}, f32[104,256]{1,0:T(8,128)S(1)}, u32[]{:S(2)}, u32[]{:S(2)}) collective-permute-start(f32[104,256]{1,0:T(8,128)} %shard_map.105.refs_0_), channel_id=1, source_target_pairs={{0,12},{4,0},{8,4},{12,8},{1,13},{5,1},{9,5},{13,9},{2,14},{6,2},{... | collective-permute-start | bytes 319496 | tf_op jit(solution)/shard_map/ppermute | solution.py:270
  10.6 0.8 %convert_bitcast_fusion = f32[32,256]{1,0:T(8,128)S(1)} fusion(s32[1,32,256]{2,1,0:T(8,128)} %sea_ref.1), kind=kLoop, calls=%fused_computation.21 | loop fusion | flops 8192 | bytes 65536 | tf_op jit(solution)/shard_map/mul | solution.py:288
  12.2 2.5 %collective-permute-start = (f32[1600]{0:T(1024)S(1)}, f32[1600]{0:T(1024)S(1)}, u32[]{:S(2)}, u32[]{:S(2)}) collective-permute-start(f32[1600]{0:T(1024)S(1)} %reshape.107), channel_id=1, source_target_pairs={{1,0},{2,1},{3,2},{0,3},{5,4},{6,5},{7,6},{4,7},{9,8},{10,9},{11,1... | collective-permute-start | bytes 19208 | tf_op jit(solution)/shard_map/ppermute | solution.py:31
  15.2 0.9 %collective-permute-done = f32[1600]{0:T(1024)S(1)} collective-permute-done((f32[1600]{0:T(1024)S(1)}, f32[1600]{0:T(1024)S(1)}, u32[]{:S(2)}, u32[]{:S(2)}) %collective-permute-start) | collective-permute-done | bytes 6432 | tf_op jit(solution)/shard_map/ppermute | solution.py:31
  16.0 0.4 reshape.108
  16.4 3.1 %collective-permute-done.1 = f32[1600]{0:T(1024)S(1)} collective-permute-done((f32[1600]{0:T(1024)S(1)}, f32[1600]{0:T(1024)S(1)}, u32[]{:S(2)}, u32[]{:S(2)}) %collective-permute-start.1) | collective-permute-done | bytes 6432 | tf_op jit(solution)/shard_map/ppermute | solution.py:31
  19.5 0.4 reshape.110
  20.1 1.3 %collective-permute-start.2 = (f32[19200]{0:T(1024)S(1)}, f32[19200]{0:T(1024)S(1)}, u32[]{:S(2)}, u32[]{:S(2)}) collective-permute-start(f32[19200]{0:T(1024)S(1)} %reshape.111), channel_id=1, source_target_pairs={{4,0},{8,4},{12,8},{5,1},{9,5},{13,9},{6,2},{10,6},{14,10},{7,3},{... | collective-permute-start | bytes 230408 | tf_op jit(solution)/shard_map/ppermute | solution.py:31
  21.5 4.6 %collective-permute-start.3 = (f32[19200]{0:T(1024)S(1)}, f32[19200]{0:T(1024)S(1)}, u32[]{:S(2)}, u32[]{:S(2)}) collective-permute-start(f32[19200]{0:T(1024)S(1)} %reshape.113), channel_id=1, source_target_pairs={{0,4},{4,8},{8,12},{1,5},{5,9},{9,13},{2,6},{6,10},{10,14},{3,7},{... | collective-permute-start | bytes 230408 | tf_op jit(solution)/shard_map/ppermute | solution.py:31
  26.1 0.3 collective-permute-done.2
  26.5 1.6 %collective-permute-done.3 = f32[19200]{0:T(1024)S(1)} collective-permute-done((f32[19200]{0:T(1024)S(1)}, f32[19200]{0:T(1024)S(1)}, u32[]{:S(2)}, u32[]{:S(2)}) %collective-permute-start.3) | collective-permute-done | bytes 76832 | tf_op jit(solution)/shard_map/ppermute | solution.py:31
  28.2 0.6 %copy-done.3 = f32[104,256]{1,0:T(8,128)} copy-done((f32[104,256]{1,0:T(8,128)}, f32[104,256]{1,0:T(8,128)S(1)}, u32[]{:S(2)}) %copy-start.3) | copy-done | bytes 106520
  28.9 7.4 %shard_map.106 = f32[4,3,32,256]{3,2,1,0:T(8,128)} custom-call(s32[1]{0:T(128)} %bitcast.4.lat_ref, f32[104,256]{1,0:T(8,128)} %shard_map.105.refs_0_, f32[104,256]{1,0:T(8,128)} %copy-done.3, f32[104,256]{1,0:T(8,128)} %copy-done.4, f32[104,256]{1,0:T(8,128)} %copy-done.5, f32[1,8,256,256]{3,2,1,0:T(8,128)} %refs_4_.1), custom_call_target="tpu_custom_call" | custom-call | tf_op jit(solution)/shard_map/pallas_call | solution.py:209
  36.3 1.1 %dynamic-slice_bitcast_fusion.2 = (f32[3,32,256]{2,1,0:T(8,128)S(1)}, f32[3,32,256]{2,1,0:T(8,128)S(1)}, f32[3,32,256]{2,1,0:T(8,128)S(1)}, f32[3,32,256]{2,1,0:T(8,128)S(1)}) fusion(f32[4,3,32,256]{3,2,1,0:T(8,128)} %shard_map.106, s32[]{:T(128)S(6)} %select_n.70, s32[]{:T(128)S(6)} %select_n.74, s32[]{:T(128)S(6)} %select_n.72, s32[]{:T(128)S(6)} %select_n.68), kind=kLoop, calls=%fused_computation.13 | loop fusion | bytes 786448 | tf_op jit(solution)/shard_map/squeeze | solution.py:283
  37.6 1.5 %collective-permute-start.8 = (f32[3,32,256]{2,1,0:T(8,128)S(1)}, f32[3,32,256]{2,1,0:T(8,128)S(1)}, u32[]{:S(2)}, u32[]{:S(2)}) collective-permute-start(f32[3,32,256]{2,1,0:T(8,128)S(1)} %get-tuple-element.6), channel_id=1, source_target_pairs={{0,17},{1,18},{2,19},{3,16},{16,1},{17,2},{18,3},{19,0},{4,21},{5,... | collective-permute-start | bytes 294920 | tf_op jit(solution)/shard_map/ppermute | solution.py:283
  39.2 0.6 %collective-permute-start.9 = (f32[3,32,256]{2,1,0:T(8,128)S(1)}, f32[3,32,256]{2,1,0:T(8,128)S(1)}, u32[]{:S(2)}, u32[]{:S(2)}) collective-permute-start(f32[3,32,256]{2,1,0:T(8,128)S(1)} %get-tuple-element.8), channel_id=1, source_target_pairs={{0,18},{1,19},{2,16},{3,17},{16,2},{17,3},{18,0},{19,1},{4,22},{5,... | collective-permute-start | bytes 294920 | tf_op jit(solution)/shard_map/ppermute | solution.py:283
  39.8 1.5 %pad_maximum_fusion.wide_ref = f32[25,40,384]{2,1,0:T(8,128)} fusion(f32[25,2,384]{2,1,0:T(2,128)S(1)} %reshape.114, f32[25,2,384]{2,1,0:T(2,128)S(1)} %reshape.112, f32[25,32,2]{2,1,0:T(8,128)S(1)} %reshape.110, f32[25,32,124]{2,1,0:T(8,128)S(1)} %broadcast_in_dim.24, f32[25,32,2]{2,1,0:T(8,128)S(1)} %reshape.108, f32[1,32,256]{2,1,0:T(8,128)S(1)} %convert_select_fusion, ...), kind=kLoop, calls=%fused_computation | loop fusion | flops 2688000 | bytes 2918560 | tf_op jit(solution)/shard_map/concatenate | solution.py:46
  41.3 0.7 %broadcast_in_dim.10.row_ref = f32[2,40,384]{2,1,0:T(8,128)} broadcast(f32[2,40]{1,0:T(2,128)S(1)} %pad_maximum_fusion.8), dimensions={0,1} | broadcast | bytes 123200 | tf_op jit(solution)/shard_map/broadcast_in_dim | solution.py:304
  42.0 4.3 %shard_map.104 = f32[1,3,8,32,256]{4,3,2,1,0:T(8,128)} custom-call(f32[1,4,8]{2,1,0:T(4,128)} %coef_ref.1, f32[2,40,384]{2,1,0:T(8,128)} %broadcast_in_dim.10.row_ref, f32[25,40,384]{2,1,0:T(8,128)} %pad_maximum_fusion.wide_ref), custom_call_target="tpu_custom_call" | custom-call | tf_op jit(solution)/shard_map/pallas_call | solution.py:103
  46.4 0.7 %multiply_bitcast_fusion = f32[1,3,32,256]{3,2,1,0:T(8,128)} fusion(f32[3,32,256]{2,1,0:T(8,128)S(1)} %collective-permute-done.10, f32[3,32,256]{2,1,0:T(8,128)S(1)} %collective-permute-done.9, f32[3,32,256]{2,1,0:T(8,128)S(1)} %collective-permute-done.7, f32[3,32,256]{2,1,0:T(8,128)S(1)} %collective-permute-done.8, f32[32,256]{1,0:T(8,128)S(1)} %convert_bitcast_fusion), kind=kLoop, calls=%fused_computation.10 | loop fusion | flops 98304 | bytes 524288 | tf_op jit(solution)/shard_map/broadcast_in_dim | solution.py:306
  (41 shorter events, 2.0 us)
Async XLA Ops:
  0.6 10.8 %copy-start.2 = (s32[1,32,256]{2,1,0:T(8,128)S(1)}, s32[1,32,256]{2,1,0:T(8,128)}, u32[]{:S(2)}) copy-start(s32[1,32,256]{2,1,0:T(8,128)} %sea_ref.1) | copy-start | bytes 98308
  0.6 10.7 %copy-start = (f32[1,3,8,32,256]{4,3,2,1,0:T(8,128)S(1)}, f32[1,3,8,32,256]{4,3,2,1,0:T(8,128)}, u32[]{:S(2)}) copy-start(f32[1,3,8,32,256]{4,3,2,1,0:T(8,128)} %ground_ref.1) | copy-start | bytes 2359300
  3.7 7.9 %copy-start.1 = (f32[1,3,32,256]{3,2,1,0:T(8,128)S(1)}, f32[1,3,32,256]{3,2,1,0:T(8,128)}, u32[]{:S(2)}) copy-start(f32[1,3,32,256]{3,2,1,0:T(8,128)} %previous_ref.1) | copy-start | bytes 294916
  3.7 24.5 %collective-permute-start.4 = (f32[104,256]{1,0:T(8,128)}, f32[104,256]{1,0:T(8,128)S(1)}, u32[]{:S(2)}, u32[]{:S(2)}) collective-permute-start(f32[104,256]{1,0:T(8,128)} %shard_map.105.refs_0_), channel_id=1, source_target_pairs={{0,4},{4,8},{8,12},{12,0},{1,5},{5,9},{9,13},{13,1},{2,6},{6,10},{... | collective-permute-start | bytes 319496 | tf_op jit(solution)/shard_map/ppermute | solution.py:270
  6.7 21.5 %collective-permute-start.5 = (f32[104,256]{1,0:T(8,128)}, f32[104,256]{1,0:T(8,128)S(1)}, u32[]{:S(2)}, u32[]{:S(2)}) collective-permute-start(f32[104,256]{1,0:T(8,128)} %shard_map.105.refs_0_), channel_id=1, source_target_pairs={{0,8},{4,12},{8,0},{12,4},{1,9},{5,13},{9,1},{13,5},{2,10},{6,14},... | collective-permute-start | bytes 319496 | tf_op jit(solution)/shard_map/ppermute | solution.py:270
  9.3 18.9 %collective-permute-start.6 = (f32[104,256]{1,0:T(8,128)}, f32[104,256]{1,0:T(8,128)S(1)}, u32[]{:S(2)}, u32[]{:S(2)}) collective-permute-start(f32[104,256]{1,0:T(8,128)} %shard_map.105.refs_0_), channel_id=1, source_target_pairs={{0,12},{4,0},{8,4},{12,8},{1,13},{5,1},{9,5},{13,9},{2,14},{6,2},{... | collective-permute-start | bytes 319496 | tf_op jit(solution)/shard_map/ppermute | solution.py:270
  12.2 3.9 %collective-permute-start = (f32[1600]{0:T(1024)S(1)}, f32[1600]{0:T(1024)S(1)}, u32[]{:S(2)}, u32[]{:S(2)}) collective-permute-start(f32[1600]{0:T(1024)S(1)} %reshape.107), channel_id=1, source_target_pairs={{1,0},{2,1},{3,2},{0,3},{5,4},{6,5},{7,6},{4,7},{9,8},{10,9},{11,1... | collective-permute-start | bytes 19208 | tf_op jit(solution)/shard_map/ppermute | solution.py:31
  14.9 4.6 %collective-permute-start.1 = (f32[1600]{0:T(1024)S(1)}, f32[1600]{0:T(1024)S(1)}, u32[]{:S(2)}, u32[]{:S(2)}) collective-permute-start(f32[1600]{0:T(1024)S(1)} %reshape.109), channel_id=1, source_target_pairs={{0,1},{1,2},{2,3},{3,0},{4,5},{5,6},{6,7},{7,4},{8,9},{9,10},{10,1... | collective-permute-start | bytes 19208 | tf_op jit(solution)/shard_map/ppermute | solution.py:31
  20.1 6.3 %collective-permute-start.2 = (f32[19200]{0:T(1024)S(1)}, f32[19200]{0:T(1024)S(1)}, u32[]{:S(2)}, u32[]{:S(2)}) collective-permute-start(f32[19200]{0:T(1024)S(1)} %reshape.111), channel_id=1, source_target_pairs={{4,0},{8,4},{12,8},{5,1},{9,5},{13,9},{6,2},{10,6},{14,10},{7,3},{... | collective-permute-start | bytes 230408 | tf_op jit(solution)/shard_map/ppermute | solution.py:31
  21.5 6.6 %collective-permute-start.3 = (f32[19200]{0:T(1024)S(1)}, f32[19200]{0:T(1024)S(1)}, u32[]{:S(2)}, u32[]{:S(2)}) collective-permute-start(f32[19200]{0:T(1024)S(1)} %reshape.113), channel_id=1, source_target_pairs={{0,4},{4,8},{8,12},{1,5},{5,9},{9,13},{2,6},{6,10},{10,14},{3,7},{... | collective-permute-start | bytes 230408 | tf_op jit(solution)/shard_map/ppermute | solution.py:31
  28.1 0.6 %copy-start.3 = (f32[104,256]{1,0:T(8,128)}, f32[104,256]{1,0:T(8,128)S(1)}, u32[]{:S(2)}) copy-start(f32[104,256]{1,0:T(8,128)S(1)} %collective-permute-done.4.refs_1_) | copy-start | bytes 319492
  28.2 0.7 %copy-start.4 = (f32[104,256]{1,0:T(8,128)}, f32[104,256]{1,0:T(8,128)S(1)}, u32[]{:S(2)}) copy-start(f32[104,256]{1,0:T(8,128)S(1)} %collective-permute-done.5.refs_2_) | copy-start | bytes 319492
  28.2 0.7 %copy-start.5 = (f32[104,256]{1,0:T(8,128)}, f32[104,256]{1,0:T(8,128)S(1)}, u32[]{:S(2)}) copy-start(f32[104,256]{1,0:T(8,128)S(1)} %collective-permute-done.6.refs_3_) | copy-start | bytes 319492
  37.4 9.0 %collective-permute-start.10 = (f32[3,32,256]{2,1,0:T(8,128)S(1)}, f32[3,32,256]{2,1,0:T(8,128)S(1)}, u32[]{:S(2)}, u32[]{:S(2)}) collective-permute-start(f32[3,32,256]{2,1,0:T(8,128)S(1)} %get-tuple-element.7), channel_id=1, source_target_pairs={{0,19},{1,16},{2,17},{3,18},{16,3},{17,0},{18,1},{19,2},{4,23},{5,... | collective-permute-start | bytes 294920 | tf_op jit(solution)/shard_map/ppermute | solution.py:283
  37.4 8.9 %collective-permute-start.7 = (f32[3,32,256]{2,1,0:T(8,128)S(1)}, f32[3,32,256]{2,1,0:T(8,128)S(1)}, u32[]{:S(2)}, u32[]{:S(2)}) collective-permute-start(f32[3,32,256]{2,1,0:T(8,128)S(1)} %get-tuple-element.9), channel_id=1, source_target_pairs={{0,16},{1,17},{2,18},{3,19},{16,0},{17,1},{18,2},{19,3},{4,20},{5,... | collective-permute-start | bytes 294920 | tf_op jit(solution)/shard_map/ppermute | solution.py:283
  37.6 8.7 %collective-permute-start.8 = (f32[3,32,256]{2,1,0:T(8,128)S(1)}, f32[3,32,256]{2,1,0:T(8,128)S(1)}, u32[]{:S(2)}, u32[]{:S(2)}) collective-permute-start(f32[3,32,256]{2,1,0:T(8,128)S(1)} %get-tuple-element.6), channel_id=1, source_target_pairs={{0,17},{1,18},{2,19},{3,16},{16,1},{17,2},{18,3},{19,0},{4,21},{5,... | collective-permute-start | bytes 294920 | tf_op jit(solution)/shard_map/ppermute | solution.py:283
  39.2 7.2 %collective-permute-start.9 = (f32[3,32,256]{2,1,0:T(8,128)S(1)}, f32[3,32,256]{2,1,0:T(8,128)S(1)}, u32[]{:S(2)}, u32[]{:S(2)}) collective-permute-start(f32[3,32,256]{2,1,0:T(8,128)S(1)} %get-tuple-element.8), channel_id=1, source_target_pairs={{0,18},{1,19},{2,16},{3,17},{16,2},{17,3},{18,0},{19,1},{4,22},{5,... | collective-permute-start | bytes 294920 | tf_op jit(solution)/shard_map/ppermute | solution.py:283

commit v7 on v6

--- a/solution.py
+++ b/solution.py
@@ -51,23 +51,26 @@
 def stencil_kernel(coef_ref, row_ref, wide_ref, out_ref, mid_ref):
     field_count, level_count, row_count, col_count = out_ref.shape[1:]
     wide_rows, wide_cols = wide_ref.shape[1:]
-    turning = row_ref[0]
-    keep = wide_ref[field_count * level_count] * row_ref[1]
-
-    def step(read, write):
+    turning_wide = jnp.broadcast_to(row_ref[0], (wide_rows, wide_cols))
+    keep_wide = wide_ref[field_count * level_count] * jnp.broadcast_to(row_ref[1], (wide_rows, wide_cols))
+
+    def step(read, write, rows, cols):
+        turning = turning_wide[:rows, :cols]
+        keep = keep_wide[:rows, :cols]
         for field in range(field_count):
             for level in range(level_count):
                 diffuse = coef_ref[0, 0, level]
                 advect_east = coef_ref[0, 1, level]
                 advect_north = coef_ref[0, 2, level]
                 mixing = coef_ref[0, 3, level]
-                center = read(field, level)
-                north = pltpu.roll(center, wide_rows - 1, 0)
-                south = pltpu.roll(center, 1, 0)
-                east = pltpu.roll(center, wide_cols - 1, 1)
-                west = pltpu.roll(center, 1, 1)
-                above = read(field, min(level + 1, level_count - 1))
-                below = read(field, max(level - 1, 0))
+                whole = read(field, level)
+                north = pltpu.roll(whole, wide_rows - 1, 0)[:rows, :cols]
+                south = pltpu.roll(whole, 1, 0)[:rows, :cols]
+                east = pltpu.roll(whole, wide_cols - 1, 1)[:rows, :cols]
+                west = pltpu.roll(whole, 1, 1)[:rows, :cols]
+                center = whole[:rows, :cols]
+                above = read(field, min(level + 1, level_count - 1))[:rows, :cols]
+                below = read(field, max(level - 1, 0))[:rows, :cols]
                 laplace = north + south + east + west - 4.0 * center
                 updated = (
                     center
@@ -77,9 +80,9 @@
                     + mixing * (above + below - 2.0 * center)
                 )
                 if field == 0:
-                    updated = updated + turning * read(1, level)
+                    updated = updated + turning * read(1, level)[:rows, :cols]
                 elif field == 1:
-                    updated = updated + (-turning) * read(0, level)
+                    updated = updated + (-turning) * read(0, level)[:rows, :cols]
                 write(field, level, updated * keep)
 
     def from_wide(field, level):
@@ -92,10 +95,10 @@
         return mid_ref[field * level_count + level]
 
     def to_out(field, level, value):
-        out_ref[0, field, level] = value[:row_count, :col_count]
-
-    step(from_wide, to_mid)
-    step(from_mid, to_out)
+        out_ref[0, field, level] = value
+
+    step(from_wide, to_mid, wide_rows, wide_cols)
+    step(from_mid, to_out, row_count, col_count)
 
 
 def dynamics(coeffs, row_terms, wide, field_count, level_count, row_count, col_count):
@@ -157,13 +160,14 @@
     )(flag, state, surface, sea_mask, links)
 
 
-def remap_kernel(link_count, source_count, lat_ref, *refs):
+def remap_kernel(link_count, source_count, place_ref, *refs):
     source_refs = refs[:source_count]
     table_ref, out_ref, rows_ref, combo_ref = refs[source_count:]
     tile_count = table_ref.shape[1]
     owner_count, field_count, row_count, col_count = out_ref.shape
     base = field_count * row_count
-    my_lat = lat_ref[0]
+    my_lat = place_ref[0]
+    my_lon = place_ref[1]
     for source in range(source_count):
         rows_ref[source * base : (source + 1) * base, :] = source_refs[source][:base, :]
     for tile in range(tile_count):
@@ -183,7 +187,9 @@
         dest, src_row, dst_row, tile = table[0:1], table[1:2], table[2:3], table[3:4]
         low = my_lat * owner_count
         valid = (dest >= low) & (dest < low + owner_count)
-        dest_col = (dest - low) * row_count + dst_row
+        shift = dest - low - my_lon
+        shift = jnp.where(shift < 0, shift + owner_count, shift)
+        dest_col = shift * row_count + dst_row
         pick_col = (source * tile_count + tile) * row_count + src_row
         to_rows = (
             (lax.broadcasted_iota(jnp.int32, (owner_count * row_count, link_count), 0) == dest_col)
@@ -270,8 +276,8 @@
         lax.ppermute(payload, "lat", [(i, (i + shift) % lat_count) for i in range(lat_count)])
         for shift in range(1, lat_count)
     ]
-    lat = lax.axis_index("lat").astype(jnp.int32).reshape(1)
-    partial = remapped(lat, sources, remap_weights, lon_count, field_count, row_count, links.shape[1])
+    place = jnp.stack([lax.axis_index("lat"), lax.axis_index("lon")]).astype(jnp.int32)
+    partial = remapped(place, sources, remap_weights, lon_count, field_count, row_count, links.shape[1])
     pieces = []
     for shift in range(lon_count):
         route = [
@@ -279,8 +285,7 @@
             for g in range(2)
             for j in range(lon_count)
         ]
-        owner_lon = (lax.axis_index("lon") + shift) % lon_count
-        pieces.append(lax.ppermute(partial[owner_lon], ("grp", "lon"), route))
+        pieces.append(lax.ppermute(partial[shift], ("grp", "lon"), route))
     imported = functools.reduce(jnp.add, pieces) * sea_float
 
     gain = jnp.where(ocean_side, ocean_gain, air_gain)
@@ -301,7 +306,7 @@
     )
     coriolis = coriolis_scale * jnp.sin(latitude)
     inside = ((row_index >= 0) & (row_index < total_rows)).astype(jnp.float32)
-    row_terms = jnp.broadcast_to(jnp.stack([coriolis, inside])[:, :, None], (2, wide_rows, wide_cols))
+    row_terms = jnp.stack([coriolis, inside])[:, :, None]
     fields = dynamics(coeffs, row_terms, wide, field_count, level_count, row_count, col_count)
     return (fields, imported[None])
 

time: 47.4 us -> 46.5 us (0.981)
  waiting for transfers between devices: 5.91 us -> 4.69 us
  local copies, waits for them, and re-layouts: 4.16 us -> 4.75 us
    ppermute x4, waiting for transfers between devices: 5.89 us -> 4.58 us  [shifted(): flat = lax.ppermute(part.reshape(-1), axis, route)]
    mul x1, other arithmetic: 0.76 us -> 0.01 us  [body(): sea_float * (gain * previous - damping * fields[:, 0])]
    another operation x1, other arithmetic: 0.01 us -> 0.65 us  [body(): jnp.stack([lax.axis_index('lat'), lax.axis_index('lon')]).astype(jnp.int32)]
    unnamed x13, local copies, waits for them, and re-layouts: 0.76 us -> 1.35 us
where the time goes in v7:
time: 46.5 us; the launch traced here: 46.2 us
  starting transfers between devices  17.8 us (38%)
  Pallas kernels  13.3 us (29%)
  local copies, waits for them, and re-layouts  4.75 us (10%)
  other arithmetic  4.74 us (10%)
  waiting for transfers between devices  4.69 us (10%)
  between operations  0.9 us (2%)
    ppermute x4, starting transfers between devices, shifted(): flat = lax.ppermute(part.reshape(-1), axis, route)  8.4 us
    pallas_call x1, Pallas kernels, remapped(): pl.pallas_call(functools.partial(remap_kernel, link_count, source_count),...  7.44 us
    ppermute x3, starting transfers between devices, body(): lax.ppermute(payload, 'lat', [(i, (i + shift) % lat_count) for i in range...  6.96 us
    ppermute x4, waiting for transfers between devices, shifted(): flat = lax.ppermute(part.reshape(-1), axis, route)  4.58 us
    pallas_call x1, Pallas kernels, dynamics(): pl.pallas_call(stencil_kernel, out_shape=jax.ShapeDtypeStruct((1, field_c...  4.27 us
    ppermute x4, starting transfers between devices, body(): pieces.append(lax.ppermute(partial[shift], ('grp', 'lon'), route))  2.41 us
    pallas_call x1, Pallas kernels, exported_block(): pl.pallas_call(export_kernel, out_shape=jax.ShapeDtypeStruct((field_count...  1.64 us
    concatenate x1, other arithmetic, with_halo(): jnp.concatenate([cells, shifted(head, 'lat', False, False), gap, shifted(...  1.51 us
  transfers between devices with their start and end apart: 11, of which 4 were waited for; matrix products, arithmetic and copies ran while one was open for 11% of the time, Pallas kernels for 9%

profile of v7, /device:TPU:0, one launch (start us, length us, event | category | flops | bytes accessed | tf_op | source)
XLA Modules:
  0.0 46.2 jit_solution(14316602118774848638)
XLA Ops:
  0.7 1.4 %add_convert_fusion.link_ref = f32[4,128]{1,0:T(4,128)} fusion(s32[1,128]{1,0:T(1,128)} %param.17, s32[1,128]{1,0:T(1,128)} %param.16, s32[1,128]{1,0:T(1,128)} %param.15, s32[1,128]{1,0:T(1,128)} %bitcast.33), kind=kLoop, calls=%fused_computation.23 | loop fusion | flops 2048 | bytes 4096 | tf_op jit(solution)/shard_map/convert_element_type | solution.py:270
  2.0 1.6 %shard_map.105.refs_0_ = f32[104,256]{1,0:T(8,128)} custom-call(s32[1]{0:T(128)} %bitcast.7.flag_ref, f32[1,3,8,32,256]{4,3,2,1,0:T(8,128)} %ground_ref.1, f32[1,3,32,256]{3,2,1,0:T(8,128)} %previous_ref.1, s32[1,32,256]{2,1,0:T(8,128)} %sea_ref.1, f32[4,128]{1,0:T(4,128)} %add_convert_fusion.link_ref), custom_call_target="tpu_custom_call" | custom-call | tf_op jit(solution)/shard_map/pallas_call | solution.py:147
  3.7 3.0 %collective-permute-start.4 = (f32[104,256]{1,0:T(8,128)}, f32[104,256]{1,0:T(8,128)S(1)}, u32[]{:S(2)}, u32[]{:S(2)}) collective-permute-start(f32[104,256]{1,0:T(8,128)} %shard_map.105.refs_0_), channel_id=1, source_target_pairs={{0,4},{4,8},{8,12},{12,0},{1,5},{5,9},{9,13},{13,1},{2,6},{6,10},{... | collective-permute-start | bytes 319496 | tf_op jit(solution)/shard_map/ppermute | solution.py:276
  6.7 2.6 %collective-permute-start.5 = (f32[104,256]{1,0:T(8,128)}, f32[104,256]{1,0:T(8,128)S(1)}, u32[]{:S(2)}, u32[]{:S(2)}) collective-permute-start(f32[104,256]{1,0:T(8,128)} %shard_map.105.refs_0_), channel_id=1, source_target_pairs={{0,8},{4,12},{8,0},{12,4},{1,9},{5,13},{9,1},{13,5},{2,10},{6,14},... | collective-permute-start | bytes 319496 | tf_op jit(solution)/shard_map/ppermute | solution.py:276
  9.3 1.3 %collective-permute-start.6 = (f32[104,256]{1,0:T(8,128)}, f32[104,256]{1,0:T(8,128)S(1)}, u32[]{:S(2)}, u32[]{:S(2)}) collective-permute-start(f32[104,256]{1,0:T(8,128)} %shard_map.105.refs_0_), channel_id=1, source_target_pairs={{0,12},{4,0},{8,4},{12,8},{1,13},{5,1},{9,5},{13,9},{2,14},{6,2},{... | collective-permute-start | bytes 319496 | tf_op jit(solution)/shard_map/ppermute | solution.py:276
  11.2 0.2 reshape.103
  11.4 2.5 %collective-permute-start = (f32[1600]{0:T(1024)S(1)}, f32[1600]{0:T(1024)S(1)}, u32[]{:S(2)}, u32[]{:S(2)}) collective-permute-start(f32[1600]{0:T(1024)S(1)} %reshape.103), channel_id=1, source_target_pairs={{1,0},{2,1},{3,2},{0,3},{5,4},{6,5},{7,6},{4,7},{9,8},{10,9},{11,1... | collective-permute-start | bytes 19208 | tf_op jit(solution)/shard_map/ppermute | solution.py:31
  14.3 0.7 %copy.16.row_ref = f32[2,40,1]{2,1,0:T(8,128)} copy(f32[2,40,1]{1,0,2:T(2,128)S(1)} %maximum_bitcast_fusion) | data formatting | bytes 640 | tf_op jit(solution)/shard_map/broadcast_in_dim | solution.py:309
  15.3 0.4 reshape.104
  15.6 3.1 %collective-permute-done.1 = f32[1600]{0:T(1024)S(1)} collective-permute-done((f32[1600]{0:T(1024)S(1)}, f32[1600]{0:T(1024)S(1)}, u32[]{:S(2)}, u32[]{:S(2)}) %collective-permute-start.1) | collective-permute-done | bytes 6432 | tf_op jit(solution)/shard_map/ppermute | solution.py:31
  18.7 0.4 reshape.106
  19.4 1.3 %collective-permute-start.2 = (f32[19200]{0:T(1024)S(1)}, f32[19200]{0:T(1024)S(1)}, u32[]{:S(2)}, u32[]{:S(2)}) collective-permute-start(f32[19200]{0:T(1024)S(1)} %reshape.107), channel_id=1, source_target_pairs={{4,0},{8,4},{12,8},{5,1},{9,5},{13,9},{6,2},{10,6},{14,10},{7,3},{... | collective-permute-start | bytes 230408 | tf_op jit(solution)/shard_map/ppermute | solution.py:31
  20.8 4.6 %collective-permute-start.3 = (f32[19200]{0:T(1024)S(1)}, f32[19200]{0:T(1024)S(1)}, u32[]{:S(2)}, u32[]{:S(2)}) collective-permute-start(f32[19200]{0:T(1024)S(1)} %reshape.109), channel_id=1, source_target_pairs={{0,4},{4,8},{8,12},{1,5},{5,9},{9,13},{2,6},{6,10},{10,14},{3,7},{... | collective-permute-start | bytes 230408 | tf_op jit(solution)/shard_map/ppermute | solution.py:31
  25.3 0.7 %pad_add_fusion.place_ref = s32[2]{0:T(128)} fusion(s32[1]{0:T(128)} %bitcast.6, s32[1]{0:T(128)} %bitcast.5), kind=kLoop, calls=%fused_computation.27 | loop fusion | flops 2 | bytes 16 | tf_op jit(solution)/shard_map/stack | solution.py:279
  26.0 1.3 %collective-permute-done.3 = f32[19200]{0:T(1024)S(1)} collective-permute-done((f32[19200]{0:T(1024)S(1)}, f32[19200]{0:T(1024)S(1)}, u32[]{:S(2)}, u32[]{:S(2)}) %collective-permute-start.3) | collective-permute-done | bytes 76832 | tf_op jit(solution)/shard_map/ppermute | solution.py:31
  27.4 0.6 %copy-done.3 = f32[104,256]{1,0:T(8,128)} copy-done((f32[104,256]{1,0:T(8,128)}, f32[104,256]{1,0:T(8,128)S(1)}, u32[]{:S(2)}) %copy-start.3) | copy-done | bytes 106520
  28.1 0.6 %copy-done.5 = f32[104,256]{1,0:T(8,128)} copy-done((f32[104,256]{1,0:T(8,128)}, f32[104,256]{1,0:T(8,128)S(1)}, u32[]{:S(2)}) %copy-start.5) | copy-done | bytes 106520
  28.7 7.4 %shard_map.106 = f32[4,3,32,256]{3,2,1,0:T(8,128)} custom-call(s32[2]{0:T(128)} %pad_add_fusion.place_ref, f32[104,256]{1,0:T(8,128)} %shard_map.105.refs_0_, f32[104,256]{1,0:T(8,128)} %copy-done.3, f32[104,256]{1,0:T(8,128)} %copy-done.4, f32[104,256]{1,0:T(8,128)} %copy-done.5, f32[1,8,256,256]{3,2,1,0:T(8,128)} %refs_4_.1), custom_call_target="tpu_custom_call" | custom-call | tf_op jit(solution)/shard_map/pallas_call | solution.py:215
  36.1 1.1 %slice_bitcast_fusion.2 = (f32[3,32,256]{2,1,0:T(8,128)S(1)}, f32[3,32,256]{2,1,0:T(8,128)S(1)}, f32[3,32,256]{2,1,0:T(8,128)S(1)}, f32[3,32,256]{2,1,0:T(8,128)S(1)}) fusion(f32[4,3,32,256]{3,2,1,0:T(8,128)} %shard_map.106), kind=kLoop, calls=%fused_computation.9 | loop fusion | bytes 786432 | tf_op jit(solution)/shard_map/squeeze | solution.py:288
  37.5 1.5 %collective-permute-start.8 = (f32[3,32,256]{2,1,0:T(8,128)S(1)}, f32[3,32,256]{2,1,0:T(8,128)S(1)}, u32[]{:S(2)}, u32[]{:S(2)}) collective-permute-start(f32[3,32,256]{2,1,0:T(8,128)S(1)} %get-tuple-element.6), channel_id=1, source_target_pairs={{0,17},{1,18},{2,19},{3,16},{16,1},{17,2},{18,3},{19,0},{4,21},{5,... | collective-permute-start | bytes 294920 | tf_op jit(solution)/shard_map/ppermute | solution.py:288
  39.0 0.6 %collective-permute-start.9 = (f32[3,32,256]{2,1,0:T(8,128)S(1)}, f32[3,32,256]{2,1,0:T(8,128)S(1)}, u32[]{:S(2)}, u32[]{:S(2)}) collective-permute-start(f32[3,32,256]{2,1,0:T(8,128)S(1)} %get-tuple-element.8), channel_id=1, source_target_pairs={{0,18},{1,19},{2,16},{3,17},{16,2},{17,3},{18,0},{19,1},{4,22},{5,... | collective-permute-start | bytes 294920 | tf_op jit(solution)/shard_map/ppermute | solution.py:288
  39.6 1.5 %pad_maximum_fusion.wide_ref = f32[25,40,384]{2,1,0:T(8,128)} fusion(f32[25,2,384]{2,1,0:T(2,128)S(1)} %reshape.110, f32[25,2,384]{2,1,0:T(2,128)S(1)} %reshape.108, f32[25,32,2]{2,1,0:T(8,128)S(1)} %reshape.106, f32[25,32,124]{2,1,0:T(8,128)S(1)} %broadcast_in_dim.21, f32[25,32,2]{2,1,0:T(8,128)S(1)} %reshape.104, f32[1,32,256]{2,1,0:T(8,128)S(1)} %convert_select_fusion, ...), kind=kLoop, calls=%fused_computation | loop fusion | flops 2688000 | bytes 2918560 | tf_op jit(solution)/shard_map/concatenate | solution.py:46
  41.1 4.3 %shard_map.104 = f32[1,3,8,32,256]{4,3,2,1,0:T(8,128)} custom-call(f32[1,4,8]{2,1,0:T(4,128)} %coef_ref.1, f32[2,40,1]{2,1,0:T(8,128)} %copy.16.row_ref, f32[25,40,384]{2,1,0:T(8,128)} %pad_maximum_fusion.wide_ref), custom_call_target="tpu_custom_call" | custom-call | tf_op jit(solution)/shard_map/pallas_call | solution.py:106
  45.5 0.7 %multiply_bitcast_fusion = f32[1,3,32,256]{3,2,1,0:T(8,128)} fusion(f32[3,32,256]{2,1,0:T(8,128)S(1)} %collective-permute-done.10, f32[3,32,256]{2,1,0:T(8,128)S(1)} %collective-permute-done.9, f32[3,32,256]{2,1,0:T(8,128)S(1)} %collective-permute-done.7, f32[3,32,256]{2,1,0:T(8,128)S(1)} %collective-permute-done.8, f32[32,256]{1,0:T(8,128)S(1)} %convert_bitcast_fusion), kind=kLoop, calls=%fused_computation.14 | loop fusion | flops 98304 | bytes 524288 | tf_op jit(solution)/shard_map/broadcast_in_dim | solution.py:311
  (42 shorter events, 2.0 us)
Async XLA Ops:
  0.6 10.0 %copy-start = (f32[1,3,8,32,256]{4,3,2,1,0:T(8,128)S(1)}, f32[1,3,8,32,256]{4,3,2,1,0:T(8,128)}, u32[]{:S(2)}) copy-start(f32[1,3,8,32,256]{4,3,2,1,0:T(8,128)} %ground_ref.1) | copy-start | bytes 2359300
  0.6 10.0 %copy-start.2 = (s32[1,32,256]{2,1,0:T(8,128)S(1)}, s32[1,32,256]{2,1,0:T(8,128)}, u32[]{:S(2)}) copy-start(s32[1,32,256]{2,1,0:T(8,128)} %sea_ref.1) | copy-start | bytes 98308
  3.7 7.1 %copy-start.1 = (f32[1,3,32,256]{3,2,1,0:T(8,128)S(1)}, f32[1,3,32,256]{3,2,1,0:T(8,128)}, u32[]{:S(2)}) copy-start(f32[1,3,32,256]{3,2,1,0:T(8,128)} %previous_ref.1) | copy-start | bytes 294916
  3.7 23.7 %collective-permute-start.4 = (f32[104,256]{1,0:T(8,128)}, f32[104,256]{1,0:T(8,128)S(1)}, u32[]{:S(2)}, u32[]{:S(2)}) collective-permute-start(f32[104,256]{1,0:T(8,128)} %shard_map.105.refs_0_), channel_id=1, source_target_pairs={{0,4},{4,8},{8,12},{12,0},{1,5},{5,9},{9,13},{13,1},{2,6},{6,10},{... | collective-permute-start | bytes 319496 | tf_op jit(solution)/shard_map/ppermute | solution.py:276
  6.7 20.7 %collective-permute-start.5 = (f32[104,256]{1,0:T(8,128)}, f32[104,256]{1,0:T(8,128)S(1)}, u32[]{:S(2)}, u32[]{:S(2)}) collective-permute-start(f32[104,256]{1,0:T(8,128)} %shard_map.105.refs_0_), channel_id=1, source_target_pairs={{0,8},{4,12},{8,0},{12,4},{1,9},{5,13},{9,1},{13,5},{2,10},{6,14},... | collective-permute-start | bytes 319496 | tf_op jit(solution)/shard_map/ppermute | solution.py:276
  9.3 18.1 %collective-permute-start.6 = (f32[104,256]{1,0:T(8,128)}, f32[104,256]{1,0:T(8,128)S(1)}, u32[]{:S(2)}, u32[]{:S(2)}) collective-permute-start(f32[104,256]{1,0:T(8,128)} %shard_map.105.refs_0_), channel_id=1, source_target_pairs={{0,12},{4,0},{8,4},{12,8},{1,13},{5,1},{9,5},{13,9},{2,14},{6,2},{... | collective-permute-start | bytes 319496 | tf_op jit(solution)/shard_map/ppermute | solution.py:276
  11.4 3.9 %collective-permute-start = (f32[1600]{0:T(1024)S(1)}, f32[1600]{0:T(1024)S(1)}, u32[]{:S(2)}, u32[]{:S(2)}) collective-permute-start(f32[1600]{0:T(1024)S(1)} %reshape.103), channel_id=1, source_target_pairs={{1,0},{2,1},{3,2},{0,3},{5,4},{6,5},{7,6},{4,7},{9,8},{10,9},{11,1... | collective-permute-start | bytes 19208 | tf_op jit(solution)/shard_map/ppermute | solution.py:31
  14.1 4.6 %collective-permute-start.1 = (f32[1600]{0:T(1024)S(1)}, f32[1600]{0:T(1024)S(1)}, u32[]{:S(2)}, u32[]{:S(2)}) collective-permute-start(f32[1600]{0:T(1024)S(1)} %reshape.105), channel_id=1, source_target_pairs={{0,1},{1,2},{2,3},{3,0},{4,5},{5,6},{6,7},{7,4},{8,9},{9,10},{10,1... | collective-permute-start | bytes 19208 | tf_op jit(solution)/shard_map/ppermute | solution.py:31
  19.4 6.6 %collective-permute-start.2 = (f32[19200]{0:T(1024)S(1)}, f32[19200]{0:T(1024)S(1)}, u32[]{:S(2)}, u32[]{:S(2)}) collective-permute-start(f32[19200]{0:T(1024)S(1)} %reshape.107), channel_id=1, source_target_pairs={{4,0},{8,4},{12,8},{5,1},{9,5},{13,9},{6,2},{10,6},{14,10},{7,3},{... | collective-permute-start | bytes 230408 | tf_op jit(solution)/shard_map/ppermute | solution.py:31
  20.8 6.6 %collective-permute-start.3 = (f32[19200]{0:T(1024)S(1)}, f32[19200]{0:T(1024)S(1)}, u32[]{:S(2)}, u32[]{:S(2)}) collective-permute-start(f32[19200]{0:T(1024)S(1)} %reshape.109), channel_id=1, source_target_pairs={{0,4},{4,8},{8,12},{1,5},{5,9},{9,13},{2,6},{6,10},{10,14},{3,7},{... | collective-permute-start | bytes 230408 | tf_op jit(solution)/shard_map/ppermute | solution.py:31
  27.4 0.6 %copy-start.3 = (f32[104,256]{1,0:T(8,128)}, f32[104,256]{1,0:T(8,128)S(1)}, u32[]{:S(2)}) copy-start(f32[104,256]{1,0:T(8,128)S(1)} %collective-permute-done.4.refs_1_) | copy-start | bytes 319492
  27.4 0.7 %copy-start.4 = (f32[104,256]{1,0:T(8,128)}, f32[104,256]{1,0:T(8,128)S(1)}, u32[]{:S(2)}) copy-start(f32[104,256]{1,0:T(8,128)S(1)} %collective-permute-done.5.refs_2_) | copy-start | bytes 319492
  28.1 0.6 %copy-start.5 = (f32[104,256]{1,0:T(8,128)}, f32[104,256]{1,0:T(8,128)S(1)}, u32[]{:S(2)}) copy-start(f32[104,256]{1,0:T(8,128)S(1)} %collective-permute-done.6.refs_3_) | copy-start | bytes 319492
  37.2 8.2 %collective-permute-start.10 = (f32[3,32,256]{2,1,0:T(8,128)S(1)}, f32[3,32,256]{2,1,0:T(8,128)S(1)}, u32[]{:S(2)}, u32[]{:S(2)}) collective-permute-start(f32[3,32,256]{2,1,0:T(8,128)S(1)} %get-tuple-element.7), channel_id=1, source_target_pairs={{0,19},{1,16},{2,17},{3,18},{16,3},{17,0},{18,1},{19,2},{4,23},{5,... | collective-permute-start | bytes 294920 | tf_op jit(solution)/shard_map/ppermute | solution.py:288
  37.3 8.1 %collective-permute-start.7 = (f32[3,32,256]{2,1,0:T(8,128)S(1)}, f32[3,32,256]{2,1,0:T(8,128)S(1)}, u32[]{:S(2)}, u32[]{:S(2)}) collective-permute-start(f32[3,32,256]{2,1,0:T(8,128)S(1)} %get-tuple-element.9), channel_id=1, source_target_pairs={{0,16},{1,17},{2,18},{3,19},{16,0},{17,1},{18,2},{19,3},{4,20},{5,... | collective-permute-start | bytes 294920 | tf_op jit(solution)/shard_map/ppermute | solution.py:288
  37.5 7.9 %collective-permute-start.8 = (f32[3,32,256]{2,1,0:T(8,128)S(1)}, f32[3,32,256]{2,1,0:T(8,128)S(1)}, u32[]{:S(2)}, u32[]{:S(2)}) collective-permute-start(f32[3,32,256]{2,1,0:T(8,128)S(1)} %get-tuple-element.6), channel_id=1, source_target_pairs={{0,17},{1,18},{2,19},{3,16},{16,1},{17,2},{18,3},{19,0},{4,21},{5,... | collective-permute-start | bytes 294920 | tf_op jit(solution)/shard_map/ppermute | solution.py:288
  39.0 6.5 %collective-permute-start.9 = (f32[3,32,256]{2,1,0:T(8,128)S(1)}, f32[3,32,256]{2,1,0:T(8,128)S(1)}, u32[]{:S(2)}, u32[]{:S(2)}) collective-permute-start(f32[3,32,256]{2,1,0:T(8,128)S(1)} %get-tuple-element.8), channel_id=1, source_target_pairs={{0,18},{1,19},{2,16},{3,17},{16,2},{17,3},{18,0},{19,1},{4,22},{5,... | collective-permute-start | bytes 294920 | tf_op jit(solution)/shard_map/ppermute | solution.py:288

commit v8 on v7

--- a/solution.py
+++ b/solution.py
@@ -272,10 +272,9 @@
     payload = exported_block(flag, state, surface, sea_mask, links)
     lat_count = lax.axis_size("lat")
     lon_count = lax.axis_size("lon")
-    sources = [payload] + [
-        lax.ppermute(payload, "lat", [(i, (i + shift) % lat_count) for i in range(lat_count)])
-        for shift in range(1, lat_count)
-    ]
+    copies = jnp.broadcast_to(payload[None], (lat_count,) + payload.shape)
+    gathered = lax.all_to_all(copies, "lat", split_axis=0, concat_axis=0, tiled=True)
+    sources = [gathered[i] for i in range(lat_count)]
     place = jnp.stack([lax.axis_index("lat"), lax.axis_index("lon")]).astype(jnp.int32)
     partial = remapped(place, sources, remap_weights, lon_count, field_count, row_count, links.shape[1])
     pieces = []

time: 46.5 us -> 49.5 us (1.065)
  local copies, waits for them, and re-layouts: 4.75 us -> 6.65 us
  waiting for transfers between devices: 4.69 us -> 5.33 us
    ppermute x3 -> x0, starting transfers between devices: 6.96 us -> none  [body(): lax.ppermute(payload, 'lat', [(i, (i + shift) % lat_count) for i in range...]
    all_to_all x0 -> x1, starting transfers between devices: none -> 6.32 us  [body(): lax.all_to_all(copies, 'lat', split_axis=0, concat_axis=0, tiled=True)]
    broadcast_in_dim x0 -> x1, local copies, waits for them, and re-layouts: none -> 1.69 us  [body(): copies = jnp.broadcast_to(payload[None], (lat_count,) + payload.shape)]
    ppermute x4, starting transfers between devices: 2.41 us -> 3.62 us  [body(): pieces.append(lax.ppermute(partial[shift], ('grp', 'lon'), route))]
    squeeze x0 -> x1, local copies, waits for them, and re-layouts: none -> 0.76 us  [body(): sources = [gathered[i] for i in range(lat_count)]]
    ppermute x4, waiting for transfers between devices: 4.58 us -> 5.32 us  [shifted(): flat = lax.ppermute(part.reshape(-1), axis, route)]
    unnamed x13 -> x7, local copies, waits for them, and re-layouts: 1.35 us -> 0.8 us
  transfers between devices with their start and end apart: 11 -> 9, of which waited for: 4 -> 3; matrix products, arithmetic and copies ran while one was open for 11% -> 10% of each run, Pallas kernels for 9% -> 9%
where the time goes in v8:
time: 49.5 us; the launch traced here: 49 us
  starting transfers between devices  18.2 us (37%)
  Pallas kernels  13.4 us (27%)
  local copies, waits for them, and re-layouts  6.65 us (13%)
  waiting for transfers between devices  5.33 us (11%)
  other arithmetic  4.67 us (9%)
  between operations  0.83 us (2%)
    ppermute x4, starting transfers between devices, shifted(): flat = lax.ppermute(part.reshape(-1), axis, route)  8.25 us
    pallas_call x1, Pallas kernels, remapped(): pl.pallas_call(functools.partial(remap_kernel, link_count, source_count),...  7.44 us
    all_to_all x1, starting transfers between devices, body(): lax.all_to_all(copies, 'lat', split_axis=0, concat_axis=0, tiled=True)  6.32 us
    ppermute x4, waiting for transfers between devices, shifted(): flat = lax.ppermute(part.reshape(-1), axis, route)  5.32 us
    pallas_call x1, Pallas kernels, dynamics(): pl.pallas_call(stencil_kernel, out_shape=jax.ShapeDtypeStruct((1, field_c...  4.27 us
    ppermute x4, starting transfers between devices, body(): pieces.append(lax.ppermute(partial[shift], ('grp', 'lon'), route))  3.62 us
    broadcast_in_dim x1, local copies, waits for them, and re-layouts, body(): copies = jnp.broadcast_to(payload[None], (lat_count,) + payload.shape)  1.69 us
    pallas_call x1, Pallas kernels, exported_block(): pl.pallas_call(export_kernel, out_shape=jax.ShapeDtypeStruct((field_count...  1.64 us
  transfers between devices with their start and end apart: 9, of which 3 were waited for; matrix products, arithmetic and copies ran while one was open for 10% of the time, Pallas kernels for 9%

profile of v8, /device:TPU:0, one launch (start us, length us, event | category | flops | bytes accessed | tf_op | source)
XLA Modules:
  0.0 49.0 jit_solution(16643669263528066793)
XLA Ops:
  0.6 1.4 %add_convert_fusion.link_ref = f32[4,128]{1,0:T(4,128)} fusion(s32[1,128]{1,0:T(1,128)} %param.17, s32[1,128]{1,0:T(1,128)} %param.16, s32[1,128]{1,0:T(1,128)} %param.15, s32[1,128]{1,0:T(1,128)} %bitcast.41), kind=kLoop, calls=%fused_computation.27 | loop fusion | flops 2048 | bytes 4096 | tf_op jit(solution)/shard_map/convert_element_type | solution.py:270
  2.0 1.6 %shard_map.105 = f32[104,256]{1,0:T(8,128)} custom-call(s32[1]{0:T(128)} %bitcast.7.flag_ref, f32[1,3,8,32,256]{4,3,2,1,0:T(8,128)} %ground_ref.1, f32[1,3,32,256]{3,2,1,0:T(8,128)} %previous_ref.1, s32[1,32,256]{2,1,0:T(8,128)} %sea_ref.1, f32[4,128]{1,0:T(4,128)} %add_convert_fusion.link_ref), custom_call_target="tpu_custom_call" | custom-call | tf_op jit(solution)/shard_map/pallas_call | solution.py:147
  3.7 1.7 %broadcast_in_dim.29 = f32[4,104,256]{2,1,0:T(8,128)} broadcast(f32[104,256]{1,0:T(8,128)} %shard_map.105), dimensions={1,2} | broadcast | bytes 532480 | tf_op jit(solution)/shard_map/broadcast_in_dim | solution.py:275
  5.3 6.3 %all-to-all-start = ((f32[4,104,256]{2,1,0:T(8,128)}), f32[4,104,256]{2,1,0:T(8,128)S(1)}, u32[]{:S(2)}, u32[]{:S(2)}) async-start(f32[4,104,256]{2,1,0:T(8,128)} %broadcast_in_dim.29), calls=%async_computation | async-start | bytes 851968 | tf_op jit(solution)/shard_map/all_to_all | solution.py:276
  11.8 0.7 %copy-done.1 = f32[1,3,32,256]{3,2,1,0:T(8,128)S(1)} copy-done((f32[1,3,32,256]{3,2,1,0:T(8,128)S(1)}, f32[1,3,32,256]{3,2,1,0:T(8,128)}, u32[]{:S(2)}) %copy-start.1) | copy-done | bytes 98328
  12.9 0.2 reshape.106
  13.2 1.5 %collective-permute-start.1 = (f32[1600]{0:T(1024)S(1)}, f32[1600]{0:T(1024)S(1)}, u32[]{:S(2)}, u32[]{:S(2)}) collective-permute-start(f32[1600]{0:T(1024)S(1)} %reshape.106), channel_id=1, source_target_pairs={{0,1},{1,2},{2,3},{3,0},{4,5},{5,6},{6,7},{7,4},{8,9},{9,10},{10,1... | collective-permute-start | bytes 19208 | tf_op jit(solution)/shard_map/ppermute | solution.py:31
  14.9 1.5 %collective-permute-start = (f32[1600]{0:T(1024)S(1)}, f32[1600]{0:T(1024)S(1)}, u32[]{:S(2)}, u32[]{:S(2)}) collective-permute-start(f32[1600]{0:T(1024)S(1)} %reshape.104), channel_id=1, source_target_pairs={{1,0},{2,1},{3,2},{0,3},{5,4},{6,5},{7,6},{4,7},{9,8},{10,9},{11,1... | collective-permute-start | bytes 19208 | tf_op jit(solution)/shard_map/ppermute | solution.py:31
  16.5 0.7 %copy.16.row_ref = f32[2,40,1]{2,1,0:T(8,128)} copy(f32[2,40,1]{1,0,2:T(2,128)S(1)} %maximum_bitcast_fusion) | data formatting | bytes 640 | tf_op jit(solution)/shard_map/broadcast_in_dim | solution.py:308
  17.3 0.5 collective-permute-done.1
  17.8 0.4 reshape.107
  18.1 0.5 %collective-permute-done = f32[1600]{0:T(1024)S(1)} collective-permute-done((f32[1600]{0:T(1024)S(1)}, f32[1600]{0:T(1024)S(1)}, u32[]{:S(2)}, u32[]{:S(2)}) %collective-permute-start) | collective-permute-done | bytes 6432 | tf_op jit(solution)/shard_map/ppermute | solution.py:31
  18.6 0.4 reshape.105
  19.3 3.9 %collective-permute-start.3 = (f32[19200]{0:T(1024)S(1)}, f32[19200]{0:T(1024)S(1)}, u32[]{:S(2)}, u32[]{:S(2)}) collective-permute-start(f32[19200]{0:T(1024)S(1)} %reshape.110), channel_id=1, source_target_pairs={{0,4},{4,8},{8,12},{1,5},{5,9},{9,13},{2,6},{6,10},{10,14},{3,7},{... | collective-permute-start | bytes 230408 | tf_op jit(solution)/shard_map/ppermute | solution.py:31
  23.3 1.3 %collective-permute-start.2 = (f32[19200]{0:T(1024)S(1)}, f32[19200]{0:T(1024)S(1)}, u32[]{:S(2)}, u32[]{:S(2)}) collective-permute-start(f32[19200]{0:T(1024)S(1)} %reshape.108), channel_id=1, source_target_pairs={{4,0},{8,4},{12,8},{5,1},{9,5},{13,9},{6,2},{10,6},{14,10},{7,3},{... | collective-permute-start | bytes 230408 | tf_op jit(solution)/shard_map/ppermute | solution.py:31
  24.6 0.6 %pad_add_fusion.place_ref = s32[2]{0:T(128)} fusion(s32[1]{0:T(128)} %bitcast.6, s32[1]{0:T(128)} %bitcast.5), kind=kLoop, calls=%fused_computation.31 | loop fusion | flops 2 | bytes 16 | tf_op jit(solution)/shard_map/stack | solution.py:278
  25.3 4.3 %collective-permute-done.2 = f32[19200]{0:T(1024)S(1)} collective-permute-done((f32[19200]{0:T(1024)S(1)}, f32[19200]{0:T(1024)S(1)}, u32[]{:S(2)}, u32[]{:S(2)}) %collective-permute-start.2) | collective-permute-done | bytes 76832 | tf_op jit(solution)/shard_map/ppermute | solution.py:31
  29.6 0.8 %slice_bitcast_fusion = (f32[104,256]{1,0:T(8,128)}, f32[104,256]{1,0:T(8,128)}, f32[104,256]{1,0:T(8,128)}, f32[104,256]{1,0:T(8,128)}) fusion(f32[4,104,256]{2,1,0:T(8,128)S(1)} %all-to-all-done), kind=kLoop, calls=%fused_computation.7 | loop fusion | bytes 851968 | tf_op jit(solution)/shard_map/squeeze | solution.py:277
  30.4 7.4 %shard_map.106 = f32[4,3,32,256]{3,2,1,0:T(8,128)} custom-call(s32[2]{0:T(128)} %pad_add_fusion.place_ref, f32[104,256]{1,0:T(8,128)} %get-tuple-element.9.refs_0_, f32[104,256]{1,0:T(8,128)} %get-tuple-element.8.refs_1_, f32[104,256]{1,0:T(8,128)} %get-tuple-element.7.refs_2_, f32[104,256]{1,0:T(8,128)} %get-tuple-element.6.refs_3_, f32[1,8,256,256]{3,2,1,0:T(8,128)} %refs_4_.1), custom_call_target="tpu_custom_call" | custom-call | tf_op jit(solution)/shard_map/pallas_call | solution.py:215
  37.9 1.1 %slice_bitcast_fusion.6 = (f32[3,32,256]{2,1,0:T(8,128)S(1)}, f32[3,32,256]{2,1,0:T(8,128)S(1)}, f32[3,32,256]{2,1,0:T(8,128)S(1)}, f32[3,32,256]{2,1,0:T(8,128)S(1)}) fusion(f32[4,3,32,256]{3,2,1,0:T(8,128)} %shard_map.106), kind=kLoop, calls=%fused_computation.13 | loop fusion | bytes 786432 | tf_op jit(solution)/shard_map/squeeze | solution.py:287
  39.0 3.6 %collective-permute-start.6 = (f32[3,32,256]{2,1,0:T(8,128)S(1)}, f32[3,32,256]{2,1,0:T(8,128)S(1)}, u32[]{:S(2)}, u32[]{:S(2)}) collective-permute-start(f32[3,32,256]{2,1,0:T(8,128)S(1)} %get-tuple-element.12), channel_id=1, source_target_pairs={{0,18},{1,19},{2,16},{3,17},{16,2},{17,3},{18,0},{19,1},{4,22},{5,... | collective-permute-start | bytes 294920 | tf_op jit(solution)/shard_map/ppermute | solution.py:287
  42.6 1.5 %pad_maximum_fusion.wide_ref = f32[25,40,384]{2,1,0:T(8,128)} fusion(f32[25,2,384]{2,1,0:T(2,128)S(1)} %reshape.111, f32[25,2,384]{2,1,0:T(2,128)S(1)} %reshape.109, f32[25,32,2]{2,1,0:T(8,128)S(1)} %reshape.107, f32[25,32,124]{2,1,0:T(8,128)S(1)} %broadcast_in_dim.27, f32[25,32,2]{2,1,0:T(8,128)S(1)} %reshape.105, f32[1,32,256]{2,1,0:T(8,128)S(1)} %convert_select_fusion, ...), kind=kLoop, calls=%fused_computation | loop fusion | flops 2688000 | bytes 2918560 | tf_op jit(solution)/shard_map/concatenate | solution.py:46
  44.1 4.3 %shard_map.104 = f32[1,3,8,32,256]{4,3,2,1,0:T(8,128)} custom-call(f32[1,4,8]{2,1,0:T(4,128)} %coef_ref.1, f32[2,40,1]{2,1,0:T(8,128)} %copy.16.row_ref, f32[25,40,384]{2,1,0:T(8,128)} %pad_maximum_fusion.wide_ref), custom_call_target="tpu_custom_call" | custom-call | tf_op jit(solution)/shard_map/pallas_call | solution.py:106
  48.4 0.7 %multiply_bitcast_fusion = f32[1,3,32,256]{3,2,1,0:T(8,128)} fusion(f32[3,32,256]{2,1,0:T(8,128)S(1)} %collective-permute-done.7, f32[3,32,256]{2,1,0:T(8,128)S(1)} %collective-permute-done.6, f32[3,32,256]{2,1,0:T(8,128)S(1)} %collective-permute-done.4, f32[3,32,256]{2,1,0:T(8,128)S(1)} %collective-permute-done.5, f32[32,256]{1,0:T(8,128)S(1)} %convert_bitcast_fusion), kind=kLoop, calls=%fused_computation.18 | loop fusion | flops 98304 | bytes 524288 | tf_op jit(solution)/shard_map/broadcast_in_dim | solution.py:310
  (34 shorter events, 1.4 us)
Async XLA Ops:
  0.6 11.0 %copy-start = (f32[1,3,8,32,256]{4,3,2,1,0:T(8,128)S(1)}, f32[1,3,8,32,256]{4,3,2,1,0:T(8,128)}, u32[]{:S(2)}) copy-start(f32[1,3,8,32,256]{4,3,2,1,0:T(8,128)} %ground_ref.1) | copy-start | bytes 2359300
  3.7 8.1 %copy-start.2 = (s32[1,32,256]{2,1,0:T(8,128)S(1)}, s32[1,32,256]{2,1,0:T(8,128)}, u32[]{:S(2)}) copy-start(s32[1,32,256]{2,1,0:T(8,128)} %sea_ref.1) | copy-start | bytes 98308
  5.3 24.3 %all-to-all-start = ((f32[4,104,256]{2,1,0:T(8,128)}), f32[4,104,256]{2,1,0:T(8,128)S(1)}, u32[]{:S(2)}, u32[]{:S(2)}) async-start(f32[4,104,256]{2,1,0:T(8,128)} %broadcast_in_dim.29), calls=%async_computation | async-start | bytes 851968 | tf_op jit(solution)/shard_map/all_to_all | solution.py:276
  11.7 0.9 %copy-start.1 = (f32[1,3,32,256]{3,2,1,0:T(8,128)S(1)}, f32[1,3,32,256]{3,2,1,0:T(8,128)}, u32[]{:S(2)}) copy-start(f32[1,3,32,256]{3,2,1,0:T(8,128)} %previous_ref.1) | copy-start | bytes 294916
  13.2 4.6 %collective-permute-start.1 = (f32[1600]{0:T(1024)S(1)}, f32[1600]{0:T(1024)S(1)}, u32[]{:S(2)}, u32[]{:S(2)}) collective-permute-start(f32[1600]{0:T(1024)S(1)} %reshape.106), channel_id=1, source_target_pairs={{0,1},{1,2},{2,3},{3,0},{4,5},{5,6},{6,7},{7,4},{8,9},{9,10},{10,1... | collective-permute-start | bytes 19208 | tf_op jit(solution)/shard_map/ppermute | solution.py:31
  14.9 3.7 %collective-permute-start = (f32[1600]{0:T(1024)S(1)}, f32[1600]{0:T(1024)S(1)}, u32[]{:S(2)}, u32[]{:S(2)}) collective-permute-start(f32[1600]{0:T(1024)S(1)} %reshape.104), channel_id=1, source_target_pairs={{1,0},{2,1},{3,2},{0,3},{5,4},{6,5},{7,6},{4,7},{9,8},{10,9},{11,1... | collective-permute-start | bytes 19208 | tf_op jit(solution)/shard_map/ppermute | solution.py:31
  19.3 5.9 %collective-permute-start.3 = (f32[19200]{0:T(1024)S(1)}, f32[19200]{0:T(1024)S(1)}, u32[]{:S(2)}, u32[]{:S(2)}) collective-permute-start(f32[19200]{0:T(1024)S(1)} %reshape.110), channel_id=1, source_target_pairs={{0,4},{4,8},{8,12},{1,5},{5,9},{9,13},{2,6},{6,10},{10,14},{3,7},{... | collective-permute-start | bytes 230408 | tf_op jit(solution)/shard_map/ppermute | solution.py:31
  23.3 6.3 %collective-permute-start.2 = (f32[19200]{0:T(1024)S(1)}, f32[19200]{0:T(1024)S(1)}, u32[]{:S(2)}, u32[]{:S(2)}) collective-permute-start(f32[19200]{0:T(1024)S(1)} %reshape.108), channel_id=1, source_target_pairs={{4,0},{8,4},{12,8},{5,1},{9,5},{13,9},{6,2},{10,6},{14,10},{7,3},{... | collective-permute-start | bytes 230408 | tf_op jit(solution)/shard_map/ppermute | solution.py:31
  38.9 9.4 %collective-permute-start.7 = (f32[3,32,256]{2,1,0:T(8,128)S(1)}, f32[3,32,256]{2,1,0:T(8,128)S(1)}, u32[]{:S(2)}, u32[]{:S(2)}) collective-permute-start(f32[3,32,256]{2,1,0:T(8,128)S(1)} %get-tuple-element.11), channel_id=1, source_target_pairs={{0,19},{1,16},{2,17},{3,18},{16,3},{17,0},{18,1},{19,2},{4,23},{5,... | collective-permute-start | bytes 294920 | tf_op jit(solution)/shard_map/ppermute | solution.py:287
  39.0 9.3 %collective-permute-start.6 = (f32[3,32,256]{2,1,0:T(8,128)S(1)}, f32[3,32,256]{2,1,0:T(8,128)S(1)}, u32[]{:S(2)}, u32[]{:S(2)}) collective-permute-start(f32[3,32,256]{2,1,0:T(8,128)S(1)} %get-tuple-element.12), channel_id=1, source_target_pairs={{0,18},{1,19},{2,16},{3,17},{16,2},{17,3},{18,0},{19,1},{4,22},{5,... | collective-permute-start | bytes 294920 | tf_op jit(solution)/shard_map/ppermute | solution.py:287
  42.5 5.8 %collective-permute-start.4 = (f32[3,32,256]{2,1,0:T(8,128)S(1)}, f32[3,32,256]{2,1,0:T(8,128)S(1)}, u32[]{:S(2)}, u32[]{:S(2)}) collective-permute-start(f32[3,32,256]{2,1,0:T(8,128)S(1)} %get-tuple-element.13), channel_id=1, source_target_pairs={{0,16},{1,17},{2,18},{3,19},{16,0},{17,1},{18,2},{19,3},{4,20},{5,... | collective-permute-start | bytes 294920 | tf_op jit(solution)/shard_map/ppermute | solution.py:287
  42.5 5.8 %collective-permute-start.5 = (f32[3,32,256]{2,1,0:T(8,128)S(1)}, f32[3,32,256]{2,1,0:T(8,128)S(1)}, u32[]{:S(2)}, u32[]{:S(2)}) collective-permute-start(f32[3,32,256]{2,1,0:T(8,128)S(1)} %get-tuple-element.10), channel_id=1, source_target_pairs={{0,17},{1,18},{2,19},{3,16},{16,1},{17,2},{18,3},{19,0},{4,21},{5,... | collective-permute-start | bytes 294920 | tf_op jit(solution)/shard_map/ppermute | solution.py:287

commit v9 on v7

--- a/solution.py
+++ b/solution.py
@@ -48,11 +48,11 @@
     )
 
 
-def stencil_kernel(coef_ref, row_ref, wide_ref, out_ref, mid_ref):
+def stencil_kernel(coef_ref, wide_ref, out_ref, mid_ref):
     field_count, level_count, row_count, col_count = out_ref.shape[1:]
     wide_rows, wide_cols = wide_ref.shape[1:]
-    turning_wide = jnp.broadcast_to(row_ref[0], (wide_rows, wide_cols))
-    keep_wide = wide_ref[field_count * level_count] * jnp.broadcast_to(row_ref[1], (wide_rows, wide_cols))
+    turning_wide = wide_ref[field_count * level_count + 1]
+    keep_wide = wide_ref[field_count * level_count] * wide_ref[field_count * level_count + 2]
 
     def step(read, write, rows, cols):
         turning = turning_wide[:rows, :cols]
@@ -101,7 +101,7 @@
     step(from_mid, to_out, row_count, col_count)
 
 
-def dynamics(coeffs, row_terms, wide, field_count, level_count, row_count, col_count):
+def dynamics(coeffs, wide, field_count, level_count, row_count, col_count):
     planes, wide_rows, wide_cols = wide.shape
     return pl.pallas_call(
         stencil_kernel,
@@ -109,12 +109,11 @@
         in_specs=[
             pl.BlockSpec(memory_space=pltpu.SMEM),
             pl.BlockSpec(memory_space=pltpu.VMEM),
-            pl.BlockSpec(memory_space=pltpu.VMEM),
         ],
         out_specs=pl.BlockSpec(memory_space=pltpu.VMEM),
-        scratch_shapes=[pltpu.VMEM((planes - 1, wide_rows, wide_cols), jnp.float32)],
+        scratch_shapes=[pltpu.VMEM((planes - 3, wide_rows, wide_cols), jnp.float32)],
         interpret=INTERPRET,
-    )(coeffs, row_terms, wide)
+    )(coeffs, wide)
 
 
 def export_kernel(flag_ref, ground_ref, previous_ref, sea_ref, link_ref, out_ref):
@@ -162,17 +161,27 @@
 
 def remap_kernel(link_count, source_count, place_ref, *refs):
     source_refs = refs[:source_count]
-    table_ref, out_ref, rows_ref, combo_ref = refs[source_count:]
+    table_ref = refs[source_count]
     tile_count = table_ref.shape[1]
-    owner_count, field_count, row_count, col_count = out_ref.shape
+    out_refs = refs[source_count + 1 : -4]
+    rows_ref, combo_ref, weight_ref, copy_sems = refs[-4:]
+    owner_count = len(out_refs)
+    field_count, row_count, col_count = out_refs[0].shape
+    copies = [
+        pltpu.make_async_copy(table_ref.at[0, tile], weight_ref.at[tile], copy_sems.at[tile])
+        for tile in range(tile_count)
+    ]
+    for copy in copies:
+        copy.start()
     base = field_count * row_count
     my_lat = place_ref[0]
     my_lon = place_ref[1]
     for source in range(source_count):
         rows_ref[source * base : (source + 1) * base, :] = source_refs[source][:base, :]
     for tile in range(tile_count):
+        copies[tile].wait()
         weighted = jnp.dot(
-            rows_ref[...], table_ref[0, tile], precision=HIGHEST, preferred_element_type=jnp.float32
+            rows_ref[...], weight_ref[tile], precision=HIGHEST, preferred_element_type=jnp.float32
         )
         for source in range(source_count):
             for c in range(field_count):
@@ -204,7 +213,7 @@
     for c in range(field_count):
         summed = jnp.dot(into, combo_ref[c], precision=HIGHEST, preferred_element_type=jnp.float32)
         for owner in range(owner_count):
-            out_ref[owner, c] = summed[owner * row_count : (owner + 1) * row_count]
+            out_refs[owner][c] = summed[owner * row_count : (owner + 1) * row_count]
 
 
 def remapped(lat, sources, remap_weights, owner_count, field_count, row_count, link_count):
@@ -214,14 +223,21 @@
     vmem = pl.BlockSpec(memory_space=pltpu.VMEM)
     return pl.pallas_call(
         functools.partial(remap_kernel, link_count, source_count),
-        out_shape=jax.ShapeDtypeStruct((owner_count, field_count, row_count, col_count), jnp.float32),
-        in_specs=[pl.BlockSpec(memory_space=pltpu.SMEM)] + [vmem] * (source_count + 1),
-        out_specs=vmem,
+        out_shape=[
+            jax.ShapeDtypeStruct((field_count, row_count, col_count), jnp.float32)
+            for owner in range(owner_count)
+        ],
+        in_specs=[pl.BlockSpec(memory_space=pltpu.SMEM)]
+        + [vmem] * source_count
+        + [pl.BlockSpec(memory_space=pl.ANY)],
+        out_specs=[vmem] * owner_count,
         scratch_shapes=[
             pltpu.VMEM((source_count * field_count * row_count, col_count), jnp.float32),
             pltpu.VMEM(
                 (field_count, source_count * tile_count * row_count, col_count), jnp.float32
             ),
+            pltpu.VMEM(remap_weights.shape[1:], jnp.float32),
+            pltpu.SemaphoreType.DMA((tile_count,)),
         ],
         interpret=INTERPRET,
     )(lat, *sources, remap_weights)
@@ -306,8 +322,9 @@
     )
     coriolis = coriolis_scale * jnp.sin(latitude)
     inside = ((row_index >= 0) & (row_index < total_rows)).astype(jnp.float32)
-    row_terms = jnp.stack([coriolis, inside])[:, :, None]
-    fields = dynamics(coeffs, row_terms, wide, field_count, level_count, row_count, col_count)
+    row_terms = jnp.broadcast_to(jnp.stack([coriolis, inside])[:, :, None], (2, wide_rows, wide_cols))
+    wide = jnp.concatenate([wide, row_terms], 0)
+    fields = dynamics(coeffs, wide, field_count, level_count, row_count, col_count)
     return (fields, imported[None])
 
 

time: 46.5 us -> 49.9 us (1.073)
  Pallas kernels: 13.3 us -> 16.4 us
  waiting for transfers between devices: 4.69 us -> 5.32 us
  local copies, waits for them, and re-layouts: 4.75 us -> 4.19 us
    pallas_call x1, Pallas kernels: 7.44 us -> 10.5 us  [remapped(): pl.pallas_call(functools.partial(remap_kernel, link_count, source_count),...]
    unnamed x13 -> x11, local copies, waits for them, and re-layouts: 1.35 us -> 2.48 us
    squeeze x1 -> x0, local copies, waits for them, and re-layouts: 1.06 us -> none  [body(): pieces.append(lax.ppermute(partial[shift], ('grp', 'lon'), route))]
    ppermute x4, waiting for transfers between devices: 4.58 us -> 5.29 us  [shifted(): flat = lax.ppermute(part.reshape(-1), axis, route)]
    broadcast_in_dim x1, local copies, waits for them, and re-layouts: 0.72 us -> 0.07 us  [body(): jnp.broadcast_to(jnp.stack([coriolis, inside])[:, :, None], (2, wide_rows...]
  transfers between devices with their start and end apart: 11 -> 11, of which waited for: 4 -> 3; matrix products, arithmetic and copies ran while one was open for 11% -> 12% of each run, Pallas kernels for 9% -> 9%
where the time goes in v9:
time: 49.9 us; the launch traced here: 49.5 us
  starting transfers between devices  17.8 us (36%)
  Pallas kernels  16.4 us (33%)
  waiting for transfers between devices  5.32 us (11%)
  other arithmetic  4.86 us (10%)
  local copies, waits for them, and re-layouts  4.19 us (8%)
  between operations  0.9 us (2%)
    pallas_call x1, Pallas kernels, remapped(): pl.pallas_call(functools.partial(remap_kernel, link_count, source_count),...  10.5 us
    ppermute x4, starting transfers between devices, shifted(): flat = lax.ppermute(part.reshape(-1), axis, route)  8.4 us
    ppermute x3, starting transfers between devices, body(): lax.ppermute(payload, 'lat', [(i, (i + shift) % lat_count) for i in range...  6.96 us
    ppermute x4, waiting for transfers between devices, shifted(): flat = lax.ppermute(part.reshape(-1), axis, route)  5.29 us
    pallas_call x1, Pallas kernels, dynamics(): pl.pallas_call(stencil_kernel, out_shape=jax.ShapeDtypeStruct((1, field_c...  4.29 us
    unnamed x11, local copies, waits for them, and re-layouts  2.48 us
    ppermute x4, starting transfers between devices, body(): pieces.append(lax.ppermute(partial[shift], ('grp', 'lon'), route))  2.41 us
    concatenate x1, other arithmetic, body(): wide = jnp.concatenate([wide, row_terms], 0)  1.7 us
  transfers between devices with their start and end apart: 11, of which 3 were waited for; matrix products, arithmetic and copies ran while one was open for 12% of the time, Pallas kernels for 9%

profile of v9, /device:TPU:0, one launch (start us, length us, event | category | flops | bytes accessed | tf_op | source)
XLA Modules:
  0.0 49.5 jit_solution(16752928320988858645)
XLA Ops:
  0.6 1.3 %add_convert_fusion.link_ref = f32[4,128]{1,0:T(4,128)} fusion(s32[1,128]{1,0:T(1,128)} %param.17, s32[1,128]{1,0:T(1,128)} %param.16, s32[1,128]{1,0:T(1,128)} %param.15, s32[1,128]{1,0:T(1,128)} %bitcast.23), kind=kLoop, calls=%fused_computation.19 | loop fusion | flops 2048 | bytes 4096 | tf_op jit(solution)/shard_map/convert_element_type | solution.py:286
  1.9 1.6 %shard_map.105.refs_0_ = f32[104,256]{1,0:T(8,128)} custom-call(s32[1]{0:T(128)} %bitcast.6.flag_ref, f32[1,3,8,32,256]{4,3,2,1,0:T(8,128)} %ground_ref.1, f32[1,3,32,256]{3,2,1,0:T(8,128)} %previous_ref.1, s32[1,32,256]{2,1,0:T(8,128)} %sea_ref.1, f32[4,128]{1,0:T(4,128)} %add_convert_fusion.link_ref), custom_call_target="tpu_custom_call" | custom-call | tf_op jit(solution)/shard_map/pallas_call | solution.py:146
  3.6 3.0 %collective-permute-start.4 = (f32[104,256]{1,0:T(8,128)}, f32[104,256]{1,0:T(8,128)S(1)}, u32[]{:S(2)}, u32[]{:S(2)}) collective-permute-start(f32[104,256]{1,0:T(8,128)} %shard_map.105.refs_0_), channel_id=1, source_target_pairs={{0,4},{4,8},{8,12},{12,0},{1,5},{5,9},{9,13},{13,1},{2,6},{6,10},{... | collective-permute-start | bytes 319496 | tf_op jit(solution)/shard_map/ppermute | solution.py:292
  6.6 2.6 %collective-permute-start.5 = (f32[104,256]{1,0:T(8,128)}, f32[104,256]{1,0:T(8,128)S(1)}, u32[]{:S(2)}, u32[]{:S(2)}) collective-permute-start(f32[104,256]{1,0:T(8,128)} %shard_map.105.refs_0_), channel_id=1, source_target_pairs={{0,8},{4,12},{8,0},{12,4},{1,9},{5,13},{9,1},{13,5},{2,10},{6,14},... | collective-permute-start | bytes 319496 | tf_op jit(solution)/shard_map/ppermute | solution.py:292
  9.2 1.3 %collective-permute-start.6 = (f32[104,256]{1,0:T(8,128)}, f32[104,256]{1,0:T(8,128)S(1)}, u32[]{:S(2)}, u32[]{:S(2)}) collective-permute-start(f32[104,256]{1,0:T(8,128)} %shard_map.105.refs_0_), channel_id=1, source_target_pairs={{0,12},{4,0},{8,4},{12,8},{1,13},{5,1},{9,5},{13,9},{2,14},{6,2},{... | collective-permute-start | bytes 319496 | tf_op jit(solution)/shard_map/ppermute | solution.py:292
  10.5 1.2 %copy.16 = f32[1,3,8,32,256]{4,3,1,2,0:T(8,128)S(1)} copy(f32[1,3,8,32,256]{4,3,2,1,0:T(8,128)} %ground_ref.1) | data formatting | bytes 1572864 | tf_op args[0]
  12.2 0.2 reshape.104
  12.5 2.5 %collective-permute-start = (f32[1600]{0:T(1024)S(1)}, f32[1600]{0:T(1024)S(1)}, u32[]{:S(2)}, u32[]{:S(2)}) collective-permute-start(f32[1600]{0:T(1024)S(1)} %reshape.104), channel_id=1, source_target_pairs={{1,0},{2,1},{3,2},{0,3},{5,4},{6,5},{7,6},{4,7},{9,8},{10,9},{11,1... | collective-permute-start | bytes 19208 | tf_op jit(solution)/shard_map/ppermute | solution.py:31
  15.4 0.9 %collective-permute-done = f32[1600]{0:T(1024)S(1)} collective-permute-done((f32[1600]{0:T(1024)S(1)}, f32[1600]{0:T(1024)S(1)}, u32[]{:S(2)}, u32[]{:S(2)}) %collective-permute-start) | collective-permute-done | bytes 6432 | tf_op jit(solution)/shard_map/ppermute | solution.py:31
  16.3 0.4 reshape.105
  16.7 3.1 %collective-permute-done.1 = f32[1600]{0:T(1024)S(1)} collective-permute-done((f32[1600]{0:T(1024)S(1)}, f32[1600]{0:T(1024)S(1)}, u32[]{:S(2)}, u32[]{:S(2)}) %collective-permute-start.1) | collective-permute-done | bytes 6432 | tf_op jit(solution)/shard_map/ppermute | solution.py:31
  19.8 0.4 reshape.107
  20.5 1.3 %collective-permute-start.2 = (f32[19200]{0:T(1024)S(1)}, f32[19200]{0:T(1024)S(1)}, u32[]{:S(2)}, u32[]{:S(2)}) collective-permute-start(f32[19200]{0:T(1024)S(1)} %reshape.108), channel_id=1, source_target_pairs={{4,0},{8,4},{12,8},{5,1},{9,5},{13,9},{6,2},{10,6},{14,10},{7,3},{... | collective-permute-start | bytes 230408 | tf_op jit(solution)/shard_map/ppermute | solution.py:31
  21.8 4.6 %collective-permute-start.3 = (f32[19200]{0:T(1024)S(1)}, f32[19200]{0:T(1024)S(1)}, u32[]{:S(2)}, u32[]{:S(2)}) collective-permute-start(f32[19200]{0:T(1024)S(1)} %reshape.110), channel_id=1, source_target_pairs={{0,4},{4,8},{8,12},{1,5},{5,9},{9,13},{2,6},{6,10},{10,14},{3,7},{... | collective-permute-start | bytes 230408 | tf_op jit(solution)/shard_map/ppermute | solution.py:31
  26.4 0.7 %pad_add_fusion.place_ref = s32[2]{0:T(128)} fusion(s32[1]{0:T(128)} %bitcast.5, s32[1]{0:T(128)} %bitcast.4), kind=kLoop, calls=%fused_computation.23 | loop fusion | flops 2 | bytes 16 | tf_op jit(solution)/shard_map/stack | solution.py:295
  27.1 1.3 %collective-permute-done.3 = f32[19200]{0:T(1024)S(1)} collective-permute-done((f32[19200]{0:T(1024)S(1)}, f32[19200]{0:T(1024)S(1)}, u32[]{:S(2)}, u32[]{:S(2)}) %collective-permute-start.3) | collective-permute-done | bytes 76832 | tf_op jit(solution)/shard_map/ppermute | solution.py:31
  28.5 0.6 %copy-done.2 = f32[104,256]{1,0:T(8,128)} copy-done((f32[104,256]{1,0:T(8,128)}, f32[104,256]{1,0:T(8,128)S(1)}, u32[]{:S(2)}) %copy-start.2) | copy-done | bytes 106520
  29.1 0.6 %copy-done.4 = f32[104,256]{1,0:T(8,128)} copy-done((f32[104,256]{1,0:T(8,128)}, f32[104,256]{1,0:T(8,128)S(1)}, u32[]{:S(2)}) %copy-start.4) | copy-done | bytes 106520
  29.8 10.5 %shard_map.106 = (f32[3,32,256]{2,1,0:T(8,128)}, f32[3,32,256]{2,1,0:T(8,128)}, f32[3,32,256]{2,1,0:T(8,128)}, f32[3,32,256]{2,1,0:T(8,128)}) custom-call(s32[2]{0:T(128)} %pad_add_fusion.place_ref, f32[104,256]{1,0:T(8,128)} %shard_map.105.refs_0_, f32[104,256]{1,0:T(8,128)} %copy-done.2, f32[104,256]{1,0:T(8,128)} %copy-done.3, f32[104,256]{1,0:T(8,128)} %copy-done.4, ...), custom_call_target="tpu_custom_call" | custom-call | tf_op jit(solution)/shard_map/pallas_call | solution.py:224
  40.6 1.5 %collective-permute-start.8 = (f32[3,32,256]{2,1,0:T(8,128)}, f32[3,32,256]{2,1,0:T(8,128)S(1)}, u32[]{:S(2)}, u32[]{:S(2)}) collective-permute-start(f32[3,32,256]{2,1,0:T(8,128)} %get-tuple-element.7), channel_id=1, source_target_pairs={{0,17},{1,18},{2,19},{3,16},{16,1},{17,2},{18,3},{19,0},{4,21},{5,... | collective-permute-start | bytes 294920 | tf_op jit(solution)/shard_map/ppermute | solution.py:304
  42.1 0.6 %collective-permute-start.9 = (f32[3,32,256]{2,1,0:T(8,128)}, f32[3,32,256]{2,1,0:T(8,128)S(1)}, u32[]{:S(2)}, u32[]{:S(2)}) collective-permute-start(f32[3,32,256]{2,1,0:T(8,128)} %get-tuple-element.8), channel_id=1, source_target_pairs={{0,18},{1,19},{2,16},{3,17},{16,2},{17,3},{18,0},{19,1},{4,22},{5,... | collective-permute-start | bytes 294920 | tf_op jit(solution)/shard_map/ppermute | solution.py:304
  42.8 1.7 %pad_maximum_fusion.wide_ref = f32[27,40,384]{2,1,0:T(8,128)} fusion(f32[2,40,384]{2,1,0:T(8,128)S(1)} %broadcast_in_dim.25, f32[25,2,384]{2,1,0:T(2,128)S(1)} %reshape.111, f32[25,2,384]{2,1,0:T(2,128)S(1)} %reshape.109, f32[25,32,2]{2,1,0:T(8,128)S(1)} %reshape.107, f32[25,32,124]{2,1,0:T(8,128)S(1)} %broadcast_in_dim.11, f32[25,32,2]{2,1,0:T(8,128)S(1)} %reshape.105, ...), kind=kLoop, calls=%fused_computation | loop fusion | flops 3317760 | bytes 3168480 | tf_op jit(solution)/shard_map/concatenate | solution.py:326
  44.5 4.3 %shard_map.104 = f32[1,3,8,32,256]{4,3,2,1,0:T(8,128)} custom-call(f32[1,4,8]{2,1,0:T(4,128)} %coef_ref.1, f32[27,40,384]{2,1,0:T(8,128)} %pad_maximum_fusion.wide_ref), custom_call_target="tpu_custom_call" | custom-call | tf_op jit(solution)/shard_map/pallas_call | solution.py:106
  48.8 0.7 %multiply_bitcast_fusion = f32[1,3,32,256]{3,2,1,0:T(8,128)} fusion(f32[3,32,256]{2,1,0:T(8,128)S(1)} %collective-permute-done.10, f32[3,32,256]{2,1,0:T(8,128)S(1)} %collective-permute-done.9, f32[3,32,256]{2,1,0:T(8,128)S(1)} %collective-permute-done.7, f32[3,32,256]{2,1,0:T(8,128)S(1)} %collective-permute-done.8, f32[32,256]{1,0:T(8,128)S(1)} %convert_bitcast_fusion), kind=kLoop, calls=%fused_computation.10 | loop fusion | flops 98304 | bytes 524288 | tf_op jit(solution)/shard_map/broadcast_in_dim | solution.py:328
  (39 shorter events, 1.7 us)
Async XLA Ops:
  0.6 11.1 %copy-start.1 = (s32[1,32,256]{2,1,0:T(8,128)S(1)}, s32[1,32,256]{2,1,0:T(8,128)}, u32[]{:S(2)}) copy-start(s32[1,32,256]{2,1,0:T(8,128)} %sea_ref.1) | copy-start | bytes 98308
  3.6 8.3 %copy-start = (f32[1,3,32,256]{3,2,1,0:T(8,128)S(1)}, f32[1,3,32,256]{3,2,1,0:T(8,128)}, u32[]{:S(2)}) copy-start(f32[1,3,32,256]{3,2,1,0:T(8,128)} %previous_ref.1) | copy-start | bytes 294916
  3.6 24.9 %collective-permute-start.4 = (f32[104,256]{1,0:T(8,128)}, f32[104,256]{1,0:T(8,128)S(1)}, u32[]{:S(2)}, u32[]{:S(2)}) collective-permute-start(f32[104,256]{1,0:T(8,128)} %shard_map.105.refs_0_), channel_id=1, source_target_pairs={{0,4},{4,8},{8,12},{12,0},{1,5},{5,9},{9,13},{13,1},{2,6},{6,10},{... | collective-permute-start | bytes 319496 | tf_op jit(solution)/shard_map/ppermute | solution.py:292
  6.6 21.9 %collective-permute-start.5 = (f32[104,256]{1,0:T(8,128)}, f32[104,256]{1,0:T(8,128)S(1)}, u32[]{:S(2)}, u32[]{:S(2)}) collective-permute-start(f32[104,256]{1,0:T(8,128)} %shard_map.105.refs_0_), channel_id=1, source_target_pairs={{0,8},{4,12},{8,0},{12,4},{1,9},{5,13},{9,1},{13,5},{2,10},{6,14},... | collective-permute-start | bytes 319496 | tf_op jit(solution)/shard_map/ppermute | solution.py:292
  9.2 19.3 %collective-permute-start.6 = (f32[104,256]{1,0:T(8,128)}, f32[104,256]{1,0:T(8,128)S(1)}, u32[]{:S(2)}, u32[]{:S(2)}) collective-permute-start(f32[104,256]{1,0:T(8,128)} %shard_map.105.refs_0_), channel_id=1, source_target_pairs={{0,12},{4,0},{8,4},{12,8},{1,13},{5,1},{9,5},{13,9},{2,14},{6,2},{... | collective-permute-start | bytes 319496 | tf_op jit(solution)/shard_map/ppermute | solution.py:292
  12.5 3.9 %collective-permute-start = (f32[1600]{0:T(1024)S(1)}, f32[1600]{0:T(1024)S(1)}, u32[]{:S(2)}, u32[]{:S(2)}) collective-permute-start(f32[1600]{0:T(1024)S(1)} %reshape.104), channel_id=1, source_target_pairs={{1,0},{2,1},{3,2},{0,3},{5,4},{6,5},{7,6},{4,7},{9,8},{10,9},{11,1... | collective-permute-start | bytes 19208 | tf_op jit(solution)/shard_map/ppermute | solution.py:31
  15.2 4.6 %collective-permute-start.1 = (f32[1600]{0:T(1024)S(1)}, f32[1600]{0:T(1024)S(1)}, u32[]{:S(2)}, u32[]{:S(2)}) collective-permute-start(f32[1600]{0:T(1024)S(1)} %reshape.106), channel_id=1, source_target_pairs={{0,1},{1,2},{2,3},{3,0},{4,5},{5,6},{6,7},{7,4},{8,9},{9,10},{10,1... | collective-permute-start | bytes 19208 | tf_op jit(solution)/shard_map/ppermute | solution.py:31
  20.5 6.6 %collective-permute-start.2 = (f32[19200]{0:T(1024)S(1)}, f32[19200]{0:T(1024)S(1)}, u32[]{:S(2)}, u32[]{:S(2)}) collective-permute-start(f32[19200]{0:T(1024)S(1)} %reshape.108), channel_id=1, source_target_pairs={{4,0},{8,4},{12,8},{5,1},{9,5},{13,9},{6,2},{10,6},{14,10},{7,3},{... | collective-permute-start | bytes 230408 | tf_op jit(solution)/shard_map/ppermute | solution.py:31
  21.8 6.6 %collective-permute-start.3 = (f32[19200]{0:T(1024)S(1)}, f32[19200]{0:T(1024)S(1)}, u32[]{:S(2)}, u32[]{:S(2)}) collective-permute-start(f32[19200]{0:T(1024)S(1)} %reshape.110), channel_id=1, source_target_pairs={{0,4},{4,8},{8,12},{1,5},{5,9},{9,13},{2,6},{6,10},{10,14},{3,7},{... | collective-permute-start | bytes 230408 | tf_op jit(solution)/shard_map/ppermute | solution.py:31
  28.4 0.6 %copy-start.2 = (f32[104,256]{1,0:T(8,128)}, f32[104,256]{1,0:T(8,128)S(1)}, u32[]{:S(2)}) copy-start(f32[104,256]{1,0:T(8,128)S(1)} %collective-permute-done.4.refs_1_) | copy-start | bytes 319492
  28.5 0.7 %copy-start.3 = (f32[104,256]{1,0:T(8,128)}, f32[104,256]{1,0:T(8,128)S(1)}, u32[]{:S(2)}) copy-start(f32[104,256]{1,0:T(8,128)S(1)} %collective-permute-done.5.refs_2_) | copy-start | bytes 319492
  29.1 0.6 %copy-start.4 = (f32[104,256]{1,0:T(8,128)}, f32[104,256]{1,0:T(8,128)S(1)}, u32[]{:S(2)}) copy-start(f32[104,256]{1,0:T(8,128)S(1)} %collective-permute-done.6.refs_3_) | copy-start | bytes 319492
  40.3 8.5 %collective-permute-start.10 = (f32[3,32,256]{2,1,0:T(8,128)}, f32[3,32,256]{2,1,0:T(8,128)S(1)}, u32[]{:S(2)}, u32[]{:S(2)}) collective-permute-start(f32[3,32,256]{2,1,0:T(8,128)} %get-tuple-element.9), channel_id=1, source_target_pairs={{0,19},{1,16},{2,17},{3,18},{16,3},{17,0},{18,1},{19,2},{4,23},{5,... | collective-permute-start | bytes 294920 | tf_op jit(solution)/shard_map/ppermute | solution.py:304
  40.4 8.4 %collective-permute-start.7 = (f32[3,32,256]{2,1,0:T(8,128)}, f32[3,32,256]{2,1,0:T(8,128)S(1)}, u32[]{:S(2)}, u32[]{:S(2)}) collective-permute-start(f32[3,32,256]{2,1,0:T(8,128)} %get-tuple-element.6), channel_id=1, source_target_pairs={{0,16},{1,17},{2,18},{3,19},{16,0},{17,1},{18,2},{19,3},{4,20},{5,... | collective-permute-start | bytes 294920 | tf_op jit(solution)/shard_map/ppermute | solution.py:304
  40.6 8.2 %collective-permute-start.8 = (f32[3,32,256]{2,1,0:T(8,128)}, f32[3,32,256]{2,1,0:T(8,128)S(1)}, u32[]{:S(2)}, u32[]{:S(2)}) collective-permute-start(f32[3,32,256]{2,1,0:T(8,128)} %get-tuple-element.7), channel_id=1, source_target_pairs={{0,17},{1,18},{2,19},{3,16},{16,1},{17,2},{18,3},{19,0},{4,21},{5,... | collective-permute-start | bytes 294920 | tf_op jit(solution)/shard_map/ppermute | solution.py:304
  42.1 6.7 %collective-permute-start.9 = (f32[3,32,256]{2,1,0:T(8,128)}, f32[3,32,256]{2,1,0:T(8,128)S(1)}, u32[]{:S(2)}, u32[]{:S(2)}) collective-permute-start(f32[3,32,256]{2,1,0:T(8,128)} %get-tuple-element.8), channel_id=1, source_target_pairs={{0,18},{1,19},{2,16},{3,17},{16,2},{17,3},{18,0},{19,1},{4,22},{5,... | collective-permute-start | bytes 294920 | tf_op jit(solution)/shard_map/ppermute | solution.py:304

commit v10 on v7

--- a/solution.py
+++ b/solution.py
@@ -63,6 +63,11 @@
                 advect_east = coef_ref[0, 1, level]
                 advect_north = coef_ref[0, 2, level]
                 mixing = coef_ref[0, 3, level]
+                own_weight = 1.0 - 4.0 * diffuse - 2.0 * mixing
+                north_weight = diffuse - advect_north
+                south_weight = diffuse + advect_north
+                east_weight = diffuse - advect_east
+                west_weight = diffuse + advect_east
                 whole = read(field, level)
                 north = pltpu.roll(whole, wide_rows - 1, 0)[:rows, :cols]
                 south = pltpu.roll(whole, 1, 0)[:rows, :cols]
@@ -71,13 +76,13 @@
                 center = whole[:rows, :cols]
                 above = read(field, min(level + 1, level_count - 1))[:rows, :cols]
                 below = read(field, max(level - 1, 0))[:rows, :cols]
-                laplace = north + south + east + west - 4.0 * center
                 updated = (
-                    center
-                    + diffuse * laplace
-                    - advect_east * (east - west)
-                    - advect_north * (north - south)
-                    + mixing * (above + below - 2.0 * center)
+                    own_weight * center
+                    + north_weight * north
+                    + south_weight * south
+                    + east_weight * east
+                    + west_weight * west
+                    + mixing * (above + below)
                 )
                 if field == 0:
                     updated = updated + turning * read(1, level)[:rows, :cols]
@@ -162,9 +167,12 @@
 
 def remap_kernel(link_count, source_count, place_ref, *refs):
     source_refs = refs[:source_count]
-    table_ref, out_ref, rows_ref, combo_ref = refs[source_count:]
+    table_ref = refs[source_count]
     tile_count = table_ref.shape[1]
-    owner_count, field_count, row_count, col_count = out_ref.shape
+    out_refs = refs[source_count + 1 : -2]
+    rows_ref, combo_ref = refs[-2:]
+    owner_count = len(out_refs)
+    field_count, row_count, col_count = out_refs[0].shape
     base = field_count * row_count
     my_lat = place_ref[0]
     my_lon = place_ref[1]
@@ -204,7 +212,7 @@
     for c in range(field_count):
         summed = jnp.dot(into, combo_ref[c], precision=HIGHEST, preferred_element_type=jnp.float32)
         for owner in range(owner_count):
-            out_ref[owner, c] = summed[owner * row_count : (owner + 1) * row_count]
+            out_refs[owner][c] = summed[owner * row_count : (owner + 1) * row_count]
 
 
 def remapped(lat, sources, remap_weights, owner_count, field_count, row_count, link_count):
@@ -214,9 +222,12 @@
     vmem = pl.BlockSpec(memory_space=pltpu.VMEM)
     return pl.pallas_call(
         functools.partial(remap_kernel, link_count, source_count),
-        out_shape=jax.ShapeDtypeStruct((owner_count, field_count, row_count, col_count), jnp.float32),
+        out_shape=[
+            jax.ShapeDtypeStruct((field_count, row_count, col_count), jnp.float32)
+            for owner in range(owner_count)
+        ],
         in_specs=[pl.BlockSpec(memory_space=pltpu.SMEM)] + [vmem] * (source_count + 1),
-        out_specs=vmem,
+        out_specs=[vmem] * owner_count,
         scratch_shapes=[
             pltpu.VMEM((source_count * field_count * row_count, col_count), jnp.float32),
             pltpu.VMEM(

time: 46.5 us -> 45.5 us (0.978)
  local copies, waits for them, and re-layouts: 4.75 us -> 3.68 us
    squeeze x1 -> x0, local copies, waits for them, and re-layouts: 1.06 us -> none  [body(): pieces.append(lax.ppermute(partial[shift], ('grp', 'lon'), route))]
where the time goes in v10:
time: 45.5 us; the launch traced here: 45.2 us
  starting transfers between devices  17.7 us (39%)
  Pallas kernels  13.1 us (29%)
  waiting for transfers between devices  5.14 us (11%)
  other arithmetic  4.73 us (10%)
  local copies, waits for them, and re-layouts  3.68 us (8%)
  between operations  0.88 us (2%)
    ppermute x4, starting transfers between devices, shifted(): flat = lax.ppermute(part.reshape(-1), axis, route)  8.4 us
    pallas_call x1, Pallas kernels, remapped(): pl.pallas_call(functools.partial(remap_kernel, link_count, source_count),...  7.4 us
    ppermute x3, starting transfers between devices, body(): lax.ppermute(payload, 'lat', [(i, (i + shift) % lat_count) for i in range...  6.96 us
    ppermute x4, waiting for transfers between devices, shifted(): flat = lax.ppermute(part.reshape(-1), axis, route)  4.59 us
    pallas_call x1, Pallas kernels, dynamics(): pl.pallas_call(stencil_kernel, out_shape=jax.ShapeDtypeStruct((1, field_c...  4.03 us
    ppermute x4, starting transfers between devices, body(): pieces.append(lax.ppermute(partial[shift], ('grp', 'lon'), route))  2.37 us
    pallas_call x1, Pallas kernels, exported_block(): pl.pallas_call(export_kernel, out_shape=jax.ShapeDtypeStruct((field_count...  1.63 us
    concatenate x1, other arithmetic, with_halo(): jnp.concatenate([cells, shifted(head, 'lat', False, False), gap, shifted(...  1.51 us
  transfers between devices with their start and end apart: 11, of which 4 were waited for; matrix products, arithmetic and copies ran while one was open for 11% of the time, Pallas kernels for 9%

profile of v10, /device:TPU:0, one launch (start us, length us, event | category | flops | bytes accessed | tf_op | source)
XLA Modules:
  0.0 45.2 jit_solution(16447931058295166415)
XLA Ops:
  0.7 1.4 %add_convert_fusion.link_ref = f32[4,128]{1,0:T(4,128)} fusion(s32[1,128]{1,0:T(1,128)} %param.17, s32[1,128]{1,0:T(1,128)} %param.16, s32[1,128]{1,0:T(1,128)} %param.15, s32[1,128]{1,0:T(1,128)} %bitcast.25), kind=kLoop, calls=%fused_computation.19 | loop fusion | flops 2048 | bytes 4096 | tf_op jit(solution)/shard_map/convert_element_type | solution.py:281
  2.0 1.6 %shard_map.105.refs_0_ = f32[104,256]{1,0:T(8,128)} custom-call(s32[1]{0:T(128)} %bitcast.7.flag_ref, f32[1,3,8,32,256]{4,3,2,1,0:T(8,128)} %ground_ref.1, f32[1,3,32,256]{3,2,1,0:T(8,128)} %previous_ref.1, s32[1,32,256]{2,1,0:T(8,128)} %sea_ref.1, f32[4,128]{1,0:T(4,128)} %add_convert_fusion.link_ref), custom_call_target="tpu_custom_call" | custom-call | tf_op jit(solution)/shard_map/pallas_call | solution.py:152
  3.7 3.0 %collective-permute-start.4 = (f32[104,256]{1,0:T(8,128)}, f32[104,256]{1,0:T(8,128)S(1)}, u32[]{:S(2)}, u32[]{:S(2)}) collective-permute-start(f32[104,256]{1,0:T(8,128)} %shard_map.105.refs_0_), channel_id=1, source_target_pairs={{0,4},{4,8},{8,12},{12,0},{1,5},{5,9},{9,13},{13,1},{2,6},{6,10},{... | collective-permute-start | bytes 319496 | tf_op jit(solution)/shard_map/ppermute | solution.py:287
  6.7 2.6 %collective-permute-start.5 = (f32[104,256]{1,0:T(8,128)}, f32[104,256]{1,0:T(8,128)S(1)}, u32[]{:S(2)}, u32[]{:S(2)}) collective-permute-start(f32[104,256]{1,0:T(8,128)} %shard_map.105.refs_0_), channel_id=1, source_target_pairs={{0,8},{4,12},{8,0},{12,4},{1,9},{5,13},{9,1},{13,5},{2,10},{6,14},... | collective-permute-start | bytes 319496 | tf_op jit(solution)/shard_map/ppermute | solution.py:287
  9.3 1.3 %collective-permute-start.6 = (f32[104,256]{1,0:T(8,128)}, f32[104,256]{1,0:T(8,128)S(1)}, u32[]{:S(2)}, u32[]{:S(2)}) collective-permute-start(f32[104,256]{1,0:T(8,128)} %shard_map.105.refs_0_), channel_id=1, source_target_pairs={{0,12},{4,0},{8,4},{12,8},{1,13},{5,1},{9,5},{13,9},{2,14},{6,2},{... | collective-permute-start | bytes 319496 | tf_op jit(solution)/shard_map/ppermute | solution.py:287
  11.2 0.2 reshape.103
  11.4 2.5 %collective-permute-start = (f32[1600]{0:T(1024)S(1)}, f32[1600]{0:T(1024)S(1)}, u32[]{:S(2)}, u32[]{:S(2)}) collective-permute-start(f32[1600]{0:T(1024)S(1)} %reshape.103), channel_id=1, source_target_pairs={{1,0},{2,1},{3,2},{0,3},{5,4},{6,5},{7,6},{4,7},{9,8},{10,9},{11,1... | collective-permute-start | bytes 19208 | tf_op jit(solution)/shard_map/ppermute | solution.py:31
  14.3 0.7 %copy.16.row_ref = f32[2,40,1]{2,1,0:T(8,128)} copy(f32[2,40,1]{1,0,2:T(2,128)S(1)} %maximum_bitcast_fusion) | data formatting | bytes 640 | tf_op jit(solution)/shard_map/broadcast_in_dim | solution.py:320
  15.3 0.4 reshape.104
  15.6 3.1 %collective-permute-done.1 = f32[1600]{0:T(1024)S(1)} collective-permute-done((f32[1600]{0:T(1024)S(1)}, f32[1600]{0:T(1024)S(1)}, u32[]{:S(2)}, u32[]{:S(2)}) %collective-permute-start.1) | collective-permute-done | bytes 6432 | tf_op jit(solution)/shard_map/ppermute | solution.py:31
  18.7 0.4 reshape.106
  19.4 1.3 %collective-permute-start.2 = (f32[19200]{0:T(1024)S(1)}, f32[19200]{0:T(1024)S(1)}, u32[]{:S(2)}, u32[]{:S(2)}) collective-permute-start(f32[19200]{0:T(1024)S(1)} %reshape.107), channel_id=1, source_target_pairs={{4,0},{8,4},{12,8},{5,1},{9,5},{13,9},{6,2},{10,6},{14,10},{7,3},{... | collective-permute-start | bytes 230408 | tf_op jit(solution)/shard_map/ppermute | solution.py:31
  20.8 4.6 %collective-permute-start.3 = (f32[19200]{0:T(1024)S(1)}, f32[19200]{0:T(1024)S(1)}, u32[]{:S(2)}, u32[]{:S(2)}) collective-permute-start(f32[19200]{0:T(1024)S(1)} %reshape.109), channel_id=1, source_target_pairs={{0,4},{4,8},{8,12},{1,5},{5,9},{9,13},{2,6},{6,10},{10,14},{3,7},{... | collective-permute-start | bytes 230408 | tf_op jit(solution)/shard_map/ppermute | solution.py:31
  25.3 0.6 %pad_add_fusion.place_ref = s32[2]{0:T(128)} fusion(s32[1]{0:T(128)} %bitcast.6, s32[1]{0:T(128)} %bitcast.5), kind=kLoop, calls=%fused_computation.23 | loop fusion | flops 2 | bytes 16 | tf_op jit(solution)/shard_map/stack | solution.py:290
  26.0 1.3 %collective-permute-done.3 = f32[19200]{0:T(1024)S(1)} collective-permute-done((f32[19200]{0:T(1024)S(1)}, f32[19200]{0:T(1024)S(1)}, u32[]{:S(2)}, u32[]{:S(2)}) %collective-permute-start.3) | collective-permute-done | bytes 76832 | tf_op jit(solution)/shard_map/ppermute | solution.py:31
  27.4 0.6 %copy-done.3 = f32[104,256]{1,0:T(8,128)} copy-done((f32[104,256]{1,0:T(8,128)}, f32[104,256]{1,0:T(8,128)S(1)}, u32[]{:S(2)}) %copy-start.3) | copy-done | bytes 106520
  28.0 0.6 %copy-done.5 = f32[104,256]{1,0:T(8,128)} copy-done((f32[104,256]{1,0:T(8,128)}, f32[104,256]{1,0:T(8,128)S(1)}, u32[]{:S(2)}) %copy-start.5) | copy-done | bytes 106520
  28.7 7.4 %shard_map.106 = (f32[3,32,256]{2,1,0:T(8,128)}, f32[3,32,256]{2,1,0:T(8,128)}, f32[3,32,256]{2,1,0:T(8,128)}, f32[3,32,256]{2,1,0:T(8,128)}) custom-call(s32[2]{0:T(128)} %pad_add_fusion.place_ref, f32[104,256]{1,0:T(8,128)} %shard_map.105.refs_0_, f32[104,256]{1,0:T(8,128)} %copy-done.3, f32[104,256]{1,0:T(8,128)} %copy-done.4, f32[104,256]{1,0:T(8,128)} %copy-done.5, ...), custom_call_target="tpu_custom_call" | custom-call | tf_op jit(solution)/shard_map/pallas_call | solution.py:223
  36.3 1.5 %collective-permute-start.8 = (f32[3,32,256]{2,1,0:T(8,128)}, f32[3,32,256]{2,1,0:T(8,128)S(1)}, u32[]{:S(2)}, u32[]{:S(2)}) collective-permute-start(f32[3,32,256]{2,1,0:T(8,128)} %get-tuple-element.7), channel_id=1, source_target_pairs={{0,17},{1,18},{2,19},{3,16},{16,1},{17,2},{18,3},{19,0},{4,21},{5,... | collective-permute-start | bytes 294920 | tf_op jit(solution)/shard_map/ppermute | solution.py:299
  37.8 0.6 %collective-permute-start.9 = (f32[3,32,256]{2,1,0:T(8,128)}, f32[3,32,256]{2,1,0:T(8,128)S(1)}, u32[]{:S(2)}, u32[]{:S(2)}) collective-permute-start(f32[3,32,256]{2,1,0:T(8,128)} %get-tuple-element.8), channel_id=1, source_target_pairs={{0,18},{1,19},{2,16},{3,17},{16,2},{17,3},{18,0},{19,1},{4,22},{5,... | collective-permute-start | bytes 294920 | tf_op jit(solution)/shard_map/ppermute | solution.py:299
  38.4 1.5 %pad_maximum_fusion.wide_ref = f32[25,40,384]{2,1,0:T(8,128)} fusion(f32[25,2,384]{2,1,0:T(2,128)S(1)} %reshape.110, f32[25,2,384]{2,1,0:T(2,128)S(1)} %reshape.108, f32[25,32,2]{2,1,0:T(8,128)S(1)} %reshape.106, f32[25,32,124]{2,1,0:T(8,128)S(1)} %broadcast_in_dim.21, f32[25,32,2]{2,1,0:T(8,128)S(1)} %reshape.104, f32[1,32,256]{2,1,0:T(8,128)S(1)} %convert_select_fusion, ...), kind=kLoop, calls=%fused_computation | loop fusion | flops 2688000 | bytes 2918560 | tf_op jit(solution)/shard_map/concatenate | solution.py:46
  40.0 4.0 %shard_map.104 = f32[1,3,8,32,256]{4,3,2,1,0:T(8,128)} custom-call(f32[1,4,8]{2,1,0:T(4,128)} %coef_ref.1, f32[2,40,1]{2,1,0:T(8,128)} %copy.16.row_ref, f32[25,40,384]{2,1,0:T(8,128)} %pad_maximum_fusion.wide_ref), custom_call_target="tpu_custom_call" | custom-call | tf_op jit(solution)/shard_map/pallas_call | solution.py:111
  44.0 0.5 %collective-permute-done.9 = f32[3,32,256]{2,1,0:T(8,128)S(1)} collective-permute-done((f32[3,32,256]{2,1,0:T(8,128)}, f32[3,32,256]{2,1,0:T(8,128)S(1)}, u32[]{:S(2)}, u32[]{:S(2)}) %collective-permute-start.9) | collective-permute-done | bytes 98336 | tf_op jit(solution)/shard_map/ppermute | solution.py:299
  44.5 0.7 %multiply_bitcast_fusion = f32[1,3,32,256]{3,2,1,0:T(8,128)} fusion(f32[3,32,256]{2,1,0:T(8,128)S(1)} %collective-permute-done.10, f32[3,32,256]{2,1,0:T(8,128)S(1)} %collective-permute-done.9, f32[3,32,256]{2,1,0:T(8,128)S(1)} %collective-permute-done.7, f32[3,32,256]{2,1,0:T(8,128)S(1)} %collective-permute-done.8, f32[32,256]{1,0:T(8,128)S(1)} %convert_bitcast_fusion), kind=kLoop, calls=%fused_computation.10 | loop fusion | flops 98304 | bytes 524288 | tf_op jit(solution)/shard_map/broadcast_in_dim | solution.py:322
  (41 shorter events, 1.8 us)
Async XLA Ops:
  0.6 10.0 %copy-start = (f32[1,3,8,32,256]{4,3,2,1,0:T(8,128)S(1)}, f32[1,3,8,32,256]{4,3,2,1,0:T(8,128)}, u32[]{:S(2)}) copy-start(f32[1,3,8,32,256]{4,3,2,1,0:T(8,128)} %ground_ref.1) | copy-start | bytes 2359300
  0.6 10.0 %copy-start.2 = (s32[1,32,256]{2,1,0:T(8,128)S(1)}, s32[1,32,256]{2,1,0:T(8,128)}, u32[]{:S(2)}) copy-start(s32[1,32,256]{2,1,0:T(8,128)} %sea_ref.1) | copy-start | bytes 98308
  3.6 7.1 %copy-start.1 = (f32[1,3,32,256]{3,2,1,0:T(8,128)S(1)}, f32[1,3,32,256]{3,2,1,0:T(8,128)}, u32[]{:S(2)}) copy-start(f32[1,3,32,256]{3,2,1,0:T(8,128)} %previous_ref.1) | copy-start | bytes 294916
  3.7 23.7 %collective-permute-start.4 = (f32[104,256]{1,0:T(8,128)}, f32[104,256]{1,0:T(8,128)S(1)}, u32[]{:S(2)}, u32[]{:S(2)}) collective-permute-start(f32[104,256]{1,0:T(8,128)} %shard_map.105.refs_0_), channel_id=1, source_target_pairs={{0,4},{4,8},{8,12},{12,0},{1,5},{5,9},{9,13},{13,1},{2,6},{6,10},{... | collective-permute-start | bytes 319496 | tf_op jit(solution)/shard_map/ppermute | solution.py:287
  6.7 20.7 %collective-permute-start.5 = (f32[104,256]{1,0:T(8,128)}, f32[104,256]{1,0:T(8,128)S(1)}, u32[]{:S(2)}, u32[]{:S(2)}) collective-permute-start(f32[104,256]{1,0:T(8,128)} %shard_map.105.refs_0_), channel_id=1, source_target_pairs={{0,8},{4,12},{8,0},{12,4},{1,9},{5,13},{9,1},{13,5},{2,10},{6,14},... | collective-permute-start | bytes 319496 | tf_op jit(solution)/shard_map/ppermute | solution.py:287
  9.3 18.1 %collective-permute-start.6 = (f32[104,256]{1,0:T(8,128)}, f32[104,256]{1,0:T(8,128)S(1)}, u32[]{:S(2)}, u32[]{:S(2)}) collective-permute-start(f32[104,256]{1,0:T(8,128)} %shard_map.105.refs_0_), channel_id=1, source_target_pairs={{0,12},{4,0},{8,4},{12,8},{1,13},{5,1},{9,5},{13,9},{2,14},{6,2},{... | collective-permute-start | bytes 319496 | tf_op jit(solution)/shard_map/ppermute | solution.py:287
  11.4 3.9 %collective-permute-start = (f32[1600]{0:T(1024)S(1)}, f32[1600]{0:T(1024)S(1)}, u32[]{:S(2)}, u32[]{:S(2)}) collective-permute-start(f32[1600]{0:T(1024)S(1)} %reshape.103), channel_id=1, source_target_pairs={{1,0},{2,1},{3,2},{0,3},{5,4},{6,5},{7,6},{4,7},{9,8},{10,9},{11,1... | collective-permute-start | bytes 19208 | tf_op jit(solution)/shard_map/ppermute | solution.py:31
  14.1 4.6 %collective-permute-start.1 = (f32[1600]{0:T(1024)S(1)}, f32[1600]{0:T(1024)S(1)}, u32[]{:S(2)}, u32[]{:S(2)}) collective-permute-start(f32[1600]{0:T(1024)S(1)} %reshape.105), channel_id=1, source_target_pairs={{0,1},{1,2},{2,3},{3,0},{4,5},{5,6},{6,7},{7,4},{8,9},{9,10},{10,1... | collective-permute-start | bytes 19208 | tf_op jit(solution)/shard_map/ppermute | solution.py:31
  19.4 6.6 %collective-permute-start.2 = (f32[19200]{0:T(1024)S(1)}, f32[19200]{0:T(1024)S(1)}, u32[]{:S(2)}, u32[]{:S(2)}) collective-permute-start(f32[19200]{0:T(1024)S(1)} %reshape.107), channel_id=1, source_target_pairs={{4,0},{8,4},{12,8},{5,1},{9,5},{13,9},{6,2},{10,6},{14,10},{7,3},{... | collective-permute-start | bytes 230408 | tf_op jit(solution)/shard_map/ppermute | solution.py:31
  20.8 6.6 %collective-permute-start.3 = (f32[19200]{0:T(1024)S(1)}, f32[19200]{0:T(1024)S(1)}, u32[]{:S(2)}, u32[]{:S(2)}) collective-permute-start(f32[19200]{0:T(1024)S(1)} %reshape.109), channel_id=1, source_target_pairs={{0,4},{4,8},{8,12},{1,5},{5,9},{9,13},{2,6},{6,10},{10,14},{3,7},{... | collective-permute-start | bytes 230408 | tf_op jit(solution)/shard_map/ppermute | solution.py:31
  27.4 0.7 %copy-start.3 = (f32[104,256]{1,0:T(8,128)}, f32[104,256]{1,0:T(8,128)S(1)}, u32[]{:S(2)}) copy-start(f32[104,256]{1,0:T(8,128)S(1)} %collective-permute-done.4.refs_1_) | copy-start | bytes 319492
  27.4 0.7 %copy-start.4 = (f32[104,256]{1,0:T(8,128)}, f32[104,256]{1,0:T(8,128)S(1)}, u32[]{:S(2)}) copy-start(f32[104,256]{1,0:T(8,128)S(1)} %collective-permute-done.5.refs_2_) | copy-start | bytes 319492
  28.0 0.6 %copy-start.5 = (f32[104,256]{1,0:T(8,128)}, f32[104,256]{1,0:T(8,128)S(1)}, u32[]{:S(2)}) copy-start(f32[104,256]{1,0:T(8,128)S(1)} %collective-permute-done.6.refs_3_) | copy-start | bytes 319492
  36.1 7.9 %collective-permute-start.10 = (f32[3,32,256]{2,1,0:T(8,128)}, f32[3,32,256]{2,1,0:T(8,128)S(1)}, u32[]{:S(2)}, u32[]{:S(2)}) collective-permute-start(f32[3,32,256]{2,1,0:T(8,128)} %get-tuple-element.9), channel_id=1, source_target_pairs={{0,19},{1,16},{2,17},{3,18},{16,3},{17,0},{18,1},{19,2},{4,23},{5,... | collective-permute-start | bytes 294920 | tf_op jit(solution)/shard_map/ppermute | solution.py:299
  36.1 7.9 %collective-permute-start.7 = (f32[3,32,256]{2,1,0:T(8,128)}, f32[3,32,256]{2,1,0:T(8,128)S(1)}, u32[]{:S(2)}, u32[]{:S(2)}) collective-permute-start(f32[3,32,256]{2,1,0:T(8,128)} %get-tuple-element.6), channel_id=1, source_target_pairs={{0,16},{1,17},{2,18},{3,19},{16,0},{17,1},{18,2},{19,3},{4,20},{5,... | collective-permute-start | bytes 294920 | tf_op jit(solution)/shard_map/ppermute | solution.py:299
  36.3 7.7 %collective-permute-start.8 = (f32[3,32,256]{2,1,0:T(8,128)}, f32[3,32,256]{2,1,0:T(8,128)S(1)}, u32[]{:S(2)}, u32[]{:S(2)}) collective-permute-start(f32[3,32,256]{2,1,0:T(8,128)} %get-tuple-element.7), channel_id=1, source_target_pairs={{0,17},{1,18},{2,19},{3,16},{16,1},{17,2},{18,3},{19,0},{4,21},{5,... | collective-permute-start | bytes 294920 | tf_op jit(solution)/shard_map/ppermute | solution.py:299
  37.8 6.7 %collective-permute-start.9 = (f32[3,32,256]{2,1,0:T(8,128)}, f32[3,32,256]{2,1,0:T(8,128)S(1)}, u32[]{:S(2)}, u32[]{:S(2)}) collective-permute-start(f32[3,32,256]{2,1,0:T(8,128)} %get-tuple-element.8), channel_id=1, source_target_pairs={{0,18},{1,19},{2,16},{3,17},{16,2},{17,3},{18,0},{19,1},{4,22},{5,... | collective-permute-start | bytes 294920 | tf_op jit(solution)/shard_map/ppermute | solution.py:299

commit v11 on v10

--- a/solution.py
+++ b/solution.py
@@ -180,7 +180,7 @@
         rows_ref[source * base : (source + 1) * base, :] = source_refs[source][:base, :]
     for tile in range(tile_count):
         weighted = jnp.dot(
-            rows_ref[...], table_ref[0, tile], precision=HIGHEST, preferred_element_type=jnp.float32
+            rows_ref[...], table_ref[0, tile], precision=lax.Precision.HIGH, preferred_element_type=jnp.float32
         )
         for source in range(source_count):
             for c in range(field_count):
@@ -210,7 +210,7 @@
             to_rows, from_rows, (((1,), (1,)), ((), ())), preferred_element_type=jnp.float32
         )
     for c in range(field_count):
-        summed = jnp.dot(into, combo_ref[c], precision=HIGHEST, preferred_element_type=jnp.float32)
+        summed = jnp.dot(into, combo_ref[c], precision=lax.Precision.HIGH, preferred_element_type=jnp.float32)
         for owner in range(owner_count):
             out_refs[owner][c] = summed[owner * row_count : (owner + 1) * row_count]
 

time: 45.5 us -> 43.3 us (0.952)
  Pallas kernels: 13.1 us -> 10.9 us
    pallas_call x1, Pallas kernels: 7.4 us -> 5.24 us  [remapped(): pl.pallas_call(functools.partial(remap_kernel, link_count, source_count),...]
  transfers between devices with their start and end apart: 11 -> 11, of which waited for: 4 -> 4; matrix products, arithmetic and copies ran while one was open for 11% -> 12% of each run, Pallas kernels for 9% -> 9%
where the time goes in v11:
time: 43.3 us; the launch traced here: 43 us
  starting transfers between devices  17.7 us (41%)
  Pallas kernels  10.9 us (25%)
  waiting for transfers between devices  5.15 us (12%)
  other arithmetic  4.73 us (11%)
  local copies, waits for them, and re-layouts  3.68 us (8%)
  between operations  0.88 us (2%)
    ppermute x4, starting transfers between devices, shifted(): flat = lax.ppermute(part.reshape(-1), axis, route)  8.4 us
    ppermute x3, starting transfers between devices, body(): lax.ppermute(payload, 'lat', [(i, (i + shift) % lat_count) for i in range...  6.96 us
    pallas_call x1, Pallas kernels, remapped(): pl.pallas_call(functools.partial(remap_kernel, link_count, source_count),...  5.24 us
    ppermute x4, waiting for transfers between devices, shifted(): flat = lax.ppermute(part.reshape(-1), axis, route)  4.59 us
    pallas_call x1, Pallas kernels, dynamics(): pl.pallas_call(stencil_kernel, out_shape=jax.ShapeDtypeStruct((1, field_c...  4.03 us
    ppermute x4, starting transfers between devices, body(): pieces.append(lax.ppermute(partial[shift], ('grp', 'lon'), route))  2.36 us
    pallas_call x1, Pallas kernels, exported_block(): pl.pallas_call(export_kernel, out_shape=jax.ShapeDtypeStruct((field_count...  1.63 us
    concatenate x1, other arithmetic, with_halo(): jnp.concatenate([cells, shifted(head, 'lat', False, False), gap, shifted(...  1.51 us
  transfers between devices with their start and end apart: 11, of which 4 were waited for; matrix products, arithmetic and copies ran while one was open for 12% of the time, Pallas kernels for 9%

profile of v11, /device:TPU:0, one launch (start us, length us, event | category | flops | bytes accessed | tf_op | source)
XLA Modules:
  0.0 43.0 jit_solution(6536787845390736802)
XLA Ops:
  0.7 1.4 %add_convert_fusion.link_ref = f32[4,128]{1,0:T(4,128)} fusion(s32[1,128]{1,0:T(1,128)} %param.17, s32[1,128]{1,0:T(1,128)} %param.16, s32[1,128]{1,0:T(1,128)} %param.15, s32[1,128]{1,0:T(1,128)} %bitcast.25), kind=kLoop, calls=%fused_computation.19 | loop fusion | flops 2048 | bytes 4096 | tf_op jit(solution)/shard_map/convert_element_type | solution.py:281
  2.0 1.6 %shard_map.105.refs_0_ = f32[104,256]{1,0:T(8,128)} custom-call(s32[1]{0:T(128)} %bitcast.7.flag_ref, f32[1,3,8,32,256]{4,3,2,1,0:T(8,128)} %ground_ref.1, f32[1,3,32,256]{3,2,1,0:T(8,128)} %previous_ref.1, s32[1,32,256]{2,1,0:T(8,128)} %sea_ref.1, f32[4,128]{1,0:T(4,128)} %add_convert_fusion.link_ref), custom_call_target="tpu_custom_call" | custom-call | tf_op jit(solution)/shard_map/pallas_call | solution.py:152
  3.7 3.0 %collective-permute-start.4 = (f32[104,256]{1,0:T(8,128)}, f32[104,256]{1,0:T(8,128)S(1)}, u32[]{:S(2)}, u32[]{:S(2)}) collective-permute-start(f32[104,256]{1,0:T(8,128)} %shard_map.105.refs_0_), channel_id=1, source_target_pairs={{0,4},{4,8},{8,12},{12,0},{1,5},{5,9},{9,13},{13,1},{2,6},{6,10},{... | collective-permute-start | bytes 319496 | tf_op jit(solution)/shard_map/ppermute | solution.py:287
  6.7 2.6 %collective-permute-start.5 = (f32[104,256]{1,0:T(8,128)}, f32[104,256]{1,0:T(8,128)S(1)}, u32[]{:S(2)}, u32[]{:S(2)}) collective-permute-start(f32[104,256]{1,0:T(8,128)} %shard_map.105.refs_0_), channel_id=1, source_target_pairs={{0,8},{4,12},{8,0},{12,4},{1,9},{5,13},{9,1},{13,5},{2,10},{6,14},... | collective-permute-start | bytes 319496 | tf_op jit(solution)/shard_map/ppermute | solution.py:287
  9.3 1.3 %collective-permute-start.6 = (f32[104,256]{1,0:T(8,128)}, f32[104,256]{1,0:T(8,128)S(1)}, u32[]{:S(2)}, u32[]{:S(2)}) collective-permute-start(f32[104,256]{1,0:T(8,128)} %shard_map.105.refs_0_), channel_id=1, source_target_pairs={{0,12},{4,0},{8,4},{12,8},{1,13},{5,1},{9,5},{13,9},{2,14},{6,2},{... | collective-permute-start | bytes 319496 | tf_op jit(solution)/shard_map/ppermute | solution.py:287
  11.2 0.2 reshape.103
  11.4 2.5 %collective-permute-start = (f32[1600]{0:T(1024)S(1)}, f32[1600]{0:T(1024)S(1)}, u32[]{:S(2)}, u32[]{:S(2)}) collective-permute-start(f32[1600]{0:T(1024)S(1)} %reshape.103), channel_id=1, source_target_pairs={{1,0},{2,1},{3,2},{0,3},{5,4},{6,5},{7,6},{4,7},{9,8},{10,9},{11,1... | collective-permute-start | bytes 19208 | tf_op jit(solution)/shard_map/ppermute | solution.py:31
  14.3 0.7 %copy.16.row_ref = f32[2,40,1]{2,1,0:T(8,128)} copy(f32[2,40,1]{1,0,2:T(2,128)S(1)} %maximum_bitcast_fusion) | data formatting | bytes 640 | tf_op jit(solution)/shard_map/broadcast_in_dim | solution.py:320
  15.3 0.4 reshape.104
  15.6 3.1 %collective-permute-done.1 = f32[1600]{0:T(1024)S(1)} collective-permute-done((f32[1600]{0:T(1024)S(1)}, f32[1600]{0:T(1024)S(1)}, u32[]{:S(2)}, u32[]{:S(2)}) %collective-permute-start.1) | collective-permute-done | bytes 6432 | tf_op jit(solution)/shard_map/ppermute | solution.py:31
  18.7 0.4 reshape.106
  19.4 1.3 %collective-permute-start.2 = (f32[19200]{0:T(1024)S(1)}, f32[19200]{0:T(1024)S(1)}, u32[]{:S(2)}, u32[]{:S(2)}) collective-permute-start(f32[19200]{0:T(1024)S(1)} %reshape.107), channel_id=1, source_target_pairs={{4,0},{8,4},{12,8},{5,1},{9,5},{13,9},{6,2},{10,6},{14,10},{7,3},{... | collective-permute-start | bytes 230408 | tf_op jit(solution)/shard_map/ppermute | solution.py:31
  20.8 4.6 %collective-permute-start.3 = (f32[19200]{0:T(1024)S(1)}, f32[19200]{0:T(1024)S(1)}, u32[]{:S(2)}, u32[]{:S(2)}) collective-permute-start(f32[19200]{0:T(1024)S(1)} %reshape.109), channel_id=1, source_target_pairs={{0,4},{4,8},{8,12},{1,5},{5,9},{9,13},{2,6},{6,10},{10,14},{3,7},{... | collective-permute-start | bytes 230408 | tf_op jit(solution)/shard_map/ppermute | solution.py:31
  25.3 0.6 %pad_add_fusion.place_ref = s32[2]{0:T(128)} fusion(s32[1]{0:T(128)} %bitcast.6, s32[1]{0:T(128)} %bitcast.5), kind=kLoop, calls=%fused_computation.23 | loop fusion | flops 2 | bytes 16 | tf_op jit(solution)/shard_map/stack | solution.py:290
  26.0 1.3 %collective-permute-done.3 = f32[19200]{0:T(1024)S(1)} collective-permute-done((f32[19200]{0:T(1024)S(1)}, f32[19200]{0:T(1024)S(1)}, u32[]{:S(2)}, u32[]{:S(2)}) %collective-permute-start.3) | collective-permute-done | bytes 76832 | tf_op jit(solution)/shard_map/ppermute | solution.py:31
  27.4 0.6 %copy-done.3 = f32[104,256]{1,0:T(8,128)} copy-done((f32[104,256]{1,0:T(8,128)}, f32[104,256]{1,0:T(8,128)S(1)}, u32[]{:S(2)}) %copy-start.3) | copy-done | bytes 106520
  28.0 0.6 %copy-done.5 = f32[104,256]{1,0:T(8,128)} copy-done((f32[104,256]{1,0:T(8,128)}, f32[104,256]{1,0:T(8,128)S(1)}, u32[]{:S(2)}) %copy-start.5) | copy-done | bytes 106520
  28.7 5.2 %shard_map.106 = (f32[3,32,256]{2,1,0:T(8,128)}, f32[3,32,256]{2,1,0:T(8,128)}, f32[3,32,256]{2,1,0:T(8,128)}, f32[3,32,256]{2,1,0:T(8,128)}) custom-call(s32[2]{0:T(128)} %pad_add_fusion.place_ref, f32[104,256]{1,0:T(8,128)} %shard_map.105.refs_0_, f32[104,256]{1,0:T(8,128)} %copy-done.3, f32[104,256]{1,0:T(8,128)} %copy-done.4, f32[104,256]{1,0:T(8,128)} %copy-done.5, ...), custom_call_target="tpu_custom_call" | custom-call | tf_op jit(solution)/shard_map/pallas_call | solution.py:223
  34.1 1.5 %collective-permute-start.8 = (f32[3,32,256]{2,1,0:T(8,128)}, f32[3,32,256]{2,1,0:T(8,128)S(1)}, u32[]{:S(2)}, u32[]{:S(2)}) collective-permute-start(f32[3,32,256]{2,1,0:T(8,128)} %get-tuple-element.7), channel_id=1, source_target_pairs={{0,17},{1,18},{2,19},{3,16},{16,1},{17,2},{18,3},{19,0},{4,21},{5,... | collective-permute-start | bytes 294920 | tf_op jit(solution)/shard_map/ppermute | solution.py:299
  35.7 0.6 %collective-permute-start.9 = (f32[3,32,256]{2,1,0:T(8,128)}, f32[3,32,256]{2,1,0:T(8,128)S(1)}, u32[]{:S(2)}, u32[]{:S(2)}) collective-permute-start(f32[3,32,256]{2,1,0:T(8,128)} %get-tuple-element.8), channel_id=1, source_target_pairs={{0,18},{1,19},{2,16},{3,17},{16,2},{17,3},{18,0},{19,1},{4,22},{5,... | collective-permute-start | bytes 294920 | tf_op jit(solution)/shard_map/ppermute | solution.py:299
  36.3 1.5 %pad_maximum_fusion.wide_ref = f32[25,40,384]{2,1,0:T(8,128)} fusion(f32[25,2,384]{2,1,0:T(2,128)S(1)} %reshape.110, f32[25,2,384]{2,1,0:T(2,128)S(1)} %reshape.108, f32[25,32,2]{2,1,0:T(8,128)S(1)} %reshape.106, f32[25,32,124]{2,1,0:T(8,128)S(1)} %broadcast_in_dim.21, f32[25,32,2]{2,1,0:T(8,128)S(1)} %reshape.104, f32[1,32,256]{2,1,0:T(8,128)S(1)} %convert_select_fusion, ...), kind=kLoop, calls=%fused_computation | loop fusion | flops 2688000 | bytes 2918560 | tf_op jit(solution)/shard_map/concatenate | solution.py:46
  37.8 4.0 %shard_map.104 = f32[1,3,8,32,256]{4,3,2,1,0:T(8,128)} custom-call(f32[1,4,8]{2,1,0:T(4,128)} %coef_ref.1, f32[2,40,1]{2,1,0:T(8,128)} %copy.16.row_ref, f32[25,40,384]{2,1,0:T(8,128)} %pad_maximum_fusion.wide_ref), custom_call_target="tpu_custom_call" | custom-call | tf_op jit(solution)/shard_map/pallas_call | solution.py:111
  41.8 0.5 %collective-permute-done.9 = f32[3,32,256]{2,1,0:T(8,128)S(1)} collective-permute-done((f32[3,32,256]{2,1,0:T(8,128)}, f32[3,32,256]{2,1,0:T(8,128)S(1)}, u32[]{:S(2)}, u32[]{:S(2)}) %collective-permute-start.9) | collective-permute-done | bytes 98336 | tf_op jit(solution)/shard_map/ppermute | solution.py:299
  42.4 0.7 %multiply_bitcast_fusion = f32[1,3,32,256]{3,2,1,0:T(8,128)} fusion(f32[3,32,256]{2,1,0:T(8,128)S(1)} %collective-permute-done.10, f32[3,32,256]{2,1,0:T(8,128)S(1)} %collective-permute-done.9, f32[3,32,256]{2,1,0:T(8,128)S(1)} %collective-permute-done.7, f32[3,32,256]{2,1,0:T(8,128)S(1)} %collective-permute-done.8, f32[32,256]{1,0:T(8,128)S(1)} %convert_bitcast_fusion), kind=kLoop, calls=%fused_computation.10 | loop fusion | flops 98304 | bytes 524288 | tf_op jit(solution)/shard_map/broadcast_in_dim | solution.py:322
  (41 shorter events, 1.8 us)
Async XLA Ops:
  0.6 10.0 %copy-start = (f32[1,3,8,32,256]{4,3,2,1,0:T(8,128)S(1)}, f32[1,3,8,32,256]{4,3,2,1,0:T(8,128)}, u32[]{:S(2)}) copy-start(f32[1,3,8,32,256]{4,3,2,1,0:T(8,128)} %ground_ref.1) | copy-start | bytes 2359300
  0.6 10.0 %copy-start.2 = (s32[1,32,256]{2,1,0:T(8,128)S(1)}, s32[1,32,256]{2,1,0:T(8,128)}, u32[]{:S(2)}) copy-start(s32[1,32,256]{2,1,0:T(8,128)} %sea_ref.1) | copy-start | bytes 98308
  3.6 7.1 %copy-start.1 = (f32[1,3,32,256]{3,2,1,0:T(8,128)S(1)}, f32[1,3,32,256]{3,2,1,0:T(8,128)}, u32[]{:S(2)}) copy-start(f32[1,3,32,256]{3,2,1,0:T(8,128)} %previous_ref.1) | copy-start | bytes 294916
  3.7 23.7 %collective-permute-start.4 = (f32[104,256]{1,0:T(8,128)}, f32[104,256]{1,0:T(8,128)S(1)}, u32[]{:S(2)}, u32[]{:S(2)}) collective-permute-start(f32[104,256]{1,0:T(8,128)} %shard_map.105.refs_0_), channel_id=1, source_target_pairs={{0,4},{4,8},{8,12},{12,0},{1,5},{5,9},{9,13},{13,1},{2,6},{6,10},{... | collective-permute-start | bytes 319496 | tf_op jit(solution)/shard_map/ppermute | solution.py:287
  6.7 20.7 %collective-permute-start.5 = (f32[104,256]{1,0:T(8,128)}, f32[104,256]{1,0:T(8,128)S(1)}, u32[]{:S(2)}, u32[]{:S(2)}) collective-permute-start(f32[104,256]{1,0:T(8,128)} %shard_map.105.refs_0_), channel_id=1, source_target_pairs={{0,8},{4,12},{8,0},{12,4},{1,9},{5,13},{9,1},{13,5},{2,10},{6,14},... | collective-permute-start | bytes 319496 | tf_op jit(solution)/shard_map/ppermute | solution.py:287
  9.3 18.1 %collective-permute-start.6 = (f32[104,256]{1,0:T(8,128)}, f32[104,256]{1,0:T(8,128)S(1)}, u32[]{:S(2)}, u32[]{:S(2)}) collective-permute-start(f32[104,256]{1,0:T(8,128)} %shard_map.105.refs_0_), channel_id=1, source_target_pairs={{0,12},{4,0},{8,4},{12,8},{1,13},{5,1},{9,5},{13,9},{2,14},{6,2},{... | collective-permute-start | bytes 319496 | tf_op jit(solution)/shard_map/ppermute | solution.py:287
  11.4 3.9 %collective-permute-start = (f32[1600]{0:T(1024)S(1)}, f32[1600]{0:T(1024)S(1)}, u32[]{:S(2)}, u32[]{:S(2)}) collective-permute-start(f32[1600]{0:T(1024)S(1)} %reshape.103), channel_id=1, source_target_pairs={{1,0},{2,1},{3,2},{0,3},{5,4},{6,5},{7,6},{4,7},{9,8},{10,9},{11,1... | collective-permute-start | bytes 19208 | tf_op jit(solution)/shard_map/ppermute | solution.py:31
  14.1 4.6 %collective-permute-start.1 = (f32[1600]{0:T(1024)S(1)}, f32[1600]{0:T(1024)S(1)}, u32[]{:S(2)}, u32[]{:S(2)}) collective-permute-start(f32[1600]{0:T(1024)S(1)} %reshape.105), channel_id=1, source_target_pairs={{0,1},{1,2},{2,3},{3,0},{4,5},{5,6},{6,7},{7,4},{8,9},{9,10},{10,1... | collective-permute-start | bytes 19208 | tf_op jit(solution)/shard_map/ppermute | solution.py:31
  19.4 6.6 %collective-permute-start.2 = (f32[19200]{0:T(1024)S(1)}, f32[19200]{0:T(1024)S(1)}, u32[]{:S(2)}, u32[]{:S(2)}) collective-permute-start(f32[19200]{0:T(1024)S(1)} %reshape.107), channel_id=1, source_target_pairs={{4,0},{8,4},{12,8},{5,1},{9,5},{13,9},{6,2},{10,6},{14,10},{7,3},{... | collective-permute-start | bytes 230408 | tf_op jit(solution)/shard_map/ppermute | solution.py:31
  20.8 6.6 %collective-permute-start.3 = (f32[19200]{0:T(1024)S(1)}, f32[19200]{0:T(1024)S(1)}, u32[]{:S(2)}, u32[]{:S(2)}) collective-permute-start(f32[19200]{0:T(1024)S(1)} %reshape.109), channel_id=1, source_target_pairs={{0,4},{4,8},{8,12},{1,5},{5,9},{9,13},{2,6},{6,10},{10,14},{3,7},{... | collective-permute-start | bytes 230408 | tf_op jit(solution)/shard_map/ppermute | solution.py:31
  27.4 0.7 %copy-start.3 = (f32[104,256]{1,0:T(8,128)}, f32[104,256]{1,0:T(8,128)S(1)}, u32[]{:S(2)}) copy-start(f32[104,256]{1,0:T(8,128)S(1)} %collective-permute-done.4.refs_1_) | copy-start | bytes 319492
  27.4 0.7 %copy-start.4 = (f32[104,256]{1,0:T(8,128)}, f32[104,256]{1,0:T(8,128)S(1)}, u32[]{:S(2)}) copy-start(f32[104,256]{1,0:T(8,128)S(1)} %collective-permute-done.5.refs_2_) | copy-start | bytes 319492
  28.0 0.6 %copy-start.5 = (f32[104,256]{1,0:T(8,128)}, f32[104,256]{1,0:T(8,128)S(1)}, u32[]{:S(2)}) copy-start(f32[104,256]{1,0:T(8,128)S(1)} %collective-permute-done.6.refs_3_) | copy-start | bytes 319492
  33.9 7.9 %collective-permute-start.10 = (f32[3,32,256]{2,1,0:T(8,128)}, f32[3,32,256]{2,1,0:T(8,128)S(1)}, u32[]{:S(2)}, u32[]{:S(2)}) collective-permute-start(f32[3,32,256]{2,1,0:T(8,128)} %get-tuple-element.9), channel_id=1, source_target_pairs={{0,19},{1,16},{2,17},{3,18},{16,3},{17,0},{18,1},{19,2},{4,23},{5,... | collective-permute-start | bytes 294920 | tf_op jit(solution)/shard_map/ppermute | solution.py:299
  33.9 7.9 %collective-permute-start.7 = (f32[3,32,256]{2,1,0:T(8,128)}, f32[3,32,256]{2,1,0:T(8,128)S(1)}, u32[]{:S(2)}, u32[]{:S(2)}) collective-permute-start(f32[3,32,256]{2,1,0:T(8,128)} %get-tuple-element.6), channel_id=1, source_target_pairs={{0,16},{1,17},{2,18},{3,19},{16,0},{17,1},{18,2},{19,3},{4,20},{5,... | collective-permute-start | bytes 294920 | tf_op jit(solution)/shard_map/ppermute | solution.py:299
  34.1 7.7 %collective-permute-start.8 = (f32[3,32,256]{2,1,0:T(8,128)}, f32[3,32,256]{2,1,0:T(8,128)S(1)}, u32[]{:S(2)}, u32[]{:S(2)}) collective-permute-start(f32[3,32,256]{2,1,0:T(8,128)} %get-tuple-element.7), channel_id=1, source_target_pairs={{0,17},{1,18},{2,19},{3,16},{16,1},{17,2},{18,3},{19,0},{4,21},{5,... | collective-permute-start | bytes 294920 | tf_op jit(solution)/shard_map/ppermute | solution.py:299
  35.7 6.7 %collective-permute-start.9 = (f32[3,32,256]{2,1,0:T(8,128)}, f32[3,32,256]{2,1,0:T(8,128)S(1)}, u32[]{:S(2)}, u32[]{:S(2)}) collective-permute-start(f32[3,32,256]{2,1,0:T(8,128)} %get-tuple-element.8), channel_id=1, source_target_pairs={{0,18},{1,19},{2,16},{3,17},{16,2},{17,3},{18,0},{19,1},{4,22},{5,... | collective-permute-start | bytes 294920 | tf_op jit(solution)/shard_map/ppermute | solution.py:299

commit v12 on v11

--- a/solution.py
+++ b/solution.py
@@ -30,22 +30,6 @@
         route = [((i + 1) % count, i) for i in range(ends)]
     flat = lax.ppermute(part.reshape(-1), axis, route)
     return flat.reshape(part.shape)
-
-
-def with_halo(cells, width, wide_cols, wide_rows):
-    planes, rows, cols = cells.shape
-    head = cells[:, :, :width]
-    tail = cells[:, :, -width:]
-    gap = jnp.zeros((planes, rows, wide_cols - cols - 2 * width), cells.dtype)
-    cells = jnp.concatenate(
-        [cells, shifted(head, "lon", True, False), gap, shifted(tail, "lon", True, True)], axis=2
-    )
-    head = cells[:, :width, :]
-    tail = cells[:, rows - width : rows, :]
-    gap = jnp.zeros((planes, wide_rows - rows - 2 * width, wide_cols), cells.dtype)
-    return jnp.concatenate(
-        [cells, shifted(head, "lat", False, False), gap, shifted(tail, "lat", False, True)], axis=1
-    )
 
 
 def stencil_kernel(coef_ref, row_ref, wide_ref, out_ref, mid_ref):
@@ -273,8 +257,6 @@
     ocean_side = lax.axis_index("grp") == 1
     first_row = lax.axis_index("lat") * row_count
     total_rows = row_count * lax.axis_size("lat")
-    peer_count = lax.axis_size("lat") * lax.axis_size("lon")
-    width = field_count * col_count
 
     links = jnp.stack(
         [link_dest[0, :, 0], link_src_row[0], link_dst_row[0], link_tile[0]]
@@ -283,10 +265,41 @@
     payload = exported_block(flag, state, surface, sea_mask, links)
     lat_count = lax.axis_size("lat")
     lon_count = lax.axis_size("lon")
-    sources = [payload] + [
-        lax.ppermute(payload, "lat", [(i, (i + shift) % lat_count) for i in range(lat_count)])
-        for shift in range(1, lat_count)
-    ]
+    gain = jnp.where(ocean_side, ocean_gain, air_gain)
+    damping = jnp.where(ocean_side, 0.0, air_gain)
+    ground = fields[:, 0] + sea_float * (gain * previous - damping * fields[:, 0])
+    fields = jnp.concatenate([ground[:, None], fields[:, 1:]], 1)
+    state_mask = jnp.where(ocean_side, sea_float, jnp.ones_like(sea_float))
+    planes = jnp.concatenate(
+        [fields.reshape(field_count * level_count, row_count, col_count), state_mask[None]], 0
+    )
+    plane_count = planes.shape[0]
+    width = SUBSTEPS
+    edge_rows = plane_count * width
+    edge_pad = -(-edge_rows // 8) * 8 - edge_rows
+    head = planes[:, :width, :].reshape(edge_rows, col_count)
+    tail = planes[:, row_count - width :, :].reshape(edge_rows, col_count)
+    gap_rows = jnp.zeros((edge_pad, col_count), jnp.float32)
+    base = payload.shape[0]
+    sources = [payload]
+    south = north = None
+    for shift in range(1, lat_count):
+        parts = [payload]
+        if shift == 1:
+            parts += [tail, gap_rows]
+        if shift == lat_count - 1:
+            parts += [head, gap_rows]
+        sent = jnp.concatenate(parts, 0) if len(parts) > 1 else payload
+        got = lax.ppermute(sent, "lat", [(i, (i + shift) % lat_count) for i in range(lat_count)])
+        sources.append(got)
+        if shift == 1:
+            south = got[base : base + edge_rows]
+        if shift == lat_count - 1:
+            start = base + (edge_rows + edge_pad if shift == 1 else 0)
+            north = got[start : start + edge_rows]
+    my_lat = lax.axis_index("lat")
+    south = south.reshape(plane_count, width, col_count) * (my_lat > 0).astype(jnp.float32)
+    north = north.reshape(plane_count, width, col_count) * (my_lat < lat_count - 1).astype(jnp.float32)
     place = jnp.stack([lax.axis_index("lat"), lax.axis_index("lon")]).astype(jnp.int32)
     partial = remapped(place, sources, remap_weights, lon_count, field_count, row_count, links.shape[1])
     pieces = []
@@ -299,17 +312,20 @@
         pieces.append(lax.ppermute(partial[shift], ("grp", "lon"), route))
     imported = functools.reduce(jnp.add, pieces) * sea_float
 
-    gain = jnp.where(ocean_side, ocean_gain, air_gain)
-    damping = jnp.where(ocean_side, 0.0, air_gain)
-    ground = fields[:, 0] + sea_float * (gain * previous - damping * fields[:, 0])
-    fields = jnp.concatenate([ground[:, None], fields[:, 1:]], 1)
-    state_mask = jnp.where(ocean_side, sea_float, jnp.ones_like(sea_float))
-    planes = jnp.concatenate(
-        [fields.reshape(field_count * level_count, row_count, col_count), state_mask[None]], 0
-    )
     wide_rows = -(-(row_count + 4 * SUBSTEPS) // 8) * 8
     wide_cols = -(-(col_count + 4 * SUBSTEPS) // 128) * 128
-    wide = with_halo(planes, SUBSTEPS, wide_cols, wide_rows)
+    row_gap = jnp.zeros((plane_count, wide_rows - row_count - 2 * width, col_count), jnp.float32)
+    stacked = jnp.concatenate([planes, north, row_gap, south], 1)
+    col_gap = jnp.zeros((plane_count, wide_rows, wide_cols - col_count - 2 * width), jnp.float32)
+    wide = jnp.concatenate(
+        [
+            stacked,
+            shifted(stacked[:, :, :width], "lon", True, False),
+            col_gap,
+            shifted(stacked[:, :, col_count - width :], "lon", True, True),
+        ],
+        2,
+    )
     local = jnp.arange(wide_rows, dtype=jnp.int32)
     row_index = first_row + jnp.where(local < wide_rows // 2 + row_count // 2, local, local - wide_rows)
     latitude = jnp.pi * (

time: 43.3 us -> 41.7 us (0.963)
  starting transfers between devices: 17.7 us -> 12.6 us
  waiting for transfers between devices: 5.15 us -> 8.19 us
  local copies, waits for them, and re-layouts: 3.68 us -> 4.33 us
    ppermute x3, waiting for transfers between devices: 0.01 us -> 8.18 us  [body(): lax.ppermute(sent, 'lat', [(i, (i + shift) % lat_count) for i in range(la...]
    ppermute x4 -> x2, starting transfers between devices: 8.4 us -> 2.6 us  [shifted(): flat = lax.ppermute(part.reshape(-1), axis, route)]
    ppermute x4 -> x2, waiting for transfers between devices: 4.59 us -> 0.01 us  [shifted(): flat = lax.ppermute(part.reshape(-1), axis, route)]
    ppermute x4, starting transfers between devices: 2.36 us -> 3.84 us  [body(): pieces.append(lax.ppermute(partial[shift], ('grp', 'lon'), route))]
    ppermute x3, starting transfers between devices: 6.96 us -> 6.11 us  [body(): lax.ppermute(sent, 'lat', [(i, (i + shift) % lat_count) for i in range(la...]
    ppermute x4, waiting for transfers between devices: 0.55 us -> 0.01 us  [body(): pieces.append(lax.ppermute(partial[shift], ('grp', 'lon'), route))]
    unnamed x13 -> x15, local copies, waits for them, and re-layouts: 1.34 us -> 1.56 us
    reshape x4 -> x2, local copies, waits for them, and re-layouts: 0.8 us -> 0.91 us  [shifted(): return flat.reshape(part.shape)]
  transfers between devices with their start and end apart: 11 -> 9, of which waited for: 4 -> 1; matrix products, arithmetic and copies ran while one was open for 12% -> 13% of each run, Pallas kernels for 9% -> 22%
where the time goes in v12:
time: 41.7 us; the launch traced here: 41.5 us
  starting transfers between devices  12.6 us (30%)
  Pallas kernels  10.9 us (26%)
  waiting for transfers between devices  8.19 us (20%)
  other arithmetic  4.56 us (11%)
  local copies, waits for them, and re-layouts  4.33 us (10%)
  between operations  0.91 us (2%)
    ppermute x3, waiting for transfers between devices, body(): lax.ppermute(sent, 'lat', [(i, (i + shift) % lat_count) for i in range(la...  8.18 us
    ppermute x3, starting transfers between devices, body(): lax.ppermute(sent, 'lat', [(i, (i + shift) % lat_count) for i in range(la...  6.11 us
    pallas_call x1, Pallas kernels, remapped(): pl.pallas_call(functools.partial(remap_kernel, link_count, source_count),...  5.28 us
    pallas_call x1, Pallas kernels, dynamics(): pl.pallas_call(stencil_kernel, out_shape=jax.ShapeDtypeStruct((1, field_c...  4.03 us
    ppermute x4, starting transfers between devices, body(): pieces.append(lax.ppermute(partial[shift], ('grp', 'lon'), route))  3.84 us
    ppermute x2, starting transfers between devices, shifted(): flat = lax.ppermute(part.reshape(-1), axis, route)  2.6 us
    pallas_call x1, Pallas kernels, exported_block(): pl.pallas_call(export_kernel, out_shape=jax.ShapeDtypeStruct((field_count...  1.63 us
    unnamed x15, local copies, waits for them, and re-layouts  1.56 us
  transfers between devices with their start and end apart: 9, of which 1 were waited for; matrix products, arithmetic and copies ran while one was open for 13% of the time, Pallas kernels for 22%

profile of v12, /device:TPU:0, one launch (start us, length us, event | category | flops | bytes accessed | tf_op | source)
XLA Modules:
  0.0 41.5 jit_solution(16306168132567735924)
XLA Ops:
  0.7 1.4 %add_convert_fusion.link_ref = f32[4,128]{1,0:T(4,128)} fusion(s32[1,128]{1,0:T(1,128)} %param.17, s32[1,128]{1,0:T(1,128)} %param.16, s32[1,128]{1,0:T(1,128)} %param.15, s32[1,128]{1,0:T(1,128)} %bitcast.25), kind=kLoop, calls=%fused_computation.19 | loop fusion | flops 2048 | bytes 4096 | tf_op jit(solution)/shard_map/convert_element_type | solution.py:263
  2.0 1.6 %shard_map.104.refs_0_ = f32[104,256]{1,0:T(8,128)} custom-call(s32[1]{0:T(128)} %bitcast.5.flag_ref, f32[1,3,8,32,256]{4,3,2,1,0:T(8,128)} %ground_ref.1, f32[1,3,32,256]{3,2,1,0:T(8,128)} %previous_ref.1, s32[1,32,256]{2,1,0:T(8,128)} %sea_ref.1, f32[4,128]{1,0:T(4,128)} %add_convert_fusion.link_ref), custom_call_target="tpu_custom_call" | custom-call | tf_op jit(solution)/shard_map/pallas_call | solution.py:136
  3.7 4.0 %collective-permute-start.4 = (f32[104,256]{1,0:T(8,128)}, f32[104,256]{1,0:T(8,128)S(1)}, u32[]{:S(2)}, u32[]{:S(2)}) collective-permute-start(f32[104,256]{1,0:T(8,128)} %shard_map.104.refs_0_), channel_id=1, source_target_pairs={{0,8},{4,12},{8,0},{12,4},{1,9},{5,13},{9,1},{13,5},{2,10},{6,14},... | collective-permute-start | bytes 319496 | tf_op jit(solution)/shard_map/ppermute | solution.py:293
  8.3 0.6 %copy-done.1 = f32[104,256]{1,0:T(8,128)S(1)} copy-done((f32[104,256]{1,0:T(8,128)S(1)}, f32[104,256]{1,0:T(8,128)}, u32[]{:S(2)}) %copy-start.1) | copy-done | bytes 106520
  9.0 1.8 %collective-permute-start = (f32[160,256]{1,0:T(8,128)S(1)}, f32[160,256]{1,0:T(8,128)S(1)}, u32[]{:S(2)}, u32[]{:S(2)}) collective-permute-start(f32[160,256]{1,0:T(8,128)S(1)} %get-tuple-element.14), channel_id=1, source_target_pairs={{0,12},{4,0},{8,4},{12,8},{1,13},{5,1},{9,5},{13,9},{2,14},{6,2},{... | collective-permute-start | bytes 491528 | tf_op jit(solution)/shard_map/ppermute | solution.py:293
  10.7 0.3 collective-permute-start.1
  11.1 8.2 %collective-permute-done.refs_3_ = f32[160,256]{1,0:T(8,128)S(1)} collective-permute-done((f32[160,256]{1,0:T(8,128)S(1)}, f32[160,256]{1,0:T(8,128)S(1)}, u32[]{:S(2)}, u32[]{:S(2)}) %collective-permute-start) | collective-permute-done | bytes 163872 | tf_op jit(solution)/shard_map/ppermute | solution.py:293
  19.6 0.2 fusion.5
  19.8 0.2 copy-done.3
  20.0 0.3 reshape.106
  20.3 2.5 %collective-permute-start.2 = (f32[2000]{0:T(1024)S(1)}, f32[2000]{0:T(1024)S(1)}, u32[]{:S(2)}, u32[]{:S(2)}) collective-permute-start(f32[2000]{0:T(1024)S(1)} %reshape.106), channel_id=1, source_target_pairs={{1,0},{2,1},{3,2},{0,3},{5,4},{6,5},{7,6},{4,7},{9,8},{10,9},{11,1... | collective-permute-start | bytes 24008 | tf_op jit(solution)/shard_map/ppermute | solution.py:31
  22.9 0.3 reshape.108
  23.2 0.6 %pad_add_fusion.place_ref = s32[2]{0:T(128)} fusion(s32[1]{0:T(128)} %bitcast.8, s32[1]{0:T(128)} %bitcast.7), kind=kLoop, calls=%fused_computation.23 | loop fusion | flops 2 | bytes 16 | tf_op jit(solution)/shard_map/stack | solution.py:303
  23.9 0.7 %copy.16.row_ref = f32[2,40,1]{2,1,0:T(8,128)} copy(f32[2,40,1]{1,0,2:T(2,128)S(1)} %maximum_bitcast_fusion) | data formatting | bytes 640 | tf_op jit(solution)/shard_map/broadcast_in_dim | solution.py:336
  24.6 0.6 %copy-done.6 = f32[104,256]{1,0:T(8,128)} copy-done((f32[104,256]{1,0:T(8,128)}, f32[104,256]{1,0:T(8,128)S(1)}, u32[]{:S(2)}) %copy-start.6) | copy-done | bytes 106520
  25.2 5.3 %shard_map.106 = (f32[3,32,256]{2,1,0:T(8,128)}, f32[3,32,256]{2,1,0:T(8,128)}, f32[3,32,256]{2,1,0:T(8,128)}, f32[3,32,256]{2,1,0:T(8,128)}) custom-call(s32[2]{0:T(128)} %pad_add_fusion.place_ref, f32[104,256]{1,0:T(8,128)} %shard_map.104.refs_0_, f32[160,256]{1,0:T(8,128)} %copy-done.4, f32[104,256]{1,0:T(8,128)} %copy-done.6, f32[160,256]{1,0:T(8,128)} %copy-done.3, ...), custom_call_target="tpu_custom_call" | custom-call | tf_op jit(solution)/shard_map/pallas_call | solution.py:207
  30.5 2.1 %collective-permute-start.6 = (f32[3,32,256]{2,1,0:T(8,128)}, f32[3,32,256]{2,1,0:T(8,128)S(1)}, u32[]{:S(2)}, u32[]{:S(2)}) collective-permute-start(f32[3,32,256]{2,1,0:T(8,128)} %get-tuple-element.7), channel_id=1, source_target_pairs={{0,17},{1,18},{2,19},{3,16},{16,1},{17,2},{18,3},{19,0},{4,21},{5,... | collective-permute-start | bytes 294920 | tf_op jit(solution)/shard_map/ppermute | solution.py:312
  32.6 1.1 %collective-permute-start.7 = (f32[3,32,256]{2,1,0:T(8,128)}, f32[3,32,256]{2,1,0:T(8,128)S(1)}, u32[]{:S(2)}, u32[]{:S(2)}) collective-permute-start(f32[3,32,256]{2,1,0:T(8,128)} %get-tuple-element.8), channel_id=1, source_target_pairs={{0,18},{1,19},{2,16},{3,17},{16,2},{17,3},{18,0},{19,1},{4,22},{5,... | collective-permute-start | bytes 294920 | tf_op jit(solution)/shard_map/ppermute | solution.py:312
  33.7 0.6 %collective-permute-start.8 = (f32[3,32,256]{2,1,0:T(8,128)}, f32[3,32,256]{2,1,0:T(8,128)S(1)}, u32[]{:S(2)}, u32[]{:S(2)}) collective-permute-start(f32[3,32,256]{2,1,0:T(8,128)} %get-tuple-element.9), channel_id=1, source_target_pairs={{0,19},{1,16},{2,17},{3,18},{16,3},{17,0},{18,1},{19,2},{4,23},{5,... | collective-permute-start | bytes 294920 | tf_op jit(solution)/shard_map/ppermute | solution.py:312
  34.4 0.5 %reshape.107 = f32[25,40,2]{2,1,0:T(8,128)S(1)} reshape(f32[2000]{0:T(1024)S(1)} %collective-permute-done.2) | data formatting | bytes 16000 | tf_op jit(solution)/shard_map/reshape | solution.py:32
  34.8 0.5 %reshape.109 = f32[25,40,2]{2,1,0:T(8,128)S(1)} reshape(f32[2000]{0:T(1024)S(1)} %collective-permute-done.3) | data formatting | bytes 16000 | tf_op jit(solution)/shard_map/reshape | solution.py:32
  35.3 1.5 %pad_maximum_fusion.wide_ref = f32[25,40,384]{2,1,0:T(8,128)} fusion(f32[25,40,2]{2,1,0:T(8,128)S(1)} %reshape.109, f32[25,40,2]{2,1,0:T(8,128)S(1)} %reshape.107, f32[25,2,256]{2,1,0:T(2,128)S(1)} %mul.110, f32[25,4,256]{2,1,0:T(4,128)S(1)} %broadcast_in_dim.25, f32[25,2,256]{2,1,0:T(2,128)S(1)} %mul.107, f32[1,32,256]{2,1,0:T(8,128)S(1)} %convert_select_fusion, ...), kind=kLoop, calls=%fused_computation | loop fusion | flops 2688000 | bytes 2577536 | tf_op jit(solution)/shard_map/concatenate | solution.py:320
  36.8 4.0 %shard_map.105 = f32[1,3,8,32,256]{4,3,2,1,0:T(8,128)} custom-call(f32[1,4,8]{2,1,0:T(4,128)} %coef_ref.1, f32[2,40,1]{2,1,0:T(8,128)} %copy.16.row_ref, f32[25,40,384]{2,1,0:T(8,128)} %pad_maximum_fusion.wide_ref), custom_call_target="tpu_custom_call" | custom-call | tf_op jit(solution)/shard_map/pallas_call | solution.py:95
  40.8 0.7 %multiply_bitcast_fusion = f32[1,3,32,256]{3,2,1,0:T(8,128)} fusion(f32[3,32,256]{2,1,0:T(8,128)S(1)} %collective-permute-done.8, f32[3,32,256]{2,1,0:T(8,128)S(1)} %collective-permute-done.7, f32[3,32,256]{2,1,0:T(8,128)S(1)} %collective-permute-done.5, f32[3,32,256]{2,1,0:T(8,128)S(1)} %collective-permute-done.6, f32[32,256]{1,0:T(8,128)S(1)} %convert_bitcast_fusion), kind=kLoop, calls=%fused_computation.11 | loop fusion | flops 98304 | bytes 524288 | tf_op jit(solution)/shard_map/broadcast_in_dim | solution.py:338
  (45 shorter events, 1.1 us)
Async XLA Ops:
  0.6 7.1 %copy-start = (f32[1,3,8,32,256]{4,3,2,1,0:T(8,128)S(1)}, f32[1,3,8,32,256]{4,3,2,1,0:T(8,128)}, u32[]{:S(2)}) copy-start(f32[1,3,8,32,256]{4,3,2,1,0:T(8,128)} %ground_ref.1) | copy-start | bytes 2359300
  0.6 7.1 %copy-start.5 = (s32[1,32,256]{2,1,0:T(8,128)S(1)}, s32[1,32,256]{2,1,0:T(8,128)}, u32[]{:S(2)}) copy-start(s32[1,32,256]{2,1,0:T(8,128)} %sea_ref.1) | copy-start | bytes 98308
  3.7 4.2 %copy-start.2 = (f32[1,3,32,256]{3,2,1,0:T(8,128)S(1)}, f32[1,3,32,256]{3,2,1,0:T(8,128)}, u32[]{:S(2)}) copy-start(f32[1,3,32,256]{3,2,1,0:T(8,128)} %previous_ref.1) | copy-start | bytes 294916
  3.7 20.9 %collective-permute-start.4 = (f32[104,256]{1,0:T(8,128)}, f32[104,256]{1,0:T(8,128)S(1)}, u32[]{:S(2)}, u32[]{:S(2)}) collective-permute-start(f32[104,256]{1,0:T(8,128)} %shard_map.104.refs_0_), channel_id=1, source_target_pairs={{0,8},{4,12},{8,0},{12,4},{1,9},{5,13},{9,1},{13,5},{2,10},{6,14},... | collective-permute-start | bytes 319496 | tf_op jit(solution)/shard_map/ppermute | solution.py:293
  8.0 0.9 %copy-start.1 = (f32[104,256]{1,0:T(8,128)S(1)}, f32[104,256]{1,0:T(8,128)}, u32[]{:S(2)}) copy-start(f32[104,256]{1,0:T(8,128)} %shard_map.104.refs_0_) | copy-start | bytes 319492
  9.0 10.3 %collective-permute-start = (f32[160,256]{1,0:T(8,128)S(1)}, f32[160,256]{1,0:T(8,128)S(1)}, u32[]{:S(2)}, u32[]{:S(2)}) collective-permute-start(f32[160,256]{1,0:T(8,128)S(1)} %get-tuple-element.14), channel_id=1, source_target_pairs={{0,12},{4,0},{8,4},{12,8},{1,13},{5,1},{9,5},{13,9},{2,14},{6,2},{... | collective-permute-start | bytes 491528 | tf_op jit(solution)/shard_map/ppermute | solution.py:293
  10.7 8.6 %collective-permute-start.1 = (f32[160,256]{1,0:T(8,128)S(1)}, f32[160,256]{1,0:T(8,128)S(1)}, u32[]{:S(2)}, u32[]{:S(2)}) collective-permute-start(f32[160,256]{1,0:T(8,128)S(1)} %get-tuple-element.15), channel_id=1, source_target_pairs={{0,4},{4,8},{8,12},{12,0},{1,5},{5,9},{9,13},{13,1},{2,6},{6,10},{... | collective-permute-start | bytes 491528 | tf_op jit(solution)/shard_map/ppermute | solution.py:293
  19.3 0.7 %copy-start.3 = (f32[160,256]{1,0:T(8,128)}, f32[160,256]{1,0:T(8,128)S(1)}, u32[]{:S(2)}) copy-start(f32[160,256]{1,0:T(8,128)S(1)} %collective-permute-done.refs_3_) | copy-start | bytes 491524
  19.4 0.7 %copy-start.4 = (f32[160,256]{1,0:T(8,128)}, f32[160,256]{1,0:T(8,128)S(1)}, u32[]{:S(2)}) copy-start(f32[160,256]{1,0:T(8,128)S(1)} %collective-permute-done.1.refs_1_) | copy-start | bytes 491524
  20.3 13.4 %collective-permute-start.2 = (f32[2000]{0:T(1024)S(1)}, f32[2000]{0:T(1024)S(1)}, u32[]{:S(2)}, u32[]{:S(2)}) collective-permute-start(f32[2000]{0:T(1024)S(1)} %reshape.106), channel_id=1, source_target_pairs={{1,0},{2,1},{3,2},{0,3},{5,4},{6,5},{7,6},{4,7},{9,8},{10,9},{11,1... | collective-permute-start | bytes 24008 | tf_op jit(solution)/shard_map/ppermute | solution.py:31
  23.1 11.7 %collective-permute-start.3 = (f32[2000]{0:T(1024)S(1)}, f32[2000]{0:T(1024)S(1)}, u32[]{:S(2)}, u32[]{:S(2)}) collective-permute-start(f32[2000]{0:T(1024)S(1)} %reshape.108), channel_id=1, source_target_pairs={{0,1},{1,2},{2,3},{3,0},{4,5},{5,6},{6,7},{7,4},{8,9},{9,10},{10,1... | collective-permute-start | bytes 24008 | tf_op jit(solution)/shard_map/ppermute | solution.py:31
  24.6 0.6 %copy-start.6 = (f32[104,256]{1,0:T(8,128)}, f32[104,256]{1,0:T(8,128)S(1)}, u32[]{:S(2)}) copy-start(f32[104,256]{1,0:T(8,128)S(1)} %collective-permute-done.4.refs_2_) | copy-start | bytes 319492
  30.5 10.3 %collective-permute-start.5 = (f32[3,32,256]{2,1,0:T(8,128)}, f32[3,32,256]{2,1,0:T(8,128)S(1)}, u32[]{:S(2)}, u32[]{:S(2)}) collective-permute-start(f32[3,32,256]{2,1,0:T(8,128)} %get-tuple-element.6), channel_id=1, source_target_pairs={{0,16},{1,17},{2,18},{3,19},{16,0},{17,1},{18,2},{19,3},{4,20},{5,... | collective-permute-start | bytes 294920 | tf_op jit(solution)/shard_map/ppermute | solution.py:312
  30.5 10.3 %collective-permute-start.6 = (f32[3,32,256]{2,1,0:T(8,128)}, f32[3,32,256]{2,1,0:T(8,128)S(1)}, u32[]{:S(2)}, u32[]{:S(2)}) collective-permute-start(f32[3,32,256]{2,1,0:T(8,128)} %get-tuple-element.7), channel_id=1, source_target_pairs={{0,17},{1,18},{2,19},{3,16},{16,1},{17,2},{18,3},{19,0},{4,21},{5,... | collective-permute-start | bytes 294920 | tf_op jit(solution)/shard_map/ppermute | solution.py:312
  32.6 8.2 %collective-permute-start.7 = (f32[3,32,256]{2,1,0:T(8,128)}, f32[3,32,256]{2,1,0:T(8,128)S(1)}, u32[]{:S(2)}, u32[]{:S(2)}) collective-permute-start(f32[3,32,256]{2,1,0:T(8,128)} %get-tuple-element.8), channel_id=1, source_target_pairs={{0,18},{1,19},{2,16},{3,17},{16,2},{17,3},{18,0},{19,1},{4,22},{5,... | collective-permute-start | bytes 294920 | tf_op jit(solution)/shard_map/ppermute | solution.py:312
  33.7 7.1 %collective-permute-start.8 = (f32[3,32,256]{2,1,0:T(8,128)}, f32[3,32,256]{2,1,0:T(8,128)S(1)}, u32[]{:S(2)}, u32[]{:S(2)}) collective-permute-start(f32[3,32,256]{2,1,0:T(8,128)} %get-tuple-element.9), channel_id=1, source_target_pairs={{0,19},{1,16},{2,17},{3,18},{16,3},{17,0},{18,1},{19,2},{4,23},{5,... | collective-permute-start | bytes 294920 | tf_op jit(solution)/shard_map/ppermute | solution.py:312

commit v13 on v12

--- a/solution.py
+++ b/solution.py
@@ -32,11 +32,19 @@
     return flat.reshape(part.shape)
 
 
-def stencil_kernel(coef_ref, row_ref, wide_ref, out_ref, mid_ref):
+def stencil_kernel(total_rows, coef_ref, place_ref, wide_ref, out_ref, mid_ref):
     field_count, level_count, row_count, col_count = out_ref.shape[1:]
     wide_rows, wide_cols = wide_ref.shape[1:]
-    turning_wide = jnp.broadcast_to(row_ref[0], (wide_rows, wide_cols))
-    keep_wide = wide_ref[field_count * level_count] * jnp.broadcast_to(row_ref[1], (wide_rows, wide_cols))
+    local = lax.broadcasted_iota(jnp.int32, (wide_rows, wide_cols), 0)
+    row_index = place_ref[1] * row_count + jnp.where(
+        local < wide_rows // 2 + row_count // 2, local, local - wide_rows
+    )
+    latitude = jnp.pi * (
+        -1.0 / 3.0 + 2.0 / 3.0 * (row_index.astype(jnp.float32) + 0.5) / total_rows
+    )
+    turning_wide = coriolis_scale * jnp.sin(latitude)
+    inside = ((row_index >= 0) & (row_index < total_rows)).astype(jnp.float32)
+    keep_wide = wide_ref[field_count * level_count] * inside
 
     def step(read, write, rows, cols):
         turning = turning_wide[:rows, :cols]
@@ -90,20 +98,20 @@
     step(from_mid, to_out, row_count, col_count)
 
 
-def dynamics(coeffs, row_terms, wide, field_count, level_count, row_count, col_count):
+def dynamics(coeffs, place, wide, field_count, level_count, row_count, col_count, total_rows):
     planes, wide_rows, wide_cols = wide.shape
     return pl.pallas_call(
-        stencil_kernel,
+        functools.partial(stencil_kernel, total_rows),
         out_shape=jax.ShapeDtypeStruct((1, field_count, level_count, row_count, col_count), jnp.float32),
         in_specs=[
             pl.BlockSpec(memory_space=pltpu.SMEM),
-            pl.BlockSpec(memory_space=pltpu.VMEM),
+            pl.BlockSpec(memory_space=pltpu.SMEM),
             pl.BlockSpec(memory_space=pltpu.VMEM),
         ],
         out_specs=pl.BlockSpec(memory_space=pltpu.VMEM),
         scratch_shapes=[pltpu.VMEM((planes - 1, wide_rows, wide_cols), jnp.float32)],
         interpret=INTERPRET,
-    )(coeffs, row_terms, wide)
+    )(coeffs, place, wide)
 
 
 def export_kernel(flag_ref, ground_ref, previous_ref, sea_ref, link_ref, out_ref):
@@ -158,8 +166,8 @@
     owner_count = len(out_refs)
     field_count, row_count, col_count = out_refs[0].shape
     base = field_count * row_count
-    my_lat = place_ref[0]
-    my_lon = place_ref[1]
+    my_lat = place_ref[1]
+    my_lon = place_ref[2]
     for source in range(source_count):
         rows_ref[source * base : (source + 1) * base, :] = source_refs[source][:base, :]
     for tile in range(tile_count):
@@ -261,8 +269,8 @@
     links = jnp.stack(
         [link_dest[0, :, 0], link_src_row[0], link_dst_row[0], link_tile[0]]
     ).astype(jnp.float32)
-    flag = lax.axis_index("grp").astype(jnp.int32).reshape(1)
-    payload = exported_block(flag, state, surface, sea_mask, links)
+    place = jnp.stack([lax.axis_index(axis) for axis in ("grp", "lat", "lon")]).astype(jnp.int32)
+    payload = exported_block(place, state, surface, sea_mask, links)
     lat_count = lax.axis_size("lat")
     lon_count = lax.axis_size("lon")
     gain = jnp.where(ocean_side, ocean_gain, air_gain)
@@ -300,7 +308,6 @@
     my_lat = lax.axis_index("lat")
     south = south.reshape(plane_count, width, col_count) * (my_lat > 0).astype(jnp.float32)
     north = north.reshape(plane_count, width, col_count) * (my_lat < lat_count - 1).astype(jnp.float32)
-    place = jnp.stack([lax.axis_index("lat"), lax.axis_index("lon")]).astype(jnp.int32)
     partial = remapped(place, sources, remap_weights, lon_count, field_count, row_count, links.shape[1])
     pieces = []
     for shift in range(lon_count):
@@ -326,15 +333,9 @@
         ],
         2,
     )
-    local = jnp.arange(wide_rows, dtype=jnp.int32)
-    row_index = first_row + jnp.where(local < wide_rows // 2 + row_count // 2, local, local - wide_rows)
-    latitude = jnp.pi * (
-        -1.0 / 3.0 + 2.0 / 3.0 * (row_index.astype(jnp.float32) + 0.5) / total_rows
-    )
-    coriolis = coriolis_scale * jnp.sin(latitude)
-    inside = ((row_index >= 0) & (row_index < total_rows)).astype(jnp.float32)
-    row_terms = jnp.stack([coriolis, inside])[:, :, None]
-    fields = dynamics(coeffs, row_terms, wide, field_count, level_count, row_count, col_count)
+    fields = dynamics(
+        coeffs, place, wide, field_count, level_count, row_count, col_count, total_rows
+    )
     return (fields, imported[None])
 
 

time: 41.7 us -> 44.5 us (1.067)
  other arithmetic: 4.56 us -> 6.13 us
  waiting for transfers between devices: 8.19 us -> 9.22 us
    ppermute x3, waiting for transfers between devices: 8.18 us -> 9.2 us  [body(): lax.ppermute(sent, 'lat', [(i, (i + shift) % lat_count) for i in range(la...]
    concatenate x1, other arithmetic: 0.09 us -> 0.98 us  [body(): sent = jnp.concatenate(parts, 0) if len(parts) > 1 else payload]
    mul x1, other arithmetic: 0.01 us -> 0.8 us  [body(): sea_float * (gain * previous - damping * fields[:, 0])]
    convert_element_type x1, other arithmetic: 1.36 us -> 0.59 us  [body(): links = jnp.stack([link_dest[0, :, 0], link_src_row[0], link_dst_row[0],...]
    select_n x1, other arithmetic: 0.01 us -> 0.76 us  [body(): state_mask = jnp.where(ocean_side, sea_float, jnp.ones_like(sea_float))]
    broadcast_in_dim x1 -> x0, local copies, waits for them, and re-layouts: 0.71 us -> none  [body(): row_terms = jnp.stack([coriolis, inside])[:, :, None]]
    unnamed x15 -> x17, local copies, waits for them, and re-layouts: 1.56 us -> 2.1 us
  transfers between devices with their start and end apart: 9 -> 9, of which waited for: 1 -> 2; matrix products, arithmetic and copies ran while one was open for 13% -> 8% of each run, Pallas kernels for 22% -> 21%
where the time goes in v13:
time: 44.5 us; the launch traced here: 43.9 us
  starting transfers between devices  12.5 us (28%)
  Pallas kernels  11 us (25%)
  waiting for transfers between devices  9.22 us (21%)
  other arithmetic  6.13 us (14%)
  local copies, waits for them, and re-layouts  4.16 us (9%)
  between operations  0.86 us (2%)
    ppermute x3, waiting for transfers between devices, body(): lax.ppermute(sent, 'lat', [(i, (i + shift) % lat_count) for i in range(la...  9.2 us
    ppermute x3, starting transfers between devices, body(): lax.ppermute(sent, 'lat', [(i, (i + shift) % lat_count) for i in range(la...  6.11 us
    pallas_call x1, Pallas kernels, remapped(): pl.pallas_call(functools.partial(remap_kernel, link_count, source_count),...  5.3 us
    pallas_call x1, Pallas kernels, dynamics(): pl.pallas_call(functools.partial(stencil_kernel, total_rows), out_shape=j...  4.05 us
    ppermute x4, starting transfers between devices, body(): pieces.append(lax.ppermute(partial[shift], ('grp', 'lon'), route))  3.84 us
    ppermute x2, starting transfers between devices, shifted(): flat = lax.ppermute(part.reshape(-1), axis, route)  2.55 us
    unnamed x17, local copies, waits for them, and re-layouts  2.1 us
    pallas_call x1, Pallas kernels, exported_block(): pl.pallas_call(export_kernel, out_shape=jax.ShapeDtypeStruct((field_count...  1.64 us
  transfers between devices with their start and end apart: 9, of which 2 were waited for; matrix products, arithmetic and copies ran while one was open for 8% of the time, Pallas kernels for 21%

profile of v13, /device:TPU:0, one launch (start us, length us, event | category | flops | bytes accessed | tf_op | source)
XLA Modules:
  0.0 43.9 jit_solution(10406978330022767320)
XLA Ops:
  0.6 0.8 %convert_bitcast_fusion = f32[32,256]{1,0:T(8,128)S(1)} fusion(s32[1,32,256]{2,1,0:T(8,128)} %sea_ref.1), kind=kLoop, calls=%fused_computation.17 | loop fusion | flops 8192 | bytes 65536 | tf_op jit(solution)/shard_map/mul | solution.py:278
  1.4 0.8 %convert_select_fusion = f32[1,32,256]{2,1,0:T(8,128)S(1)} fusion(s32[1,32,256]{2,1,0:T(8,128)} %sea_ref.1, pred[]{:T(512)S(6)} %eq.3), kind=kLoop, calls=%fused_computation.16 | loop fusion | flops 16384 | bytes 65537 | tf_op jit(solution)/shard_map/jit(_where)/select_n | solution.py:280
  2.2 1.2 %copy.16 = f32[1,3,8,32,256]{4,3,1,2,0:T(8,128)S(1)} copy(f32[1,3,8,32,256]{4,3,2,1,0:T(8,128)} %ground_ref.1) | data formatting | bytes 1572864 | tf_op args[0]
  3.9 0.6 %pad_add_fusion.flag_ref.place_ref = s32[3]{0:T(128)} fusion(s32[1]{0:T(128)} %bitcast.2, s32[1]{0:T(128)} %bitcast.1, s32[1]{0:T(128)} %bitcast), kind=kLoop, calls=%fused_computation.19 | loop fusion | flops 6 | bytes 24 | tf_op jit(solution)/shard_map/stack | solution.py:272
  4.5 0.6 %add_convert_fusion.link_ref = f32[4,128]{1,0:T(4,128)} fusion(s32[1,128]{1,0:T(1,128)S(1)} %copy-done.4, s32[1,128]{1,0:T(1,128)S(1)} %copy-done.5, s32[1,128]{1,0:T(1,128)S(1)} %copy-done.6, s32[1,128]{1,0:T(1,128)S(1)} %bitcast.23), kind=kLoop, calls=%fused_computation.18 | loop fusion | flops 2048 | bytes 4096 | tf_op jit(solution)/shard_map/convert_element_type | solution.py:271
  5.1 1.6 %shard_map.104.refs_0_ = f32[104,256]{1,0:T(8,128)} custom-call(s32[3]{0:T(128)} %pad_add_fusion.flag_ref.place_ref, f32[1,3,8,32,256]{4,3,2,1,0:T(8,128)} %ground_ref.1, f32[1,3,32,256]{3,2,1,0:T(8,128)} %previous_ref.1, s32[1,32,256]{2,1,0:T(8,128)} %sea_ref.1, f32[4,128]{1,0:T(4,128)} %add_convert_fusion.link_ref), custom_call_target="tpu_custom_call" | custom-call | tf_op jit(solution)/shard_map/pallas_call | solution.py:144
  6.7 1.0 %fusion = (f32[160,256]{1,0:T(8,128)S(1)}, f32[160,256]{1,0:T(8,128)S(1)}) fusion(f32[104,256]{1,0:T(8,128)} %shard_map.104.refs_0_, f32[50,256]{1,0:T(8,128)S(1)} %reshape.44, f32[160]{0:T(256)S(1)} %pad.18.clone, f32[50,256]{1,0:T(8,128)S(1)} %reshape.45), kind=kLoop, calls=%fused_computation.6 | loop fusion | flops 163840 | bytes 537216 | tf_op jit(solution)/shard_map/concatenate | solution.py:300
  7.7 5.1 %collective-permute-start = (f32[160,256]{1,0:T(8,128)S(1)}, f32[160,256]{1,0:T(8,128)S(1)}, u32[]{:S(2)}, u32[]{:S(2)}) collective-permute-start(f32[160,256]{1,0:T(8,128)S(1)} %get-tuple-element.14), channel_id=1, source_target_pairs={{0,12},{4,0},{8,4},{12,8},{1,13},{5,1},{9,5},{13,9},{2,14},{6,2},{... | collective-permute-start | bytes 491528 | tf_op jit(solution)/shard_map/ppermute | solution.py:301
  12.8 1.0 %collective-permute-start.1 = (f32[160,256]{1,0:T(8,128)S(1)}, f32[160,256]{1,0:T(8,128)S(1)}, u32[]{:S(2)}, u32[]{:S(2)}) collective-permute-start(f32[160,256]{1,0:T(8,128)S(1)} %get-tuple-element.15), channel_id=1, source_target_pairs={{0,4},{4,8},{8,12},{12,0},{1,5},{5,9},{9,13},{13,1},{2,6},{6,10},{... | collective-permute-start | bytes 491528 | tf_op jit(solution)/shard_map/ppermute | solution.py:301
  13.9 3.6 %collective-permute-done.refs_3_ = f32[160,256]{1,0:T(8,128)S(1)} collective-permute-done((f32[160,256]{1,0:T(8,128)S(1)}, f32[160,256]{1,0:T(8,128)S(1)}, u32[]{:S(2)}, u32[]{:S(2)}) %collective-permute-start) | collective-permute-done | bytes 163872 | tf_op jit(solution)/shard_map/ppermute | solution.py:301
  17.5 5.6 %collective-permute-done.1.refs_1_ = f32[160,256]{1,0:T(8,128)S(1)} collective-permute-done((f32[160,256]{1,0:T(8,128)S(1)}, f32[160,256]{1,0:T(8,128)S(1)}, u32[]{:S(2)}, u32[]{:S(2)}) %collective-permute-start.1) | collective-permute-done | bytes 163872 | tf_op jit(solution)/shard_map/ppermute | solution.py:301
  23.8 0.3 reshape.46
  24.0 2.5 %collective-permute-start.2 = (f32[2000]{0:T(1024)S(1)}, f32[2000]{0:T(1024)S(1)}, u32[]{:S(2)}, u32[]{:S(2)}) collective-permute-start(f32[2000]{0:T(1024)S(1)} %reshape.46), channel_id=1, source_target_pairs={{1,0},{2,1},{3,2},{0,3},{5,4},{6,5},{7,6},{4,7},{9,8},{10,9},{11,1... | collective-permute-start | bytes 24008 | tf_op jit(solution)/shard_map/ppermute | solution.py:31
  26.5 0.3 reshape.48
  26.9 0.6 %copy-done.3 = f32[104,256]{1,0:T(8,128)} copy-done((f32[104,256]{1,0:T(8,128)}, f32[104,256]{1,0:T(8,128)S(1)}, u32[]{:S(2)}) %copy-start.3) | copy-done | bytes 106520
  27.6 5.3 %shard_map.106 = (f32[3,32,256]{2,1,0:T(8,128)}, f32[3,32,256]{2,1,0:T(8,128)}, f32[3,32,256]{2,1,0:T(8,128)}, f32[3,32,256]{2,1,0:T(8,128)}) custom-call(s32[3]{0:T(128)} %pad_add_fusion.flag_ref.place_ref, f32[104,256]{1,0:T(8,128)} %shard_map.104.refs_0_, f32[160,256]{1,0:T(8,128)} %copy-done.2, f32[104,256]{1,0:T(8,128)} %copy-done.3, ...), custom_call_target="tpu_custom_call" | custom-call | tf_op jit(solution)/shard_map/pallas_call | solution.py:215
  32.9 2.1 %collective-permute-start.6 = (f32[3,32,256]{2,1,0:T(8,128)}, f32[3,32,256]{2,1,0:T(8,128)S(1)}, u32[]{:S(2)}, u32[]{:S(2)}) collective-permute-start(f32[3,32,256]{2,1,0:T(8,128)} %get-tuple-element.7), channel_id=1, source_target_pairs={{0,17},{1,18},{2,19},{3,16},{16,1},{17,2},{18,3},{19,0},{4,21},{5,... | collective-permute-start | bytes 294920 | tf_op jit(solution)/shard_map/ppermute | solution.py:319
  34.9 1.1 %collective-permute-start.7 = (f32[3,32,256]{2,1,0:T(8,128)}, f32[3,32,256]{2,1,0:T(8,128)S(1)}, u32[]{:S(2)}, u32[]{:S(2)}) collective-permute-start(f32[3,32,256]{2,1,0:T(8,128)} %get-tuple-element.8), channel_id=1, source_target_pairs={{0,18},{1,19},{2,16},{3,17},{16,2},{17,3},{18,0},{19,1},{4,22},{5,... | collective-permute-start | bytes 294920 | tf_op jit(solution)/shard_map/ppermute | solution.py:319
  36.1 0.6 %collective-permute-start.8 = (f32[3,32,256]{2,1,0:T(8,128)}, f32[3,32,256]{2,1,0:T(8,128)S(1)}, u32[]{:S(2)}, u32[]{:S(2)}) collective-permute-start(f32[3,32,256]{2,1,0:T(8,128)} %get-tuple-element.9), channel_id=1, source_target_pairs={{0,19},{1,16},{2,17},{3,18},{16,3},{17,0},{18,1},{19,2},{4,23},{5,... | collective-permute-start | bytes 294920 | tf_op jit(solution)/shard_map/ppermute | solution.py:319
  36.7 0.5 %reshape.47 = f32[25,40,2]{2,1,0:T(8,128)S(1)} reshape(f32[2000]{0:T(1024)S(1)} %collective-permute-done.2) | data formatting | bytes 16000 | tf_op jit(solution)/shard_map/reshape | solution.py:32
  37.2 0.5 %reshape.49 = f32[25,40,2]{2,1,0:T(8,128)S(1)} reshape(f32[2000]{0:T(1024)S(1)} %collective-permute-done.3) | data formatting | bytes 16000 | tf_op jit(solution)/shard_map/reshape | solution.py:32
  37.7 1.5 %pad_maximum_fusion.wide_ref = f32[25,40,384]{2,1,0:T(8,128)} fusion(f32[25,40,2]{2,1,0:T(8,128)S(1)} %reshape.49, f32[25,40,2]{2,1,0:T(8,128)S(1)} %reshape.47, f32[25,2,256]{2,1,0:T(2,128)S(1)} %mul.73, f32[25,4,256]{2,1,0:T(4,128)S(1)} %broadcast_in_dim.21, f32[25,2,256]{2,1,0:T(2,128)S(1)} %mul.70, f32[1,32,256]{2,1,0:T(8,128)S(1)} %convert_select_fusion, ...), kind=kLoop, calls=%fused_computation | loop fusion | flops 2688000 | bytes 2577536 | tf_op jit(solution)/shard_map/concatenate | solution.py:327
  39.1 4.0 %shard_map.105 = f32[1,3,8,32,256]{4,3,2,1,0:T(8,128)} custom-call(f32[1,4,8]{2,1,0:T(4,128)} %coef_ref.1, s32[3]{0:T(128)} %pad_add_fusion.flag_ref.place_ref, f32[25,40,384]{2,1,0:T(8,128)} %pad_maximum_fusion.wide_ref), custom_call_target="tpu_custom_call" | custom-call | tf_op jit(solution)/shard_map/pallas_call | solution.py:103
  43.2 0.7 %multiply_bitcast_fusion = f32[1,3,32,256]{3,2,1,0:T(8,128)} fusion(f32[3,32,256]{2,1,0:T(8,128)S(1)} %collective-permute-done.8, f32[3,32,256]{2,1,0:T(8,128)S(1)} %collective-permute-done.7, f32[3,32,256]{2,1,0:T(8,128)S(1)} %collective-permute-done.5, f32[3,32,256]{2,1,0:T(8,128)S(1)} %collective-permute-done.6, f32[32,256]{1,0:T(8,128)S(1)} %convert_bitcast_fusion), kind=kLoop, calls=%fused_computation.11 | loop fusion | flops 98304 | bytes 524288 | tf_op jit(solution)/shard_map/broadcast_in_dim | solution.py:339
  (43 shorter events, 1.3 us)
Async XLA Ops:
  0.6 2.8 %copy-start = (f32[1,3,32,256]{3,2,1,0:T(8,128)S(1)}, f32[1,3,32,256]{3,2,1,0:T(8,128)}, u32[]{:S(2)}) copy-start(f32[1,3,32,256]{3,2,1,0:T(8,128)} %previous_ref.1) | copy-start | bytes 294916
  3.6 0.9 %copy-start.4 = (s32[1,128]{1,0:T(1,128)S(1)}, s32[1,128]{1,0:T(1,128)}, u32[]{:S(2)}) copy-start(s32[1,128]{1,0:T(1,128)} %param.17) | copy-start | bytes 1540
  3.6 0.9 %copy-start.5 = (s32[1,128]{1,0:T(1,128)S(1)}, s32[1,128]{1,0:T(1,128)}, u32[]{:S(2)}) copy-start(s32[1,128]{1,0:T(1,128)} %param.16) | copy-start | bytes 1540
  3.6 0.9 %copy-start.6 = (s32[1,128]{1,0:T(1,128)S(1)}, s32[1,128]{1,0:T(1,128)}, u32[]{:S(2)}) copy-start(s32[1,128]{1,0:T(1,128)} %param.15) | copy-start | bytes 1540
  3.6 0.9 %copy-start.7 = (s32[1,128,1]{1,2,0:T(1,128)S(1)}, s32[1,128,1]{1,2,0:T(1,128)}, u32[]{:S(2)}) copy-start(s32[1,128,1]{1,2,0:T(1,128)} %param.14) | copy-start | bytes 1540
  7.7 9.8 %collective-permute-start = (f32[160,256]{1,0:T(8,128)S(1)}, f32[160,256]{1,0:T(8,128)S(1)}, u32[]{:S(2)}, u32[]{:S(2)}) collective-permute-start(f32[160,256]{1,0:T(8,128)S(1)} %get-tuple-element.14), channel_id=1, source_target_pairs={{0,12},{4,0},{8,4},{12,8},{1,13},{5,1},{9,5},{13,9},{2,14},{6,2},{... | collective-permute-start | bytes 491528 | tf_op jit(solution)/shard_map/ppermute | solution.py:301
  12.8 14.1 %collective-permute-start.4 = (f32[104,256]{1,0:T(8,128)}, f32[104,256]{1,0:T(8,128)S(1)}, u32[]{:S(2)}, u32[]{:S(2)}) collective-permute-start(f32[104,256]{1,0:T(8,128)} %shard_map.104.refs_0_), channel_id=1, source_target_pairs={{0,8},{4,12},{8,0},{12,4},{1,9},{5,13},{9,1},{13,5},{2,10},{6,14},... | collective-permute-start | bytes 319496 | tf_op jit(solution)/shard_map/ppermute | solution.py:301
  12.8 10.3 %collective-permute-start.1 = (f32[160,256]{1,0:T(8,128)S(1)}, f32[160,256]{1,0:T(8,128)S(1)}, u32[]{:S(2)}, u32[]{:S(2)}) collective-permute-start(f32[160,256]{1,0:T(8,128)S(1)} %get-tuple-element.15), channel_id=1, source_target_pairs={{0,4},{4,8},{8,12},{12,0},{1,5},{5,9},{9,13},{13,1},{2,6},{6,10},{... | collective-permute-start | bytes 491528 | tf_op jit(solution)/shard_map/ppermute | solution.py:301
  17.5 6.0 %copy-start.1 = (f32[160,256]{1,0:T(8,128)}, f32[160,256]{1,0:T(8,128)S(1)}, u32[]{:S(2)}) copy-start(f32[160,256]{1,0:T(8,128)S(1)} %collective-permute-done.refs_3_) | copy-start | bytes 491524
  23.1 0.7 %copy-start.2 = (f32[160,256]{1,0:T(8,128)}, f32[160,256]{1,0:T(8,128)S(1)}, u32[]{:S(2)}) copy-start(f32[160,256]{1,0:T(8,128)S(1)} %collective-permute-done.1.refs_1_) | copy-start | bytes 491524
  24.0 12.0 %collective-permute-start.2 = (f32[2000]{0:T(1024)S(1)}, f32[2000]{0:T(1024)S(1)}, u32[]{:S(2)}, u32[]{:S(2)}) collective-permute-start(f32[2000]{0:T(1024)S(1)} %reshape.46), channel_id=1, source_target_pairs={{1,0},{2,1},{3,2},{0,3},{5,4},{6,5},{7,6},{4,7},{9,8},{10,9},{11,1... | collective-permute-start | bytes 24008 | tf_op jit(solution)/shard_map/ppermute | solution.py:31
  26.8 10.4 %collective-permute-start.3 = (f32[2000]{0:T(1024)S(1)}, f32[2000]{0:T(1024)S(1)}, u32[]{:S(2)}, u32[]{:S(2)}) collective-permute-start(f32[2000]{0:T(1024)S(1)} %reshape.48), channel_id=1, source_target_pairs={{0,1},{1,2},{2,3},{3,0},{4,5},{5,6},{6,7},{7,4},{8,9},{9,10},{10,1... | collective-permute-start | bytes 24008 | tf_op jit(solution)/shard_map/ppermute | solution.py:31
  26.9 0.6 %copy-start.3 = (f32[104,256]{1,0:T(8,128)}, f32[104,256]{1,0:T(8,128)S(1)}, u32[]{:S(2)}) copy-start(f32[104,256]{1,0:T(8,128)S(1)} %collective-permute-done.4.refs_2_) | copy-start | bytes 319492
  32.9 10.3 %collective-permute-start.5 = (f32[3,32,256]{2,1,0:T(8,128)}, f32[3,32,256]{2,1,0:T(8,128)S(1)}, u32[]{:S(2)}, u32[]{:S(2)}) collective-permute-start(f32[3,32,256]{2,1,0:T(8,128)} %get-tuple-element.6), channel_id=1, source_target_pairs={{0,16},{1,17},{2,18},{3,19},{16,0},{17,1},{18,2},{19,3},{4,20},{5,... | collective-permute-start | bytes 294920 | tf_op jit(solution)/shard_map/ppermute | solution.py:319
  32.9 10.3 %collective-permute-start.6 = (f32[3,32,256]{2,1,0:T(8,128)}, f32[3,32,256]{2,1,0:T(8,128)S(1)}, u32[]{:S(2)}, u32[]{:S(2)}) collective-permute-start(f32[3,32,256]{2,1,0:T(8,128)} %get-tuple-element.7), channel_id=1, source_target_pairs={{0,17},{1,18},{2,19},{3,16},{16,1},{17,2},{18,3},{19,0},{4,21},{5,... | collective-permute-start | bytes 294920 | tf_op jit(solution)/shard_map/ppermute | solution.py:319
  34.9 8.2 %collective-permute-start.7 = (f32[3,32,256]{2,1,0:T(8,128)}, f32[3,32,256]{2,1,0:T(8,128)S(1)}, u32[]{:S(2)}, u32[]{:S(2)}) collective-permute-start(f32[3,32,256]{2,1,0:T(8,128)} %get-tuple-element.8), channel_id=1, source_target_pairs={{0,18},{1,19},{2,16},{3,17},{16,2},{17,3},{18,0},{19,1},{4,22},{5,... | collective-permute-start | bytes 294920 | tf_op jit(solution)/shard_map/ppermute | solution.py:319
  36.1 7.1 %collective-permute-start.8 = (f32[3,32,256]{2,1,0:T(8,128)}, f32[3,32,256]{2,1,0:T(8,128)S(1)}, u32[]{:S(2)}, u32[]{:S(2)}) collective-permute-start(f32[3,32,256]{2,1,0:T(8,128)} %get-tuple-element.9), channel_id=1, source_target_pairs={{0,19},{1,16},{2,17},{3,18},{16,3},{17,0},{18,1},{19,2},{4,23},{5,... | collective-permute-start | bytes 294920 | tf_op jit(solution)/shard_map/ppermute | solution.py:319

commit v14 on v13

--- a/solution.py
+++ b/solution.py
@@ -114,8 +114,11 @@
     )(coeffs, place, wide)
 
 
-def export_kernel(flag_ref, ground_ref, previous_ref, sea_ref, link_ref, out_ref):
+def export_kernel(
+    flag_ref, ground_ref, head_ref, tail_ref, previous_ref, sea_ref, link_ref, mid_ref, up_ref, down_ref
+):
     field_count, row_count, col_count = previous_ref.shape[1:]
+    level_count = head_ref.shape[2]
     link_fields, link_count = link_ref.shape
     ground = ground_ref[0, :, 0]
     previous = previous_ref[0]
@@ -129,32 +132,70 @@
         drag_coeff * wind_speed * slip_north,
         heat_coeff * wind_speed * (previous[2] - ground[2]),
     ]
-    for c in range(field_count):
-        out_ref[c * row_count : (c + 1) * row_count, :] = (
-            ground[c] * ocean + bulk_flux[c] * (1.0 - ocean)
-        ) * sea_float
     base = field_count * row_count
-    out_ref[base : base + 8, :] = jnp.zeros((8, col_count), jnp.float32)
-    out_ref[base : base + link_fields, :link_count] = link_ref[...]
-
-
-def exported_block(flag, state, surface, sea_mask, links):
+    for out_ref in (mid_ref, up_ref, down_ref):
+        for c in range(field_count):
+            out_ref[c * row_count : (c + 1) * row_count, :] = (
+                ground[c] * ocean + bulk_flux[c] * (1.0 - ocean)
+            ) * sea_float
+        out_ref[base : base + 8, :] = jnp.zeros((8, col_count), jnp.float32)
+        out_ref[base : base + link_fields, :link_count] = link_ref[...]
+    gain = air_gain + (ocean_gain - air_gain) * ocean
+    damping = air_gain * (1.0 - ocean)
+    width = SUBSTEPS
+    per_tile = 8 // width
+    row_ids = lax.broadcasted_iota(jnp.int32, (8, col_count), 0)
+    for edge_ref, out_ref, first in ((tail_ref, up_ref, 8 - width), (head_ref, down_ref, 0)):
+        edge_prev = previous_ref[0, :, pl.ds(row_count - 8 if first else 0, 8), :]
+        edge_sea = sea_ref[0, pl.ds(row_count - 8 if first else 0, 8), :].astype(jnp.float32)
+        planes = []
+        for c in range(field_count):
+            for level in range(level_count):
+                value = edge_ref[0, c, level]
+                if level == 0:
+                    value = value + edge_sea * (gain * edge_prev[c] - damping * value)
+                planes.append(value)
+        planes.append(edge_sea * ocean + (1.0 - ocean))
+        tile_count = -(-len(planes) // per_tile)
+        for tile in range(tile_count):
+            packed = jnp.zeros((8, col_count), jnp.float32)
+            for slot in range(per_tile):
+                plane = tile * per_tile + slot
+                if plane >= len(planes):
+                    break
+                offset = slot * width
+                moved = pltpu.roll(planes[plane], (offset - first) % 8, 0)
+                packed = jnp.where((row_ids >= offset) & (row_ids < offset + width), moved, packed)
+            out_ref[base + 8 * (tile + 1) : base + 8 * (tile + 2), :] = packed
+
+
+def exported_block(flag, state, surface, sea_mask, links, edge_rows):
     field_count, row_count, col_count = surface.shape[1:]
+    level_count = state.shape[2]
     vmem = pl.BlockSpec(memory_space=pltpu.VMEM)
+    base = field_count * row_count + 8
+    wide_rows = base + -(-edge_rows // 8) * 8
+    last = row_count // 8 - 1
     return pl.pallas_call(
         export_kernel,
-        out_shape=jax.ShapeDtypeStruct((field_count * row_count + 8, col_count), jnp.float32),
+        out_shape=[
+            jax.ShapeDtypeStruct((base, col_count), jnp.float32),
+            jax.ShapeDtypeStruct((wide_rows, col_count), jnp.float32),
+            jax.ShapeDtypeStruct((wide_rows, col_count), jnp.float32),
+        ],
         in_specs=[
             pl.BlockSpec(memory_space=pltpu.SMEM),
             pl.BlockSpec((1, field_count, 1, row_count, col_count), lambda i: (0, 0, 0, 0, 0)),
+            pl.BlockSpec((1, field_count, level_count, 8, col_count), lambda i: (0, 0, 0, 0, 0)),
+            pl.BlockSpec((1, field_count, level_count, 8, col_count), lambda i: (0, 0, 0, last, 0)),
             vmem,
             vmem,
             vmem,
         ],
-        out_specs=vmem,
+        out_specs=[vmem, vmem, vmem],
         grid=(1,),
         interpret=INTERPRET,
-    )(flag, state, surface, sea_mask, links)
+    )(flag, state, state, state, surface, sea_mask, links)
 
 
 def remap_kernel(link_count, source_count, place_ref, *refs):
@@ -270,9 +311,13 @@
         [link_dest[0, :, 0], link_src_row[0], link_dst_row[0], link_tile[0]]
     ).astype(jnp.float32)
     place = jnp.stack([lax.axis_index(axis) for axis in ("grp", "lat", "lon")]).astype(jnp.int32)
-    payload = exported_block(place, state, surface, sea_mask, links)
     lat_count = lax.axis_size("lat")
     lon_count = lax.axis_size("lon")
+    plane_count = field_count * level_count + 1
+    width = SUBSTEPS
+    edge_rows = plane_count * width
+    payload, upward, downward = exported_block(place, state, surface, sea_mask, links, edge_rows)
+    base = payload.shape[0]
     gain = jnp.where(ocean_side, ocean_gain, air_gain)
     damping = jnp.where(ocean_side, 0.0, air_gain)
     ground = fields[:, 0] + sea_float * (gain * previous - damping * fields[:, 0])
@@ -281,30 +326,15 @@
     planes = jnp.concatenate(
         [fields.reshape(field_count * level_count, row_count, col_count), state_mask[None]], 0
     )
-    plane_count = planes.shape[0]
-    width = SUBSTEPS
-    edge_rows = plane_count * width
-    edge_pad = -(-edge_rows // 8) * 8 - edge_rows
-    head = planes[:, :width, :].reshape(edge_rows, col_count)
-    tail = planes[:, row_count - width :, :].reshape(edge_rows, col_count)
-    gap_rows = jnp.zeros((edge_pad, col_count), jnp.float32)
-    base = payload.shape[0]
     sources = [payload]
-    south = north = None
     for shift in range(1, lat_count):
-        parts = [payload]
-        if shift == 1:
-            parts += [tail, gap_rows]
-        if shift == lat_count - 1:
-            parts += [head, gap_rows]
-        sent = jnp.concatenate(parts, 0) if len(parts) > 1 else payload
+        sent = upward if shift == 1 else downward if shift == lat_count - 1 else payload
         got = lax.ppermute(sent, "lat", [(i, (i + shift) % lat_count) for i in range(lat_count)])
         sources.append(got)
         if shift == 1:
             south = got[base : base + edge_rows]
         if shift == lat_count - 1:
-            start = base + (edge_rows + edge_pad if shift == 1 else 0)
-            north = got[start : start + edge_rows]
+            north = got[base : base + edge_rows]
     my_lat = lax.axis_index("lat")
     south = south.reshape(plane_count, width, col_count) * (my_lat > 0).astype(jnp.float32)
     north = north.reshape(plane_count, width, col_count) * (my_lat < lat_count - 1).astype(jnp.float32)

time: 44.5 us -> 40.9 us (0.919)
  other arithmetic: 6.13 us -> 4.26 us
  local copies, waits for them, and re-layouts: 4.16 us -> 2.88 us
    unnamed x17 -> x13, local copies, waits for them, and re-layouts: 2.1 us -> 0.98 us
    concatenate x1 -> x0, other arithmetic: 0.98 us -> none  [body(): sent = jnp.concatenate(parts, 0) if len(parts) > 1 else payload]
    mul x1, other arithmetic: 0.8 us -> 0.01 us  [body(): sea_float * (gain * previous - damping * fields[:, 0])]
    select_n x1, other arithmetic: 0.76 us -> 0.01 us  [body(): state_mask = jnp.where(ocean_side, sea_float, jnp.ones_like(sea_float))]
    convert_element_type x1, other arithmetic: 0.59 us -> 1.29 us  [body(): links = jnp.stack([link_dest[0, :, 0], link_src_row[0], link_dst_row[0],...]
  transfers between devices with their start and end apart: 9 -> 9, of which waited for: 2 -> 2; matrix products, arithmetic and copies ran while one was open for 8% -> 9% of each run, Pallas kernels for 21% -> 23%
where the time goes in v14:
time: 40.9 us; the launch traced here: 40.7 us
  starting transfers between devices  12.4 us (30%)
  Pallas kernels  11.3 us (28%)
  waiting for transfers between devices  9 us (22%)
  other arithmetic  4.26 us (10%)
  local copies, waits for them, and re-layouts  2.88 us (7%)
  between operations  0.83 us (2%)
    ppermute x3, waiting for transfers between devices, body(): lax.ppermute(sent, 'lat', [(i, (i + shift) % lat_count) for i in range(la...  8.98 us
    ppermute x3, starting transfers between devices, body(): lax.ppermute(sent, 'lat', [(i, (i + shift) % lat_count) for i in range(la...  6.06 us
    pallas_call x1, Pallas kernels, remapped(): pl.pallas_call(functools.partial(remap_kernel, link_count, source_count),...  5.29 us
    pallas_call x1, Pallas kernels, dynamics(): pl.pallas_call(functools.partial(stencil_kernel, total_rows), out_shape=j...  4.05 us
    ppermute x4, starting transfers between devices, body(): pieces.append(lax.ppermute(partial[shift], ('grp', 'lon'), route))  3.83 us
    ppermute x2, starting transfers between devices, shifted(): flat = lax.ppermute(part.reshape(-1), axis, route)  2.54 us
    pallas_call x1, Pallas kernels, exported_block(): pl.pallas_call(export_kernel, out_shape=[jax.ShapeDtypeStruct((base, col_...  1.93 us
    concatenate x1, other arithmetic, body(): jnp.concatenate([stacked, shifted(stacked[:, :, :width], 'lon', True, Fal...  1.46 us
  transfers between devices with their start and end apart: 9, of which 2 were waited for; matrix products, arithmetic and copies ran while one was open for 9% of the time, Pallas kernels for 23%

profile of v14, /device:TPU:0, one launch (start us, length us, event | category | flops | bytes accessed | tf_op | source)
XLA Modules:
  0.0 40.7 jit_solution(8041732316851045462)
XLA Ops:
  0.7 0.6 %pad_add_fusion.flag_ref.place_ref = s32[3]{0:T(128)} fusion(s32[1]{0:T(128)} %bitcast.2, s32[1]{0:T(128)} %bitcast.1, s32[1]{0:T(128)} %bitcast), kind=kLoop, calls=%fused_computation.13 | loop fusion | flops 6 | bytes 24 | tf_op jit(solution)/shard_map/stack | solution.py:313
  1.3 1.3 %add_convert_fusion.link_ref = f32[4,128]{1,0:T(4,128)} fusion(s32[1,128]{1,0:T(1,128)} %param.17, s32[1,128]{1,0:T(1,128)} %param.16, s32[1,128]{1,0:T(1,128)} %param.15, s32[1,128]{1,0:T(1,128)} %bitcast.22), kind=kLoop, calls=%fused_computation.12 | loop fusion | flops 2048 | bytes 4096 | tf_op jit(solution)/shard_map/convert_element_type | solution.py:312
  2.5 1.9 %shard_map.104 = (f32[104,256]{1,0:T(8,128)}, f32[160,256]{1,0:T(8,128)}, f32[160,256]{1,0:T(8,128)}) custom-call(s32[3]{0:T(128)} %pad_add_fusion.flag_ref.place_ref, f32[1,3,8,32,256]{4,3,2,1,0:T(8,128)} %tail_ref.1, f32[1,3,8,32,256]{4,3,2,1,0:T(8,128)} %tail_ref.1, f32[1,3,8,32,256]{4,3,2,1,0:T(8,128)} %tail_ref.1, f32[1,3,32,256]{3,2,1,0:T(8,128)} %previous_ref.1, ...), custom_call_target="tpu_custom_call" | custom-call | tf_op jit(solution)/shard_map/pallas_call | solution.py:179
  4.5 4.0 %collective-permute-start.4 = (f32[104,256]{1,0:T(8,128)}, f32[104,256]{1,0:T(8,128)S(1)}, u32[]{:S(2)}, u32[]{:S(2)}) collective-permute-start(f32[104,256]{1,0:T(8,128)} %get-tuple-element.11.refs_0_), channel_id=1, source_target_pairs={{0,8},{4,12},{8,0},{12,4},{1,9},{5,13},{9,1},{13,5},{2,10},{6,14},... | collective-permute-start | bytes 319496 | tf_op jit(solution)/shard_map/ppermute | solution.py:332
  8.5 1.3 %collective-permute-start = (f32[160,256]{1,0:T(8,128)}, f32[160,256]{1,0:T(8,128)S(1)}, u32[]{:S(2)}, u32[]{:S(2)}) collective-permute-start(f32[160,256]{1,0:T(8,128)} %get-tuple-element.9), channel_id=1, source_target_pairs={{0,12},{4,0},{8,4},{12,8},{1,13},{5,1},{9,5},{13,9},{2,14},{6,2},{... | collective-permute-start | bytes 491528 | tf_op jit(solution)/shard_map/ppermute | solution.py:332
  9.9 0.7 %collective-permute-start.1 = (f32[160,256]{1,0:T(8,128)}, f32[160,256]{1,0:T(8,128)S(1)}, u32[]{:S(2)}, u32[]{:S(2)}) collective-permute-start(f32[160,256]{1,0:T(8,128)} %get-tuple-element.10), channel_id=1, source_target_pairs={{0,4},{4,8},{8,12},{12,0},{1,5},{5,9},{9,13},{13,1},{2,6},{6,10},{... | collective-permute-start | bytes 491528 | tf_op jit(solution)/shard_map/ppermute | solution.py:332
  10.9 4.9 %collective-permute-done.refs_3_ = f32[160,256]{1,0:T(8,128)S(1)} collective-permute-done((f32[160,256]{1,0:T(8,128)}, f32[160,256]{1,0:T(8,128)S(1)}, u32[]{:S(2)}, u32[]{:S(2)}) %collective-permute-start) | collective-permute-done | bytes 163872 | tf_op jit(solution)/shard_map/ppermute | solution.py:332
  15.8 4.1 %collective-permute-done.1.refs_1_ = f32[160,256]{1,0:T(8,128)S(1)} collective-permute-done((f32[160,256]{1,0:T(8,128)}, f32[160,256]{1,0:T(8,128)S(1)}, u32[]{:S(2)}, u32[]{:S(2)}) %collective-permute-start.1) | collective-permute-done | bytes 163872 | tf_op jit(solution)/shard_map/ppermute | solution.py:332
  20.0 0.1 pad_maximum_fusion.1
  20.1 0.2 fusion.2
  20.4 0.3 copy-done.3
  20.6 0.3 reshape.38
  20.9 2.5 %collective-permute-start.2 = (f32[2000]{0:T(1024)S(1)}, f32[2000]{0:T(1024)S(1)}, u32[]{:S(2)}, u32[]{:S(2)}) collective-permute-start(f32[2000]{0:T(1024)S(1)} %reshape.38), channel_id=1, source_target_pairs={{1,0},{2,1},{3,2},{0,3},{5,4},{6,5},{7,6},{4,7},{9,8},{10,9},{11,1... | collective-permute-start | bytes 24008 | tf_op jit(solution)/shard_map/ppermute | solution.py:31
  23.4 0.3 reshape.40
  23.8 0.6 %copy-done.5 = f32[104,256]{1,0:T(8,128)} copy-done((f32[104,256]{1,0:T(8,128)}, f32[104,256]{1,0:T(8,128)S(1)}, u32[]{:S(2)}) %copy-start.5) | copy-done | bytes 106520
  24.4 5.3 %shard_map.106 = (f32[3,32,256]{2,1,0:T(8,128)}, f32[3,32,256]{2,1,0:T(8,128)}, f32[3,32,256]{2,1,0:T(8,128)}, f32[3,32,256]{2,1,0:T(8,128)}) custom-call(s32[3]{0:T(128)} %pad_add_fusion.flag_ref.place_ref, f32[104,256]{1,0:T(8,128)} %get-tuple-element.11.refs_0_, f32[160,256]{1,0:T(8,128)} %copy-done.3, f32[104,256]{1,0:T(8,128)} %copy-done.5, ...), custom_call_target="tpu_custom_call" | custom-call | tf_op jit(solution)/shard_map/pallas_call | solution.py:256
  29.7 2.1 %collective-permute-start.6 = (f32[3,32,256]{2,1,0:T(8,128)}, f32[3,32,256]{2,1,0:T(8,128)S(1)}, u32[]{:S(2)}, u32[]{:S(2)}) collective-permute-start(f32[3,32,256]{2,1,0:T(8,128)} %get-tuple-element.13), channel_id=1, source_target_pairs={{0,17},{1,18},{2,19},{3,16},{16,1},{17,2},{18,3},{19,0},{4,21},{5,... | collective-permute-start | bytes 294920 | tf_op jit(solution)/shard_map/ppermute | solution.py:349
  31.8 1.1 %collective-permute-start.7 = (f32[3,32,256]{2,1,0:T(8,128)}, f32[3,32,256]{2,1,0:T(8,128)S(1)}, u32[]{:S(2)}, u32[]{:S(2)}) collective-permute-start(f32[3,32,256]{2,1,0:T(8,128)} %get-tuple-element.14), channel_id=1, source_target_pairs={{0,18},{1,19},{2,16},{3,17},{16,2},{17,3},{18,0},{19,1},{4,22},{5,... | collective-permute-start | bytes 294920 | tf_op jit(solution)/shard_map/ppermute | solution.py:349
  32.9 0.6 %collective-permute-start.8 = (f32[3,32,256]{2,1,0:T(8,128)}, f32[3,32,256]{2,1,0:T(8,128)S(1)}, u32[]{:S(2)}, u32[]{:S(2)}) collective-permute-start(f32[3,32,256]{2,1,0:T(8,128)} %get-tuple-element.15), channel_id=1, source_target_pairs={{0,19},{1,16},{2,17},{3,18},{16,3},{17,0},{18,1},{19,2},{4,23},{5,... | collective-permute-start | bytes 294920 | tf_op jit(solution)/shard_map/ppermute | solution.py:349
  33.5 0.5 %reshape.39 = f32[25,40,2]{2,1,0:T(8,128)S(1)} reshape(f32[2000]{0:T(1024)S(1)} %collective-permute-done.2) | data formatting | bytes 16000 | tf_op jit(solution)/shard_map/reshape | solution.py:32
  34.0 0.5 %reshape.41 = f32[25,40,2]{2,1,0:T(8,128)S(1)} reshape(f32[2000]{0:T(1024)S(1)} %collective-permute-done.3) | data formatting | bytes 16000 | tf_op jit(solution)/shard_map/reshape | solution.py:32
  34.5 1.5 %pad_maximum_fusion.wide_ref = f32[25,40,384]{2,1,0:T(8,128)} fusion(f32[25,40,2]{2,1,0:T(8,128)S(1)} %reshape.41, f32[25,40,2]{2,1,0:T(8,128)S(1)} %reshape.39, f32[25,2,256]{2,1,0:T(2,128)S(1)} %mul.73, f32[25,4,256]{2,1,0:T(4,128)S(1)} %broadcast_in_dim.17, f32[25,2,256]{2,1,0:T(2,128)S(1)} %mul.70, f32[1,32,256]{2,1,0:T(8,128)S(1)} %convert_select_fusion, ...), kind=kLoop, calls=%fused_computation | loop fusion | flops 2688000 | bytes 2577536 | tf_op jit(solution)/shard_map/concatenate | solution.py:357
  35.9 4.0 %shard_map.105 = f32[1,3,8,32,256]{4,3,2,1,0:T(8,128)} custom-call(f32[1,4,8]{2,1,0:T(4,128)} %coef_ref.1, s32[3]{0:T(128)} %pad_add_fusion.flag_ref.place_ref, f32[25,40,384]{2,1,0:T(8,128)} %pad_maximum_fusion.wide_ref), custom_call_target="tpu_custom_call" | custom-call | tf_op jit(solution)/shard_map/pallas_call | solution.py:103
  40.0 0.7 %multiply_bitcast_fusion = f32[1,3,32,256]{3,2,1,0:T(8,128)} fusion(f32[3,32,256]{2,1,0:T(8,128)S(1)} %collective-permute-done.8, f32[3,32,256]{2,1,0:T(8,128)S(1)} %collective-permute-done.7, f32[3,32,256]{2,1,0:T(8,128)S(1)} %collective-permute-done.5, f32[3,32,256]{2,1,0:T(8,128)S(1)} %collective-permute-done.6, f32[32,256]{1,0:T(8,128)S(1)} %convert_bitcast_fusion), kind=kLoop, calls=%fused_computation.7 | loop fusion | flops 98304 | bytes 524288 | tf_op jit(solution)/shard_map/broadcast_in_dim | solution.py:369
  (33 shorter events, 0.5 us)
Async XLA Ops:
  0.6 9.9 %copy-start.4 = (s32[1,32,256]{2,1,0:T(8,128)S(1)}, s32[1,32,256]{2,1,0:T(8,128)}, u32[]{:S(2)}) copy-start(s32[1,32,256]{2,1,0:T(8,128)} %sea_ref.1) | copy-start | bytes 98308
  0.6 9.9 %copy-start = (f32[1,3,8,32,256]{4,3,2,1,0:T(8,128)S(1)}, f32[1,3,8,32,256]{4,3,2,1,0:T(8,128)}, u32[]{:S(2)}) copy-start(f32[1,3,8,32,256]{4,3,2,1,0:T(8,128)} %tail_ref.1) | copy-start | bytes 2359300
  4.5 6.2 %copy-start.1 = (f32[1,3,32,256]{3,2,1,0:T(8,128)S(1)}, f32[1,3,32,256]{3,2,1,0:T(8,128)}, u32[]{:S(2)}) copy-start(f32[1,3,32,256]{3,2,1,0:T(8,128)} %previous_ref.1) | copy-start | bytes 294916
  4.5 19.3 %collective-permute-start.4 = (f32[104,256]{1,0:T(8,128)}, f32[104,256]{1,0:T(8,128)S(1)}, u32[]{:S(2)}, u32[]{:S(2)}) collective-permute-start(f32[104,256]{1,0:T(8,128)} %get-tuple-element.11.refs_0_), channel_id=1, source_target_pairs={{0,8},{4,12},{8,0},{12,4},{1,9},{5,13},{9,1},{13,5},{2,10},{6,14},... | collective-permute-start | bytes 319496 | tf_op jit(solution)/shard_map/ppermute | solution.py:332
  8.5 7.3 %collective-permute-start = (f32[160,256]{1,0:T(8,128)}, f32[160,256]{1,0:T(8,128)S(1)}, u32[]{:S(2)}, u32[]{:S(2)}) collective-permute-start(f32[160,256]{1,0:T(8,128)} %get-tuple-element.9), channel_id=1, source_target_pairs={{0,12},{4,0},{8,4},{12,8},{1,13},{5,1},{9,5},{13,9},{2,14},{6,2},{... | collective-permute-start | bytes 491528 | tf_op jit(solution)/shard_map/ppermute | solution.py:332
  9.9 10.1 %collective-permute-start.1 = (f32[160,256]{1,0:T(8,128)}, f32[160,256]{1,0:T(8,128)S(1)}, u32[]{:S(2)}, u32[]{:S(2)}) collective-permute-start(f32[160,256]{1,0:T(8,128)} %get-tuple-element.10), channel_id=1, source_target_pairs={{0,4},{4,8},{8,12},{12,0},{1,5},{5,9},{9,13},{13,1},{2,6},{6,10},{... | collective-permute-start | bytes 491528 | tf_op jit(solution)/shard_map/ppermute | solution.py:332
  15.8 4.6 %copy-start.2 = (f32[160,256]{1,0:T(8,128)}, f32[160,256]{1,0:T(8,128)S(1)}, u32[]{:S(2)}) copy-start(f32[160,256]{1,0:T(8,128)S(1)} %collective-permute-done.refs_3_) | copy-start | bytes 491524
  19.9 0.7 %copy-start.3 = (f32[160,256]{1,0:T(8,128)}, f32[160,256]{1,0:T(8,128)S(1)}, u32[]{:S(2)}) copy-start(f32[160,256]{1,0:T(8,128)S(1)} %collective-permute-done.1.refs_1_) | copy-start | bytes 491524
  20.9 12.0 %collective-permute-start.2 = (f32[2000]{0:T(1024)S(1)}, f32[2000]{0:T(1024)S(1)}, u32[]{:S(2)}, u32[]{:S(2)}) collective-permute-start(f32[2000]{0:T(1024)S(1)} %reshape.38), channel_id=1, source_target_pairs={{1,0},{2,1},{3,2},{0,3},{5,4},{6,5},{7,6},{4,7},{9,8},{10,9},{11,1... | collective-permute-start | bytes 24008 | tf_op jit(solution)/shard_map/ppermute | solution.py:31
  23.6 10.4 %collective-permute-start.3 = (f32[2000]{0:T(1024)S(1)}, f32[2000]{0:T(1024)S(1)}, u32[]{:S(2)}, u32[]{:S(2)}) collective-permute-start(f32[2000]{0:T(1024)S(1)} %reshape.40), channel_id=1, source_target_pairs={{0,1},{1,2},{2,3},{3,0},{4,5},{5,6},{6,7},{7,4},{8,9},{9,10},{10,1... | collective-permute-start | bytes 24008 | tf_op jit(solution)/shard_map/ppermute | solution.py:31
  23.8 0.6 %copy-start.5 = (f32[104,256]{1,0:T(8,128)}, f32[104,256]{1,0:T(8,128)S(1)}, u32[]{:S(2)}) copy-start(f32[104,256]{1,0:T(8,128)S(1)} %collective-permute-done.4.refs_2_) | copy-start | bytes 319492
  29.7 10.3 %collective-permute-start.5 = (f32[3,32,256]{2,1,0:T(8,128)}, f32[3,32,256]{2,1,0:T(8,128)S(1)}, u32[]{:S(2)}, u32[]{:S(2)}) collective-permute-start(f32[3,32,256]{2,1,0:T(8,128)} %get-tuple-element.12), channel_id=1, source_target_pairs={{0,16},{1,17},{2,18},{3,19},{16,0},{17,1},{18,2},{19,3},{4,20},{5,... | collective-permute-start | bytes 294920 | tf_op jit(solution)/shard_map/ppermute | solution.py:349
  29.7 10.3 %collective-permute-start.6 = (f32[3,32,256]{2,1,0:T(8,128)}, f32[3,32,256]{2,1,0:T(8,128)S(1)}, u32[]{:S(2)}, u32[]{:S(2)}) collective-permute-start(f32[3,32,256]{2,1,0:T(8,128)} %get-tuple-element.13), channel_id=1, source_target_pairs={{0,17},{1,18},{2,19},{3,16},{16,1},{17,2},{18,3},{19,0},{4,21},{5,... | collective-permute-start | bytes 294920 | tf_op jit(solution)/shard_map/ppermute | solution.py:349
  31.8 8.2 %collective-permute-start.7 = (f32[3,32,256]{2,1,0:T(8,128)}, f32[3,32,256]{2,1,0:T(8,128)S(1)}, u32[]{:S(2)}, u32[]{:S(2)}) collective-permute-start(f32[3,32,256]{2,1,0:T(8,128)} %get-tuple-element.14), channel_id=1, source_target_pairs={{0,18},{1,19},{2,16},{3,17},{16,2},{17,3},{18,0},{19,1},{4,22},{5,... | collective-permute-start | bytes 294920 | tf_op jit(solution)/shard_map/ppermute | solution.py:349
  32.9 7.1 %collective-permute-start.8 = (f32[3,32,256]{2,1,0:T(8,128)}, f32[3,32,256]{2,1,0:T(8,128)S(1)}, u32[]{:S(2)}, u32[]{:S(2)}) collective-permute-start(f32[3,32,256]{2,1,0:T(8,128)} %get-tuple-element.15), channel_id=1, source_target_pairs={{0,19},{1,16},{2,17},{3,18},{16,3},{17,0},{18,1},{19,2},{4,23},{5,... | collective-permute-start | bytes 294920 | tf_op jit(solution)/shard_map/ppermute | solution.py:349

commit v15 on v14

--- a/solution.py
+++ b/solution.py
@@ -198,7 +198,36 @@
     )(flag, state, state, state, surface, sea_mask, links)
 
 
-def remap_kernel(link_count, source_count, place_ref, *refs):
+def own_kernel(payload_ref, table_ref, out_ref):
+    tile_count = table_ref.shape[1]
+    field_count, picks, col_count = out_ref.shape
+    row_count = picks // tile_count
+    base = field_count * row_count
+    for tile in range(tile_count):
+        weighted = jnp.dot(
+            payload_ref[:base, :], table_ref[0, tile], precision=lax.Precision.HIGH,
+            preferred_element_type=jnp.float32,
+        )
+        for c in range(field_count):
+            out_ref[c, tile * row_count : (tile + 1) * row_count, :] = weighted[
+                c * row_count : (c + 1) * row_count
+            ]
+
+
+def own_products(payload, remap_weights, field_count, row_count):
+    tile_count = remap_weights.shape[1]
+    col_count = payload.shape[1]
+    vmem = pl.BlockSpec(memory_space=pltpu.VMEM)
+    return pl.pallas_call(
+        own_kernel,
+        out_shape=jax.ShapeDtypeStruct((field_count, tile_count * row_count, col_count), jnp.float32),
+        in_specs=[vmem, vmem],
+        out_specs=vmem,
+        interpret=INTERPRET,
+    )(payload, remap_weights)
+
+
+def remap_kernel(link_count, source_count, place_ref, own_ref, *refs):
     source_refs = refs[:source_count]
     table_ref = refs[source_count]
     tile_count = table_ref.shape[1]
@@ -209,17 +238,17 @@
     base = field_count * row_count
     my_lat = place_ref[1]
     my_lon = place_ref[2]
-    for source in range(source_count):
-        rows_ref[source * base : (source + 1) * base, :] = source_refs[source][:base, :]
+    for source in range(1, source_count):
+        rows_ref[(source - 1) * base : source * base, :] = source_refs[source][:base, :]
     for tile in range(tile_count):
         weighted = jnp.dot(
             rows_ref[...], table_ref[0, tile], precision=lax.Precision.HIGH, preferred_element_type=jnp.float32
         )
-        for source in range(source_count):
+        for source in range(1, source_count):
             for c in range(field_count):
-                first = (source * tile_count + tile) * row_count
+                first = ((source - 1) * tile_count + tile) * row_count
                 combo_ref[c, first : first + row_count, :] = weighted[
-                    source * base + c * row_count : source * base + (c + 1) * row_count
+                    (source - 1) * base + c * row_count : (source - 1) * base + (c + 1) * row_count
                 ]
     pick_count = source_count * tile_count * row_count
     into = jnp.zeros((owner_count * row_count, pick_count), jnp.float32)
@@ -243,12 +272,19 @@
             to_rows, from_rows, (((1,), (1,)), ((), ())), preferred_element_type=jnp.float32
         )
     for c in range(field_count):
-        summed = jnp.dot(into, combo_ref[c], precision=lax.Precision.HIGH, preferred_element_type=jnp.float32)
+        own_picks = tile_count * row_count
+        summed = jnp.dot(
+            into[:, :own_picks], own_ref[c], precision=lax.Precision.HIGH,
+            preferred_element_type=jnp.float32,
+        ) + jnp.dot(
+            into[:, own_picks:], combo_ref[c], precision=lax.Precision.HIGH,
+            preferred_element_type=jnp.float32,
+        )
         for owner in range(owner_count):
             out_refs[owner][c] = summed[owner * row_count : (owner + 1) * row_count]
 
 
-def remapped(lat, sources, remap_weights, owner_count, field_count, row_count, link_count):
+def remapped(lat, own, sources, remap_weights, owner_count, field_count, row_count, link_count):
     source_count = len(sources)
     col_count = sources[0].shape[1]
     tile_count = remap_weights.shape[1]
@@ -259,16 +295,16 @@
             jax.ShapeDtypeStruct((field_count, row_count, col_count), jnp.float32)
             for owner in range(owner_count)
         ],
-        in_specs=[pl.BlockSpec(memory_space=pltpu.SMEM)] + [vmem] * (source_count + 1),
+        in_specs=[pl.BlockSpec(memory_space=pltpu.SMEM)] + [vmem] * (source_count + 2),
         out_specs=[vmem] * owner_count,
         scratch_shapes=[
-            pltpu.VMEM((source_count * field_count * row_count, col_count), jnp.float32),
+            pltpu.VMEM(((source_count - 1) * field_count * row_count, col_count), jnp.float32),
             pltpu.VMEM(
-                (field_count, source_count * tile_count * row_count, col_count), jnp.float32
+                (field_count, (source_count - 1) * tile_count * row_count, col_count), jnp.float32
             ),
         ],
         interpret=INTERPRET,
-    )(lat, *sources, remap_weights)
+    )(lat, own, *sources, remap_weights)
 
 
 def surface_export(ground, previous, sea_float, ocean_side):
@@ -338,7 +374,8 @@
     my_lat = lax.axis_index("lat")
     south = south.reshape(plane_count, width, col_count) * (my_lat > 0).astype(jnp.float32)
     north = north.reshape(plane_count, width, col_count) * (my_lat < lat_count - 1).astype(jnp.float32)
-    partial = remapped(place, sources, remap_weights, lon_count, field_count, row_count, links.shape[1])
+    own = own_products(payload, remap_weights, field_count, row_count)
+    partial = remapped(place, own, sources, remap_weights, lon_count, field_count, row_count, links.shape[1])
     pieces = []
     for shift in range(lon_count):
         route = [

time: 40.9 us -> 44.1 us (1.078)
  Pallas kernels: 11.3 us -> 14.4 us
    pallas_call x0 -> x1, Pallas kernels: none -> 3.19 us  [own_products(): pl.pallas_call(own_kernel, out_shape=jax.ShapeDtypeStruct((field_count, t...]
  transfers between devices with their start and end apart: 9 -> 9, of which waited for: 2 -> 2; matrix products, arithmetic and copies ran while one was open for 9% -> 8% of each run, Pallas kernels for 23% -> 28%
where the time goes in v15:
time: 44.1 us; the launch traced here: 43.9 us
  Pallas kernels  14.4 us (33%)
  starting transfers between devices  12.5 us (28%)
  waiting for transfers between devices  9 us (20%)
  other arithmetic  4.26 us (10%)
  local copies, waits for them, and re-layouts  2.89 us (7%)
  between operations  0.83 us (2%)
    ppermute x3, waiting for transfers between devices, body(): lax.ppermute(sent, 'lat', [(i, (i + shift) % lat_count) for i in range(la...  8.98 us
    ppermute x3, starting transfers between devices, body(): lax.ppermute(sent, 'lat', [(i, (i + shift) % lat_count) for i in range(la...  6.06 us
    pallas_call x1, Pallas kernels, remapped(): pl.pallas_call(functools.partial(remap_kernel, link_count, source_count),...  5.26 us
    pallas_call x1, Pallas kernels, dynamics(): pl.pallas_call(functools.partial(stencil_kernel, total_rows), out_shape=j...  4.05 us
    ppermute x4, starting transfers between devices, body(): pieces.append(lax.ppermute(partial[shift], ('grp', 'lon'), route))  3.85 us
    pallas_call x1, Pallas kernels, own_products(): pl.pallas_call(own_kernel, out_shape=jax.ShapeDtypeStruct((field_count, t...  3.19 us
    ppermute x2, starting transfers between devices, shifted(): flat = lax.ppermute(part.reshape(-1), axis, route)  2.54 us
    pallas_call x1, Pallas kernels, exported_block(): pl.pallas_call(export_kernel, out_shape=[jax.ShapeDtypeStruct((base, col_...  1.93 us
  transfers between devices with their start and end apart: 9, of which 2 were waited for; matrix products, arithmetic and copies ran while one was open for 8% of the time, Pallas kernels for 28%

profile of v15, /device:TPU:0, one launch (start us, length us, event | category | flops | bytes accessed | tf_op | source)
XLA Modules:
  0.0 43.9 jit_solution(5663740388719158680)
XLA Ops:
  0.7 0.6 %pad_add_fusion.flag_ref.place_ref = s32[3]{0:T(128)} fusion(s32[1]{0:T(128)} %bitcast.2, s32[1]{0:T(128)} %bitcast.1, s32[1]{0:T(128)} %bitcast), kind=kLoop, calls=%fused_computation.13 | loop fusion | flops 6 | bytes 24 | tf_op jit(solution)/shard_map/stack | solution.py:349
  1.3 1.3 %add_convert_fusion.link_ref = f32[4,128]{1,0:T(4,128)} fusion(s32[1,128]{1,0:T(1,128)} %param.17, s32[1,128]{1,0:T(1,128)} %param.16, s32[1,128]{1,0:T(1,128)} %param.15, s32[1,128]{1,0:T(1,128)} %bitcast.22), kind=kLoop, calls=%fused_computation.12 | loop fusion | flops 2048 | bytes 4096 | tf_op jit(solution)/shard_map/convert_element_type | solution.py:348
  2.5 1.9 %shard_map.104 = (f32[104,256]{1,0:T(8,128)}, f32[160,256]{1,0:T(8,128)}, f32[160,256]{1,0:T(8,128)}) custom-call(s32[3]{0:T(128)} %pad_add_fusion.flag_ref.place_ref, f32[1,3,8,32,256]{4,3,2,1,0:T(8,128)} %tail_ref.1, f32[1,3,8,32,256]{4,3,2,1,0:T(8,128)} %tail_ref.1, f32[1,3,8,32,256]{4,3,2,1,0:T(8,128)} %tail_ref.1, f32[1,3,32,256]{3,2,1,0:T(8,128)} %previous_ref.1, ...), custom_call_target="tpu_custom_call" | custom-call | tf_op jit(solution)/shard_map/pallas_call | solution.py:179
  4.5 4.0 %collective-permute-start.4 = (f32[104,256]{1,0:T(8,128)}, f32[104,256]{1,0:T(8,128)S(1)}, u32[]{:S(2)}, u32[]{:S(2)}) collective-permute-start(f32[104,256]{1,0:T(8,128)} %get-tuple-element.11.payload_ref.refs_0_), channel_id=1, source_target_pairs={{0,8},{4,12},{8,0},{12,4},{1,9},{5,13},{9,1},{13,5},{2,10},{6,14},... | collective-permute-start | bytes 319496 | tf_op jit(solution)/shard_map/ppermute | solution.py:368
  8.5 1.3 %collective-permute-start = (f32[160,256]{1,0:T(8,128)}, f32[160,256]{1,0:T(8,128)S(1)}, u32[]{:S(2)}, u32[]{:S(2)}) collective-permute-start(f32[160,256]{1,0:T(8,128)} %get-tuple-element.9), channel_id=1, source_target_pairs={{0,12},{4,0},{8,4},{12,8},{1,13},{5,1},{9,5},{13,9},{2,14},{6,2},{... | collective-permute-start | bytes 491528 | tf_op jit(solution)/shard_map/ppermute | solution.py:368
  9.9 0.7 %collective-permute-start.1 = (f32[160,256]{1,0:T(8,128)}, f32[160,256]{1,0:T(8,128)S(1)}, u32[]{:S(2)}, u32[]{:S(2)}) collective-permute-start(f32[160,256]{1,0:T(8,128)} %get-tuple-element.10), channel_id=1, source_target_pairs={{0,4},{4,8},{8,12},{12,0},{1,5},{5,9},{9,13},{13,1},{2,6},{6,10},{... | collective-permute-start | bytes 491528 | tf_op jit(solution)/shard_map/ppermute | solution.py:368
  10.9 4.9 %collective-permute-done.refs_3_ = f32[160,256]{1,0:T(8,128)S(1)} collective-permute-done((f32[160,256]{1,0:T(8,128)}, f32[160,256]{1,0:T(8,128)S(1)}, u32[]{:S(2)}, u32[]{:S(2)}) %collective-permute-start) | collective-permute-done | bytes 163872 | tf_op jit(solution)/shard_map/ppermute | solution.py:368
  15.8 4.1 %collective-permute-done.1.refs_1_ = f32[160,256]{1,0:T(8,128)S(1)} collective-permute-done((f32[160,256]{1,0:T(8,128)}, f32[160,256]{1,0:T(8,128)S(1)}, u32[]{:S(2)}, u32[]{:S(2)}) %collective-permute-start.1) | collective-permute-done | bytes 163872 | tf_op jit(solution)/shard_map/ppermute | solution.py:368
  20.1 0.2 fusion.2
  20.4 0.3 copy-done.3
  20.6 0.3 reshape.38
  20.9 2.5 %collective-permute-start.2 = (f32[2000]{0:T(1024)S(1)}, f32[2000]{0:T(1024)S(1)}, u32[]{:S(2)}, u32[]{:S(2)}) collective-permute-start(f32[2000]{0:T(1024)S(1)} %reshape.38), channel_id=1, source_target_pairs={{1,0},{2,1},{3,2},{0,3},{5,4},{6,5},{7,6},{4,7},{9,8},{10,9},{11,1... | collective-permute-start | bytes 24008 | tf_op jit(solution)/shard_map/ppermute | solution.py:31
  23.4 0.3 reshape.40
  23.7 3.2 %shard_map.106.own_ref = f32[3,256,256]{2,1,0:T(8,128)} custom-call(f32[104,256]{1,0:T(8,128)} %get-tuple-element.11.payload_ref.refs_0_, f32[1,8,256,256]{3,2,1,0:T(8,128)} %refs_4_.1), custom_call_target="tpu_custom_call" | custom-call | tf_op jit(solution)/shard_map/pallas_call | solution.py:221
  27.0 0.6 %copy-done.5 = f32[104,256]{1,0:T(8,128)} copy-done((f32[104,256]{1,0:T(8,128)}, f32[104,256]{1,0:T(8,128)S(1)}, u32[]{:S(2)}) %copy-start.5) | copy-done | bytes 106520
  27.6 5.3 %shard_map.107 = (f32[3,32,256]{2,1,0:T(8,128)}, f32[3,32,256]{2,1,0:T(8,128)}, f32[3,32,256]{2,1,0:T(8,128)}, f32[3,32,256]{2,1,0:T(8,128)}) custom-call(s32[3]{0:T(128)} %pad_add_fusion.flag_ref.place_ref, f32[3,256,256]{2,1,0:T(8,128)} %shard_map.106.own_ref, f32[104,256]{1,0:T(8,128)} %get-tuple-element.11.payload_ref.refs_0_, f32[160,256]{1,0:T(8,128)} %copy-done.3, ...), custom_call_target="tpu_custom_call" | custom-call | tf_op jit(solution)/shard_map/pallas_call | solution.py:292
  32.9 2.1 %collective-permute-start.6 = (f32[3,32,256]{2,1,0:T(8,128)}, f32[3,32,256]{2,1,0:T(8,128)S(1)}, u32[]{:S(2)}, u32[]{:S(2)}) collective-permute-start(f32[3,32,256]{2,1,0:T(8,128)} %get-tuple-element.13), channel_id=1, source_target_pairs={{0,17},{1,18},{2,19},{3,16},{16,1},{17,2},{18,3},{19,0},{4,21},{5,... | collective-permute-start | bytes 294920 | tf_op jit(solution)/shard_map/ppermute | solution.py:386
  34.9 1.2 %collective-permute-start.7 = (f32[3,32,256]{2,1,0:T(8,128)}, f32[3,32,256]{2,1,0:T(8,128)S(1)}, u32[]{:S(2)}, u32[]{:S(2)}) collective-permute-start(f32[3,32,256]{2,1,0:T(8,128)} %get-tuple-element.14), channel_id=1, source_target_pairs={{0,18},{1,19},{2,16},{3,17},{16,2},{17,3},{18,0},{19,1},{4,22},{5,... | collective-permute-start | bytes 294920 | tf_op jit(solution)/shard_map/ppermute | solution.py:386
  36.1 0.6 %collective-permute-start.8 = (f32[3,32,256]{2,1,0:T(8,128)}, f32[3,32,256]{2,1,0:T(8,128)S(1)}, u32[]{:S(2)}, u32[]{:S(2)}) collective-permute-start(f32[3,32,256]{2,1,0:T(8,128)} %get-tuple-element.15), channel_id=1, source_target_pairs={{0,19},{1,16},{2,17},{3,18},{16,3},{17,0},{18,1},{19,2},{4,23},{5,... | collective-permute-start | bytes 294920 | tf_op jit(solution)/shard_map/ppermute | solution.py:386
  36.7 0.5 %reshape.39 = f32[25,40,2]{2,1,0:T(8,128)S(1)} reshape(f32[2000]{0:T(1024)S(1)} %collective-permute-done.2) | data formatting | bytes 16000 | tf_op jit(solution)/shard_map/reshape | solution.py:32
  37.2 0.5 %reshape.41 = f32[25,40,2]{2,1,0:T(8,128)S(1)} reshape(f32[2000]{0:T(1024)S(1)} %collective-permute-done.3) | data formatting | bytes 16000 | tf_op jit(solution)/shard_map/reshape | solution.py:32
  37.7 1.5 %pad_maximum_fusion.wide_ref = f32[25,40,384]{2,1,0:T(8,128)} fusion(f32[25,40,2]{2,1,0:T(8,128)S(1)} %reshape.41, f32[25,40,2]{2,1,0:T(8,128)S(1)} %reshape.39, f32[25,2,256]{2,1,0:T(2,128)S(1)} %mul.73, f32[25,4,256]{2,1,0:T(4,128)S(1)} %broadcast_in_dim.17, f32[25,2,256]{2,1,0:T(2,128)S(1)} %mul.70, f32[1,32,256]{2,1,0:T(8,128)S(1)} %convert_select_fusion, ...), kind=kLoop, calls=%fused_computation | loop fusion | flops 2688000 | bytes 2577536 | tf_op jit(solution)/shard_map/concatenate | solution.py:394
  39.1 4.0 %shard_map.105 = f32[1,3,8,32,256]{4,3,2,1,0:T(8,128)} custom-call(f32[1,4,8]{2,1,0:T(4,128)} %coef_ref.1, s32[3]{0:T(128)} %pad_add_fusion.flag_ref.place_ref, f32[25,40,384]{2,1,0:T(8,128)} %pad_maximum_fusion.wide_ref), custom_call_target="tpu_custom_call" | custom-call | tf_op jit(solution)/shard_map/pallas_call | solution.py:103
  43.2 0.7 %multiply_bitcast_fusion = f32[1,3,32,256]{3,2,1,0:T(8,128)} fusion(f32[3,32,256]{2,1,0:T(8,128)S(1)} %collective-permute-done.8, f32[3,32,256]{2,1,0:T(8,128)S(1)} %collective-permute-done.7, f32[3,32,256]{2,1,0:T(8,128)S(1)} %collective-permute-done.5, f32[3,32,256]{2,1,0:T(8,128)S(1)} %collective-permute-done.6, f32[32,256]{1,0:T(8,128)S(1)} %convert_bitcast_fusion), kind=kLoop, calls=%fused_computation.7 | loop fusion | flops 98304 | bytes 524288 | tf_op jit(solution)/shard_map/broadcast_in_dim | solution.py:406
  (34 shorter events, 0.7 us)
Async XLA Ops:
  0.6 9.9 %copy-start.4 = (s32[1,32,256]{2,1,0:T(8,128)S(1)}, s32[1,32,256]{2,1,0:T(8,128)}, u32[]{:S(2)}) copy-start(s32[1,32,256]{2,1,0:T(8,128)} %sea_ref.1) | copy-start | bytes 98308
  0.6 9.9 %copy-start = (f32[1,3,8,32,256]{4,3,2,1,0:T(8,128)S(1)}, f32[1,3,8,32,256]{4,3,2,1,0:T(8,128)}, u32[]{:S(2)}) copy-start(f32[1,3,8,32,256]{4,3,2,1,0:T(8,128)} %tail_ref.1) | copy-start | bytes 2359300
  4.5 6.2 %copy-start.1 = (f32[1,3,32,256]{3,2,1,0:T(8,128)S(1)}, f32[1,3,32,256]{3,2,1,0:T(8,128)}, u32[]{:S(2)}) copy-start(f32[1,3,32,256]{3,2,1,0:T(8,128)} %previous_ref.1) | copy-start | bytes 294916
  4.5 22.5 %collective-permute-start.4 = (f32[104,256]{1,0:T(8,128)}, f32[104,256]{1,0:T(8,128)S(1)}, u32[]{:S(2)}, u32[]{:S(2)}) collective-permute-start(f32[104,256]{1,0:T(8,128)} %get-tuple-element.11.payload_ref.refs_0_), channel_id=1, source_target_pairs={{0,8},{4,12},{8,0},{12,4},{1,9},{5,13},{9,1},{13,5},{2,10},{6,14},... | collective-permute-start | bytes 319496 | tf_op jit(solution)/shard_map/ppermute | solution.py:368
  8.5 7.3 %collective-permute-start = (f32[160,256]{1,0:T(8,128)}, f32[160,256]{1,0:T(8,128)S(1)}, u32[]{:S(2)}, u32[]{:S(2)}) collective-permute-start(f32[160,256]{1,0:T(8,128)} %get-tuple-element.9), channel_id=1, source_target_pairs={{0,12},{4,0},{8,4},{12,8},{1,13},{5,1},{9,5},{13,9},{2,14},{6,2},{... | collective-permute-start | bytes 491528 | tf_op jit(solution)/shard_map/ppermute | solution.py:368
  9.9 10.1 %collective-permute-start.1 = (f32[160,256]{1,0:T(8,128)}, f32[160,256]{1,0:T(8,128)S(1)}, u32[]{:S(2)}, u32[]{:S(2)}) collective-permute-start(f32[160,256]{1,0:T(8,128)} %get-tuple-element.10), channel_id=1, source_target_pairs={{0,4},{4,8},{8,12},{12,0},{1,5},{5,9},{9,13},{13,1},{2,6},{6,10},{... | collective-permute-start | bytes 491528 | tf_op jit(solution)/shard_map/ppermute | solution.py:368
  15.8 4.6 %copy-start.2 = (f32[160,256]{1,0:T(8,128)}, f32[160,256]{1,0:T(8,128)S(1)}, u32[]{:S(2)}) copy-start(f32[160,256]{1,0:T(8,128)S(1)} %collective-permute-done.refs_3_) | copy-start | bytes 491524
  19.9 0.7 %copy-start.3 = (f32[160,256]{1,0:T(8,128)}, f32[160,256]{1,0:T(8,128)S(1)}, u32[]{:S(2)}) copy-start(f32[160,256]{1,0:T(8,128)S(1)} %collective-permute-done.1.refs_1_) | copy-start | bytes 491524
  20.9 15.3 %collective-permute-start.2 = (f32[2000]{0:T(1024)S(1)}, f32[2000]{0:T(1024)S(1)}, u32[]{:S(2)}, u32[]{:S(2)}) collective-permute-start(f32[2000]{0:T(1024)S(1)} %reshape.38), channel_id=1, source_target_pairs={{1,0},{2,1},{3,2},{0,3},{5,4},{6,5},{7,6},{4,7},{9,8},{10,9},{11,1... | collective-permute-start | bytes 24008 | tf_op jit(solution)/shard_map/ppermute | solution.py:31
  23.6 13.6 %collective-permute-start.3 = (f32[2000]{0:T(1024)S(1)}, f32[2000]{0:T(1024)S(1)}, u32[]{:S(2)}, u32[]{:S(2)}) collective-permute-start(f32[2000]{0:T(1024)S(1)} %reshape.40), channel_id=1, source_target_pairs={{0,1},{1,2},{2,3},{3,0},{4,5},{5,6},{6,7},{7,4},{8,9},{9,10},{10,1... | collective-permute-start | bytes 24008 | tf_op jit(solution)/shard_map/ppermute | solution.py:31
  27.0 0.6 %copy-start.5 = (f32[104,256]{1,0:T(8,128)}, f32[104,256]{1,0:T(8,128)S(1)}, u32[]{:S(2)}) copy-start(f32[104,256]{1,0:T(8,128)S(1)} %collective-permute-done.4.refs_2_) | copy-start | bytes 319492
  32.9 10.3 %collective-permute-start.5 = (f32[3,32,256]{2,1,0:T(8,128)}, f32[3,32,256]{2,1,0:T(8,128)S(1)}, u32[]{:S(2)}, u32[]{:S(2)}) collective-permute-start(f32[3,32,256]{2,1,0:T(8,128)} %get-tuple-element.12), channel_id=1, source_target_pairs={{0,16},{1,17},{2,18},{3,19},{16,0},{17,1},{18,2},{19,3},{4,20},{5,... | collective-permute-start | bytes 294920 | tf_op jit(solution)/shard_map/ppermute | solution.py:386
  32.9 10.3 %collective-permute-start.6 = (f32[3,32,256]{2,1,0:T(8,128)}, f32[3,32,256]{2,1,0:T(8,128)S(1)}, u32[]{:S(2)}, u32[]{:S(2)}) collective-permute-start(f32[3,32,256]{2,1,0:T(8,128)} %get-tuple-element.13), channel_id=1, source_target_pairs={{0,17},{1,18},{2,19},{3,16},{16,1},{17,2},{18,3},{19,0},{4,21},{5,... | collective-permute-start | bytes 294920 | tf_op jit(solution)/shard_map/ppermute | solution.py:386
  34.9 8.2 %collective-permute-start.7 = (f32[3,32,256]{2,1,0:T(8,128)}, f32[3,32,256]{2,1,0:T(8,128)S(1)}, u32[]{:S(2)}, u32[]{:S(2)}) collective-permute-start(f32[3,32,256]{2,1,0:T(8,128)} %get-tuple-element.14), channel_id=1, source_target_pairs={{0,18},{1,19},{2,16},{3,17},{16,2},{17,3},{18,0},{19,1},{4,22},{5,... | collective-permute-start | bytes 294920 | tf_op jit(solution)/shard_map/ppermute | solution.py:386
  36.1 7.1 %collective-permute-start.8 = (f32[3,32,256]{2,1,0:T(8,128)}, f32[3,32,256]{2,1,0:T(8,128)S(1)}, u32[]{:S(2)}, u32[]{:S(2)}) collective-permute-start(f32[3,32,256]{2,1,0:T(8,128)} %get-tuple-element.15), channel_id=1, source_target_pairs={{0,19},{1,16},{2,17},{3,18},{16,3},{17,0},{18,1},{19,2},{4,23},{5,... | collective-permute-start | bytes 294920 | tf_op jit(solution)/shard_map/ppermute | solution.py:386

commit v16 on v14

--- a/solution.py
+++ b/solution.py
@@ -115,11 +115,18 @@
 
 
 def export_kernel(
-    flag_ref, ground_ref, head_ref, tail_ref, previous_ref, sea_ref, link_ref, mid_ref, up_ref, down_ref
+    flag_ref, ground_ref, head_ref, tail_ref, previous_ref, sea_ref, dest_ref, src_ref, dst_ref,
+    tile_ref, mid_ref, up_ref, down_ref
 ):
     field_count, row_count, col_count = previous_ref.shape[1:]
     level_count = head_ref.shape[2]
-    link_fields, link_count = link_ref.shape
+    link_count = src_ref.shape[1]
+    dest_col = dest_ref[0].astype(jnp.float32)
+    dest_row = jnp.transpose(jnp.broadcast_to(dest_col, (link_count, link_count)))[0:1, :]
+    link_rows = jnp.concatenate(
+        [dest_row] + [ref[...].astype(jnp.float32) for ref in (src_ref, dst_ref, tile_ref)], 0
+    )
+    link_fields = link_rows.shape[0]
     ground = ground_ref[0, :, 0]
     previous = previous_ref[0]
     sea_float = sea_ref[0].astype(jnp.float32)
@@ -139,7 +146,7 @@
                 ground[c] * ocean + bulk_flux[c] * (1.0 - ocean)
             ) * sea_float
         out_ref[base : base + 8, :] = jnp.zeros((8, col_count), jnp.float32)
-        out_ref[base : base + link_fields, :link_count] = link_ref[...]
+        out_ref[base : base + link_fields, :link_count] = link_rows
     gain = air_gain + (ocean_gain - air_gain) * ocean
     damping = air_gain * (1.0 - ocean)
     width = SUBSTEPS
@@ -170,6 +177,7 @@
 
 
 def exported_block(flag, state, surface, sea_mask, links, edge_rows):
+    link_dest, link_src_row, link_dst_row, link_tile = links
     field_count, row_count, col_count = surface.shape[1:]
     level_count = state.shape[2]
     vmem = pl.BlockSpec(memory_space=pltpu.VMEM)
@@ -191,11 +199,14 @@
             vmem,
             vmem,
             vmem,
+            vmem,
+            vmem,
+            vmem,
         ],
         out_specs=[vmem, vmem, vmem],
         grid=(1,),
         interpret=INTERPRET,
-    )(flag, state, state, state, surface, sea_mask, links)
+    )(flag, state, state, state, surface, sea_mask, link_dest, link_src_row, link_dst_row, link_tile)
 
 
 def remap_kernel(link_count, source_count, place_ref, *refs):
@@ -307,9 +318,7 @@
     first_row = lax.axis_index("lat") * row_count
     total_rows = row_count * lax.axis_size("lat")
 
-    links = jnp.stack(
-        [link_dest[0, :, 0], link_src_row[0], link_dst_row[0], link_tile[0]]
-    ).astype(jnp.float32)
+    links = (link_dest, link_src_row, link_dst_row, link_tile)
     place = jnp.stack([lax.axis_index(axis) for axis in ("grp", "lat", "lon")]).astype(jnp.int32)
     lat_count = lax.axis_size("lat")
     lon_count = lax.axis_size("lon")
@@ -338,7 +347,7 @@
     my_lat = lax.axis_index("lat")
     south = south.reshape(plane_count, width, col_count) * (my_lat > 0).astype(jnp.float32)
     north = north.reshape(plane_count, width, col_count) * (my_lat < lat_count - 1).astype(jnp.float32)
-    partial = remapped(place, sources, remap_weights, lon_count, field_count, row_count, links.shape[1])
+    partial = remapped(place, sources, remap_weights, lon_count, field_count, row_count, link_src_row.shape[1])
     pieces = []
     for shift in range(lon_count):
         route = [

time: 40.9 us -> 41.2 us (level)
  local copies, waits for them, and re-layouts: 2.88 us -> 4.35 us
  other arithmetic: 4.26 us -> 2.97 us
    unnamed x13 -> x14, local copies, waits for them, and re-layouts: 0.98 us -> 2.44 us
    convert_element_type x1 -> x0, other arithmetic: 1.29 us -> none  [body(): links = jnp.stack([link_dest[0, :, 0], link_src_row[0], link_dst_row[0],...]
where the time goes in v16:
time: 41.2 us; the launch traced here: 41 us
  starting transfers between devices  12.4 us (30%)
  Pallas kernels  11.4 us (28%)
  waiting for transfers between devices  9 us (22%)
  local copies, waits for them, and re-layouts  4.35 us (11%)
  other arithmetic  2.97 us (7%)
  between operations  0.84 us (2%)
    ppermute x3, waiting for transfers between devices, body(): lax.ppermute(sent, 'lat', [(i, (i + shift) % lat_count) for i in range(la...  8.98 us
    ppermute x3, starting transfers between devices, body(): lax.ppermute(sent, 'lat', [(i, (i + shift) % lat_count) for i in range(la...  6.06 us
    pallas_call x1, Pallas kernels, remapped(): pl.pallas_call(functools.partial(remap_kernel, link_count, source_count),...  5.28 us
    pallas_call x1, Pallas kernels, dynamics(): pl.pallas_call(functools.partial(stencil_kernel, total_rows), out_shape=j...  4.05 us
    ppermute x4, starting transfers between devices, body(): pieces.append(lax.ppermute(partial[shift], ('grp', 'lon'), route))  3.84 us
    ppermute x2, starting transfers between devices, shifted(): flat = lax.ppermute(part.reshape(-1), axis, route)  2.54 us
    unnamed x14, local copies, waits for them, and re-layouts  2.44 us
    pallas_call x1, Pallas kernels, exported_block(): pl.pallas_call(export_kernel, out_shape=[jax.ShapeDtypeStruct((base, col_...  2.08 us
  transfers between devices with their start and end apart: 9, of which 2 were waited for; matrix products, arithmetic and copies ran while one was open for 9% of the time, Pallas kernels for 23%

profile of v16, /device:TPU:0, one launch (start us, length us, event | category | flops | bytes accessed | tf_op | source)
XLA Modules:
  0.0 41.0 jit_solution(12253497476659659130)
XLA Ops:
  0.7 1.5 %copy.16.dest_ref = s32[1,128,1]{2,1,0:T(8,128)} copy(s32[1,128,1]{1,2,0:T(1,128)} %param.14) | data formatting | bytes 1024 | tf_op args[5]
  2.1 0.6 %pad_add_fusion.flag_ref.place_ref = s32[3]{0:T(128)} fusion(s32[1]{0:T(128)} %bitcast.2, s32[1]{0:T(128)} %bitcast.1, s32[1]{0:T(128)} %bitcast), kind=kLoop, calls=%fused_computation.12 | loop fusion | flops 6 | bytes 24 | tf_op jit(solution)/shard_map/stack | solution.py:322
  2.7 2.1 %shard_map.104 = (f32[104,256]{1,0:T(8,128)}, f32[160,256]{1,0:T(8,128)}, f32[160,256]{1,0:T(8,128)}) custom-call(s32[3]{0:T(128)} %pad_add_fusion.flag_ref.place_ref, f32[1,3,8,32,256]{4,3,2,1,0:T(8,128)} %tail_ref.1, f32[1,3,8,32,256]{4,3,2,1,0:T(8,128)} %tail_ref.1, f32[1,3,8,32,256]{4,3,2,1,0:T(8,128)} %tail_ref.1, f32[1,3,32,256]{3,2,1,0:T(8,128)} %previous_ref.1, ...), custom_call_target="tpu_custom_call" | custom-call | tf_op jit(solution)/shard_map/pallas_call | solution.py:187
  4.8 4.0 %collective-permute-start.4 = (f32[104,256]{1,0:T(8,128)}, f32[104,256]{1,0:T(8,128)S(1)}, u32[]{:S(2)}, u32[]{:S(2)}) collective-permute-start(f32[104,256]{1,0:T(8,128)} %get-tuple-element.11.refs_0_), channel_id=1, source_target_pairs={{0,8},{4,12},{8,0},{12,4},{1,9},{5,13},{9,1},{13,5},{2,10},{6,14},... | collective-permute-start | bytes 319496 | tf_op jit(solution)/shard_map/ppermute | solution.py:341
  8.8 1.3 %collective-permute-start = (f32[160,256]{1,0:T(8,128)}, f32[160,256]{1,0:T(8,128)S(1)}, u32[]{:S(2)}, u32[]{:S(2)}) collective-permute-start(f32[160,256]{1,0:T(8,128)} %get-tuple-element.9), channel_id=1, source_target_pairs={{0,12},{4,0},{8,4},{12,8},{1,13},{5,1},{9,5},{13,9},{2,14},{6,2},{... | collective-permute-start | bytes 491528 | tf_op jit(solution)/shard_map/ppermute | solution.py:341
  10.2 0.7 %collective-permute-start.1 = (f32[160,256]{1,0:T(8,128)}, f32[160,256]{1,0:T(8,128)S(1)}, u32[]{:S(2)}, u32[]{:S(2)}) collective-permute-start(f32[160,256]{1,0:T(8,128)} %get-tuple-element.10), channel_id=1, source_target_pairs={{0,4},{4,8},{8,12},{12,0},{1,5},{5,9},{9,13},{13,1},{2,6},{6,10},{... | collective-permute-start | bytes 491528 | tf_op jit(solution)/shard_map/ppermute | solution.py:341
  11.2 4.9 %collective-permute-done.refs_3_ = f32[160,256]{1,0:T(8,128)S(1)} collective-permute-done((f32[160,256]{1,0:T(8,128)}, f32[160,256]{1,0:T(8,128)S(1)}, u32[]{:S(2)}, u32[]{:S(2)}) %collective-permute-start) | collective-permute-done | bytes 163872 | tf_op jit(solution)/shard_map/ppermute | solution.py:341
  16.1 4.1 %collective-permute-done.1.refs_1_ = f32[160,256]{1,0:T(8,128)S(1)} collective-permute-done((f32[160,256]{1,0:T(8,128)}, f32[160,256]{1,0:T(8,128)S(1)}, u32[]{:S(2)}, u32[]{:S(2)}) %collective-permute-start.1) | collective-permute-done | bytes 163872 | tf_op jit(solution)/shard_map/ppermute | solution.py:341
  20.3 0.1 pad_maximum_fusion.1
  20.5 0.2 fusion.2
  20.7 0.3 copy-done.3
  20.9 0.3 reshape.38
  21.2 2.5 %collective-permute-start.2 = (f32[2000]{0:T(1024)S(1)}, f32[2000]{0:T(1024)S(1)}, u32[]{:S(2)}, u32[]{:S(2)}) collective-permute-start(f32[2000]{0:T(1024)S(1)} %reshape.38), channel_id=1, source_target_pairs={{1,0},{2,1},{3,2},{0,3},{5,4},{6,5},{7,6},{4,7},{9,8},{10,9},{11,1... | collective-permute-start | bytes 24008 | tf_op jit(solution)/shard_map/ppermute | solution.py:31
  23.7 0.3 reshape.40
  24.1 0.6 %copy-done.5 = f32[104,256]{1,0:T(8,128)} copy-done((f32[104,256]{1,0:T(8,128)}, f32[104,256]{1,0:T(8,128)S(1)}, u32[]{:S(2)}) %copy-start.5) | copy-done | bytes 106520
  24.7 5.3 %shard_map.106 = (f32[3,32,256]{2,1,0:T(8,128)}, f32[3,32,256]{2,1,0:T(8,128)}, f32[3,32,256]{2,1,0:T(8,128)}, f32[3,32,256]{2,1,0:T(8,128)}) custom-call(s32[3]{0:T(128)} %pad_add_fusion.flag_ref.place_ref, f32[104,256]{1,0:T(8,128)} %get-tuple-element.11.refs_0_, f32[160,256]{1,0:T(8,128)} %copy-done.3, f32[104,256]{1,0:T(8,128)} %copy-done.5, ...), custom_call_target="tpu_custom_call" | custom-call | tf_op jit(solution)/shard_map/pallas_call | solution.py:267
  30.0 2.1 %collective-permute-start.6 = (f32[3,32,256]{2,1,0:T(8,128)}, f32[3,32,256]{2,1,0:T(8,128)S(1)}, u32[]{:S(2)}, u32[]{:S(2)}) collective-permute-start(f32[3,32,256]{2,1,0:T(8,128)} %get-tuple-element.13), channel_id=1, source_target_pairs={{0,17},{1,18},{2,19},{3,16},{16,1},{17,2},{18,3},{19,0},{4,21},{5,... | collective-permute-start | bytes 294920 | tf_op jit(solution)/shard_map/ppermute | solution.py:358
  32.1 1.1 %collective-permute-start.7 = (f32[3,32,256]{2,1,0:T(8,128)}, f32[3,32,256]{2,1,0:T(8,128)S(1)}, u32[]{:S(2)}, u32[]{:S(2)}) collective-permute-start(f32[3,32,256]{2,1,0:T(8,128)} %get-tuple-element.14), channel_id=1, source_target_pairs={{0,18},{1,19},{2,16},{3,17},{16,2},{17,3},{18,0},{19,1},{4,22},{5,... | collective-permute-start | bytes 294920 | tf_op jit(solution)/shard_map/ppermute | solution.py:358
  33.2 0.6 %collective-permute-start.8 = (f32[3,32,256]{2,1,0:T(8,128)}, f32[3,32,256]{2,1,0:T(8,128)S(1)}, u32[]{:S(2)}, u32[]{:S(2)}) collective-permute-start(f32[3,32,256]{2,1,0:T(8,128)} %get-tuple-element.15), channel_id=1, source_target_pairs={{0,19},{1,16},{2,17},{3,18},{16,3},{17,0},{18,1},{19,2},{4,23},{5,... | collective-permute-start | bytes 294920 | tf_op jit(solution)/shard_map/ppermute | solution.py:358
  33.9 0.5 %reshape.39 = f32[25,40,2]{2,1,0:T(8,128)S(1)} reshape(f32[2000]{0:T(1024)S(1)} %collective-permute-done.2) | data formatting | bytes 16000 | tf_op jit(solution)/shard_map/reshape | solution.py:32
  34.3 0.5 %reshape.41 = f32[25,40,2]{2,1,0:T(8,128)S(1)} reshape(f32[2000]{0:T(1024)S(1)} %collective-permute-done.3) | data formatting | bytes 16000 | tf_op jit(solution)/shard_map/reshape | solution.py:32
  34.8 1.5 %pad_maximum_fusion.wide_ref = f32[25,40,384]{2,1,0:T(8,128)} fusion(f32[25,40,2]{2,1,0:T(8,128)S(1)} %reshape.41, f32[25,40,2]{2,1,0:T(8,128)S(1)} %reshape.39, f32[25,2,256]{2,1,0:T(2,128)S(1)} %mul.73, f32[25,4,256]{2,1,0:T(4,128)S(1)} %broadcast_in_dim.17, f32[25,2,256]{2,1,0:T(2,128)S(1)} %mul.70, f32[1,32,256]{2,1,0:T(8,128)S(1)} %convert_select_fusion, ...), kind=kLoop, calls=%fused_computation | loop fusion | flops 2688000 | bytes 2577536 | tf_op jit(solution)/shard_map/concatenate | solution.py:366
  36.3 4.0 %shard_map.105 = f32[1,3,8,32,256]{4,3,2,1,0:T(8,128)} custom-call(f32[1,4,8]{2,1,0:T(4,128)} %coef_ref.1, s32[3]{0:T(128)} %pad_add_fusion.flag_ref.place_ref, f32[25,40,384]{2,1,0:T(8,128)} %pad_maximum_fusion.wide_ref), custom_call_target="tpu_custom_call" | custom-call | tf_op jit(solution)/shard_map/pallas_call | solution.py:103
  40.3 0.7 %multiply_bitcast_fusion = f32[1,3,32,256]{3,2,1,0:T(8,128)} fusion(f32[3,32,256]{2,1,0:T(8,128)S(1)} %collective-permute-done.8, f32[3,32,256]{2,1,0:T(8,128)S(1)} %collective-permute-done.7, f32[3,32,256]{2,1,0:T(8,128)S(1)} %collective-permute-done.5, f32[3,32,256]{2,1,0:T(8,128)S(1)} %collective-permute-done.6, f32[32,256]{1,0:T(8,128)S(1)} %convert_bitcast_fusion), kind=kLoop, calls=%fused_computation.7 | loop fusion | flops 98304 | bytes 524288 | tf_op jit(solution)/shard_map/broadcast_in_dim | solution.py:378
  (33 shorter events, 0.5 us)
Async XLA Ops:
  0.6 10.2 %copy-start.4 = (s32[1,32,256]{2,1,0:T(8,128)S(1)}, s32[1,32,256]{2,1,0:T(8,128)}, u32[]{:S(2)}) copy-start(s32[1,32,256]{2,1,0:T(8,128)} %sea_ref.1) | copy-start | bytes 98308
  0.6 10.2 %copy-start = (f32[1,3,8,32,256]{4,3,2,1,0:T(8,128)S(1)}, f32[1,3,8,32,256]{4,3,2,1,0:T(8,128)}, u32[]{:S(2)}) copy-start(f32[1,3,8,32,256]{4,3,2,1,0:T(8,128)} %tail_ref.1) | copy-start | bytes 2359300
  4.8 6.2 %copy-start.1 = (f32[1,3,32,256]{3,2,1,0:T(8,128)S(1)}, f32[1,3,32,256]{3,2,1,0:T(8,128)}, u32[]{:S(2)}) copy-start(f32[1,3,32,256]{3,2,1,0:T(8,128)} %previous_ref.1) | copy-start | bytes 294916
  4.8 19.3 %collective-permute-start.4 = (f32[104,256]{1,0:T(8,128)}, f32[104,256]{1,0:T(8,128)S(1)}, u32[]{:S(2)}, u32[]{:S(2)}) collective-permute-start(f32[104,256]{1,0:T(8,128)} %get-tuple-element.11.refs_0_), channel_id=1, source_target_pairs={{0,8},{4,12},{8,0},{12,4},{1,9},{5,13},{9,1},{13,5},{2,10},{6,14},... | collective-permute-start | bytes 319496 | tf_op jit(solution)/shard_map/ppermute | solution.py:341
  8.8 7.3 %collective-permute-start = (f32[160,256]{1,0:T(8,128)}, f32[160,256]{1,0:T(8,128)S(1)}, u32[]{:S(2)}, u32[]{:S(2)}) collective-permute-start(f32[160,256]{1,0:T(8,128)} %get-tuple-element.9), channel_id=1, source_target_pairs={{0,12},{4,0},{8,4},{12,8},{1,13},{5,1},{9,5},{13,9},{2,14},{6,2},{... | collective-permute-start | bytes 491528 | tf_op jit(solution)/shard_map/ppermute | solution.py:341
  10.2 10.1 %collective-permute-start.1 = (f32[160,256]{1,0:T(8,128)}, f32[160,256]{1,0:T(8,128)S(1)}, u32[]{:S(2)}, u32[]{:S(2)}) collective-permute-start(f32[160,256]{1,0:T(8,128)} %get-tuple-element.10), channel_id=1, source_target_pairs={{0,4},{4,8},{8,12},{12,0},{1,5},{5,9},{9,13},{13,1},{2,6},{6,10},{... | collective-permute-start | bytes 491528 | tf_op jit(solution)/shard_map/ppermute | solution.py:341
  16.1 4.6 %copy-start.2 = (f32[160,256]{1,0:T(8,128)}, f32[160,256]{1,0:T(8,128)S(1)}, u32[]{:S(2)}) copy-start(f32[160,256]{1,0:T(8,128)S(1)} %collective-permute-done.refs_3_) | copy-start | bytes 491524
  20.3 0.7 %copy-start.3 = (f32[160,256]{1,0:T(8,128)}, f32[160,256]{1,0:T(8,128)S(1)}, u32[]{:S(2)}) copy-start(f32[160,256]{1,0:T(8,128)S(1)} %collective-permute-done.1.refs_1_) | copy-start | bytes 491524
  21.2 12.0 %collective-permute-start.2 = (f32[2000]{0:T(1024)S(1)}, f32[2000]{0:T(1024)S(1)}, u32[]{:S(2)}, u32[]{:S(2)}) collective-permute-start(f32[2000]{0:T(1024)S(1)} %reshape.38), channel_id=1, source_target_pairs={{1,0},{2,1},{3,2},{0,3},{5,4},{6,5},{7,6},{4,7},{9,8},{10,9},{11,1... | collective-permute-start | bytes 24008 | tf_op jit(solution)/shard_map/ppermute | solution.py:31
  23.9 10.4 %collective-permute-start.3 = (f32[2000]{0:T(1024)S(1)}, f32[2000]{0:T(1024)S(1)}, u32[]{:S(2)}, u32[]{:S(2)}) collective-permute-start(f32[2000]{0:T(1024)S(1)} %reshape.40), channel_id=1, source_target_pairs={{0,1},{1,2},{2,3},{3,0},{4,5},{5,6},{6,7},{7,4},{8,9},{9,10},{10,1... | collective-permute-start | bytes 24008 | tf_op jit(solution)/shard_map/ppermute | solution.py:31
  24.1 0.6 %copy-start.5 = (f32[104,256]{1,0:T(8,128)}, f32[104,256]{1,0:T(8,128)S(1)}, u32[]{:S(2)}) copy-start(f32[104,256]{1,0:T(8,128)S(1)} %collective-permute-done.4.refs_2_) | copy-start | bytes 319492
  30.0 10.3 %collective-permute-start.5 = (f32[3,32,256]{2,1,0:T(8,128)}, f32[3,32,256]{2,1,0:T(8,128)S(1)}, u32[]{:S(2)}, u32[]{:S(2)}) collective-permute-start(f32[3,32,256]{2,1,0:T(8,128)} %get-tuple-element.12), channel_id=1, source_target_pairs={{0,16},{1,17},{2,18},{3,19},{16,0},{17,1},{18,2},{19,3},{4,20},{5,... | collective-permute-start | bytes 294920 | tf_op jit(solution)/shard_map/ppermute | solution.py:358
  30.0 10.3 %collective-permute-start.6 = (f32[3,32,256]{2,1,0:T(8,128)}, f32[3,32,256]{2,1,0:T(8,128)S(1)}, u32[]{:S(2)}, u32[]{:S(2)}) collective-permute-start(f32[3,32,256]{2,1,0:T(8,128)} %get-tuple-element.13), channel_id=1, source_target_pairs={{0,17},{1,18},{2,19},{3,16},{16,1},{17,2},{18,3},{19,0},{4,21},{5,... | collective-permute-start | bytes 294920 | tf_op jit(solution)/shard_map/ppermute | solution.py:358
  32.1 8.2 %collective-permute-start.7 = (f32[3,32,256]{2,1,0:T(8,128)}, f32[3,32,256]{2,1,0:T(8,128)S(1)}, u32[]{:S(2)}, u32[]{:S(2)}) collective-permute-start(f32[3,32,256]{2,1,0:T(8,128)} %get-tuple-element.14), channel_id=1, source_target_pairs={{0,18},{1,19},{2,16},{3,17},{16,2},{17,3},{18,0},{19,1},{4,22},{5,... | collective-permute-start | bytes 294920 | tf_op jit(solution)/shard_map/ppermute | solution.py:358
  33.2 7.1 %collective-permute-start.8 = (f32[3,32,256]{2,1,0:T(8,128)}, f32[3,32,256]{2,1,0:T(8,128)S(1)}, u32[]{:S(2)}, u32[]{:S(2)}) collective-permute-start(f32[3,32,256]{2,1,0:T(8,128)} %get-tuple-element.15), channel_id=1, source_target_pairs={{0,19},{1,16},{2,17},{3,18},{16,3},{17,0},{18,1},{19,2},{4,23},{5,... | collective-permute-start | bytes 294920 | tf_op jit(solution)/shard_map/ppermute | solution.py:358
